TPU v7x, 32 devices: a whole 2x2x4 slice. The times are simulated.
32 devices in a mesh: groups: 2 (over x), gz: 16 (over z, y, core).
Axes of the slice: x: 2, y: 2, z: 4, core: 2. Of those that a mesh axis runs over, the one named last changes fastest.
Arguments:
- waves: bfloat16 [192, 8, 64, 256], P(('groups', 'gz')), parts along dimension 0, may hold values from -6 to 6
- potential: float32 [192, 512], P(('groups', 'gz')), parts along dimension 0, may hold values from 0.25 to 4
- domain_of: int32 [32], P('groups'), parts along dimension 0, may hold values from 0 to 7, never falling along the last dimension, each value on 1 to 9 neighbouring positions
Outputs:
- orbitals: bfloat16 [192, 8, 64, 256], P(('groups', 'gz')), parts along dimension 0
There are 2 independent parts, one for each index of `groups`. A program takes and returns all parts, laid end to end along the dimension named above; each array names one. Nothing has to cross between parts.
Inputs may be any that keep to these rules, and one draw needn't show every extreme that they name: `domain_of`: never falls; every domain holds 1 to 9 blocks, one domain exactly that many.
All inputs are finite; a program needn't handle non-finite values.
Results may differ from a plain program's by a relative error of at most 0.0038.
The roundings to bfloat16 on the way count: a program that leaves them out, or rounds other values in their place, can miss the bound.
Values may be sent and summed in bfloat16 or wider, within the bound.
No kernel may reach another device: no remote copies, remote signals or barrier semaphores. Data moves between devices by JAX's collectives and lax.ppermute only.
A program may use at most 64 MiB of HBM per device.

v0:
```python
import jax
import jax.numpy as jnp
from jax import lax
from jax.sharding import PartitionSpec as P

PANEL = 128
NX = 64
NY = 8
DOMS = 8
DEGREE = 4


COEF = (-49.0 / 18.0, 1.5, -0.15, 1.0 / 90.0)
CSHIFT = 7.0
EWIDTH = 5.0


def extended_2(block, sides, width):
    for axis, dim in sides:
        count = lax.axis_size(axis)
        forward = [(i, i + 1) for i in range(count - 1)]
        backward = [(target, source) for source, target in forward]
        low = lax.ppermute(
            lax.slice_in_dim(block, block.shape[dim] - width, None, axis=dim), axis, forward
        )
        high = lax.ppermute(lax.slice_in_dim(block, 0, width, axis=dim), axis, backward)
        block = jnp.concatenate([low, block, high], axis=dim)
    return block


def hamiltonian(extended, potential):
    inner = extended[3:-3]
    planes = inner.shape[0]
    rows_y = inner.shape[1]
    rows_x = inner.shape[2]
    padded_y = jnp.pad(inner, ((0, 0), (3, 3), (0, 0), (0, 0)))
    padded_x = jnp.pad(inner, ((0, 0), (0, 0), (3, 3), (0, 0)))
    total = 3.0 * COEF[0] * inner
    for distance in (1, 2, 3):
        along_z = (
            extended[3 + distance : 3 + distance + planes]
            + extended[3 - distance : 3 - distance + planes]
        )
        along_y = (
            padded_y[:, 3 + distance : 3 + distance + rows_y]
            + padded_y[:, 3 - distance : 3 - distance + rows_y]
        )
        along_x = (
            padded_x[:, :, 3 + distance : 3 + distance + rows_x]
            + padded_x[:, :, 3 - distance : 3 - distance + rows_x]
        )
        total = total + COEF[distance] * (along_z + along_y + along_x)
    return potential[:, :, :, None] * inner - 0.5 * total


def shards(waves, potential, domain_of):
    slabs = lax.axis_size("gz")
    position = lax.axis_index("gz")
    planes = waves.shape[0]
    bands = waves.shape[3]
    grid = potential.reshape(planes, NY, NX)
    owner = domain_of[position]
    below = jnp.where(position > 0, domain_of[jnp.maximum(position - 1, 0)] == owner, False).astype(
        jnp.float32
    )
    above = jnp.where(
        position < slabs - 1, domain_of[jnp.minimum(position + 1, slabs - 1)] == owner, False
    ).astype(jnp.float32)
    mask_three = jnp.concatenate(
        [
            jnp.broadcast_to(below, (3,)),
            jnp.ones((planes,), jnp.float32),
            jnp.broadcast_to(above, (3,)),
        ]
    )[:, None, None, None]

    def rimmed(field):
        return extended_2(field, (("gz", 0),), 3).astype(jnp.float32) * mask_three

    extended = rimmed(waves)
    image = hamiltonian(extended, grid)
    older = waves
    current = ((image - CSHIFT * extended[3:-3]) / EWIDTH).astype(jnp.bfloat16)
    for turn in range(DEGREE - 1):
        extended = rimmed(current)
        image = hamiltonian(extended, grid)
        newer = (
            2.0 / EWIDTH * (image - CSHIFT * extended[3:-3]) - older.astype(jnp.float32)
        ).astype(jnp.bfloat16)
        older, current = (current, newer)
    cells = jnp.sum((domain_of == owner).astype(jnp.float32)) * (planes * NY * NX)
    rows = current.reshape(planes * NY * NX, bands)

    def domain_total(term):
        picker = (jnp.arange(DOMS) == owner).astype(jnp.float32)
        summed = lax.psum(picker[:, None, None] * term[None], "gz")
        return jnp.sum(picker[:, None, None] * summed, axis=0)

    identity = jnp.eye(PANEL, dtype=jnp.float32)
    pieces = []
    for panel in range(bands // PANEL):
        block = rows[:, panel * PANEL : (panel + 1) * PANEL]
        if panel > 0:
            earlier = pieces[0]
            correlation = (
                domain_total(
                    jnp.einsum("ca,cb->ab", earlier, block, preferred_element_type=jnp.float32)
                )
                / cells
            )
            block = (
                block.astype(jnp.float32)
                - jnp.dot(
                    earlier, correlation.astype(jnp.bfloat16), preferred_element_type=jnp.float32
                )
            ).astype(jnp.bfloat16)
        gram = (
            domain_total(jnp.einsum("ca,cb->ab", block, block, preferred_element_type=jnp.float32))
            / cells
        )
        factor = jnp.linalg.cholesky(gram)
        inverse = jax.scipy.linalg.solve_triangular(factor, identity, lower=True)
        whitening = inverse.T.astype(jnp.bfloat16)
        pieces.append(
            jnp.dot(block, whitening, preferred_element_type=jnp.float32).astype(jnp.bfloat16)
        )
    return jnp.concatenate(pieces, axis=1).reshape(planes, NY, NX, bands)


def solution(mesh):
    return jax.shard_map(
        shards,
        mesh=mesh,
        in_specs=(P(("groups", "gz"), None, None, None), P(("groups", "gz"), None), P("groups")),
        out_specs=P(("groups", "gz"), None, None, None),
        check_vma=False,
    )
```

profile of v0, /device:TPU:0, one launch (start us, length us, event | category | flops | bytes accessed | tf_op | source)
XLA Modules:
  0.0 492.9 jit_solution(13511593628192767567)
XLA Ops:
  6.5 2.8 fusion.114
  9.3 2.4 collective-permute-start
  11.8 1.3 collective-permute-start.1
  13.1 0.7 fusion.115
  16.2 2.0 collective-permute-done.1
  18.3 0.7 convert_multiply_fusion.3
  19.0 0.2 slice.356
  19.2 6.6 %fusion.11 = bf16[6,8,64,256]{3,2,1,0:T(8,128)(2,1)S(1)} fusion(f32[6,8,64,256]{3,2,1,0:T(8,128)S(1)} %slice.356, f32[12,8,64,256]{3,2,1,0:T(8,128)S(1)} %convert_multiply_fusion.3, f32[6,8,64]{2,1,0:T(8,128)S(1)} %mul.191), kind=kLoop, calls=%fused_computation.66 | loop fusion | flops 22806528 | bytes 23605248 | tf_op jit(solution)/shard_map/convert_element_type | solution.py:83
  25.8 0.2 fusion.113
  26.0 15.7 %collective-permute-start.2 = (bf16[3,8,64,256]{3,2,1,0:T(8,128)(2,1)S(1)}, bf16[3,8,64,256]{3,2,1,0:T(8,128)(2,1)S(1)}, u32[]{:S(2)}, u32[]{:S(2)}) collective-permute-start(bf16[3,8,64,256]{3,2,1,0:T(8,128)(2,1)S(1)} %get-tuple-element.11), channel_id=1, source_target_pairs={{0,1},{1,2},{2,3},{3,4},{4,5},{5,6},{6,7},{7,8},{8,9},{9,10},{10,1... | collective-permute-start | bytes 2359304 | tf_op jit(solution)/shard_map/ppermute | solution.py:23
  41.7 1.3 collective-permute-start.3
  43.0 0.5 collective-permute-done.2
  43.5 4.2 collective-permute-done.3
  47.7 0.7 convert_multiply_fusion.2
  48.5 2.0 slice.365
  50.5 18.8 %fusion.95 = bf16[6,8,64,256]{3,2,1,0:T(8,128)(2,1)S(1)} fusion(bf16[6,8,64,256]{3,2,1,0:T(8,128)(2,1)S(1)} %copy-done, f32[6,8,64,256]{3,2,1,0:T(8,128)} %slice.365, f32[12,8,64,256]{3,2,1,0:T(8,128)S(1)} %convert_multiply_fusion.2, f32[6,8,64]{2,1,0:T(8,128)S(1)} %mul.191), kind=kLoop, calls=%fused_computation.162 | loop fusion | flops 24379392 | bytes 25178112 | tf_op jit(solution)/shard_map/convert_element_type | solution.py:89
  69.3 0.2 fusion.112
  69.5 15.6 %collective-permute-start.4 = (bf16[3,8,64,256]{3,2,1,0:T(8,128)(2,1)S(1)}, bf16[3,8,64,256]{3,2,1,0:T(8,128)(2,1)S(1)}, u32[]{:S(2)}, u32[]{:S(2)}) collective-permute-start(bf16[3,8,64,256]{3,2,1,0:T(8,128)(2,1)S(1)} %get-tuple-element.9), channel_id=1, source_target_pairs={{0,1},{1,2},{2,3},{3,4},{4,5},{5,6},{6,7},{7,8},{8,9},{9,10},{10,1... | collective-permute-start | bytes 2359304 | tf_op jit(solution)/shard_map/ppermute | solution.py:23
  85.1 1.3 collective-permute-start.5
  86.4 0.5 collective-permute-done.4
  87.0 4.3 collective-permute-done.5
  91.2 0.7 convert_multiply_fusion.1
  92.0 2.0 slice.374
  94.0 18.8 %fusion.94 = bf16[6,8,64,256]{3,2,1,0:T(8,128)(2,1)S(1)} fusion(bf16[6,8,64,256]{3,2,1,0:T(8,128)(2,1)S(1)} %fusion.11, f32[6,8,64,256]{3,2,1,0:T(8,128)} %slice.374, f32[12,8,64,256]{3,2,1,0:T(8,128)S(1)} %convert_multiply_fusion.1, f32[6,8,64]{2,1,0:T(8,128)S(1)} %mul.191), kind=kLoop, calls=%fused_computation.161 | loop fusion | flops 24379392 | bytes 25178112 | tf_op jit(solution)/shard_map/convert_element_type | solution.py:89
  112.9 0.2 fusion.111
  113.0 15.6 %collective-permute-start.6 = (bf16[3,8,64,256]{3,2,1,0:T(8,128)(2,1)S(1)}, bf16[3,8,64,256]{3,2,1,0:T(8,128)(2,1)S(1)}, u32[]{:S(2)}, u32[]{:S(2)}) collective-permute-start(bf16[3,8,64,256]{3,2,1,0:T(8,128)(2,1)S(1)} %get-tuple-element.6), channel_id=1, source_target_pairs={{0,1},{1,2},{2,3},{3,4},{4,5},{5,6},{6,7},{7,8},{8,9},{9,10},{10,1... | collective-permute-start | bytes 2359304 | tf_op jit(solution)/shard_map/ppermute | solution.py:23
  128.7 1.3 collective-permute-start.7
  130.0 0.5 compare_convert_fusion.1
  130.5 4.3 collective-permute-done.7
  134.8 0.7 convert_multiply_fusion
  135.5 0.3 slice.383
  135.9 6.8 %fusion.93 = bf16[6,8,64,256]{3,2,1,0:T(8,128)(2,1)S(1)} fusion(bf16[6,8,64,256]{3,2,1,0:T(8,128)(2,1)S(1)} %fusion.95, f32[6,8,64,256]{3,2,1,0:T(8,128)S(1)} %slice.383, f32[12,8,64,256]{3,2,1,0:T(8,128)S(1)} %convert_multiply_fusion, f32[6,8,64]{2,1,0:T(8,128)S(1)} %mul.191), kind=kLoop, calls=%fused_computation.160 | loop fusion | flops 24379392 | bytes 25178112 | tf_op jit(solution)/shard_map/convert_element_type | solution.py:89
  142.6 0.4 fusion.99
  143.0 0.9 broadcast_multiply_fusion.2
  144.0 0.2 all-reduce.14.cloned.1.call-start
  144.2 1.2 fusion.110
  146.1 101.4 %all-reduce.12.cloned.1.call-done = f32[8,128,128]{2,1,0:T(8,128)} async-done(((f32[8,128,128]{2,1,0:T(8,128)}), f32[8,128,128]{2,1,0:T(8,128)}) %all-reduce.12.cloned.1.call-update) | async-done | bytes 524304 | tf_op jit(solution)/shard_map/psum | solution.py:96
  247.5 1.1 multiply_reduce_fusion.2
  248.7 0.1 copy.10
  248.8 0.1 copy.11
  248.9 11.7 %cholesky.44 = f32[128,128]{1,0:T(8,128)S(1)} custom-call(f32[128,128]{1,0:T(8,128)S(1)} %fusion.108), custom_call_target="Cholesky" | custom-call | tf_op jit(solution)/shard_map/jit(cholesky)/cholesky | solution.py:121
  260.6 0.6 compare_reduce_fusion.1
  261.3 0.7 fusion.103
  262.0 9.8 %custom-call.6 = f32[1,128,128]{1,2,0:T(8,128)S(1)} custom-call(f32[1,128,128]{2,1,0:T(8,128)S(1)} %fusion.103), custom_call_target="InvertDiagBlocksLowerTriangular" | custom-call | tf_op jit(solution)/shard_map/jit(_solve_triangular)/triangular_solve | solution.py:122
  271.8 0.3 convolution_convert_fusion.3
  272.1 0.4 convolution_convert_fusion.1
  272.4 0.4 fusion.96
  272.8 0.9 broadcast_multiply_fusion.1
  273.7 0.3 all-reduce.16.cloned.1.call-start
  274.0 91.0 %all-reduce.14.cloned.1.call-done = f32[8,128,128]{2,1,0:T(8,128)} async-done(((f32[8,128,128]{2,1,0:T(8,128)}), f32[8,128,128]{2,1,0:T(8,128)}) %all-reduce.14.cloned.1.call-update) | async-done | bytes 524304 | tf_op jit(solution)/shard_map/psum | solution.py:96
  365.0 1.1 multiply_reduce_fusion.1
  366.3 0.4 fusion
  366.7 0.4 fusion.116
  367.1 0.9 broadcast_multiply_fusion
  368.0 91.8 %all-reduce.16.cloned.1.call-done = f32[8,128,128]{2,1,0:T(8,128)} async-done(((f32[8,128,128]{2,1,0:T(8,128)}), f32[8,128,128]{2,1,0:T(8,128)}) %all-reduce.16.cloned.1.call-update) | async-done | bytes 524304 | tf_op jit(solution)/shard_map/psum | solution.py:96
  459.8 1.1 multiply_reduce_fusion
  461.2 11.7 %cholesky.55 = f32[128,128]{1,0:T(8,128)S(1)} custom-call(f32[128,128]{1,0:T(8,128)S(1)} %fusion.106), custom_call_target="Cholesky" | custom-call | tf_op jit(solution)/shard_map/jit(cholesky)/cholesky | solution.py:121
  472.9 0.6 compare_reduce_fusion
  473.6 0.7 fusion.104
  474.2 9.8 %custom-call.7 = f32[1,128,128]{1,2,0:T(8,128)S(1)} custom-call(f32[1,128,128]{2,1,0:T(8,128)S(1)} %fusion.104), custom_call_target="InvertDiagBlocksLowerTriangular" | custom-call | tf_op jit(solution)/shard_map/jit(_solve_triangular)/triangular_solve | solution.py:122
  484.1 0.3 convolution_convert_fusion.2
  484.3 0.4 convolution_convert_fusion
  484.7 0.1 pad_maximum_fusion
  484.8 1.6 copy.15
  (26 shorter events, 0.6 us)
Async XLA Ops:
  6.5 11.7 %copy-start = (bf16[6,8,64,256]{3,2,1,0:T(8,128)(2,1)S(1)}, bf16[6,8,64,256]{3,2,1,0:T(8,128)(2,1)}, u32[]{:S(2)}) copy-start(bf16[6,8,64,256]{3,2,1,0:T(8,128)(2,1)} %param.6) | copy-start | bytes 4718596
  6.5 6.6 %copy-start.2 = (s32[16]{0:T(128)S(1)}, s32[16]{0:T(128)}, u32[]{:S(2)}) copy-start(s32[16]{0:T(128)} %param.8) | copy-start | bytes 196
  6.5 9.5 %copy-start.1 = (f32[6,512]{1,0:T(8,128)S(1)}, f32[6,512]{1,0:T(8,128)}, u32[]{:S(2)}) copy-start(f32[6,512]{1,0:T(8,128)} %param.7) | copy-start | bytes 36868
  6.5 241.0 %all-reduce.12.cloned.1.call-start = ((), (), s32[]{:S(2)}) async-start(), calls=%async_computation | async-start | bytes 1048576 | tf_op jit(solution)/shard_map/psum | solution.py:96
  9.3 6.9 %collective-permute-start = (bf16[3,8,64,256]{3,2,1,0:T(8,128)(2,1)}, bf16[3,8,64,256]{3,2,1,0:T(8,128)(2,1)S(1)}, u32[]{:S(2)}, u32[]{:S(2)}) collective-permute-start(bf16[3,8,64,256]{3,2,1,0:T(8,128)(2,1)} %get-tuple-element.13), channel_id=1, source_target_pairs={{0,1},{1,2},{2,3},{3,4},{4,5},{5,6},{6,7},{7,8},{8,9},{9,10},{10,1... | collective-permute-start | bytes 2359304 | tf_op jit(solution)/shard_map/ppermute | solution.py:23
  11.8 6.5 %collective-permute-start.1 = (bf16[3,8,64,256]{3,2,1,0:T(8,128)(2,1)}, bf16[3,8,64,256]{3,2,1,0:T(8,128)(2,1)S(1)}, u32[]{:S(2)}, u32[]{:S(2)}) collective-permute-start(bf16[3,8,64,256]{3,2,1,0:T(8,128)(2,1)} %get-tuple-element.14), channel_id=1, source_target_pairs={{1,0},{2,1},{3,2},{4,3},{5,4},{6,5},{7,6},{8,7},{9,8},{10,9},{11,1... | collective-permute-start | bytes 2359304 | tf_op jit(solution)/shard_map/ppermute | solution.py:26
  26.0 17.6 %collective-permute-start.2 = (bf16[3,8,64,256]{3,2,1,0:T(8,128)(2,1)S(1)}, bf16[3,8,64,256]{3,2,1,0:T(8,128)(2,1)S(1)}, u32[]{:S(2)}, u32[]{:S(2)}) collective-permute-start(bf16[3,8,64,256]{3,2,1,0:T(8,128)(2,1)S(1)} %get-tuple-element.11), channel_id=1, source_target_pairs={{0,1},{1,2},{2,3},{3,4},{4,5},{5,6},{6,7},{7,8},{8,9},{9,10},{10,1... | collective-permute-start | bytes 2359304 | tf_op jit(solution)/shard_map/ppermute | solution.py:23
  41.7 6.0 %collective-permute-start.3 = (bf16[3,8,64,256]{3,2,1,0:T(8,128)(2,1)S(1)}, bf16[3,8,64,256]{3,2,1,0:T(8,128)(2,1)S(1)}, u32[]{:S(2)}, u32[]{:S(2)}) collective-permute-start(bf16[3,8,64,256]{3,2,1,0:T(8,128)(2,1)S(1)} %get-tuple-element.12), channel_id=1, source_target_pairs={{1,0},{2,1},{3,2},{4,3},{5,4},{6,5},{7,6},{8,7},{9,8},{10,9},{11,1... | collective-permute-start | bytes 2359304 | tf_op jit(solution)/shard_map/ppermute | solution.py:26
  69.5 17.5 %collective-permute-start.4 = (bf16[3,8,64,256]{3,2,1,0:T(8,128)(2,1)S(1)}, bf16[3,8,64,256]{3,2,1,0:T(8,128)(2,1)S(1)}, u32[]{:S(2)}, u32[]{:S(2)}) collective-permute-start(bf16[3,8,64,256]{3,2,1,0:T(8,128)(2,1)S(1)} %get-tuple-element.9), channel_id=1, source_target_pairs={{0,1},{1,2},{2,3},{3,4},{4,5},{5,6},{6,7},{7,8},{8,9},{9,10},{10,1... | collective-permute-start | bytes 2359304 | tf_op jit(solution)/shard_map/ppermute | solution.py:23
  85.1 6.1 %collective-permute-start.5 = (bf16[3,8,64,256]{3,2,1,0:T(8,128)(2,1)S(1)}, bf16[3,8,64,256]{3,2,1,0:T(8,128)(2,1)S(1)}, u32[]{:S(2)}, u32[]{:S(2)}) collective-permute-start(bf16[3,8,64,256]{3,2,1,0:T(8,128)(2,1)S(1)} %get-tuple-element.10), channel_id=1, source_target_pairs={{1,0},{2,1},{3,2},{4,3},{5,4},{6,5},{7,6},{8,7},{9,8},{10,9},{11,1... | collective-permute-start | bytes 2359304 | tf_op jit(solution)/shard_map/ppermute | solution.py:26
  113.0 17.5 %collective-permute-start.6 = (bf16[3,8,64,256]{3,2,1,0:T(8,128)(2,1)S(1)}, bf16[3,8,64,256]{3,2,1,0:T(8,128)(2,1)S(1)}, u32[]{:S(2)}, u32[]{:S(2)}) collective-permute-start(bf16[3,8,64,256]{3,2,1,0:T(8,128)(2,1)S(1)} %get-tuple-element.6), channel_id=1, source_target_pairs={{0,1},{1,2},{2,3},{3,4},{4,5},{5,6},{6,7},{7,8},{8,9},{9,10},{10,1... | collective-permute-start | bytes 2359304 | tf_op jit(solution)/shard_map/ppermute | solution.py:23
  128.7 6.1 %collective-permute-start.7 = (bf16[3,8,64,256]{3,2,1,0:T(8,128)(2,1)S(1)}, bf16[3,8,64,256]{3,2,1,0:T(8,128)(2,1)S(1)}, u32[]{:S(2)}, u32[]{:S(2)}) collective-permute-start(bf16[3,8,64,256]{3,2,1,0:T(8,128)(2,1)S(1)} %get-tuple-element.8), channel_id=1, source_target_pairs={{1,0},{2,1},{3,2},{4,3},{5,4},{6,5},{7,6},{8,7},{9,8},{10,9},{11,1... | collective-permute-start | bytes 2359304 | tf_op jit(solution)/shard_map/ppermute | solution.py:26
  144.0 221.1 %all-reduce.14.cloned.1.call-start = ((), (), s32[]{:S(2)}) async-start(), calls=%async_computation.1 | async-start | bytes 1048576 | tf_op jit(solution)/shard_map/psum | solution.py:96
  273.7 186.1 %all-reduce.16.cloned.1.call-start = ((), (), s32[]{:S(2)}) async-start(), calls=%async_computation.2 | async-start | bytes 1048576 | tf_op jit(solution)/shard_map/psum | solution.py:96
Sparse Core Ops, SparseCore 0:
  144.1 103.3 all-reduce.11
  273.8 91.1 all-reduce.13
  368.4 91.3 all-reduce.15
where the time goes:
time: 493 us
  waiting for transfers between devices  300 us (61%)
  other arithmetic  108 us (22%)
  starting transfers between devices  55 us (11%)
  between operations  16.5 us (3%)
  local copies, waits for them, and re-layouts  10.7 us (2%)
    psum x3, waiting for transfers between devices, domain_total(): summed = lax.psum(picker[:, None, None] * term[None], 'gz')  284 us
    ppermute x4, starting transfers between devices, extended_2(): lax.ppermute(lax.slice_in_dim(block, block.shape[dim] - width, None, axis...  49.4 us
    convert_element_type x3, other arithmetic, shards(): newer = (2.0 / EWIDTH * (image - CSHIFT * extended[3:-3]) - older.astype(...  44.4 us
    another operation x6, other arithmetic, shards(): factor = jnp.linalg.cholesky(gram)  24.8 us
    another operation x4, other arithmetic, shards(): inverse = jax.scipy.linalg.solve_triangular(factor, identity, lower=True)  20.9 us
    ppermute x4, waiting for transfers between devices, extended_2(): lax.ppermute(lax.slice_in_dim(block, 0, width, axis=dim), axis, backward)  14.7 us
  transfers between devices with their start and end apart: 11, of which 9 were waited for; matrix products, arithmetic and copies ran while one was open for 1% of the time, Pallas kernels for 0%

commit v1 on v0

--- a/solution.py
+++ b/solution.py
@@ -92,35 +92,73 @@
     rows = current.reshape(planes * NY * NX, bands)
 
     def domain_total(term):
-        picker = (jnp.arange(DOMS) == owner).astype(jnp.float32)
-        summed = lax.psum(picker[:, None, None] * term[None], "gz")
-        return jnp.sum(picker[:, None, None] * summed, axis=0)
+        forward = term
+        backward = term
+        distance = 1
+        while distance < slabs:
+            ahead = [(i, i + distance) for i in range(slabs - distance)]
+            behind = [(i + distance, i) for i in range(slabs - distance)]
+            from_low = lax.ppermute(forward, "gz", ahead)
+            from_high = lax.ppermute(backward, "gz", behind)
+            low_same = jnp.where(
+                position >= distance,
+                domain_of[jnp.maximum(position - distance, 0)] == owner,
+                False,
+            ).astype(jnp.float32)
+            high_same = jnp.where(
+                position + distance < slabs,
+                domain_of[jnp.minimum(position + distance, slabs - 1)] == owner,
+                False,
+            ).astype(jnp.float32)
+            forward = forward + low_same * from_low
+            backward = backward + high_same * from_high
+            distance *= 2
+        return forward + backward - term
 
     identity = jnp.eye(PANEL, dtype=jnp.float32)
+    panels = bands // PANEL
+    blocks = [rows[:, p * PANEL : (p + 1) * PANEL] for p in range(panels)]
+    first = blocks[0]
+    cross = jnp.einsum("ca,cb->ab", first, rows, preferred_element_type=jnp.float32)
+    cross = domain_total(cross) / cells
     pieces = []
-    for panel in range(bands // PANEL):
-        block = rows[:, panel * PANEL : (panel + 1) * PANEL]
-        if panel > 0:
-            earlier = pieces[0]
-            correlation = (
-                domain_total(
-                    jnp.einsum("ca,cb->ab", earlier, block, preferred_element_type=jnp.float32)
+    whitenings = []
+    for panel in range(panels):
+        block = blocks[panel]
+        if panel == 0:
+            gram = cross[:, :PANEL]
+        else:
+            if panel == 1:
+                correlation = jnp.dot(
+                    whitenings[0].T.astype(jnp.float32),
+                    cross[:, PANEL : 2 * PANEL],
+                    preferred_element_type=jnp.float32,
                 )
-                / cells
-            )
+            else:
+                earlier = jnp.concatenate(pieces, axis=1)
+                correlation = (
+                    domain_total(
+                        jnp.einsum("ca,cb->ab", earlier, block, preferred_element_type=jnp.float32)
+                    )
+                    / cells
+                )
+            earlier = jnp.concatenate(pieces, axis=1)
             block = (
                 block.astype(jnp.float32)
                 - jnp.dot(
                     earlier, correlation.astype(jnp.bfloat16), preferred_element_type=jnp.float32
                 )
             ).astype(jnp.bfloat16)
-        gram = (
-            domain_total(jnp.einsum("ca,cb->ab", block, block, preferred_element_type=jnp.float32))
-            / cells
-        )
+            gram = (
+                domain_total(
+                    jnp.einsum("ca,cb->ab", block, block, preferred_element_type=jnp.float32)
+                )
+                / cells
+            )
         factor = jnp.linalg.cholesky(gram)
         inverse = jax.scipy.linalg.solve_triangular(factor, identity, lower=True)
         whitening = inverse.T.astype(jnp.bfloat16)
+        whitenings.append(whitening)
         pieces.append(
             jnp.dot(block, whitening, preferred_element_type=jnp.float32).astype(jnp.bfloat16)
         )

time: 493 us -> 274 us (0.56)
  waiting for transfers between devices: 300 us -> 31.7 us
  starting transfers between devices: 55 us -> 115 us
  other arithmetic: 108 us -> 101 us
  between operations: 16.5 us -> 10.7 us
    psum x3 -> x0, waiting for transfers between devices: 284 us -> none  [domain_total(): summed = lax.psum(picker[:, None, None] * term[None], 'gz')]
    ppermute x0 -> x16, starting transfers between devices: none -> 60.9 us  [the longest x8 50.3 us: domain_total(): from_low = lax.ppermute(forward, 'gz', ahead)]
    ppermute x0 -> x16, waiting for transfers between devices: none -> 15.5 us  [the longest x8 11 us: domain_total(): from_high = lax.ppermute(backward, 'gz', behind)]
  transfers between devices with their start and end apart: 11 -> 24, of which waited for: 9 -> 17; matrix products, arithmetic and copies ran while one was open for 1% -> 1% of each run, Pallas kernels for 0% -> 0%
where the time goes in v1:
time: 274 us; the launch traced here: 273 us
  starting transfers between devices  115 us (42%)
  other arithmetic  101 us (37%)
  waiting for transfers between devices  31.7 us (12%)
  between operations  10.7 us (4%)
  local copies, waits for them, and re-layouts  10.4 us (4%)
  matrix products  2.97 us (1%)
    ppermute x8, starting transfers between devices, domain_total(): from_low = lax.ppermute(forward, 'gz', ahead)  50.3 us
    ppermute x4, starting transfers between devices, extended_2(): lax.ppermute(lax.slice_in_dim(block, block.shape[dim] - width, None, axis...  49.4 us
    convert_element_type x3, other arithmetic, shards(): newer = (2.0 / EWIDTH * (image - CSHIFT * extended[3:-3]) - older.astype(...  44.7 us
    another operation x6, other arithmetic, shards(): factor = jnp.linalg.cholesky(gram)  24.8 us
    another operation x4, other arithmetic, shards(): inverse = jax.scipy.linalg.solve_triangular(factor, identity, lower=True)  20.9 us
    ppermute x4, waiting for transfers between devices, extended_2(): lax.ppermute(lax.slice_in_dim(block, 0, width, axis=dim), axis, backward)  14.6 us
    ppermute x8, waiting for transfers between devices, domain_total(): from_high = lax.ppermute(backward, 'gz', behind)  11 us
    ppermute x8, starting transfers between devices, domain_total(): from_high = lax.ppermute(backward, 'gz', behind)  10.6 us
  transfers between devices with their start and end apart: 24, of which 17 were waited for; matrix products, arithmetic and copies ran while one was open for 1% of the time, Pallas kernels for 0%

profile of v1, /device:TPU:0, one launch (start us, length us, event | category | flops | bytes accessed | tf_op | source)
XLA Modules:
  0.0 272.7 jit_solution(5794593283005720244)
XLA Ops:
  0.0 2.8 %fusion.113 = (bf16[3,8,64,256]{3,2,1,0:T(8,128)(2,1)}, bf16[3,8,64,256]{3,2,1,0:T(8,128)(2,1)}) fusion(bf16[6,8,64,256]{3,2,1,0:T(8,128)(2,1)} %param.6), kind=kLoop, calls=%fused_computation.209 | loop fusion | bytes 3145728 | tf_op jit(solution)/shard_map/slice | solution.py:24
  2.8 2.4 collective-permute-start
  5.3 1.3 collective-permute-start.1
  6.6 0.7 fusion.114
  9.9 1.9 collective-permute-done.1
  11.7 0.7 convert_multiply_fusion.3
  12.7 6.6 %fusion.11 = bf16[6,8,64,256]{3,2,1,0:T(8,128)(2,1)S(1)} fusion(f32[6,8,64,256]{3,2,1,0:T(8,128)S(1)} %slice.364, f32[12,8,64,256]{3,2,1,0:T(8,128)S(1)} %convert_multiply_fusion.3, f32[6,8,64]{2,1,0:T(8,128)S(1)} %mul.234), kind=kLoop, calls=%fused_computation.66 | loop fusion | flops 22806528 | bytes 23605248 | tf_op jit(solution)/shard_map/convert_element_type | solution.py:83
  19.5 15.7 %collective-permute-start.2 = (bf16[3,8,64,256]{3,2,1,0:T(8,128)(2,1)S(1)}, bf16[3,8,64,256]{3,2,1,0:T(8,128)(2,1)S(1)}, u32[]{:S(2)}, u32[]{:S(2)}) collective-permute-start(bf16[3,8,64,256]{3,2,1,0:T(8,128)(2,1)S(1)} %get-tuple-element.11), channel_id=1, source_target_pairs={{0,1},{1,2},{2,3},{3,4},{4,5},{5,6},{6,7},{7,8},{8,9},{9,10},{10,1... | collective-permute-start | bytes 2359304 | tf_op jit(solution)/shard_map/ppermute | solution.py:23
  35.2 1.3 collective-permute-start.3
  36.5 0.5 collective-permute-done.2
  37.0 4.2 %collective-permute-done.3 = bf16[3,8,64,256]{3,2,1,0:T(8,128)(2,1)S(1)} collective-permute-done((bf16[3,8,64,256]{3,2,1,0:T(8,128)(2,1)S(1)}, bf16[3,8,64,256]{3,2,1,0:T(8,128)(2,1)S(1)}, u32[]{:S(2)}, u32[]{:S(2)}) %collective-permute-start.3) | collective-permute-done | bytes 786464 | tf_op jit(solution)/shard_map/ppermute | solution.py:26
  41.2 0.7 convert_multiply_fusion.2
  41.9 2.0 slice.373
  43.9 19.0 %fusion.95 = bf16[6,8,64,256]{3,2,1,0:T(8,128)(2,1)S(1)} fusion(bf16[6,8,64,256]{3,2,1,0:T(8,128)(2,1)S(1)} %copy-done, f32[6,8,64,256]{3,2,1,0:T(8,128)} %slice.373, f32[12,8,64,256]{3,2,1,0:T(8,128)S(1)} %convert_multiply_fusion.2, f32[6,8,64]{2,1,0:T(8,128)S(1)} %mul.234), kind=kLoop, calls=%fused_computation.162 | loop fusion | flops 24379392 | bytes 25178112 | tf_op jit(solution)/shard_map/convert_element_type | solution.py:89
  63.1 15.6 %collective-permute-start.4 = (bf16[3,8,64,256]{3,2,1,0:T(8,128)(2,1)S(1)}, bf16[3,8,64,256]{3,2,1,0:T(8,128)(2,1)S(1)}, u32[]{:S(2)}, u32[]{:S(2)}) collective-permute-start(bf16[3,8,64,256]{3,2,1,0:T(8,128)(2,1)S(1)} %get-tuple-element.9), channel_id=1, source_target_pairs={{0,1},{1,2},{2,3},{3,4},{4,5},{5,6},{6,7},{7,8},{8,9},{9,10},{10,1... | collective-permute-start | bytes 2359304 | tf_op jit(solution)/shard_map/ppermute | solution.py:23
  78.7 1.3 collective-permute-start.5
  80.0 0.5 collective-permute-done.4
  80.6 4.3 %collective-permute-done.5 = bf16[3,8,64,256]{3,2,1,0:T(8,128)(2,1)S(1)} collective-permute-done((bf16[3,8,64,256]{3,2,1,0:T(8,128)(2,1)S(1)}, bf16[3,8,64,256]{3,2,1,0:T(8,128)(2,1)S(1)}, u32[]{:S(2)}, u32[]{:S(2)}) %collective-permute-start.5) | collective-permute-done | bytes 786464 | tf_op jit(solution)/shard_map/ppermute | solution.py:26
  84.8 0.7 convert_multiply_fusion.1
  85.6 2.0 slice.382
  87.6 19.0 %fusion.94 = bf16[6,8,64,256]{3,2,1,0:T(8,128)(2,1)S(1)} fusion(bf16[6,8,64,256]{3,2,1,0:T(8,128)(2,1)S(1)} %fusion.11, f32[6,8,64,256]{3,2,1,0:T(8,128)} %slice.382, f32[12,8,64,256]{3,2,1,0:T(8,128)S(1)} %convert_multiply_fusion.1, f32[6,8,64]{2,1,0:T(8,128)S(1)} %mul.234), kind=kLoop, calls=%fused_computation.161 | loop fusion | flops 24379392 | bytes 25178112 | tf_op jit(solution)/shard_map/convert_element_type | solution.py:89
  106.7 15.6 %collective-permute-start.6 = (bf16[3,8,64,256]{3,2,1,0:T(8,128)(2,1)S(1)}, bf16[3,8,64,256]{3,2,1,0:T(8,128)(2,1)S(1)}, u32[]{:S(2)}, u32[]{:S(2)}) collective-permute-start(bf16[3,8,64,256]{3,2,1,0:T(8,128)(2,1)S(1)} %get-tuple-element.6), channel_id=1, source_target_pairs={{0,1},{1,2},{2,3},{3,4},{4,5},{5,6},{6,7},{7,8},{8,9},{9,10},{10,1... | collective-permute-start | bytes 2359304 | tf_op jit(solution)/shard_map/ppermute | solution.py:23
  122.3 1.3 collective-permute-start.7
  123.6 0.5 collective-permute-done.6
  124.2 4.3 %collective-permute-done.7 = bf16[3,8,64,256]{3,2,1,0:T(8,128)(2,1)S(1)} collective-permute-done((bf16[3,8,64,256]{3,2,1,0:T(8,128)(2,1)S(1)}, bf16[3,8,64,256]{3,2,1,0:T(8,128)(2,1)S(1)}, u32[]{:S(2)}, u32[]{:S(2)}) %collective-permute-start.7) | collective-permute-done | bytes 786464 | tf_op jit(solution)/shard_map/ppermute | solution.py:26
  128.5 0.7 convert_multiply_fusion
  129.5 6.8 %fusion.93 = bf16[6,8,64,256]{3,2,1,0:T(8,128)(2,1)S(1)} fusion(bf16[6,8,64,256]{3,2,1,0:T(8,128)(2,1)S(1)} %fusion.95, f32[6,8,64,256]{3,2,1,0:T(8,128)S(1)} %slice.391, f32[12,8,64,256]{3,2,1,0:T(8,128)S(1)} %convert_multiply_fusion, f32[6,8,64]{2,1,0:T(8,128)S(1)} %mul.234), kind=kLoop, calls=%fused_computation.160 | loop fusion | flops 24379392 | bytes 25178112 | tf_op jit(solution)/shard_map/convert_element_type | solution.py:89
  136.3 0.7 fusion.97
  137.0 1.3 collective-permute-start.12
  138.3 16.2 %collective-permute-start.8 = (f32[128,256]{0,1:T(8,128)S(1)}, f32[128,256]{0,1:T(8,128)S(1)}, u32[]{:S(2)}, u32[]{:S(2)}) collective-permute-start(f32[128,256]{0,1:T(8,128)S(1)} %fusion.97), channel_id=1, source_target_pairs={{0,1},{1,2},{2,3},{3,4},{4,5},{5,6},{6,7},{7,8},{8,9},{9,10},{10,1... | collective-permute-start | bytes 393224 | tf_op jit(solution)/shard_map/ppermute | solution.py:101
  154.6 0.9 collective-permute-done.8
  155.5 7.7 %collective-permute-start.9 = (f32[128,256]{0,1:T(8,128)S(1)}, f32[128,256]{0,1:T(8,128)S(1)}, u32[]{:S(2)}, u32[]{:S(2)}) collective-permute-start(f32[128,256]{0,1:T(8,128)S(1)} %get-tuple-element.15), channel_id=1, source_target_pairs={{0,2},{1,3},{2,4},{3,5},{4,6},{5,7},{6,8},{7,9},{8,10},{9,11},{10,... | collective-permute-start | bytes 393224 | tf_op jit(solution)/shard_map/ppermute | solution.py:101
  168.0 1.3 collective-permute-start.13
  169.4 5.5 %collective-permute-start.10 = (f32[128,256]{0,1:T(8,128)S(1)}, f32[128,256]{0,1:T(8,128)S(1)}, u32[]{:S(2)}, u32[]{:S(2)}) collective-permute-start(f32[128,256]{0,1:T(8,128)S(1)} %multiply_add_fusion.4), channel_id=1, source_target_pairs={{0,4},{1,5},{2,6},{3,7},{4,8},{5,9},{6,10},{7,11},{8,12},{9,13},{1... | collective-permute-start | bytes 393224 | tf_op jit(solution)/shard_map/ppermute | solution.py:101
  174.9 1.3 collective-permute-start.14
  176.2 0.9 collective-permute-done.10
  177.2 3.8 %collective-permute-start.11 = (f32[128,256]{0,1:T(8,128)S(1)}, f32[128,256]{0,1:T(8,128)S(1)}, u32[]{:S(2)}, u32[]{:S(2)}) collective-permute-start(f32[128,256]{0,1:T(8,128)S(1)} %multiply_add_fusion.3), channel_id=1, source_target_pairs={{0,8},{1,9},{2,10},{3,11},{4,12},{5,13},{6,14},{7,15},{16,24},{17,... | collective-permute-start | bytes 393224 | tf_op jit(solution)/shard_map/ppermute | solution.py:101
  181.0 0.8 collective-permute-done.14
  181.8 1.3 collective-permute-start.15
  185.4 1.2 fusion.109
  187.2 3.5 %collective-permute-done.15 = f32[128,256]{0,1:T(8,128)S(1)} collective-permute-done((f32[128,256]{0,1:T(8,128)S(1)}, f32[128,256]{0,1:T(8,128)S(1)}, u32[]{:S(2)}, u32[]{:S(2)}) %collective-permute-start.15) | collective-permute-done | bytes 131104 | tf_op jit(solution)/shard_map/ppermute | solution.py:102
  190.9 11.7 %cholesky.44 = f32[128,128]{1,0:T(8,128)S(1)} custom-call(f32[128,128]{1,0:T(8,128)S(1)} %fusion.108), custom_call_target="Cholesky" | custom-call | tf_op jit(solution)/shard_map/jit(cholesky)/cholesky | solution.py:158
  202.6 0.6 compare_reduce_fusion.1
  203.3 0.7 fusion.101
  203.9 9.8 %custom-call.6 = f32[1,128,128]{1,2,0:T(8,128)S(1)} custom-call(f32[1,128,128]{2,1,0:T(8,128)S(1)} %fusion.101), custom_call_target="InvertDiagBlocksLowerTriangular" | custom-call | tf_op jit(solution)/shard_map/jit(_solve_triangular)/triangular_solve | solution.py:159
  214.4 0.5 fusion
  215.4 1.3 collective-permute-start.20
  216.7 3.0 %collective-permute-start.16 = (f32[128,128]{0,1:T(8,128)S(1)}, f32[128,128]{0,1:T(8,128)S(1)}, u32[]{:S(2)}, u32[]{:S(2)}) collective-permute-start(f32[128,128]{0,1:T(8,128)S(1)} %fusion.115), channel_id=1, source_target_pairs={{0,1},{1,2},{2,3},{3,4},{4,5},{5,6},{6,7},{7,8},{8,9},{9,10},{10,1... | collective-permute-start | bytes 196616 | tf_op jit(solution)/shard_map/ppermute | solution.py:101
  219.7 0.9 collective-permute-done.16
  220.6 6.0 %collective-permute-start.17 = (f32[128,128]{0,1:T(8,128)S(1)}, f32[128,128]{0,1:T(8,128)S(1)}, u32[]{:S(2)}, u32[]{:S(2)}) collective-permute-start(f32[128,128]{0,1:T(8,128)S(1)} %get-tuple-element.17), channel_id=1, source_target_pairs={{0,2},{1,3},{2,4},{3,5},{4,6},{5,7},{6,8},{7,9},{8,10},{9,11},{10,... | collective-permute-start | bytes 196616 | tf_op jit(solution)/shard_map/ppermute | solution.py:101
  226.6 1.3 collective-permute-start.21
  227.9 1.2 collective-permute-done.17
  229.2 4.4 %collective-permute-start.18 = (f32[128,128]{0,1:T(8,128)S(1)}, f32[128,128]{0,1:T(8,128)S(1)}, u32[]{:S(2)}, u32[]{:S(2)}) collective-permute-start(f32[128,128]{0,1:T(8,128)S(1)} %multiply_add_fusion.10), channel_id=1, source_target_pairs={{0,4},{1,5},{2,6},{3,7},{4,8},{5,9},{6,10},{7,11},{8,12},{9,13},{1... | collective-permute-start | bytes 196616 | tf_op jit(solution)/shard_map/ppermute | solution.py:101
  233.6 1.3 collective-permute-start.22
  234.9 0.6 collective-permute-done.18
  235.4 3.7 %collective-permute-start.19 = (f32[128,128]{0,1:T(8,128)S(1)}, f32[128,128]{0,1:T(8,128)S(1)}, u32[]{:S(2)}, u32[]{:S(2)}) collective-permute-start(f32[128,128]{0,1:T(8,128)S(1)} %multiply_add_fusion.9), channel_id=1, source_target_pairs={{0,8},{1,9},{2,10},{3,11},{4,12},{5,13},{6,14},{7,15},{16,24},{17,... | collective-permute-start | bytes 196616 | tf_op jit(solution)/shard_map/ppermute | solution.py:101
  239.2 0.6 collective-permute-done.22
  239.7 1.5 collective-permute-start.23
  241.3 6.1 %collective-permute-done.23 = f32[128,128]{0,1:T(8,128)S(1)} collective-permute-done((f32[128,128]{0,1:T(8,128)S(1)}, f32[128,128]{0,1:T(8,128)S(1)}, u32[]{:S(2)}, u32[]{:S(2)}) %collective-permute-start.23) | collective-permute-done | bytes 65568 | tf_op jit(solution)/shard_map/ppermute | solution.py:102
  247.5 11.7 %cholesky.55 = f32[128,128]{1,0:T(8,128)S(1)} custom-call(f32[128,128]{1,0:T(8,128)S(1)} %fusion.106), custom_call_target="Cholesky" | custom-call | tf_op jit(solution)/shard_map/jit(cholesky)/cholesky | solution.py:158
  259.2 0.6 compare_reduce_fusion
  259.9 0.7 fusion.102
  260.5 9.8 %custom-call.7 = f32[1,128,128]{1,2,0:T(8,128)S(1)} custom-call(f32[1,128,128]{2,1,0:T(8,128)S(1)} %fusion.102), custom_call_target="InvertDiagBlocksLowerTriangular" | custom-call | tf_op jit(solution)/shard_map/jit(_solve_triangular)/triangular_solve | solution.py:159
  271.1 1.6 copy.29
  (49 shorter events, 3.6 us)
Async XLA Ops:
  0.0 11.7 %copy-start = (bf16[6,8,64,256]{3,2,1,0:T(8,128)(2,1)S(1)}, bf16[6,8,64,256]{3,2,1,0:T(8,128)(2,1)}, u32[]{:S(2)}) copy-start(bf16[6,8,64,256]{3,2,1,0:T(8,128)(2,1)} %param.6) | copy-start | bytes 4718596
  0.0 6.6 %copy-start.1 = (s32[16]{0:T(128)S(1)}, s32[16]{0:T(128)}, u32[]{:S(2)}) copy-start(s32[16]{0:T(128)} %param.8) | copy-start | bytes 196
  0.0 9.7 %copy-start.2 = (f32[6,512]{1,0:T(8,128)S(1)}, f32[6,512]{1,0:T(8,128)}, u32[]{:S(2)}) copy-start(f32[6,512]{1,0:T(8,128)} %param.7) | copy-start | bytes 36868
  2.8 7.1 %collective-permute-start = (bf16[3,8,64,256]{3,2,1,0:T(8,128)(2,1)}, bf16[3,8,64,256]{3,2,1,0:T(8,128)(2,1)S(1)}, u32[]{:S(2)}, u32[]{:S(2)}) collective-permute-start(bf16[3,8,64,256]{3,2,1,0:T(8,128)(2,1)} %get-tuple-element.13), channel_id=1, source_target_pairs={{0,1},{1,2},{2,3},{3,4},{4,5},{5,6},{6,7},{7,8},{8,9},{9,10},{10,1... | collective-permute-start | bytes 2359304 | tf_op jit(solution)/shard_map/ppermute | solution.py:23
  5.3 6.5 %collective-permute-start.1 = (bf16[3,8,64,256]{3,2,1,0:T(8,128)(2,1)}, bf16[3,8,64,256]{3,2,1,0:T(8,128)(2,1)S(1)}, u32[]{:S(2)}, u32[]{:S(2)}) collective-permute-start(bf16[3,8,64,256]{3,2,1,0:T(8,128)(2,1)} %get-tuple-element.14), channel_id=1, source_target_pairs={{1,0},{2,1},{3,2},{4,3},{5,4},{6,5},{7,6},{8,7},{9,8},{10,9},{11,1... | collective-permute-start | bytes 2359304 | tf_op jit(solution)/shard_map/ppermute | solution.py:26
  19.5 17.6 %collective-permute-start.2 = (bf16[3,8,64,256]{3,2,1,0:T(8,128)(2,1)S(1)}, bf16[3,8,64,256]{3,2,1,0:T(8,128)(2,1)S(1)}, u32[]{:S(2)}, u32[]{:S(2)}) collective-permute-start(bf16[3,8,64,256]{3,2,1,0:T(8,128)(2,1)S(1)} %get-tuple-element.11), channel_id=1, source_target_pairs={{0,1},{1,2},{2,3},{3,4},{4,5},{5,6},{6,7},{7,8},{8,9},{9,10},{10,1... | collective-permute-start | bytes 2359304 | tf_op jit(solution)/shard_map/ppermute | solution.py:23
  35.2 6.0 %collective-permute-start.3 = (bf16[3,8,64,256]{3,2,1,0:T(8,128)(2,1)S(1)}, bf16[3,8,64,256]{3,2,1,0:T(8,128)(2,1)S(1)}, u32[]{:S(2)}, u32[]{:S(2)}) collective-permute-start(bf16[3,8,64,256]{3,2,1,0:T(8,128)(2,1)S(1)} %get-tuple-element.12), channel_id=1, source_target_pairs={{1,0},{2,1},{3,2},{4,3},{5,4},{6,5},{7,6},{8,7},{9,8},{10,9},{11,1... | collective-permute-start | bytes 2359304 | tf_op jit(solution)/shard_map/ppermute | solution.py:26
  63.1 17.5 %collective-permute-start.4 = (bf16[3,8,64,256]{3,2,1,0:T(8,128)(2,1)S(1)}, bf16[3,8,64,256]{3,2,1,0:T(8,128)(2,1)S(1)}, u32[]{:S(2)}, u32[]{:S(2)}) collective-permute-start(bf16[3,8,64,256]{3,2,1,0:T(8,128)(2,1)S(1)} %get-tuple-element.9), channel_id=1, source_target_pairs={{0,1},{1,2},{2,3},{3,4},{4,5},{5,6},{6,7},{7,8},{8,9},{9,10},{10,1... | collective-permute-start | bytes 2359304 | tf_op jit(solution)/shard_map/ppermute | solution.py:23
  78.7 6.1 %collective-permute-start.5 = (bf16[3,8,64,256]{3,2,1,0:T(8,128)(2,1)S(1)}, bf16[3,8,64,256]{3,2,1,0:T(8,128)(2,1)S(1)}, u32[]{:S(2)}, u32[]{:S(2)}) collective-permute-start(bf16[3,8,64,256]{3,2,1,0:T(8,128)(2,1)S(1)} %get-tuple-element.10), channel_id=1, source_target_pairs={{1,0},{2,1},{3,2},{4,3},{5,4},{6,5},{7,6},{8,7},{9,8},{10,9},{11,1... | collective-permute-start | bytes 2359304 | tf_op jit(solution)/shard_map/ppermute | solution.py:26
  106.7 17.5 %collective-permute-start.6 = (bf16[3,8,64,256]{3,2,1,0:T(8,128)(2,1)S(1)}, bf16[3,8,64,256]{3,2,1,0:T(8,128)(2,1)S(1)}, u32[]{:S(2)}, u32[]{:S(2)}) collective-permute-start(bf16[3,8,64,256]{3,2,1,0:T(8,128)(2,1)S(1)} %get-tuple-element.6), channel_id=1, source_target_pairs={{0,1},{1,2},{2,3},{3,4},{4,5},{5,6},{6,7},{7,8},{8,9},{9,10},{10,1... | collective-permute-start | bytes 2359304 | tf_op jit(solution)/shard_map/ppermute | solution.py:23
  122.3 6.1 %collective-permute-start.7 = (bf16[3,8,64,256]{3,2,1,0:T(8,128)(2,1)S(1)}, bf16[3,8,64,256]{3,2,1,0:T(8,128)(2,1)S(1)}, u32[]{:S(2)}, u32[]{:S(2)}) collective-permute-start(bf16[3,8,64,256]{3,2,1,0:T(8,128)(2,1)S(1)} %get-tuple-element.8), channel_id=1, source_target_pairs={{1,0},{2,1},{3,2},{4,3},{5,4},{6,5},{7,6},{8,7},{9,8},{10,9},{11,1... | collective-permute-start | bytes 2359304 | tf_op jit(solution)/shard_map/ppermute | solution.py:26
  137.0 17.5 %collective-permute-start.12 = (f32[128,256]{0,1:T(8,128)S(1)}, f32[128,256]{0,1:T(8,128)S(1)}, u32[]{:S(2)}, u32[]{:S(2)}) collective-permute-start(f32[128,256]{0,1:T(8,128)S(1)} %fusion.97), channel_id=1, source_target_pairs={{1,0},{2,1},{3,2},{4,3},{5,4},{6,5},{7,6},{8,7},{9,8},{10,9},{11,1... | collective-permute-start | bytes 393224 | tf_op jit(solution)/shard_map/ppermute | solution.py:102
  138.3 17.2 %collective-permute-start.8 = (f32[128,256]{0,1:T(8,128)S(1)}, f32[128,256]{0,1:T(8,128)S(1)}, u32[]{:S(2)}, u32[]{:S(2)}) collective-permute-start(f32[128,256]{0,1:T(8,128)S(1)} %fusion.97), channel_id=1, source_target_pairs={{0,1},{1,2},{2,3},{3,4},{4,5},{5,6},{6,7},{7,8},{8,9},{9,10},{10,1... | collective-permute-start | bytes 393224 | tf_op jit(solution)/shard_map/ppermute | solution.py:101
  155.5 13.8 %collective-permute-start.9 = (f32[128,256]{0,1:T(8,128)S(1)}, f32[128,256]{0,1:T(8,128)S(1)}, u32[]{:S(2)}, u32[]{:S(2)}) collective-permute-start(f32[128,256]{0,1:T(8,128)S(1)} %get-tuple-element.15), channel_id=1, source_target_pairs={{0,2},{1,3},{2,4},{3,5},{4,6},{5,7},{6,8},{7,9},{8,10},{9,11},{10,... | collective-permute-start | bytes 393224 | tf_op jit(solution)/shard_map/ppermute | solution.py:101
  168.0 6.9 %collective-permute-start.13 = (f32[128,256]{0,1:T(8,128)S(1)}, f32[128,256]{0,1:T(8,128)S(1)}, u32[]{:S(2)}, u32[]{:S(2)}) collective-permute-start(f32[128,256]{0,1:T(8,128)S(1)} %get-tuple-element.16), channel_id=1, source_target_pairs={{2,0},{3,1},{4,2},{5,3},{6,4},{7,5},{8,6},{9,7},{10,8},{11,9},{12,... | collective-permute-start | bytes 393224 | tf_op jit(solution)/shard_map/ppermute | solution.py:102
  169.4 7.8 %collective-permute-start.10 = (f32[128,256]{0,1:T(8,128)S(1)}, f32[128,256]{0,1:T(8,128)S(1)}, u32[]{:S(2)}, u32[]{:S(2)}) collective-permute-start(f32[128,256]{0,1:T(8,128)S(1)} %multiply_add_fusion.4), channel_id=1, source_target_pairs={{0,4},{1,5},{2,6},{3,7},{4,8},{5,9},{6,10},{7,11},{8,12},{9,13},{1... | collective-permute-start | bytes 393224 | tf_op jit(solution)/shard_map/ppermute | solution.py:101
  174.9 6.9 %collective-permute-start.14 = (f32[128,256]{0,1:T(8,128)S(1)}, f32[128,256]{0,1:T(8,128)S(1)}, u32[]{:S(2)}, u32[]{:S(2)}) collective-permute-start(f32[128,256]{0,1:T(8,128)S(1)} %multiply_add_fusion.1), channel_id=1, source_target_pairs={{4,0},{5,1},{6,2},{7,3},{8,4},{9,5},{10,6},{11,7},{12,8},{13,9},{1... | collective-permute-start | bytes 393224 | tf_op jit(solution)/shard_map/ppermute | solution.py:102
  177.2 10.0 %collective-permute-start.11 = (f32[128,256]{0,1:T(8,128)S(1)}, f32[128,256]{0,1:T(8,128)S(1)}, u32[]{:S(2)}, u32[]{:S(2)}) collective-permute-start(f32[128,256]{0,1:T(8,128)S(1)} %multiply_add_fusion.3), channel_id=1, source_target_pairs={{0,8},{1,9},{2,10},{3,11},{4,12},{5,13},{6,14},{7,15},{16,24},{17,... | collective-permute-start | bytes 393224 | tf_op jit(solution)/shard_map/ppermute | solution.py:101
  181.8 8.9 %collective-permute-start.15 = (f32[128,256]{0,1:T(8,128)S(1)}, f32[128,256]{0,1:T(8,128)S(1)}, u32[]{:S(2)}, u32[]{:S(2)}) collective-permute-start(f32[128,256]{0,1:T(8,128)S(1)} %multiply_add_fusion), channel_id=1, source_target_pairs={{8,0},{9,1},{10,2},{11,3},{12,4},{13,5},{14,6},{15,7},{24,16},{25,... | collective-permute-start | bytes 393224 | tf_op jit(solution)/shard_map/ppermute | solution.py:102
  215.4 4.3 %collective-permute-start.20 = (f32[128,128]{0,1:T(8,128)S(1)}, f32[128,128]{0,1:T(8,128)S(1)}, u32[]{:S(2)}, u32[]{:S(2)}) collective-permute-start(f32[128,128]{0,1:T(8,128)S(1)} %fusion.115), channel_id=1, source_target_pairs={{1,0},{2,1},{3,2},{4,3},{5,4},{6,5},{7,6},{8,7},{9,8},{10,9},{11,1... | collective-permute-start | bytes 196616 | tf_op jit(solution)/shard_map/ppermute | solution.py:102
  216.7 3.9 %collective-permute-start.16 = (f32[128,128]{0,1:T(8,128)S(1)}, f32[128,128]{0,1:T(8,128)S(1)}, u32[]{:S(2)}, u32[]{:S(2)}) collective-permute-start(f32[128,128]{0,1:T(8,128)S(1)} %fusion.115), channel_id=1, source_target_pairs={{0,1},{1,2},{2,3},{3,4},{4,5},{5,6},{6,7},{7,8},{8,9},{9,10},{10,1... | collective-permute-start | bytes 196616 | tf_op jit(solution)/shard_map/ppermute | solution.py:101
  220.6 8.5 %collective-permute-start.17 = (f32[128,128]{0,1:T(8,128)S(1)}, f32[128,128]{0,1:T(8,128)S(1)}, u32[]{:S(2)}, u32[]{:S(2)}) collective-permute-start(f32[128,128]{0,1:T(8,128)S(1)} %get-tuple-element.17), channel_id=1, source_target_pairs={{0,2},{1,3},{2,4},{3,5},{4,6},{5,7},{6,8},{7,9},{8,10},{9,11},{10,... | collective-permute-start | bytes 196616 | tf_op jit(solution)/shard_map/ppermute | solution.py:101
  226.6 6.9 %collective-permute-start.21 = (f32[128,128]{0,1:T(8,128)S(1)}, f32[128,128]{0,1:T(8,128)S(1)}, u32[]{:S(2)}, u32[]{:S(2)}) collective-permute-start(f32[128,128]{0,1:T(8,128)S(1)} %get-tuple-element.18), channel_id=1, source_target_pairs={{2,0},{3,1},{4,2},{5,3},{6,4},{7,5},{8,6},{9,7},{10,8},{11,9},{12,... | collective-permute-start | bytes 196616 | tf_op jit(solution)/shard_map/ppermute | solution.py:102
  229.2 6.3 %collective-permute-start.18 = (f32[128,128]{0,1:T(8,128)S(1)}, f32[128,128]{0,1:T(8,128)S(1)}, u32[]{:S(2)}, u32[]{:S(2)}) collective-permute-start(f32[128,128]{0,1:T(8,128)S(1)} %multiply_add_fusion.10), channel_id=1, source_target_pairs={{0,4},{1,5},{2,6},{3,7},{4,8},{5,9},{6,10},{7,11},{8,12},{9,13},{1... | collective-permute-start | bytes 196616 | tf_op jit(solution)/shard_map/ppermute | solution.py:101
  233.6 6.2 %collective-permute-start.22 = (f32[128,128]{0,1:T(8,128)S(1)}, f32[128,128]{0,1:T(8,128)S(1)}, u32[]{:S(2)}, u32[]{:S(2)}) collective-permute-start(f32[128,128]{0,1:T(8,128)S(1)} %multiply_add_fusion.7), channel_id=1, source_target_pairs={{4,0},{5,1},{6,2},{7,3},{8,4},{9,5},{10,6},{11,7},{12,8},{13,9},{1... | collective-permute-start | bytes 196616 | tf_op jit(solution)/shard_map/ppermute | solution.py:102
  235.4 5.8 %collective-permute-start.19 = (f32[128,128]{0,1:T(8,128)S(1)}, f32[128,128]{0,1:T(8,128)S(1)}, u32[]{:S(2)}, u32[]{:S(2)}) collective-permute-start(f32[128,128]{0,1:T(8,128)S(1)} %multiply_add_fusion.9), channel_id=1, source_target_pairs={{0,8},{1,9},{2,10},{3,11},{4,12},{5,13},{6,14},{7,15},{16,24},{17,... | collective-permute-start | bytes 196616 | tf_op jit(solution)/shard_map/ppermute | solution.py:101
  239.7 7.6 %collective-permute-start.23 = (f32[128,128]{0,1:T(8,128)S(1)}, f32[128,128]{0,1:T(8,128)S(1)}, u32[]{:S(2)}, u32[]{:S(2)}) collective-permute-start(f32[128,128]{0,1:T(8,128)S(1)} %multiply_add_fusion.6), channel_id=1, source_target_pairs={{8,0},{9,1},{10,2},{11,3},{12,4},{13,5},{14,6},{15,7},{24,16},{25,... | collective-permute-start | bytes 196616 | tf_op jit(solution)/shard_map/ppermute | solution.py:102

commit v2 on v1

--- a/solution.py
+++ b/solution.py
@@ -1,6 +1,8 @@
 import jax
 import jax.numpy as jnp
 from jax import lax
+from jax.experimental import pallas as pl
+from jax.experimental.pallas import tpu as pltpu
 from jax.sharding import PartitionSpec as P
 
 PANEL = 128
@@ -13,6 +15,39 @@
 COEF = (-49.0 / 18.0, 1.5, -0.15, 1.0 / 90.0)
 CSHIFT = 7.0
 EWIDTH = 5.0
+
+
+def _lower_inverse_kernel(gram_ref, out_ref, work_ref):
+    n = gram_ref.shape[0]
+    rows = lax.broadcasted_iota(jnp.int32, (n, 2 * n), 0)
+    lanes = lax.broadcasted_iota(jnp.int32, (n, 2 * n), 1)
+    work_ref[:, :n] = gram_ref[...]
+    work_ref[:, n:] = (lax.broadcasted_iota(jnp.int32, (n, n), 0) == lax.broadcasted_iota(jnp.int32, (n, n), 1)).astype(jnp.float32)
+
+    def step(k, carry):
+        row = work_ref[pl.ds(k, 1), :]
+        lane = lax.broadcasted_iota(jnp.int32, (1, 2 * n), 1)
+        pivot = jnp.sum(jnp.where(lane == k, row, 0.0), axis=1, keepdims=True)
+        scale = 1.0 / jnp.sqrt(pivot)
+        scaled = row * scale
+        whole = work_ref[...]
+        left = whole[:, :n]
+        column = jnp.sum(jnp.where(lanes[:, :n] == k, left, 0.0), axis=1, keepdims=True) * scale
+        updated = jnp.where(rows > k, whole - column * scaled, whole)
+        work_ref[...] = jnp.where(rows == k, scaled, updated)
+        return carry
+
+    lax.fori_loop(0, n, step, 0)
+    out_ref[...] = work_ref[:, n:]
+
+
+def lower_inverse(gram):
+    n = gram.shape[0]
+    return pl.pallas_call(
+        _lower_inverse_kernel,
+        out_shape=jax.ShapeDtypeStruct((n, n), jnp.float32),
+        scratch_shapes=[pltpu.VMEM((n, 2 * n), jnp.float32)],
+    )(gram)
 
 
 def extended_2(block, sides, width):
@@ -155,8 +190,7 @@
                 )
                 / cells
             )
-        factor = jnp.linalg.cholesky(gram)
-        inverse = jax.scipy.linalg.solve_triangular(factor, identity, lower=True)
+        inverse = lower_inverse(gram)
         whitening = inverse.T.astype(jnp.bfloat16)
         whitenings.append(whitening)
         pieces.append(

time: 274 us -> 280 us (1.022)
  Pallas kernels: 0 us -> 33.9 us
  other arithmetic: 101 us -> 69.5 us
    another operation x10 -> x0, other arithmetic: 45.7 us -> none  [the longest x6 24.8 us: shards(): factor = jnp.linalg.cholesky(gram)]
    pallas_call x0 -> x2, Pallas kernels: none -> 33.9 us  [lower_inverse(): pl.pallas_call(_lower_inverse_kernel, out_shape=jax.ShapeDtypeStruct((n,...]
    convert_element_type x3, other arithmetic: 44.7 us -> 57.7 us  [shards(): newer = (2.0 / EWIDTH * (image - CSHIFT * extended[3:-3]) - older.astype(...]
  transfers between devices with their start and end apart: 24 -> 24, of which waited for: 17 -> 18; matrix products, arithmetic and copies ran while one was open for 1% -> 1% of each run, Pallas kernels for 0% -> 0%
where the time goes in v2:
time: 280 us; the launch traced here: 279 us
  starting transfers between devices  116 us (41%)
  other arithmetic  69.5 us (25%)
  Pallas kernels  33.9 us (12%)
  waiting for transfers between devices  31.1 us (11%)
  local copies, waits for them, and re-layouts  12.6 us (4%)
  between operations  11.6 us (4%)
  matrix products  4.56 us (2%)
    convert_element_type x3, other arithmetic, shards(): newer = (2.0 / EWIDTH * (image - CSHIFT * extended[3:-3]) - older.astype(...  57.7 us
    ppermute x8, starting transfers between devices, domain_total(): from_low = lax.ppermute(forward, 'gz', ahead)  50.5 us
    ppermute x4, starting transfers between devices, extended_2(): lax.ppermute(lax.slice_in_dim(block, block.shape[dim] - width, None, axis...  49.4 us
    pallas_call x2, Pallas kernels, lower_inverse(): pl.pallas_call(_lower_inverse_kernel, out_shape=jax.ShapeDtypeStruct((n,...  33.9 us
    ppermute x4, waiting for transfers between devices, extended_2(): lax.ppermute(lax.slice_in_dim(block, 0, width, axis=dim), axis, backward)  14.3 us
    ppermute x8, starting transfers between devices, domain_total(): from_high = lax.ppermute(backward, 'gz', behind)  10.5 us
    ppermute x8, waiting for transfers between devices, domain_total(): from_high = lax.ppermute(backward, 'gz', behind)  10.3 us
    convert_element_type x1, other arithmetic, shards(): current = ((image - CSHIFT * extended[3:-3]) / EWIDTH).astype(jnp.bfloat16)  6.56 us
  transfers between devices with their start and end apart: 24, of which 18 were waited for; matrix products, arithmetic and copies ran while one was open for 1% of the time, Pallas kernels for 0%

profile of v2, /device:TPU:0, one launch (start us, length us, event | category | flops | bytes accessed | tf_op | source)
XLA Modules:
  0.0 278.9 jit_solution(10191977589924848006)
XLA Ops:
  0.0 2.8 %fusion.109 = (bf16[3,8,64,256]{3,2,1,0:T(8,128)(2,1)}, bf16[3,8,64,256]{3,2,1,0:T(8,128)(2,1)}) fusion(bf16[6,8,64,256]{3,2,1,0:T(8,128)(2,1)} %param.3), kind=kLoop, calls=%fused_computation.192 | loop fusion | bytes 3145728 | tf_op jit(solution)/shard_map/slice | solution.py:59
  2.8 2.4 collective-permute-start
  5.3 1.3 collective-permute-start.1
  6.6 0.7 fusion.110
  10.1 1.6 collective-permute-done.1
  11.7 0.7 convert_multiply_fusion.3
  12.8 6.6 %fusion.11 = bf16[6,8,64,256]{3,2,1,0:T(8,128)(2,1)S(1)} fusion(f32[6,8,64,256]{3,2,1,0:T(8,128)S(1)} %slice.356, f32[12,8,64,256]{3,2,1,0:T(8,128)S(1)} %convert_multiply_fusion.3, f32[6,8,64]{2,1,0:T(8,128)S(1)} %mul.234), kind=kLoop, calls=%fused_computation.66 | loop fusion | flops 22806528 | bytes 23605248 | tf_op jit(solution)/shard_map/convert_element_type | solution.py:118
  19.6 15.7 %collective-permute-start.2 = (bf16[3,8,64,256]{3,2,1,0:T(8,128)(2,1)S(1)}, bf16[3,8,64,256]{3,2,1,0:T(8,128)(2,1)S(1)}, u32[]{:S(2)}, u32[]{:S(2)}) collective-permute-start(bf16[3,8,64,256]{3,2,1,0:T(8,128)(2,1)S(1)} %get-tuple-element.9), channel_id=1, source_target_pairs={{0,1},{1,2},{2,3},{3,4},{4,5},{5,6},{6,7},{7,8},{8,9},{9,10},{10,1... | collective-permute-start | bytes 2359304 | tf_op jit(solution)/shard_map/ppermute | solution.py:58
  35.3 1.3 collective-permute-start.3
  36.6 0.5 collective-permute-done.2
  37.2 4.2 %collective-permute-done.3 = bf16[3,8,64,256]{3,2,1,0:T(8,128)(2,1)S(1)} collective-permute-done((bf16[3,8,64,256]{3,2,1,0:T(8,128)(2,1)S(1)}, bf16[3,8,64,256]{3,2,1,0:T(8,128)(2,1)S(1)}, u32[]{:S(2)}, u32[]{:S(2)}) %collective-permute-start.3) | collective-permute-done | bytes 786464 | tf_op jit(solution)/shard_map/ppermute | solution.py:61
  41.3 0.7 convert_multiply_fusion.2
  42.1 2.0 slice.365
  44.1 19.2 %fusion.95 = bf16[6,8,64,256]{3,2,1,0:T(8,128)(2,1)S(1)} fusion(bf16[6,8,64,256]{3,2,1,0:T(8,128)(2,1)S(1)} %copy-done, f32[6,8,64,256]{3,2,1,0:T(8,128)} %slice.365, f32[12,8,64,256]{3,2,1,0:T(8,128)S(1)} %convert_multiply_fusion.2, f32[6,8,64]{2,1,0:T(8,128)S(1)} %mul.234), kind=kLoop, calls=%fused_computation.162 | loop fusion | flops 24379392 | bytes 25178112 | tf_op jit(solution)/shard_map/convert_element_type | solution.py:124
  63.5 15.6 %collective-permute-start.4 = (bf16[3,8,64,256]{3,2,1,0:T(8,128)(2,1)S(1)}, bf16[3,8,64,256]{3,2,1,0:T(8,128)(2,1)S(1)}, u32[]{:S(2)}, u32[]{:S(2)}) collective-permute-start(bf16[3,8,64,256]{3,2,1,0:T(8,128)(2,1)S(1)} %get-tuple-element.7), channel_id=1, source_target_pairs={{0,1},{1,2},{2,3},{3,4},{4,5},{5,6},{6,7},{7,8},{8,9},{9,10},{10,1... | collective-permute-start | bytes 2359304 | tf_op jit(solution)/shard_map/ppermute | solution.py:58
  79.1 1.3 collective-permute-start.5
  80.4 0.5 collective-permute-done.4
  80.9 4.3 %collective-permute-done.5 = bf16[3,8,64,256]{3,2,1,0:T(8,128)(2,1)S(1)} collective-permute-done((bf16[3,8,64,256]{3,2,1,0:T(8,128)(2,1)S(1)}, bf16[3,8,64,256]{3,2,1,0:T(8,128)(2,1)S(1)}, u32[]{:S(2)}, u32[]{:S(2)}) %collective-permute-start.5) | collective-permute-done | bytes 786464 | tf_op jit(solution)/shard_map/ppermute | solution.py:61
  85.2 0.7 convert_multiply_fusion.1
  85.9 2.0 slice.374
  87.9 19.2 %fusion.94 = bf16[6,8,64,256]{3,2,1,0:T(8,128)(2,1)S(1)} fusion(bf16[6,8,64,256]{3,2,1,0:T(8,128)(2,1)S(1)} %fusion.11, f32[6,8,64,256]{3,2,1,0:T(8,128)} %slice.374, f32[12,8,64,256]{3,2,1,0:T(8,128)S(1)} %convert_multiply_fusion.1, f32[6,8,64]{2,1,0:T(8,128)S(1)} %mul.234), kind=kLoop, calls=%fused_computation.161 | loop fusion | flops 24379392 | bytes 25178112 | tf_op jit(solution)/shard_map/convert_element_type | solution.py:124
  107.4 15.6 %collective-permute-start.6 = (bf16[3,8,64,256]{3,2,1,0:T(8,128)(2,1)S(1)}, bf16[3,8,64,256]{3,2,1,0:T(8,128)(2,1)S(1)}, u32[]{:S(2)}, u32[]{:S(2)}) collective-permute-start(bf16[3,8,64,256]{3,2,1,0:T(8,128)(2,1)S(1)} %get-tuple-element.5), channel_id=1, source_target_pairs={{0,1},{1,2},{2,3},{3,4},{4,5},{5,6},{6,7},{7,8},{8,9},{9,10},{10,1... | collective-permute-start | bytes 2359304 | tf_op jit(solution)/shard_map/ppermute | solution.py:58
  123.0 1.3 collective-permute-start.7
  124.3 0.5 collective-permute-done.6
  124.8 4.3 %collective-permute-done.7 = bf16[3,8,64,256]{3,2,1,0:T(8,128)(2,1)S(1)} collective-permute-done((bf16[3,8,64,256]{3,2,1,0:T(8,128)(2,1)S(1)}, bf16[3,8,64,256]{3,2,1,0:T(8,128)(2,1)S(1)}, u32[]{:S(2)}, u32[]{:S(2)}) %collective-permute-start.7) | collective-permute-done | bytes 786464 | tf_op jit(solution)/shard_map/ppermute | solution.py:61
  129.1 0.7 convert_multiply_fusion
  129.8 2.0 slice.383
  131.8 19.2 %fusion.93 = bf16[6,8,64,256]{3,2,1,0:T(8,128)(2,1)S(1)} fusion(bf16[6,8,64,256]{3,2,1,0:T(8,128)(2,1)S(1)} %fusion.95, f32[6,8,64,256]{3,2,1,0:T(8,128)} %slice.383, f32[12,8,64,256]{3,2,1,0:T(8,128)S(1)} %convert_multiply_fusion, f32[6,8,64]{2,1,0:T(8,128)S(1)} %mul.234), kind=kLoop, calls=%fused_computation.160 | loop fusion | flops 24379392 | bytes 25178112 | tf_op jit(solution)/shard_map/convert_element_type | solution.py:124
  151.1 0.4 fusion.97
  151.5 1.3 collective-permute-start.12
  152.8 16.2 %collective-permute-start.8 = (f32[128,256]{1,0:T(8,128)S(1)}, f32[128,256]{1,0:T(8,128)S(1)}, u32[]{:S(2)}, u32[]{:S(2)}) collective-permute-start(f32[128,256]{1,0:T(8,128)S(1)} %fusion.97), channel_id=1, source_target_pairs={{0,1},{1,2},{2,3},{3,4},{4,5},{5,6},{6,7},{7,8},{8,9},{9,10},{10,1... | collective-permute-start | bytes 393224 | tf_op jit(solution)/shard_map/ppermute | solution.py:136
  169.0 0.9 collective-permute-done.8
  170.0 7.7 %collective-permute-start.9 = (f32[128,256]{1,0:T(8,128)S(1)}, f32[128,256]{1,0:T(8,128)S(1)}, u32[]{:S(2)}, u32[]{:S(2)}) collective-permute-start(f32[128,256]{1,0:T(8,128)S(1)} %get-tuple-element.13), channel_id=1, source_target_pairs={{0,2},{1,3},{2,4},{3,5},{4,6},{5,7},{6,8},{7,9},{8,10},{9,11},{10,... | collective-permute-start | bytes 393224 | tf_op jit(solution)/shard_map/ppermute | solution.py:136
  183.0 1.3 collective-permute-start.13
  184.4 5.3 %collective-permute-start.10 = (f32[128,256]{1,0:T(8,128)S(1)}, f32[128,256]{1,0:T(8,128)S(1)}, u32[]{:S(2)}, u32[]{:S(2)}) collective-permute-start(f32[128,256]{1,0:T(8,128)S(1)} %multiply_add_fusion.4), channel_id=1, source_target_pairs={{0,4},{1,5},{2,6},{3,7},{4,8},{5,9},{6,10},{7,11},{8,12},{9,13},{1... | collective-permute-start | bytes 393224 | tf_op jit(solution)/shard_map/ppermute | solution.py:136
  189.9 1.3 collective-permute-start.14
  191.2 0.9 collective-permute-done.10
  192.2 3.8 %collective-permute-start.11 = (f32[128,256]{1,0:T(8,128)S(1)}, f32[128,256]{1,0:T(8,128)S(1)}, u32[]{:S(2)}, u32[]{:S(2)}) collective-permute-start(f32[128,256]{1,0:T(8,128)S(1)} %multiply_add_fusion.3), channel_id=1, source_target_pairs={{0,8},{1,9},{2,10},{3,11},{4,12},{5,13},{6,14},{7,15},{16,24},{17,... | collective-permute-start | bytes 393224 | tf_op jit(solution)/shard_map/ppermute | solution.py:136
  196.0 0.8 collective-permute-done.14
  196.8 1.5 collective-permute-start.15
  200.7 1.3 fusion.105
  202.7 3.0 %collective-permute-done.15 = f32[128,256]{1,0:T(8,128)S(1)} collective-permute-done((f32[128,256]{1,0:T(8,128)S(1)}, f32[128,256]{1,0:T(8,128)S(1)}, u32[]{:S(2)}, u32[]{:S(2)}) %collective-permute-start.15) | collective-permute-done | bytes 131104 | tf_op jit(solution)/shard_map/ppermute | solution.py:137
  205.7 0.6 slice.391.gram_ref
  206.4 16.9 %shard_map.37 = f32[128,128]{1,0:T(8,128)} custom-call(f32[128,128]{1,0:T(8,128)} %slice.391.gram_ref), custom_call_target="tpu_custom_call" | custom-call | tf_op jit(solution)/shard_map/pallas_call | solution.py:46
  223.3 1.2 convolution_convert_fusion.1
  224.5 1.3 fusion
  225.9 0.4 fusion.111
  226.3 1.3 collective-permute-start.20
  227.6 3.0 %collective-permute-start.16 = (f32[128,128]{1,0:T(8,128)S(1)}, f32[128,128]{1,0:T(8,128)S(1)}, u32[]{:S(2)}, u32[]{:S(2)}) collective-permute-start(f32[128,128]{1,0:T(8,128)S(1)} %fusion.111), channel_id=1, source_target_pairs={{0,1},{1,2},{2,3},{3,4},{4,5},{5,6},{6,7},{7,8},{8,9},{9,10},{10,1... | collective-permute-start | bytes 196616 | tf_op jit(solution)/shard_map/ppermute | solution.py:136
  230.6 0.9 collective-permute-done.16
  231.5 6.0 %collective-permute-start.17 = (f32[128,128]{1,0:T(8,128)S(1)}, f32[128,128]{1,0:T(8,128)S(1)}, u32[]{:S(2)}, u32[]{:S(2)}) collective-permute-start(f32[128,128]{1,0:T(8,128)S(1)} %get-tuple-element.15), channel_id=1, source_target_pairs={{0,2},{1,3},{2,4},{3,5},{4,6},{5,7},{6,8},{7,9},{8,10},{9,11},{10,... | collective-permute-start | bytes 196616 | tf_op jit(solution)/shard_map/ppermute | solution.py:136
  237.5 1.3 collective-permute-start.21
  238.8 1.2 collective-permute-done.17
  240.0 4.4 %collective-permute-start.18 = (f32[128,128]{1,0:T(8,128)S(1)}, f32[128,128]{1,0:T(8,128)S(1)}, u32[]{:S(2)}, u32[]{:S(2)}) collective-permute-start(f32[128,128]{1,0:T(8,128)S(1)} %multiply_add_fusion.10), channel_id=1, source_target_pairs={{0,4},{1,5},{2,6},{3,7},{4,8},{5,9},{6,10},{7,11},{8,12},{9,13},{1... | collective-permute-start | bytes 196616 | tf_op jit(solution)/shard_map/ppermute | solution.py:136
  244.5 1.3 collective-permute-start.22
  245.8 0.6 collective-permute-done.18
  246.3 4.1 %collective-permute-start.19 = (f32[128,128]{1,0:T(8,128)S(1)}, f32[128,128]{1,0:T(8,128)S(1)}, u32[]{:S(2)}, u32[]{:S(2)}) collective-permute-start(f32[128,128]{1,0:T(8,128)S(1)} %multiply_add_fusion.9), channel_id=1, source_target_pairs={{0,8},{1,9},{2,10},{3,11},{4,12},{5,13},{6,14},{7,15},{16,24},{17,... | collective-permute-start | bytes 196616 | tf_op jit(solution)/shard_map/ppermute | solution.py:136
  250.6 1.3 collective-permute-start.23
  251.9 0.4 collective-permute-done.19
  252.3 6.1 %collective-permute-done.23 = f32[128,128]{1,0:T(8,128)S(1)} collective-permute-done((f32[128,128]{1,0:T(8,128)S(1)}, f32[128,128]{1,0:T(8,128)S(1)}, u32[]{:S(2)}, u32[]{:S(2)}) %collective-permute-start.23) | collective-permute-done | bytes 65568 | tf_op jit(solution)/shard_map/ppermute | solution.py:137
  258.4 0.7 subtract_divide_fusion.1.gram_ref
  259.1 16.9 %shard_map.38 = f32[128,128]{1,0:T(8,128)} custom-call(f32[128,128]{1,0:T(8,128)} %subtract_divide_fusion.1.gram_ref), custom_call_target="tpu_custom_call" | custom-call | tf_op jit(solution)/shard_map/pallas_call | solution.py:46
  276.0 1.2 convolution_convert_fusion
  277.3 1.6 copy.5
  (35 shorter events, 1.8 us)
Async XLA Ops:
  0.0 11.7 %copy-start = (bf16[6,8,64,256]{3,2,1,0:T(8,128)(2,1)S(1)}, bf16[6,8,64,256]{3,2,1,0:T(8,128)(2,1)}, u32[]{:S(2)}) copy-start(bf16[6,8,64,256]{3,2,1,0:T(8,128)(2,1)} %param.3) | copy-start | bytes 4718596
  0.0 6.6 %copy-start.1 = (s32[16]{0:T(128)S(1)}, s32[16]{0:T(128)}, u32[]{:S(2)}) copy-start(s32[16]{0:T(128)} %param.5) | copy-start | bytes 196
  0.0 10.0 %copy-start.2 = (f32[6,512]{1,0:T(8,128)S(1)}, f32[6,512]{1,0:T(8,128)}, u32[]{:S(2)}) copy-start(f32[6,512]{1,0:T(8,128)} %param.4) | copy-start | bytes 36868
  2.8 7.3 %collective-permute-start = (bf16[3,8,64,256]{3,2,1,0:T(8,128)(2,1)}, bf16[3,8,64,256]{3,2,1,0:T(8,128)(2,1)S(1)}, u32[]{:S(2)}, u32[]{:S(2)}) collective-permute-start(bf16[3,8,64,256]{3,2,1,0:T(8,128)(2,1)} %get-tuple-element.11), channel_id=1, source_target_pairs={{0,1},{1,2},{2,3},{3,4},{4,5},{5,6},{6,7},{7,8},{8,9},{9,10},{10,1... | collective-permute-start | bytes 2359304 | tf_op jit(solution)/shard_map/ppermute | solution.py:58
  5.3 6.5 %collective-permute-start.1 = (bf16[3,8,64,256]{3,2,1,0:T(8,128)(2,1)}, bf16[3,8,64,256]{3,2,1,0:T(8,128)(2,1)S(1)}, u32[]{:S(2)}, u32[]{:S(2)}) collective-permute-start(bf16[3,8,64,256]{3,2,1,0:T(8,128)(2,1)} %get-tuple-element.12), channel_id=1, source_target_pairs={{1,0},{2,1},{3,2},{4,3},{5,4},{6,5},{7,6},{8,7},{9,8},{10,9},{11,1... | collective-permute-start | bytes 2359304 | tf_op jit(solution)/shard_map/ppermute | solution.py:61
  19.6 17.6 %collective-permute-start.2 = (bf16[3,8,64,256]{3,2,1,0:T(8,128)(2,1)S(1)}, bf16[3,8,64,256]{3,2,1,0:T(8,128)(2,1)S(1)}, u32[]{:S(2)}, u32[]{:S(2)}) collective-permute-start(bf16[3,8,64,256]{3,2,1,0:T(8,128)(2,1)S(1)} %get-tuple-element.9), channel_id=1, source_target_pairs={{0,1},{1,2},{2,3},{3,4},{4,5},{5,6},{6,7},{7,8},{8,9},{9,10},{10,1... | collective-permute-start | bytes 2359304 | tf_op jit(solution)/shard_map/ppermute | solution.py:58
  35.3 6.0 %collective-permute-start.3 = (bf16[3,8,64,256]{3,2,1,0:T(8,128)(2,1)S(1)}, bf16[3,8,64,256]{3,2,1,0:T(8,128)(2,1)S(1)}, u32[]{:S(2)}, u32[]{:S(2)}) collective-permute-start(bf16[3,8,64,256]{3,2,1,0:T(8,128)(2,1)S(1)} %get-tuple-element.10), channel_id=1, source_target_pairs={{1,0},{2,1},{3,2},{4,3},{5,4},{6,5},{7,6},{8,7},{9,8},{10,9},{11,1... | collective-permute-start | bytes 2359304 | tf_op jit(solution)/shard_map/ppermute | solution.py:61
  63.5 17.5 %collective-permute-start.4 = (bf16[3,8,64,256]{3,2,1,0:T(8,128)(2,1)S(1)}, bf16[3,8,64,256]{3,2,1,0:T(8,128)(2,1)S(1)}, u32[]{:S(2)}, u32[]{:S(2)}) collective-permute-start(bf16[3,8,64,256]{3,2,1,0:T(8,128)(2,1)S(1)} %get-tuple-element.7), channel_id=1, source_target_pairs={{0,1},{1,2},{2,3},{3,4},{4,5},{5,6},{6,7},{7,8},{8,9},{9,10},{10,1... | collective-permute-start | bytes 2359304 | tf_op jit(solution)/shard_map/ppermute | solution.py:58
  79.1 6.1 %collective-permute-start.5 = (bf16[3,8,64,256]{3,2,1,0:T(8,128)(2,1)S(1)}, bf16[3,8,64,256]{3,2,1,0:T(8,128)(2,1)S(1)}, u32[]{:S(2)}, u32[]{:S(2)}) collective-permute-start(bf16[3,8,64,256]{3,2,1,0:T(8,128)(2,1)S(1)} %get-tuple-element.8), channel_id=1, source_target_pairs={{1,0},{2,1},{3,2},{4,3},{5,4},{6,5},{7,6},{8,7},{9,8},{10,9},{11,1... | collective-permute-start | bytes 2359304 | tf_op jit(solution)/shard_map/ppermute | solution.py:61
  107.4 17.5 %collective-permute-start.6 = (bf16[3,8,64,256]{3,2,1,0:T(8,128)(2,1)S(1)}, bf16[3,8,64,256]{3,2,1,0:T(8,128)(2,1)S(1)}, u32[]{:S(2)}, u32[]{:S(2)}) collective-permute-start(bf16[3,8,64,256]{3,2,1,0:T(8,128)(2,1)S(1)} %get-tuple-element.5), channel_id=1, source_target_pairs={{0,1},{1,2},{2,3},{3,4},{4,5},{5,6},{6,7},{7,8},{8,9},{9,10},{10,1... | collective-permute-start | bytes 2359304 | tf_op jit(solution)/shard_map/ppermute | solution.py:58
  123.0 6.1 %collective-permute-start.7 = (bf16[3,8,64,256]{3,2,1,0:T(8,128)(2,1)S(1)}, bf16[3,8,64,256]{3,2,1,0:T(8,128)(2,1)S(1)}, u32[]{:S(2)}, u32[]{:S(2)}) collective-permute-start(bf16[3,8,64,256]{3,2,1,0:T(8,128)(2,1)S(1)} %get-tuple-element.6), channel_id=1, source_target_pairs={{1,0},{2,1},{3,2},{4,3},{5,4},{6,5},{7,6},{8,7},{9,8},{10,9},{11,1... | collective-permute-start | bytes 2359304 | tf_op jit(solution)/shard_map/ppermute | solution.py:61
  151.5 17.5 %collective-permute-start.12 = (f32[128,256]{1,0:T(8,128)S(1)}, f32[128,256]{1,0:T(8,128)S(1)}, u32[]{:S(2)}, u32[]{:S(2)}) collective-permute-start(f32[128,256]{1,0:T(8,128)S(1)} %fusion.97), channel_id=1, source_target_pairs={{1,0},{2,1},{3,2},{4,3},{5,4},{6,5},{7,6},{8,7},{9,8},{10,9},{11,1... | collective-permute-start | bytes 393224 | tf_op jit(solution)/shard_map/ppermute | solution.py:137
  152.8 17.2 %collective-permute-start.8 = (f32[128,256]{1,0:T(8,128)S(1)}, f32[128,256]{1,0:T(8,128)S(1)}, u32[]{:S(2)}, u32[]{:S(2)}) collective-permute-start(f32[128,256]{1,0:T(8,128)S(1)} %fusion.97), channel_id=1, source_target_pairs={{0,1},{1,2},{2,3},{3,4},{4,5},{5,6},{6,7},{7,8},{8,9},{9,10},{10,1... | collective-permute-start | bytes 393224 | tf_op jit(solution)/shard_map/ppermute | solution.py:136
  170.0 14.3 %collective-permute-start.9 = (f32[128,256]{1,0:T(8,128)S(1)}, f32[128,256]{1,0:T(8,128)S(1)}, u32[]{:S(2)}, u32[]{:S(2)}) collective-permute-start(f32[128,256]{1,0:T(8,128)S(1)} %get-tuple-element.13), channel_id=1, source_target_pairs={{0,2},{1,3},{2,4},{3,5},{4,6},{5,7},{6,8},{7,9},{8,10},{9,11},{10,... | collective-permute-start | bytes 393224 | tf_op jit(solution)/shard_map/ppermute | solution.py:136
  183.0 6.9 %collective-permute-start.13 = (f32[128,256]{1,0:T(8,128)S(1)}, f32[128,256]{1,0:T(8,128)S(1)}, u32[]{:S(2)}, u32[]{:S(2)}) collective-permute-start(f32[128,256]{1,0:T(8,128)S(1)} %get-tuple-element.14), channel_id=1, source_target_pairs={{2,0},{3,1},{4,2},{5,3},{6,4},{7,5},{8,6},{9,7},{10,8},{11,9},{12,... | collective-permute-start | bytes 393224 | tf_op jit(solution)/shard_map/ppermute | solution.py:137
  184.4 7.8 %collective-permute-start.10 = (f32[128,256]{1,0:T(8,128)S(1)}, f32[128,256]{1,0:T(8,128)S(1)}, u32[]{:S(2)}, u32[]{:S(2)}) collective-permute-start(f32[128,256]{1,0:T(8,128)S(1)} %multiply_add_fusion.4), channel_id=1, source_target_pairs={{0,4},{1,5},{2,6},{3,7},{4,8},{5,9},{6,10},{7,11},{8,12},{9,13},{1... | collective-permute-start | bytes 393224 | tf_op jit(solution)/shard_map/ppermute | solution.py:136
  189.9 6.9 %collective-permute-start.14 = (f32[128,256]{1,0:T(8,128)S(1)}, f32[128,256]{1,0:T(8,128)S(1)}, u32[]{:S(2)}, u32[]{:S(2)}) collective-permute-start(f32[128,256]{1,0:T(8,128)S(1)} %multiply_add_fusion.1), channel_id=1, source_target_pairs={{4,0},{5,1},{6,2},{7,3},{8,4},{9,5},{10,6},{11,7},{12,8},{13,9},{1... | collective-permute-start | bytes 393224 | tf_op jit(solution)/shard_map/ppermute | solution.py:137
  192.2 10.5 %collective-permute-start.11 = (f32[128,256]{1,0:T(8,128)S(1)}, f32[128,256]{1,0:T(8,128)S(1)}, u32[]{:S(2)}, u32[]{:S(2)}) collective-permute-start(f32[128,256]{1,0:T(8,128)S(1)} %multiply_add_fusion.3), channel_id=1, source_target_pairs={{0,8},{1,9},{2,10},{3,11},{4,12},{5,13},{6,14},{7,15},{16,24},{17,... | collective-permute-start | bytes 393224 | tf_op jit(solution)/shard_map/ppermute | solution.py:136
  196.8 8.9 %collective-permute-start.15 = (f32[128,256]{1,0:T(8,128)S(1)}, f32[128,256]{1,0:T(8,128)S(1)}, u32[]{:S(2)}, u32[]{:S(2)}) collective-permute-start(f32[128,256]{1,0:T(8,128)S(1)} %multiply_add_fusion), channel_id=1, source_target_pairs={{8,0},{9,1},{10,2},{11,3},{12,4},{13,5},{14,6},{15,7},{24,16},{25,... | collective-permute-start | bytes 393224 | tf_op jit(solution)/shard_map/ppermute | solution.py:137
  226.3 4.3 %collective-permute-start.20 = (f32[128,128]{1,0:T(8,128)S(1)}, f32[128,128]{1,0:T(8,128)S(1)}, u32[]{:S(2)}, u32[]{:S(2)}) collective-permute-start(f32[128,128]{1,0:T(8,128)S(1)} %fusion.111), channel_id=1, source_target_pairs={{1,0},{2,1},{3,2},{4,3},{5,4},{6,5},{7,6},{8,7},{9,8},{10,9},{11,1... | collective-permute-start | bytes 196616 | tf_op jit(solution)/shard_map/ppermute | solution.py:137
  227.6 3.9 %collective-permute-start.16 = (f32[128,128]{1,0:T(8,128)S(1)}, f32[128,128]{1,0:T(8,128)S(1)}, u32[]{:S(2)}, u32[]{:S(2)}) collective-permute-start(f32[128,128]{1,0:T(8,128)S(1)} %fusion.111), channel_id=1, source_target_pairs={{0,1},{1,2},{2,3},{3,4},{4,5},{5,6},{6,7},{7,8},{8,9},{9,10},{10,1... | collective-permute-start | bytes 196616 | tf_op jit(solution)/shard_map/ppermute | solution.py:136
  231.5 8.5 %collective-permute-start.17 = (f32[128,128]{1,0:T(8,128)S(1)}, f32[128,128]{1,0:T(8,128)S(1)}, u32[]{:S(2)}, u32[]{:S(2)}) collective-permute-start(f32[128,128]{1,0:T(8,128)S(1)} %get-tuple-element.15), channel_id=1, source_target_pairs={{0,2},{1,3},{2,4},{3,5},{4,6},{5,7},{6,8},{7,9},{8,10},{9,11},{10,... | collective-permute-start | bytes 196616 | tf_op jit(solution)/shard_map/ppermute | solution.py:136
  237.5 6.9 %collective-permute-start.21 = (f32[128,128]{1,0:T(8,128)S(1)}, f32[128,128]{1,0:T(8,128)S(1)}, u32[]{:S(2)}, u32[]{:S(2)}) collective-permute-start(f32[128,128]{1,0:T(8,128)S(1)} %get-tuple-element.16), channel_id=1, source_target_pairs={{2,0},{3,1},{4,2},{5,3},{6,4},{7,5},{8,6},{9,7},{10,8},{11,9},{12,... | collective-permute-start | bytes 196616 | tf_op jit(solution)/shard_map/ppermute | solution.py:137
  240.0 6.3 %collective-permute-start.18 = (f32[128,128]{1,0:T(8,128)S(1)}, f32[128,128]{1,0:T(8,128)S(1)}, u32[]{:S(2)}, u32[]{:S(2)}) collective-permute-start(f32[128,128]{1,0:T(8,128)S(1)} %multiply_add_fusion.10), channel_id=1, source_target_pairs={{0,4},{1,5},{2,6},{3,7},{4,8},{5,9},{6,10},{7,11},{8,12},{9,13},{1... | collective-permute-start | bytes 196616 | tf_op jit(solution)/shard_map/ppermute | solution.py:136
  244.5 6.2 %collective-permute-start.22 = (f32[128,128]{1,0:T(8,128)S(1)}, f32[128,128]{1,0:T(8,128)S(1)}, u32[]{:S(2)}, u32[]{:S(2)}) collective-permute-start(f32[128,128]{1,0:T(8,128)S(1)} %multiply_add_fusion.7), channel_id=1, source_target_pairs={{4,0},{5,1},{6,2},{7,3},{8,4},{9,5},{10,6},{11,7},{12,8},{13,9},{1... | collective-permute-start | bytes 196616 | tf_op jit(solution)/shard_map/ppermute | solution.py:137
  246.3 6.0 %collective-permute-start.19 = (f32[128,128]{1,0:T(8,128)S(1)}, f32[128,128]{1,0:T(8,128)S(1)}, u32[]{:S(2)}, u32[]{:S(2)}) collective-permute-start(f32[128,128]{1,0:T(8,128)S(1)} %multiply_add_fusion.9), channel_id=1, source_target_pairs={{0,8},{1,9},{2,10},{3,11},{4,12},{5,13},{6,14},{7,15},{16,24},{17,... | collective-permute-start | bytes 196616 | tf_op jit(solution)/shard_map/ppermute | solution.py:136
  250.6 7.8 %collective-permute-start.23 = (f32[128,128]{1,0:T(8,128)S(1)}, f32[128,128]{1,0:T(8,128)S(1)}, u32[]{:S(2)}, u32[]{:S(2)}) collective-permute-start(f32[128,128]{1,0:T(8,128)S(1)} %multiply_add_fusion.6), channel_id=1, source_target_pairs={{8,0},{9,1},{10,2},{11,3},{12,4},{13,5},{14,6},{15,7},{24,16},{25,... | collective-permute-start | bytes 196616 | tf_op jit(solution)/shard_map/ppermute | solution.py:137

commit v3 on v2

--- a/solution.py
+++ b/solution.py
@@ -1,3 +1,5 @@
+import functools
+
 import jax
 import jax.numpy as jnp
 from jax import lax
@@ -48,6 +50,58 @@
         out_shape=jax.ShapeDtypeStruct((n, n), jnp.float32),
         scratch_shapes=[pltpu.VMEM((n, 2 * n), jnp.float32)],
     )(gram)
+
+
+def _step_kernel(first, extended_ref, older_ref, potential_ref, out_ref):
+    z = pl.program_id(1)
+    rows_y = extended_ref.shape[1]
+    rows_x = extended_ref.shape[2]
+    place = lax.broadcasted_iota(jnp.int32, (rows_x, extended_ref.shape[3]), 0)
+
+    def plane(offset, y):
+        return extended_ref[z + 3 + offset, y].astype(jnp.float32)
+
+    for y in range(rows_y):
+        inner = plane(0, y)
+        total = 3.0 * COEF[0] * inner
+        for distance in (1, 2, 3):
+            along_z = plane(distance, y) + plane(-distance, y)
+            up = plane(0, y + distance) if y + distance < rows_y else None
+            down = plane(0, y - distance) if y - distance >= 0 else None
+            if up is None:
+                along_y = down
+            elif down is None:
+                along_y = up
+            else:
+                along_y = up + down
+            ahead = jnp.where(place + distance < rows_x, pltpu.roll(inner, rows_x - distance, 0), 0.0)
+            behind = jnp.where(place >= distance, pltpu.roll(inner, distance, 0), 0.0)
+            along_x = ahead + behind
+            total = total + COEF[distance] * (along_z + along_y + along_x)
+        image = potential_ref[0, y] * inner - 0.5 * total
+        if first:
+            newer = (image - CSHIFT * inner) / EWIDTH
+        else:
+            newer = 2.0 / EWIDTH * (image - CSHIFT * inner) - older_ref[0, y].astype(jnp.float32)
+        out_ref[0, y] = newer.astype(out_ref.dtype)
+
+
+def chebyshev_step(extended, older, potential, first):
+    planes = older.shape[0]
+    rows_y, rows_x, bands = older.shape[1:]
+    lanes = 128
+    grid = (bands // lanes, planes)
+    return pl.pallas_call(
+        functools.partial(_step_kernel, first),
+        out_shape=jax.ShapeDtypeStruct(older.shape, jnp.bfloat16),
+        grid=grid,
+        in_specs=[
+            pl.BlockSpec((planes + 6, rows_y, rows_x, lanes), lambda j, z: (0, 0, 0, j)),
+            pl.BlockSpec((1, rows_y, rows_x, lanes), lambda j, z: (z, 0, 0, j)),
+            pl.BlockSpec((1, rows_y, rows_x, lanes), lambda j, z: (z, 0, 0, 0)),
+        ],
+        out_specs=pl.BlockSpec((1, rows_y, rows_x, lanes), lambda j, z: (z, 0, 0, j)),
+    )(extended, older, potential)
 
 
 def extended_2(block, sides, width):
@@ -110,18 +164,13 @@
     )[:, None, None, None]
 
     def rimmed(field):
-        return extended_2(field, (("gz", 0),), 3).astype(jnp.float32) * mask_three
-
-    extended = rimmed(waves)
-    image = hamiltonian(extended, grid)
+        return extended_2(field, (("gz", 0),), 3) * mask_three.astype(jnp.bfloat16)
+
+    lanes = jnp.broadcast_to(grid[..., None], grid.shape + (128,))
     older = waves
-    current = ((image - CSHIFT * extended[3:-3]) / EWIDTH).astype(jnp.bfloat16)
+    current = chebyshev_step(rimmed(waves), waves, lanes, True)
     for turn in range(DEGREE - 1):
-        extended = rimmed(current)
-        image = hamiltonian(extended, grid)
-        newer = (
-            2.0 / EWIDTH * (image - CSHIFT * extended[3:-3]) - older.astype(jnp.float32)
-        ).astype(jnp.bfloat16)
+        newer = chebyshev_step(rimmed(current), older, lanes, False)
         older, current = (current, newer)
     cells = jnp.sum((domain_of == owner).astype(jnp.float32)) * (planes * NY * NX)
     rows = current.reshape(planes * NY * NX, bands)

time: 280 us -> 269 us (0.961)
  other arithmetic: 69.5 us -> 9.78 us
  Pallas kernels: 33.9 us -> 80 us
    convert_element_type x4 -> x0, other arithmetic: 64.3 us -> none  [the longest x3 57.7 us: shards(): newer = (2.0 / EWIDTH * (image - CSHIFT * extended[3:-3]) - older.astype(...]
    pallas_call x0 -> x4, Pallas kernels: none -> 46.1 us  [chebyshev_step(): pl.pallas_call(functools.partial(_step_kernel, first), out_shape=jax.Shap...]
    slice x4 -> x0, local copies, waits for them, and re-layouts: 6.33 us -> none  [hamiltonian(): inner = extended[3:-3]]
    mul x4, other arithmetic: 2.93 us -> 7.52 us  [rimmed(): return extended_2(field, (('gz', 0),), 3) * mask_three.astype(jnp.bfloat16)]
    slice x4, local copies, waits for them, and re-layouts: 3.32 us -> 7.78 us  [extended_2(): lax.slice_in_dim(block, block.shape[dim] - width, None, axis=dim)]
where the time goes in v3:
time: 269 us; the launch traced here: 267 us
  starting transfers between devices  115 us (43%)
  Pallas kernels  80 us (30%)
  waiting for transfers between devices  31.7 us (12%)
  local copies, waits for them, and re-layouts  12.4 us (5%)
  between operations  11.3 us (4%)
  other arithmetic  9.78 us (4%)
  matrix products  6.35 us (2%)
    ppermute x8, starting transfers between devices, domain_total(): from_low = lax.ppermute(forward, 'gz', ahead)  50.3 us
    ppermute x4, starting transfers between devices, extended_2(): lax.ppermute(lax.slice_in_dim(block, block.shape[dim] - width, None, axis...  49.4 us
    pallas_call x4, Pallas kernels, chebyshev_step(): pl.pallas_call(functools.partial(_step_kernel, first), out_shape=jax.Shap...  46.1 us
    pallas_call x2, Pallas kernels, lower_inverse(): pl.pallas_call(_lower_inverse_kernel, out_shape=jax.ShapeDtypeStruct((n,...  33.9 us
    ppermute x4, waiting for transfers between devices, extended_2(): lax.ppermute(lax.slice_in_dim(block, 0, width, axis=dim), axis, backward)  14.4 us
    ppermute x8, waiting for transfers between devices, domain_total(): from_high = lax.ppermute(backward, 'gz', behind)  11 us
    ppermute x8, starting transfers between devices, domain_total(): from_high = lax.ppermute(backward, 'gz', behind)  10.3 us
    slice x4, local copies, waits for them, and re-layouts, extended_2(): lax.slice_in_dim(block, block.shape[dim] - width, None, axis=dim)  7.78 us
  transfers between devices with their start and end apart: 24, of which 18 were waited for; matrix products, arithmetic and copies ran while one was open for 1% of the time, Pallas kernels for 0%

profile of v3, /device:TPU:0, one launch (start us, length us, event | category | flops | bytes accessed | tf_op | source)
XLA Modules:
  0.0 266.6 jit_solution(13575886640366454363)
XLA Ops:
  0.0 2.8 %fusion.14 = (bf16[3,8,64,256]{3,2,1,0:T(8,128)(2,1)}, bf16[3,8,64,256]{3,2,1,0:T(8,128)(2,1)}) fusion(bf16[6,8,64,256]{3,2,1,0:T(8,128)(2,1)} %older_ref.3), kind=kLoop, calls=%fused_computation.37 | loop fusion | bytes 3145728 | tf_op jit(solution)/shard_map/slice | solution.py:113
  2.8 2.4 collective-permute-start
  5.3 1.3 collective-permute-start.1
  6.6 0.7 fusion.15
  10.0 1.7 collective-permute-done.1
  11.7 1.9 maximum_multiply_fusion.extended_ref
  13.6 1.6 broadcast_in_dim.17.potential_ref
  15.2 11.4 %shard_map.37.older_ref = bf16[6,8,64,256]{3,2,1,0:T(8,128)(2,1)} custom-call(bf16[12,8,64,256]{3,2,1,0:T(8,128)(2,1)} %maximum_multiply_fusion.extended_ref, bf16[6,8,64,256]{3,2,1,0:T(8,128)(2,1)} %older_ref.3, f32[6,8,64,128]{3,2,1,0:T(8,128)} %broadcast_in_dim.17.potential_ref), custom_call_target="tpu_custom_call" | custom-call | tf_op jit(solution)/shard_map/pallas_call | solution.py:94
  26.7 1.7 fusion.13
  28.3 15.7 %collective-permute-start.2 = (bf16[3,8,64,256]{3,2,1,0:T(8,128)(2,1)S(1)}, bf16[3,8,64,256]{3,2,1,0:T(8,128)(2,1)S(1)}, u32[]{:S(2)}, u32[]{:S(2)}) collective-permute-start(bf16[3,8,64,256]{3,2,1,0:T(8,128)(2,1)S(1)} %get-tuple-element.9), channel_id=1, source_target_pairs={{0,1},{1,2},{2,3},{3,4},{4,5},{5,6},{6,7},{7,8},{8,9},{9,10},{10,1... | collective-permute-start | bytes 2359304 | tf_op jit(solution)/shard_map/ppermute | solution.py:112
  44.1 1.3 collective-permute-start.3
  45.4 0.5 collective-permute-done.2
  45.9 4.2 %collective-permute-done.3 = bf16[3,8,64,256]{3,2,1,0:T(8,128)(2,1)S(1)} collective-permute-done((bf16[3,8,64,256]{3,2,1,0:T(8,128)(2,1)S(1)}, bf16[3,8,64,256]{3,2,1,0:T(8,128)(2,1)S(1)}, u32[]{:S(2)}, u32[]{:S(2)}) %collective-permute-start.3) | collective-permute-done | bytes 786464 | tf_op jit(solution)/shard_map/ppermute | solution.py:115
  50.1 1.9 maximum_multiply_fusion.1.extended_ref
  52.0 11.5 %shard_map.38.older_ref = bf16[6,8,64,256]{3,2,1,0:T(8,128)(2,1)} custom-call(bf16[12,8,64,256]{3,2,1,0:T(8,128)(2,1)} %maximum_multiply_fusion.1.extended_ref, bf16[6,8,64,256]{3,2,1,0:T(8,128)(2,1)} %older_ref.3, f32[6,8,64,128]{3,2,1,0:T(8,128)} %broadcast_in_dim.17.potential_ref), custom_call_target="tpu_custom_call" | custom-call | tf_op jit(solution)/shard_map/pallas_call | solution.py:94
  63.5 1.7 fusion.12
  65.2 15.6 %collective-permute-start.4 = (bf16[3,8,64,256]{3,2,1,0:T(8,128)(2,1)S(1)}, bf16[3,8,64,256]{3,2,1,0:T(8,128)(2,1)S(1)}, u32[]{:S(2)}, u32[]{:S(2)}) collective-permute-start(bf16[3,8,64,256]{3,2,1,0:T(8,128)(2,1)S(1)} %get-tuple-element.7), channel_id=1, source_target_pairs={{0,1},{1,2},{2,3},{3,4},{4,5},{5,6},{6,7},{7,8},{8,9},{9,10},{10,1... | collective-permute-start | bytes 2359304 | tf_op jit(solution)/shard_map/ppermute | solution.py:112
  80.8 1.3 collective-permute-start.5
  82.1 0.5 collective-permute-done.4
  82.6 4.3 %collective-permute-done.5 = bf16[3,8,64,256]{3,2,1,0:T(8,128)(2,1)S(1)} collective-permute-done((bf16[3,8,64,256]{3,2,1,0:T(8,128)(2,1)S(1)}, bf16[3,8,64,256]{3,2,1,0:T(8,128)(2,1)S(1)}, u32[]{:S(2)}, u32[]{:S(2)}) %collective-permute-start.5) | collective-permute-done | bytes 786464 | tf_op jit(solution)/shard_map/ppermute | solution.py:115
  86.9 1.9 maximum_multiply_fusion.2.extended_ref
  88.8 11.6 %shard_map.39 = bf16[6,8,64,256]{3,2,1,0:T(8,128)(2,1)} custom-call(bf16[12,8,64,256]{3,2,1,0:T(8,128)(2,1)} %maximum_multiply_fusion.2.extended_ref, bf16[6,8,64,256]{3,2,1,0:T(8,128)(2,1)} %shard_map.37.older_ref, f32[6,8,64,128]{3,2,1,0:T(8,128)} %broadcast_in_dim.17.potential_ref), custom_call_target="tpu_custom_call" | custom-call | tf_op jit(solution)/shard_map/pallas_call | solution.py:94
  100.4 1.7 fusion.11
  102.0 15.6 %collective-permute-start.6 = (bf16[3,8,64,256]{3,2,1,0:T(8,128)(2,1)S(1)}, bf16[3,8,64,256]{3,2,1,0:T(8,128)(2,1)S(1)}, u32[]{:S(2)}, u32[]{:S(2)}) collective-permute-start(bf16[3,8,64,256]{3,2,1,0:T(8,128)(2,1)S(1)} %get-tuple-element.5), channel_id=1, source_target_pairs={{0,1},{1,2},{2,3},{3,4},{4,5},{5,6},{6,7},{7,8},{8,9},{9,10},{10,1... | collective-permute-start | bytes 2359304 | tf_op jit(solution)/shard_map/ppermute | solution.py:112
  117.6 1.3 collective-permute-start.7
  118.9 0.5 collective-permute-done.6
  119.5 4.3 %collective-permute-done.7 = bf16[3,8,64,256]{3,2,1,0:T(8,128)(2,1)S(1)} collective-permute-done((bf16[3,8,64,256]{3,2,1,0:T(8,128)(2,1)S(1)}, bf16[3,8,64,256]{3,2,1,0:T(8,128)(2,1)S(1)}, u32[]{:S(2)}, u32[]{:S(2)}) %collective-permute-start.7) | collective-permute-done | bytes 786464 | tf_op jit(solution)/shard_map/ppermute | solution.py:115
  123.8 1.9 maximum_multiply_fusion.3.extended_ref
  125.6 11.6 %shard_map.40 = bf16[6,8,64,256]{3,2,1,0:T(8,128)(2,1)} custom-call(bf16[12,8,64,256]{3,2,1,0:T(8,128)(2,1)} %maximum_multiply_fusion.3.extended_ref, bf16[6,8,64,256]{3,2,1,0:T(8,128)(2,1)} %shard_map.38.older_ref, f32[6,8,64,128]{3,2,1,0:T(8,128)} %broadcast_in_dim.17.potential_ref), custom_call_target="tpu_custom_call" | custom-call | tf_op jit(solution)/shard_map/pallas_call | solution.py:94
  137.2 2.2 fusion.2
  139.4 1.3 collective-permute-start.12
  140.7 16.2 %collective-permute-start.8 = (f32[128,256]{1,0:T(8,128)S(1)}, f32[128,256]{1,0:T(8,128)S(1)}, u32[]{:S(2)}, u32[]{:S(2)}) collective-permute-start(f32[128,256]{1,0:T(8,128)S(1)} %fusion.2), channel_id=1, source_target_pairs={{0,1},{1,2},{2,3},{3,4},{4,5},{5,6},{6,7},{7,8},{8,9},{9,10},{10,1... | collective-permute-start | bytes 393224 | tf_op jit(solution)/shard_map/ppermute | solution.py:185
  157.0 0.9 collective-permute-done.8
  157.9 7.7 %collective-permute-start.9 = (f32[128,256]{1,0:T(8,128)S(1)}, f32[128,256]{1,0:T(8,128)S(1)}, u32[]{:S(2)}, u32[]{:S(2)}) collective-permute-start(f32[128,256]{1,0:T(8,128)S(1)} %get-tuple-element.13), channel_id=1, source_target_pairs={{0,2},{1,3},{2,4},{3,5},{4,6},{5,7},{6,8},{7,9},{8,10},{9,11},{10,... | collective-permute-start | bytes 393224 | tf_op jit(solution)/shard_map/ppermute | solution.py:185
  170.8 1.3 collective-permute-start.13
  172.1 5.3 %collective-permute-start.10 = (f32[128,256]{1,0:T(8,128)S(1)}, f32[128,256]{1,0:T(8,128)S(1)}, u32[]{:S(2)}, u32[]{:S(2)}) collective-permute-start(f32[128,256]{1,0:T(8,128)S(1)} %multiply_add_fusion.4), channel_id=1, source_target_pairs={{0,4},{1,5},{2,6},{3,7},{4,8},{5,9},{6,10},{7,11},{8,12},{9,13},{1... | collective-permute-start | bytes 393224 | tf_op jit(solution)/shard_map/ppermute | solution.py:185
  177.6 1.3 collective-permute-start.14
  178.9 0.9 collective-permute-done.10
  179.9 3.8 %collective-permute-start.11 = (f32[128,256]{1,0:T(8,128)S(1)}, f32[128,256]{1,0:T(8,128)S(1)}, u32[]{:S(2)}, u32[]{:S(2)}) collective-permute-start(f32[128,256]{1,0:T(8,128)S(1)} %multiply_add_fusion.3), channel_id=1, source_target_pairs={{0,8},{1,9},{2,10},{3,11},{4,12},{5,13},{6,14},{7,15},{16,24},{17,... | collective-permute-start | bytes 393224 | tf_op jit(solution)/shard_map/ppermute | solution.py:185
  183.7 0.8 collective-permute-done.14
  184.5 1.3 collective-permute-start.15
  188.3 1.2 fusion.10
  190.2 3.2 %collective-permute-done.15 = f32[128,256]{1,0:T(8,128)S(1)} collective-permute-done((f32[128,256]{1,0:T(8,128)S(1)}, f32[128,256]{1,0:T(8,128)S(1)}, u32[]{:S(2)}, u32[]{:S(2)}) %collective-permute-start.15) | collective-permute-done | bytes 131104 | tf_op jit(solution)/shard_map/ppermute | solution.py:186
  193.5 0.6 slice.55.gram_ref
  194.1 16.9 %shard_map.41 = f32[128,128]{1,0:T(8,128)} custom-call(f32[128,128]{1,0:T(8,128)} %slice.55.gram_ref), custom_call_target="tpu_custom_call" | custom-call | tf_op jit(solution)/shard_map/pallas_call | solution.py:48
  211.0 1.2 convolution_convert_fusion.1
  212.3 1.3 fusion
  214.0 1.3 collective-permute-start.20
  215.3 3.0 %collective-permute-start.16 = (f32[128,128]{1,0:T(8,128)S(1)}, f32[128,128]{1,0:T(8,128)S(1)}, u32[]{:S(2)}, u32[]{:S(2)}) collective-permute-start(f32[128,128]{1,0:T(8,128)S(1)} %fusion.16), channel_id=1, source_target_pairs={{0,1},{1,2},{2,3},{3,4},{4,5},{5,6},{6,7},{7,8},{8,9},{9,10},{10,1... | collective-permute-start | bytes 196616 | tf_op jit(solution)/shard_map/ppermute | solution.py:185
  218.4 0.9 collective-permute-done.16
  219.3 6.0 %collective-permute-start.17 = (f32[128,128]{1,0:T(8,128)S(1)}, f32[128,128]{1,0:T(8,128)S(1)}, u32[]{:S(2)}, u32[]{:S(2)}) collective-permute-start(f32[128,128]{1,0:T(8,128)S(1)} %get-tuple-element.15), channel_id=1, source_target_pairs={{0,2},{1,3},{2,4},{3,5},{4,6},{5,7},{6,8},{7,9},{8,10},{9,11},{10,... | collective-permute-start | bytes 196616 | tf_op jit(solution)/shard_map/ppermute | solution.py:185
  225.3 1.3 collective-permute-start.21
  226.6 1.2 collective-permute-done.17
  227.8 4.4 %collective-permute-start.18 = (f32[128,128]{1,0:T(8,128)S(1)}, f32[128,128]{1,0:T(8,128)S(1)}, u32[]{:S(2)}, u32[]{:S(2)}) collective-permute-start(f32[128,128]{1,0:T(8,128)S(1)} %multiply_add_fusion.10), channel_id=1, source_target_pairs={{0,4},{1,5},{2,6},{3,7},{4,8},{5,9},{6,10},{7,11},{8,12},{9,13},{1... | collective-permute-start | bytes 196616 | tf_op jit(solution)/shard_map/ppermute | solution.py:185
  232.2 1.3 collective-permute-start.22
  233.5 0.6 collective-permute-done.18
  234.1 3.9 %collective-permute-start.19 = (f32[128,128]{1,0:T(8,128)S(1)}, f32[128,128]{1,0:T(8,128)S(1)}, u32[]{:S(2)}, u32[]{:S(2)}) collective-permute-start(f32[128,128]{1,0:T(8,128)S(1)} %multiply_add_fusion.9), channel_id=1, source_target_pairs={{0,8},{1,9},{2,10},{3,11},{4,12},{5,13},{6,14},{7,15},{16,24},{17,... | collective-permute-start | bytes 196616 | tf_op jit(solution)/shard_map/ppermute | solution.py:185
  238.0 0.4 collective-permute-done.22
  238.4 1.3 collective-permute-start.23
  239.8 6.3 %collective-permute-done.23 = f32[128,128]{1,0:T(8,128)S(1)} collective-permute-done((f32[128,128]{1,0:T(8,128)S(1)}, f32[128,128]{1,0:T(8,128)S(1)}, u32[]{:S(2)}, u32[]{:S(2)}) %collective-permute-start.23) | collective-permute-done | bytes 65568 | tf_op jit(solution)/shard_map/ppermute | solution.py:186
  246.1 0.7 subtract_divide_fusion.1.gram_ref
  246.8 16.9 %shard_map.42 = f32[128,128]{1,0:T(8,128)} custom-call(f32[128,128]{1,0:T(8,128)} %subtract_divide_fusion.1.gram_ref), custom_call_target="tpu_custom_call" | custom-call | tf_op jit(solution)/shard_map/pallas_call | solution.py:48
  263.7 1.2 convolution_convert_fusion
  265.0 1.6 copy.5
  (40 shorter events, 1.3 us)
Async XLA Ops:
  0.0 11.7 %copy-start = (bf16[6,8,64,256]{3,2,1,0:T(8,128)(2,1)S(1)}, bf16[6,8,64,256]{3,2,1,0:T(8,128)(2,1)}, u32[]{:S(2)}) copy-start(bf16[6,8,64,256]{3,2,1,0:T(8,128)(2,1)} %older_ref.3) | copy-start | bytes 4718596
  0.0 6.6 %copy-start.5 = (s32[16]{0:T(128)S(1)}, s32[16]{0:T(128)}, u32[]{:S(2)}) copy-start(s32[16]{0:T(128)} %param.5) | copy-start | bytes 196
  0.0 9.9 %copy-start.6 = (f32[6,512]{1,0:T(8,128)S(1)}, f32[6,512]{1,0:T(8,128)}, u32[]{:S(2)}) copy-start(f32[6,512]{1,0:T(8,128)} %param.4) | copy-start | bytes 36868
  2.8 7.2 %collective-permute-start = (bf16[3,8,64,256]{3,2,1,0:T(8,128)(2,1)}, bf16[3,8,64,256]{3,2,1,0:T(8,128)(2,1)S(1)}, u32[]{:S(2)}, u32[]{:S(2)}) collective-permute-start(bf16[3,8,64,256]{3,2,1,0:T(8,128)(2,1)} %get-tuple-element.11), channel_id=1, source_target_pairs={{0,1},{1,2},{2,3},{3,4},{4,5},{5,6},{6,7},{7,8},{8,9},{9,10},{10,1... | collective-permute-start | bytes 2359304 | tf_op jit(solution)/shard_map/ppermute | solution.py:112
  5.3 6.5 %collective-permute-start.1 = (bf16[3,8,64,256]{3,2,1,0:T(8,128)(2,1)}, bf16[3,8,64,256]{3,2,1,0:T(8,128)(2,1)S(1)}, u32[]{:S(2)}, u32[]{:S(2)}) collective-permute-start(bf16[3,8,64,256]{3,2,1,0:T(8,128)(2,1)} %get-tuple-element.12), channel_id=1, source_target_pairs={{1,0},{2,1},{3,2},{4,3},{5,4},{6,5},{7,6},{8,7},{9,8},{10,9},{11,1... | collective-permute-start | bytes 2359304 | tf_op jit(solution)/shard_map/ppermute | solution.py:115
  26.7 23.4 %copy-start.2 = (bf16[6,8,64,256]{3,2,1,0:T(8,128)(2,1)S(1)}, bf16[6,8,64,256]{3,2,1,0:T(8,128)(2,1)}, u32[]{:S(2)}) copy-start(bf16[6,8,64,256]{3,2,1,0:T(8,128)(2,1)} %shard_map.37.older_ref) | copy-start | bytes 4718596
  28.3 17.6 %collective-permute-start.2 = (bf16[3,8,64,256]{3,2,1,0:T(8,128)(2,1)S(1)}, bf16[3,8,64,256]{3,2,1,0:T(8,128)(2,1)S(1)}, u32[]{:S(2)}, u32[]{:S(2)}) collective-permute-start(bf16[3,8,64,256]{3,2,1,0:T(8,128)(2,1)S(1)} %get-tuple-element.9), channel_id=1, source_target_pairs={{0,1},{1,2},{2,3},{3,4},{4,5},{5,6},{6,7},{7,8},{8,9},{9,10},{10,1... | collective-permute-start | bytes 2359304 | tf_op jit(solution)/shard_map/ppermute | solution.py:112
  44.1 6.0 %collective-permute-start.3 = (bf16[3,8,64,256]{3,2,1,0:T(8,128)(2,1)S(1)}, bf16[3,8,64,256]{3,2,1,0:T(8,128)(2,1)S(1)}, u32[]{:S(2)}, u32[]{:S(2)}) collective-permute-start(bf16[3,8,64,256]{3,2,1,0:T(8,128)(2,1)S(1)} %get-tuple-element.10), channel_id=1, source_target_pairs={{1,0},{2,1},{3,2},{4,3},{5,4},{6,5},{7,6},{8,7},{9,8},{10,9},{11,1... | collective-permute-start | bytes 2359304 | tf_op jit(solution)/shard_map/ppermute | solution.py:115
  63.5 23.4 %copy-start.1 = (bf16[6,8,64,256]{3,2,1,0:T(8,128)(2,1)S(1)}, bf16[6,8,64,256]{3,2,1,0:T(8,128)(2,1)}, u32[]{:S(2)}) copy-start(bf16[6,8,64,256]{3,2,1,0:T(8,128)(2,1)} %shard_map.38.older_ref) | copy-start | bytes 4718596
  65.2 17.5 %collective-permute-start.4 = (bf16[3,8,64,256]{3,2,1,0:T(8,128)(2,1)S(1)}, bf16[3,8,64,256]{3,2,1,0:T(8,128)(2,1)S(1)}, u32[]{:S(2)}, u32[]{:S(2)}) collective-permute-start(bf16[3,8,64,256]{3,2,1,0:T(8,128)(2,1)S(1)} %get-tuple-element.7), channel_id=1, source_target_pairs={{0,1},{1,2},{2,3},{3,4},{4,5},{5,6},{6,7},{7,8},{8,9},{9,10},{10,1... | collective-permute-start | bytes 2359304 | tf_op jit(solution)/shard_map/ppermute | solution.py:112
  80.8 6.1 %collective-permute-start.5 = (bf16[3,8,64,256]{3,2,1,0:T(8,128)(2,1)S(1)}, bf16[3,8,64,256]{3,2,1,0:T(8,128)(2,1)S(1)}, u32[]{:S(2)}, u32[]{:S(2)}) collective-permute-start(bf16[3,8,64,256]{3,2,1,0:T(8,128)(2,1)S(1)} %get-tuple-element.8), channel_id=1, source_target_pairs={{1,0},{2,1},{3,2},{4,3},{5,4},{6,5},{7,6},{8,7},{9,8},{10,9},{11,1... | collective-permute-start | bytes 2359304 | tf_op jit(solution)/shard_map/ppermute | solution.py:115
  100.4 23.4 %copy-start.4 = (bf16[6,8,64,256]{3,2,1,0:T(8,128)(2,1)S(1)}, bf16[6,8,64,256]{3,2,1,0:T(8,128)(2,1)}, u32[]{:S(2)}) copy-start(bf16[6,8,64,256]{3,2,1,0:T(8,128)(2,1)} %shard_map.39) | copy-start | bytes 4718596
  102.0 17.5 %collective-permute-start.6 = (bf16[3,8,64,256]{3,2,1,0:T(8,128)(2,1)S(1)}, bf16[3,8,64,256]{3,2,1,0:T(8,128)(2,1)S(1)}, u32[]{:S(2)}, u32[]{:S(2)}) collective-permute-start(bf16[3,8,64,256]{3,2,1,0:T(8,128)(2,1)S(1)} %get-tuple-element.5), channel_id=1, source_target_pairs={{0,1},{1,2},{2,3},{3,4},{4,5},{5,6},{6,7},{7,8},{8,9},{9,10},{10,1... | collective-permute-start | bytes 2359304 | tf_op jit(solution)/shard_map/ppermute | solution.py:112
  117.6 6.1 %collective-permute-start.7 = (bf16[3,8,64,256]{3,2,1,0:T(8,128)(2,1)S(1)}, bf16[3,8,64,256]{3,2,1,0:T(8,128)(2,1)S(1)}, u32[]{:S(2)}, u32[]{:S(2)}) collective-permute-start(bf16[3,8,64,256]{3,2,1,0:T(8,128)(2,1)S(1)} %get-tuple-element.6), channel_id=1, source_target_pairs={{1,0},{2,1},{3,2},{4,3},{5,4},{6,5},{7,6},{8,7},{9,8},{10,9},{11,1... | collective-permute-start | bytes 2359304 | tf_op jit(solution)/shard_map/ppermute | solution.py:115
  137.2 73.8 %copy-start.3 = (bf16[6,8,64,256]{3,2,1,0:T(8,128)(2,1)S(1)}, bf16[6,8,64,256]{3,2,1,0:T(8,128)(2,1)}, u32[]{:S(2)}) copy-start(bf16[6,8,64,256]{3,2,1,0:T(8,128)(2,1)} %shard_map.40) | copy-start | bytes 4718596
  139.4 17.5 %collective-permute-start.12 = (f32[128,256]{1,0:T(8,128)S(1)}, f32[128,256]{1,0:T(8,128)S(1)}, u32[]{:S(2)}, u32[]{:S(2)}) collective-permute-start(f32[128,256]{1,0:T(8,128)S(1)} %fusion.2), channel_id=1, source_target_pairs={{1,0},{2,1},{3,2},{4,3},{5,4},{6,5},{7,6},{8,7},{9,8},{10,9},{11,1... | collective-permute-start | bytes 393224 | tf_op jit(solution)/shard_map/ppermute | solution.py:186
  140.7 17.2 %collective-permute-start.8 = (f32[128,256]{1,0:T(8,128)S(1)}, f32[128,256]{1,0:T(8,128)S(1)}, u32[]{:S(2)}, u32[]{:S(2)}) collective-permute-start(f32[128,256]{1,0:T(8,128)S(1)} %fusion.2), channel_id=1, source_target_pairs={{0,1},{1,2},{2,3},{3,4},{4,5},{5,6},{6,7},{7,8},{8,9},{9,10},{10,1... | collective-permute-start | bytes 393224 | tf_op jit(solution)/shard_map/ppermute | solution.py:185
  157.9 14.1 %collective-permute-start.9 = (f32[128,256]{1,0:T(8,128)S(1)}, f32[128,256]{1,0:T(8,128)S(1)}, u32[]{:S(2)}, u32[]{:S(2)}) collective-permute-start(f32[128,256]{1,0:T(8,128)S(1)} %get-tuple-element.13), channel_id=1, source_target_pairs={{0,2},{1,3},{2,4},{3,5},{4,6},{5,7},{6,8},{7,9},{8,10},{9,11},{10,... | collective-permute-start | bytes 393224 | tf_op jit(solution)/shard_map/ppermute | solution.py:185
  170.8 6.9 %collective-permute-start.13 = (f32[128,256]{1,0:T(8,128)S(1)}, f32[128,256]{1,0:T(8,128)S(1)}, u32[]{:S(2)}, u32[]{:S(2)}) collective-permute-start(f32[128,256]{1,0:T(8,128)S(1)} %get-tuple-element.14), channel_id=1, source_target_pairs={{2,0},{3,1},{4,2},{5,3},{6,4},{7,5},{8,6},{9,7},{10,8},{11,9},{12,... | collective-permute-start | bytes 393224 | tf_op jit(solution)/shard_map/ppermute | solution.py:186
  172.1 7.8 %collective-permute-start.10 = (f32[128,256]{1,0:T(8,128)S(1)}, f32[128,256]{1,0:T(8,128)S(1)}, u32[]{:S(2)}, u32[]{:S(2)}) collective-permute-start(f32[128,256]{1,0:T(8,128)S(1)} %multiply_add_fusion.4), channel_id=1, source_target_pairs={{0,4},{1,5},{2,6},{3,7},{4,8},{5,9},{6,10},{7,11},{8,12},{9,13},{1... | collective-permute-start | bytes 393224 | tf_op jit(solution)/shard_map/ppermute | solution.py:185
  177.6 6.9 %collective-permute-start.14 = (f32[128,256]{1,0:T(8,128)S(1)}, f32[128,256]{1,0:T(8,128)S(1)}, u32[]{:S(2)}, u32[]{:S(2)}) collective-permute-start(f32[128,256]{1,0:T(8,128)S(1)} %multiply_add_fusion.1), channel_id=1, source_target_pairs={{4,0},{5,1},{6,2},{7,3},{8,4},{9,5},{10,6},{11,7},{12,8},{13,9},{1... | collective-permute-start | bytes 393224 | tf_op jit(solution)/shard_map/ppermute | solution.py:186
  179.9 10.3 %collective-permute-start.11 = (f32[128,256]{1,0:T(8,128)S(1)}, f32[128,256]{1,0:T(8,128)S(1)}, u32[]{:S(2)}, u32[]{:S(2)}) collective-permute-start(f32[128,256]{1,0:T(8,128)S(1)} %multiply_add_fusion.3), channel_id=1, source_target_pairs={{0,8},{1,9},{2,10},{3,11},{4,12},{5,13},{6,14},{7,15},{16,24},{17,... | collective-permute-start | bytes 393224 | tf_op jit(solution)/shard_map/ppermute | solution.py:185
  184.5 8.9 %collective-permute-start.15 = (f32[128,256]{1,0:T(8,128)S(1)}, f32[128,256]{1,0:T(8,128)S(1)}, u32[]{:S(2)}, u32[]{:S(2)}) collective-permute-start(f32[128,256]{1,0:T(8,128)S(1)} %multiply_add_fusion), channel_id=1, source_target_pairs={{8,0},{9,1},{10,2},{11,3},{12,4},{13,5},{14,6},{15,7},{24,16},{25,... | collective-permute-start | bytes 393224 | tf_op jit(solution)/shard_map/ppermute | solution.py:186
  214.0 4.3 %collective-permute-start.20 = (f32[128,128]{1,0:T(8,128)S(1)}, f32[128,128]{1,0:T(8,128)S(1)}, u32[]{:S(2)}, u32[]{:S(2)}) collective-permute-start(f32[128,128]{1,0:T(8,128)S(1)} %fusion.16), channel_id=1, source_target_pairs={{1,0},{2,1},{3,2},{4,3},{5,4},{6,5},{7,6},{8,7},{9,8},{10,9},{11,1... | collective-permute-start | bytes 196616 | tf_op jit(solution)/shard_map/ppermute | solution.py:186
  215.3 3.9 %collective-permute-start.16 = (f32[128,128]{1,0:T(8,128)S(1)}, f32[128,128]{1,0:T(8,128)S(1)}, u32[]{:S(2)}, u32[]{:S(2)}) collective-permute-start(f32[128,128]{1,0:T(8,128)S(1)} %fusion.16), channel_id=1, source_target_pairs={{0,1},{1,2},{2,3},{3,4},{4,5},{5,6},{6,7},{7,8},{8,9},{9,10},{10,1... | collective-permute-start | bytes 196616 | tf_op jit(solution)/shard_map/ppermute | solution.py:185
  219.3 8.5 %collective-permute-start.17 = (f32[128,128]{1,0:T(8,128)S(1)}, f32[128,128]{1,0:T(8,128)S(1)}, u32[]{:S(2)}, u32[]{:S(2)}) collective-permute-start(f32[128,128]{1,0:T(8,128)S(1)} %get-tuple-element.15), channel_id=1, source_target_pairs={{0,2},{1,3},{2,4},{3,5},{4,6},{5,7},{6,8},{7,9},{8,10},{9,11},{10,... | collective-permute-start | bytes 196616 | tf_op jit(solution)/shard_map/ppermute | solution.py:185
  225.3 6.9 %collective-permute-start.21 = (f32[128,128]{1,0:T(8,128)S(1)}, f32[128,128]{1,0:T(8,128)S(1)}, u32[]{:S(2)}, u32[]{:S(2)}) collective-permute-start(f32[128,128]{1,0:T(8,128)S(1)} %get-tuple-element.16), channel_id=1, source_target_pairs={{2,0},{3,1},{4,2},{5,3},{6,4},{7,5},{8,6},{9,7},{10,8},{11,9},{12,... | collective-permute-start | bytes 196616 | tf_op jit(solution)/shard_map/ppermute | solution.py:186
  227.8 6.3 %collective-permute-start.18 = (f32[128,128]{1,0:T(8,128)S(1)}, f32[128,128]{1,0:T(8,128)S(1)}, u32[]{:S(2)}, u32[]{:S(2)}) collective-permute-start(f32[128,128]{1,0:T(8,128)S(1)} %multiply_add_fusion.10), channel_id=1, source_target_pairs={{0,4},{1,5},{2,6},{3,7},{4,8},{5,9},{6,10},{7,11},{8,12},{9,13},{1... | collective-permute-start | bytes 196616 | tf_op jit(solution)/shard_map/ppermute | solution.py:185
  232.2 6.2 %collective-permute-start.22 = (f32[128,128]{1,0:T(8,128)S(1)}, f32[128,128]{1,0:T(8,128)S(1)}, u32[]{:S(2)}, u32[]{:S(2)}) collective-permute-start(f32[128,128]{1,0:T(8,128)S(1)} %multiply_add_fusion.7), channel_id=1, source_target_pairs={{4,0},{5,1},{6,2},{7,3},{8,4},{9,5},{10,6},{11,7},{12,8},{13,9},{1... | collective-permute-start | bytes 196616 | tf_op jit(solution)/shard_map/ppermute | solution.py:186
  234.1 5.8 %collective-permute-start.19 = (f32[128,128]{1,0:T(8,128)S(1)}, f32[128,128]{1,0:T(8,128)S(1)}, u32[]{:S(2)}, u32[]{:S(2)}) collective-permute-start(f32[128,128]{1,0:T(8,128)S(1)} %multiply_add_fusion.9), channel_id=1, source_target_pairs={{0,8},{1,9},{2,10},{3,11},{4,12},{5,13},{6,14},{7,15},{16,24},{17,... | collective-permute-start | bytes 196616 | tf_op jit(solution)/shard_map/ppermute | solution.py:185
  238.4 7.8 %collective-permute-start.23 = (f32[128,128]{1,0:T(8,128)S(1)}, f32[128,128]{1,0:T(8,128)S(1)}, u32[]{:S(2)}, u32[]{:S(2)}) collective-permute-start(f32[128,128]{1,0:T(8,128)S(1)} %multiply_add_fusion.6), channel_id=1, source_target_pairs={{8,0},{9,1},{10,2},{11,3},{12,4},{13,5},{14,6},{15,7},{24,16},{25,... | collective-permute-start | bytes 196616 | tf_op jit(solution)/shard_map/ppermute | solution.py:186

commit v4 on v3

--- a/solution.py
+++ b/solution.py
@@ -21,8 +21,6 @@
 
 def _lower_inverse_kernel(gram_ref, out_ref, work_ref):
     n = gram_ref.shape[0]
-    rows = lax.broadcasted_iota(jnp.int32, (n, 2 * n), 0)
-    lanes = lax.broadcasted_iota(jnp.int32, (n, 2 * n), 1)
     work_ref[:, :n] = gram_ref[...]
     work_ref[:, n:] = (lax.broadcasted_iota(jnp.int32, (n, n), 0) == lax.broadcasted_iota(jnp.int32, (n, n), 1)).astype(jnp.float32)
 
@@ -32,11 +30,21 @@
         pivot = jnp.sum(jnp.where(lane == k, row, 0.0), axis=1, keepdims=True)
         scale = 1.0 / jnp.sqrt(pivot)
         scaled = row * scale
-        whole = work_ref[...]
-        left = whole[:, :n]
-        column = jnp.sum(jnp.where(lanes[:, :n] == k, left, 0.0), axis=1, keepdims=True) * scale
-        updated = jnp.where(rows > k, whole - column * scaled, whole)
-        work_ref[...] = jnp.where(rows == k, scaled, updated)
+        block_rows = lax.broadcasted_iota(jnp.int32, (8, 2 * n), 0)
+        block_lanes = lax.broadcasted_iota(jnp.int32, (8, n), 1)
+        for start in range(0, n, 8):
+
+            @pl.when(start + 7 >= k)
+            def _():
+                whole = work_ref[start : start + 8, :]
+                left = whole[:, :n]
+                column = (
+                    jnp.sum(jnp.where(block_lanes == k, left, 0.0), axis=1, keepdims=True) * scale
+                )
+                place = block_rows + start
+                updated = jnp.where(place > k, whole - column * scaled, whole)
+                work_ref[start : start + 8, :] = jnp.where(place == k, scaled, updated)
+
         return carry
 
     lax.fori_loop(0, n, step, 0)

time: 269 us -> 436 us (1.62)
  Pallas kernels: 80 us -> 247 us
    pallas_call x2, Pallas kernels: 33.9 us -> 201 us  [lower_inverse(): pl.pallas_call(_lower_inverse_kernel, out_shape=jax.ShapeDtypeStruct((n,...]
where the time goes in v4:
time: 436 us; the launch traced here: 434 us
  Pallas kernels  247 us (57%)
  starting transfers between devices  115 us (26%)
  waiting for transfers between devices  31.7 us (7%)
  local copies, waits for them, and re-layouts  12.4 us (3%)
  between operations  11.3 us (3%)
  other arithmetic  9.78 us (2%)
  matrix products  6.35 us (1%)
    pallas_call x2, Pallas kernels, lower_inverse(): pl.pallas_call(_lower_inverse_kernel, out_shape=jax.ShapeDtypeStruct((n,...  201 us
    ppermute x8, starting transfers between devices, domain_total(): from_low = lax.ppermute(forward, 'gz', ahead)  50.3 us
    ppermute x4, starting transfers between devices, extended_2(): lax.ppermute(lax.slice_in_dim(block, block.shape[dim] - width, None, axis...  49.4 us
    pallas_call x4, Pallas kernels, chebyshev_step(): pl.pallas_call(functools.partial(_step_kernel, first), out_shape=jax.Shap...  46.1 us
    ppermute x4, waiting for transfers between devices, extended_2(): lax.ppermute(lax.slice_in_dim(block, 0, width, axis=dim), axis, backward)  14.4 us
    ppermute x8, waiting for transfers between devices, domain_total(): from_high = lax.ppermute(backward, 'gz', behind)  11 us
    ppermute x8, starting transfers between devices, domain_total(): from_high = lax.ppermute(backward, 'gz', behind)  10.3 us
  transfers between devices with their start and end apart: 24, of which 18 were waited for; matrix products, arithmetic and copies ran while one was open for 1% of the time, Pallas kernels for 0%

profile of v4, /device:TPU:0, one launch (start us, length us, event | category | flops | bytes accessed | tf_op | source)
XLA Modules:
  0.0 434.0 jit_solution(3332138599642441890)
XLA Ops:
  0.0 2.8 fusion.14
  2.8 2.4 collective-permute-start
  5.3 1.3 collective-permute-start.1
  6.6 0.7 fusion.15
  10.0 1.7 collective-permute-done.1
  11.7 1.9 maximum_multiply_fusion.extended_ref
  13.6 1.6 broadcast_in_dim.17.potential_ref
  15.2 11.4 %shard_map.37.older_ref = bf16[6,8,64,256]{3,2,1,0:T(8,128)(2,1)} custom-call(bf16[12,8,64,256]{3,2,1,0:T(8,128)(2,1)} %maximum_multiply_fusion.extended_ref, bf16[6,8,64,256]{3,2,1,0:T(8,128)(2,1)} %older_ref.3, f32[6,8,64,128]{3,2,1,0:T(8,128)} %broadcast_in_dim.17.potential_ref), custom_call_target="tpu_custom_call" | custom-call | tf_op jit(solution)/shard_map/pallas_call | solution.py:102
  26.7 1.7 fusion.13
  28.3 15.7 %collective-permute-start.2 = (bf16[3,8,64,256]{3,2,1,0:T(8,128)(2,1)S(1)}, bf16[3,8,64,256]{3,2,1,0:T(8,128)(2,1)S(1)}, u32[]{:S(2)}, u32[]{:S(2)}) collective-permute-start(bf16[3,8,64,256]{3,2,1,0:T(8,128)(2,1)S(1)} %get-tuple-element.9), channel_id=1, source_target_pairs={{0,1},{1,2},{2,3},{3,4},{4,5},{5,6},{6,7},{7,8},{8,9},{9,10},{10,1... | collective-permute-start | bytes 2359304 | tf_op jit(solution)/shard_map/ppermute | solution.py:120
  44.1 1.3 collective-permute-start.3
  45.4 0.5 collective-permute-done.2
  45.9 4.2 collective-permute-done.3
  50.1 1.9 maximum_multiply_fusion.1.extended_ref
  52.0 11.5 %shard_map.38.older_ref = bf16[6,8,64,256]{3,2,1,0:T(8,128)(2,1)} custom-call(bf16[12,8,64,256]{3,2,1,0:T(8,128)(2,1)} %maximum_multiply_fusion.1.extended_ref, bf16[6,8,64,256]{3,2,1,0:T(8,128)(2,1)} %older_ref.3, f32[6,8,64,128]{3,2,1,0:T(8,128)} %broadcast_in_dim.17.potential_ref), custom_call_target="tpu_custom_call" | custom-call | tf_op jit(solution)/shard_map/pallas_call | solution.py:102
  63.5 1.7 fusion.12
  65.2 15.6 %collective-permute-start.4 = (bf16[3,8,64,256]{3,2,1,0:T(8,128)(2,1)S(1)}, bf16[3,8,64,256]{3,2,1,0:T(8,128)(2,1)S(1)}, u32[]{:S(2)}, u32[]{:S(2)}) collective-permute-start(bf16[3,8,64,256]{3,2,1,0:T(8,128)(2,1)S(1)} %get-tuple-element.7), channel_id=1, source_target_pairs={{0,1},{1,2},{2,3},{3,4},{4,5},{5,6},{6,7},{7,8},{8,9},{9,10},{10,1... | collective-permute-start | bytes 2359304 | tf_op jit(solution)/shard_map/ppermute | solution.py:120
  80.8 1.3 collective-permute-start.5
  82.1 0.5 collective-permute-done.4
  82.6 4.3 collective-permute-done.5
  86.9 1.9 maximum_multiply_fusion.2.extended_ref
  88.8 11.6 %shard_map.39 = bf16[6,8,64,256]{3,2,1,0:T(8,128)(2,1)} custom-call(bf16[12,8,64,256]{3,2,1,0:T(8,128)(2,1)} %maximum_multiply_fusion.2.extended_ref, bf16[6,8,64,256]{3,2,1,0:T(8,128)(2,1)} %shard_map.37.older_ref, f32[6,8,64,128]{3,2,1,0:T(8,128)} %broadcast_in_dim.17.potential_ref), custom_call_target="tpu_custom_call" | custom-call | tf_op jit(solution)/shard_map/pallas_call | solution.py:102
  100.4 1.7 fusion.11
  102.0 15.6 %collective-permute-start.6 = (bf16[3,8,64,256]{3,2,1,0:T(8,128)(2,1)S(1)}, bf16[3,8,64,256]{3,2,1,0:T(8,128)(2,1)S(1)}, u32[]{:S(2)}, u32[]{:S(2)}) collective-permute-start(bf16[3,8,64,256]{3,2,1,0:T(8,128)(2,1)S(1)} %get-tuple-element.5), channel_id=1, source_target_pairs={{0,1},{1,2},{2,3},{3,4},{4,5},{5,6},{6,7},{7,8},{8,9},{9,10},{10,1... | collective-permute-start | bytes 2359304 | tf_op jit(solution)/shard_map/ppermute | solution.py:120
  117.6 1.3 collective-permute-start.7
  118.9 0.5 collective-permute-done.6
  119.5 4.3 collective-permute-done.7
  123.8 1.9 maximum_multiply_fusion.3.extended_ref
  125.6 11.6 %shard_map.40 = bf16[6,8,64,256]{3,2,1,0:T(8,128)(2,1)} custom-call(bf16[12,8,64,256]{3,2,1,0:T(8,128)(2,1)} %maximum_multiply_fusion.3.extended_ref, bf16[6,8,64,256]{3,2,1,0:T(8,128)(2,1)} %shard_map.38.older_ref, f32[6,8,64,128]{3,2,1,0:T(8,128)} %broadcast_in_dim.17.potential_ref), custom_call_target="tpu_custom_call" | custom-call | tf_op jit(solution)/shard_map/pallas_call | solution.py:102
  137.2 2.2 fusion.2
  139.4 1.3 collective-permute-start.12
  140.7 16.2 %collective-permute-start.8 = (f32[128,256]{1,0:T(8,128)S(1)}, f32[128,256]{1,0:T(8,128)S(1)}, u32[]{:S(2)}, u32[]{:S(2)}) collective-permute-start(f32[128,256]{1,0:T(8,128)S(1)} %fusion.2), channel_id=1, source_target_pairs={{0,1},{1,2},{2,3},{3,4},{4,5},{5,6},{6,7},{7,8},{8,9},{9,10},{10,1... | collective-permute-start | bytes 393224 | tf_op jit(solution)/shard_map/ppermute | solution.py:193
  157.0 0.9 collective-permute-done.8
  157.9 7.7 %collective-permute-start.9 = (f32[128,256]{1,0:T(8,128)S(1)}, f32[128,256]{1,0:T(8,128)S(1)}, u32[]{:S(2)}, u32[]{:S(2)}) collective-permute-start(f32[128,256]{1,0:T(8,128)S(1)} %get-tuple-element.13), channel_id=1, source_target_pairs={{0,2},{1,3},{2,4},{3,5},{4,6},{5,7},{6,8},{7,9},{8,10},{9,11},{10,... | collective-permute-start | bytes 393224 | tf_op jit(solution)/shard_map/ppermute | solution.py:193
  170.8 1.3 collective-permute-start.13
  172.1 5.3 %collective-permute-start.10 = (f32[128,256]{1,0:T(8,128)S(1)}, f32[128,256]{1,0:T(8,128)S(1)}, u32[]{:S(2)}, u32[]{:S(2)}) collective-permute-start(f32[128,256]{1,0:T(8,128)S(1)} %multiply_add_fusion.4), channel_id=1, source_target_pairs={{0,4},{1,5},{2,6},{3,7},{4,8},{5,9},{6,10},{7,11},{8,12},{9,13},{1... | collective-permute-start | bytes 393224 | tf_op jit(solution)/shard_map/ppermute | solution.py:193
  177.6 1.3 collective-permute-start.14
  178.9 0.9 collective-permute-done.10
  179.9 3.8 collective-permute-start.11
  183.7 0.8 collective-permute-done.14
  184.5 1.3 collective-permute-start.15
  188.3 1.2 fusion.10
  190.2 3.2 collective-permute-done.15
  193.5 0.6 slice.55.gram_ref
  194.1 100.6 %shard_map.41 = f32[128,128]{1,0:T(8,128)} custom-call(f32[128,128]{1,0:T(8,128)} %slice.55.gram_ref), custom_call_target="tpu_custom_call" | custom-call | tf_op jit(solution)/shard_map/pallas_call | solution.py:56
  294.7 1.2 convolution_convert_fusion.1
  296.0 1.3 fusion
  297.7 1.3 collective-permute-start.20
  299.0 3.0 collective-permute-start.16
  302.1 0.9 collective-permute-done.16
  303.0 6.0 %collective-permute-start.17 = (f32[128,128]{1,0:T(8,128)S(1)}, f32[128,128]{1,0:T(8,128)S(1)}, u32[]{:S(2)}, u32[]{:S(2)}) collective-permute-start(f32[128,128]{1,0:T(8,128)S(1)} %get-tuple-element.15), channel_id=1, source_target_pairs={{0,2},{1,3},{2,4},{3,5},{4,6},{5,7},{6,8},{7,9},{8,10},{9,11},{10,... | collective-permute-start | bytes 196616 | tf_op jit(solution)/shard_map/ppermute | solution.py:193
  309.0 1.3 collective-permute-start.21
  310.3 1.2 collective-permute-done.17
  311.5 4.4 %collective-permute-start.18 = (f32[128,128]{1,0:T(8,128)S(1)}, f32[128,128]{1,0:T(8,128)S(1)}, u32[]{:S(2)}, u32[]{:S(2)}) collective-permute-start(f32[128,128]{1,0:T(8,128)S(1)} %multiply_add_fusion.10), channel_id=1, source_target_pairs={{0,4},{1,5},{2,6},{3,7},{4,8},{5,9},{6,10},{7,11},{8,12},{9,13},{1... | collective-permute-start | bytes 196616 | tf_op jit(solution)/shard_map/ppermute | solution.py:193
  315.9 1.3 collective-permute-start.22
  317.2 0.6 collective-permute-done.18
  317.8 3.9 collective-permute-start.19
  321.7 0.4 collective-permute-done.22
  322.1 1.3 collective-permute-start.23
  323.5 6.3 %collective-permute-done.23 = f32[128,128]{1,0:T(8,128)S(1)} collective-permute-done((f32[128,128]{1,0:T(8,128)S(1)}, f32[128,128]{1,0:T(8,128)S(1)}, u32[]{:S(2)}, u32[]{:S(2)}) %collective-permute-start.23) | collective-permute-done | bytes 65568 | tf_op jit(solution)/shard_map/ppermute | solution.py:194
  329.9 0.7 subtract_divide_fusion.1.gram_ref
  330.5 100.6 %shard_map.42 = f32[128,128]{1,0:T(8,128)} custom-call(f32[128,128]{1,0:T(8,128)} %subtract_divide_fusion.1.gram_ref), custom_call_target="tpu_custom_call" | custom-call | tf_op jit(solution)/shard_map/pallas_call | solution.py:56
  431.1 1.2 convolution_convert_fusion
  432.5 1.6 copy.5
  (40 shorter events, 1.3 us)
Async XLA Ops:
  0.0 11.7 %copy-start = (bf16[6,8,64,256]{3,2,1,0:T(8,128)(2,1)S(1)}, bf16[6,8,64,256]{3,2,1,0:T(8,128)(2,1)}, u32[]{:S(2)}) copy-start(bf16[6,8,64,256]{3,2,1,0:T(8,128)(2,1)} %older_ref.3) | copy-start | bytes 4718596
  0.0 6.6 %copy-start.5 = (s32[16]{0:T(128)S(1)}, s32[16]{0:T(128)}, u32[]{:S(2)}) copy-start(s32[16]{0:T(128)} %param.5) | copy-start | bytes 196
  0.0 9.9 %copy-start.6 = (f32[6,512]{1,0:T(8,128)S(1)}, f32[6,512]{1,0:T(8,128)}, u32[]{:S(2)}) copy-start(f32[6,512]{1,0:T(8,128)} %param.4) | copy-start | bytes 36868
  2.8 7.2 %collective-permute-start = (bf16[3,8,64,256]{3,2,1,0:T(8,128)(2,1)}, bf16[3,8,64,256]{3,2,1,0:T(8,128)(2,1)S(1)}, u32[]{:S(2)}, u32[]{:S(2)}) collective-permute-start(bf16[3,8,64,256]{3,2,1,0:T(8,128)(2,1)} %get-tuple-element.11), channel_id=1, source_target_pairs={{0,1},{1,2},{2,3},{3,4},{4,5},{5,6},{6,7},{7,8},{8,9},{9,10},{10,1... | collective-permute-start | bytes 2359304 | tf_op jit(solution)/shard_map/ppermute | solution.py:120
  5.3 6.5 %collective-permute-start.1 = (bf16[3,8,64,256]{3,2,1,0:T(8,128)(2,1)}, bf16[3,8,64,256]{3,2,1,0:T(8,128)(2,1)S(1)}, u32[]{:S(2)}, u32[]{:S(2)}) collective-permute-start(bf16[3,8,64,256]{3,2,1,0:T(8,128)(2,1)} %get-tuple-element.12), channel_id=1, source_target_pairs={{1,0},{2,1},{3,2},{4,3},{5,4},{6,5},{7,6},{8,7},{9,8},{10,9},{11,1... | collective-permute-start | bytes 2359304 | tf_op jit(solution)/shard_map/ppermute | solution.py:123
  26.7 23.4 %copy-start.2 = (bf16[6,8,64,256]{3,2,1,0:T(8,128)(2,1)S(1)}, bf16[6,8,64,256]{3,2,1,0:T(8,128)(2,1)}, u32[]{:S(2)}) copy-start(bf16[6,8,64,256]{3,2,1,0:T(8,128)(2,1)} %shard_map.37.older_ref) | copy-start | bytes 4718596
  28.3 17.6 %collective-permute-start.2 = (bf16[3,8,64,256]{3,2,1,0:T(8,128)(2,1)S(1)}, bf16[3,8,64,256]{3,2,1,0:T(8,128)(2,1)S(1)}, u32[]{:S(2)}, u32[]{:S(2)}) collective-permute-start(bf16[3,8,64,256]{3,2,1,0:T(8,128)(2,1)S(1)} %get-tuple-element.9), channel_id=1, source_target_pairs={{0,1},{1,2},{2,3},{3,4},{4,5},{5,6},{6,7},{7,8},{8,9},{9,10},{10,1... | collective-permute-start | bytes 2359304 | tf_op jit(solution)/shard_map/ppermute | solution.py:120
  44.1 6.0 %collective-permute-start.3 = (bf16[3,8,64,256]{3,2,1,0:T(8,128)(2,1)S(1)}, bf16[3,8,64,256]{3,2,1,0:T(8,128)(2,1)S(1)}, u32[]{:S(2)}, u32[]{:S(2)}) collective-permute-start(bf16[3,8,64,256]{3,2,1,0:T(8,128)(2,1)S(1)} %get-tuple-element.10), channel_id=1, source_target_pairs={{1,0},{2,1},{3,2},{4,3},{5,4},{6,5},{7,6},{8,7},{9,8},{10,9},{11,1... | collective-permute-start | bytes 2359304 | tf_op jit(solution)/shard_map/ppermute | solution.py:123
  63.5 23.4 %copy-start.1 = (bf16[6,8,64,256]{3,2,1,0:T(8,128)(2,1)S(1)}, bf16[6,8,64,256]{3,2,1,0:T(8,128)(2,1)}, u32[]{:S(2)}) copy-start(bf16[6,8,64,256]{3,2,1,0:T(8,128)(2,1)} %shard_map.38.older_ref) | copy-start | bytes 4718596
  65.2 17.5 %collective-permute-start.4 = (bf16[3,8,64,256]{3,2,1,0:T(8,128)(2,1)S(1)}, bf16[3,8,64,256]{3,2,1,0:T(8,128)(2,1)S(1)}, u32[]{:S(2)}, u32[]{:S(2)}) collective-permute-start(bf16[3,8,64,256]{3,2,1,0:T(8,128)(2,1)S(1)} %get-tuple-element.7), channel_id=1, source_target_pairs={{0,1},{1,2},{2,3},{3,4},{4,5},{5,6},{6,7},{7,8},{8,9},{9,10},{10,1... | collective-permute-start | bytes 2359304 | tf_op jit(solution)/shard_map/ppermute | solution.py:120
  80.8 6.1 %collective-permute-start.5 = (bf16[3,8,64,256]{3,2,1,0:T(8,128)(2,1)S(1)}, bf16[3,8,64,256]{3,2,1,0:T(8,128)(2,1)S(1)}, u32[]{:S(2)}, u32[]{:S(2)}) collective-permute-start(bf16[3,8,64,256]{3,2,1,0:T(8,128)(2,1)S(1)} %get-tuple-element.8), channel_id=1, source_target_pairs={{1,0},{2,1},{3,2},{4,3},{5,4},{6,5},{7,6},{8,7},{9,8},{10,9},{11,1... | collective-permute-start | bytes 2359304 | tf_op jit(solution)/shard_map/ppermute | solution.py:123
  100.4 23.4 %copy-start.4 = (bf16[6,8,64,256]{3,2,1,0:T(8,128)(2,1)S(1)}, bf16[6,8,64,256]{3,2,1,0:T(8,128)(2,1)}, u32[]{:S(2)}) copy-start(bf16[6,8,64,256]{3,2,1,0:T(8,128)(2,1)} %shard_map.39) | copy-start | bytes 4718596
  102.0 17.5 %collective-permute-start.6 = (bf16[3,8,64,256]{3,2,1,0:T(8,128)(2,1)S(1)}, bf16[3,8,64,256]{3,2,1,0:T(8,128)(2,1)S(1)}, u32[]{:S(2)}, u32[]{:S(2)}) collective-permute-start(bf16[3,8,64,256]{3,2,1,0:T(8,128)(2,1)S(1)} %get-tuple-element.5), channel_id=1, source_target_pairs={{0,1},{1,2},{2,3},{3,4},{4,5},{5,6},{6,7},{7,8},{8,9},{9,10},{10,1... | collective-permute-start | bytes 2359304 | tf_op jit(solution)/shard_map/ppermute | solution.py:120
  117.6 6.1 %collective-permute-start.7 = (bf16[3,8,64,256]{3,2,1,0:T(8,128)(2,1)S(1)}, bf16[3,8,64,256]{3,2,1,0:T(8,128)(2,1)S(1)}, u32[]{:S(2)}, u32[]{:S(2)}) collective-permute-start(bf16[3,8,64,256]{3,2,1,0:T(8,128)(2,1)S(1)} %get-tuple-element.6), channel_id=1, source_target_pairs={{1,0},{2,1},{3,2},{4,3},{5,4},{6,5},{7,6},{8,7},{9,8},{10,9},{11,1... | collective-permute-start | bytes 2359304 | tf_op jit(solution)/shard_map/ppermute | solution.py:123
  137.2 157.5 %copy-start.3 = (bf16[6,8,64,256]{3,2,1,0:T(8,128)(2,1)S(1)}, bf16[6,8,64,256]{3,2,1,0:T(8,128)(2,1)}, u32[]{:S(2)}) copy-start(bf16[6,8,64,256]{3,2,1,0:T(8,128)(2,1)} %shard_map.40) | copy-start | bytes 4718596
  139.4 17.5 %collective-permute-start.12 = (f32[128,256]{1,0:T(8,128)S(1)}, f32[128,256]{1,0:T(8,128)S(1)}, u32[]{:S(2)}, u32[]{:S(2)}) collective-permute-start(f32[128,256]{1,0:T(8,128)S(1)} %fusion.2), channel_id=1, source_target_pairs={{1,0},{2,1},{3,2},{4,3},{5,4},{6,5},{7,6},{8,7},{9,8},{10,9},{11,1... | collective-permute-start | bytes 393224 | tf_op jit(solution)/shard_map/ppermute | solution.py:194
  140.7 17.2 %collective-permute-start.8 = (f32[128,256]{1,0:T(8,128)S(1)}, f32[128,256]{1,0:T(8,128)S(1)}, u32[]{:S(2)}, u32[]{:S(2)}) collective-permute-start(f32[128,256]{1,0:T(8,128)S(1)} %fusion.2), channel_id=1, source_target_pairs={{0,1},{1,2},{2,3},{3,4},{4,5},{5,6},{6,7},{7,8},{8,9},{9,10},{10,1... | collective-permute-start | bytes 393224 | tf_op jit(solution)/shard_map/ppermute | solution.py:193
  157.9 14.1 %collective-permute-start.9 = (f32[128,256]{1,0:T(8,128)S(1)}, f32[128,256]{1,0:T(8,128)S(1)}, u32[]{:S(2)}, u32[]{:S(2)}) collective-permute-start(f32[128,256]{1,0:T(8,128)S(1)} %get-tuple-element.13), channel_id=1, source_target_pairs={{0,2},{1,3},{2,4},{3,5},{4,6},{5,7},{6,8},{7,9},{8,10},{9,11},{10,... | collective-permute-start | bytes 393224 | tf_op jit(solution)/shard_map/ppermute | solution.py:193
  170.8 6.9 %collective-permute-start.13 = (f32[128,256]{1,0:T(8,128)S(1)}, f32[128,256]{1,0:T(8,128)S(1)}, u32[]{:S(2)}, u32[]{:S(2)}) collective-permute-start(f32[128,256]{1,0:T(8,128)S(1)} %get-tuple-element.14), channel_id=1, source_target_pairs={{2,0},{3,1},{4,2},{5,3},{6,4},{7,5},{8,6},{9,7},{10,8},{11,9},{12,... | collective-permute-start | bytes 393224 | tf_op jit(solution)/shard_map/ppermute | solution.py:194
  172.1 7.8 %collective-permute-start.10 = (f32[128,256]{1,0:T(8,128)S(1)}, f32[128,256]{1,0:T(8,128)S(1)}, u32[]{:S(2)}, u32[]{:S(2)}) collective-permute-start(f32[128,256]{1,0:T(8,128)S(1)} %multiply_add_fusion.4), channel_id=1, source_target_pairs={{0,4},{1,5},{2,6},{3,7},{4,8},{5,9},{6,10},{7,11},{8,12},{9,13},{1... | collective-permute-start | bytes 393224 | tf_op jit(solution)/shard_map/ppermute | solution.py:193
  177.6 6.9 %collective-permute-start.14 = (f32[128,256]{1,0:T(8,128)S(1)}, f32[128,256]{1,0:T(8,128)S(1)}, u32[]{:S(2)}, u32[]{:S(2)}) collective-permute-start(f32[128,256]{1,0:T(8,128)S(1)} %multiply_add_fusion.1), channel_id=1, source_target_pairs={{4,0},{5,1},{6,2},{7,3},{8,4},{9,5},{10,6},{11,7},{12,8},{13,9},{1... | collective-permute-start | bytes 393224 | tf_op jit(solution)/shard_map/ppermute | solution.py:194
  179.9 10.3 %collective-permute-start.11 = (f32[128,256]{1,0:T(8,128)S(1)}, f32[128,256]{1,0:T(8,128)S(1)}, u32[]{:S(2)}, u32[]{:S(2)}) collective-permute-start(f32[128,256]{1,0:T(8,128)S(1)} %multiply_add_fusion.3), channel_id=1, source_target_pairs={{0,8},{1,9},{2,10},{3,11},{4,12},{5,13},{6,14},{7,15},{16,24},{17,... | collective-permute-start | bytes 393224 | tf_op jit(solution)/shard_map/ppermute | solution.py:193
  184.5 8.9 %collective-permute-start.15 = (f32[128,256]{1,0:T(8,128)S(1)}, f32[128,256]{1,0:T(8,128)S(1)}, u32[]{:S(2)}, u32[]{:S(2)}) collective-permute-start(f32[128,256]{1,0:T(8,128)S(1)} %multiply_add_fusion), channel_id=1, source_target_pairs={{8,0},{9,1},{10,2},{11,3},{12,4},{13,5},{14,6},{15,7},{24,16},{25,... | collective-permute-start | bytes 393224 | tf_op jit(solution)/shard_map/ppermute | solution.py:194
  297.7 4.3 %collective-permute-start.20 = (f32[128,128]{1,0:T(8,128)S(1)}, f32[128,128]{1,0:T(8,128)S(1)}, u32[]{:S(2)}, u32[]{:S(2)}) collective-permute-start(f32[128,128]{1,0:T(8,128)S(1)} %fusion.16), channel_id=1, source_target_pairs={{1,0},{2,1},{3,2},{4,3},{5,4},{6,5},{7,6},{8,7},{9,8},{10,9},{11,1... | collective-permute-start | bytes 196616 | tf_op jit(solution)/shard_map/ppermute | solution.py:194
  299.0 3.9 collective-permute-start.16
  303.0 8.5 %collective-permute-start.17 = (f32[128,128]{1,0:T(8,128)S(1)}, f32[128,128]{1,0:T(8,128)S(1)}, u32[]{:S(2)}, u32[]{:S(2)}) collective-permute-start(f32[128,128]{1,0:T(8,128)S(1)} %get-tuple-element.15), channel_id=1, source_target_pairs={{0,2},{1,3},{2,4},{3,5},{4,6},{5,7},{6,8},{7,9},{8,10},{9,11},{10,... | collective-permute-start | bytes 196616 | tf_op jit(solution)/shard_map/ppermute | solution.py:193
  309.0 6.9 %collective-permute-start.21 = (f32[128,128]{1,0:T(8,128)S(1)}, f32[128,128]{1,0:T(8,128)S(1)}, u32[]{:S(2)}, u32[]{:S(2)}) collective-permute-start(f32[128,128]{1,0:T(8,128)S(1)} %get-tuple-element.16), channel_id=1, source_target_pairs={{2,0},{3,1},{4,2},{5,3},{6,4},{7,5},{8,6},{9,7},{10,8},{11,9},{12,... | collective-permute-start | bytes 196616 | tf_op jit(solution)/shard_map/ppermute | solution.py:194
  311.5 6.3 %collective-permute-start.18 = (f32[128,128]{1,0:T(8,128)S(1)}, f32[128,128]{1,0:T(8,128)S(1)}, u32[]{:S(2)}, u32[]{:S(2)}) collective-permute-start(f32[128,128]{1,0:T(8,128)S(1)} %multiply_add_fusion.10), channel_id=1, source_target_pairs={{0,4},{1,5},{2,6},{3,7},{4,8},{5,9},{6,10},{7,11},{8,12},{9,13},{1... | collective-permute-start | bytes 196616 | tf_op jit(solution)/shard_map/ppermute | solution.py:193
  315.9 6.2 %collective-permute-start.22 = (f32[128,128]{1,0:T(8,128)S(1)}, f32[128,128]{1,0:T(8,128)S(1)}, u32[]{:S(2)}, u32[]{:S(2)}) collective-permute-start(f32[128,128]{1,0:T(8,128)S(1)} %multiply_add_fusion.7), channel_id=1, source_target_pairs={{4,0},{5,1},{6,2},{7,3},{8,4},{9,5},{10,6},{11,7},{12,8},{13,9},{1... | collective-permute-start | bytes 196616 | tf_op jit(solution)/shard_map/ppermute | solution.py:194
  317.8 5.8 %collective-permute-start.19 = (f32[128,128]{1,0:T(8,128)S(1)}, f32[128,128]{1,0:T(8,128)S(1)}, u32[]{:S(2)}, u32[]{:S(2)}) collective-permute-start(f32[128,128]{1,0:T(8,128)S(1)} %multiply_add_fusion.9), channel_id=1, source_target_pairs={{0,8},{1,9},{2,10},{3,11},{4,12},{5,13},{6,14},{7,15},{16,24},{17,... | collective-permute-start | bytes 196616 | tf_op jit(solution)/shard_map/ppermute | solution.py:193
  322.1 7.8 %collective-permute-start.23 = (f32[128,128]{1,0:T(8,128)S(1)}, f32[128,128]{1,0:T(8,128)S(1)}, u32[]{:S(2)}, u32[]{:S(2)}) collective-permute-start(f32[128,128]{1,0:T(8,128)S(1)} %multiply_add_fusion.6), channel_id=1, source_target_pairs={{8,0},{9,1},{10,2},{11,3},{12,4},{13,5},{14,6},{15,7},{24,16},{25,... | collective-permute-start | bytes 196616 | tf_op jit(solution)/shard_map/ppermute | solution.py:194

commit v5 on v4

--- a/solution.py
+++ b/solution.py
@@ -60,56 +60,74 @@
     )(gram)
 
 
-def _step_kernel(first, extended_ref, older_ref, potential_ref, out_ref):
+def _step_kernel(first, extended_ref, older_low_ref, older_high_ref, low_pot_ref, high_pot_ref,
+                 low_ref, high_ref):
     z = pl.program_id(1)
+    half = (extended_ref.shape[0] - 6) // 2
     rows_y = extended_ref.shape[1]
     rows_x = extended_ref.shape[2]
     place = lax.broadcasted_iota(jnp.int32, (rows_x, extended_ref.shape[3]), 0)
 
-    def plane(offset, y):
-        return extended_ref[z + 3 + offset, y].astype(jnp.float32)
-
-    for y in range(rows_y):
-        inner = plane(0, y)
-        total = 3.0 * COEF[0] * inner
-        for distance in (1, 2, 3):
-            along_z = plane(distance, y) + plane(-distance, y)
-            up = plane(0, y + distance) if y + distance < rows_y else None
-            down = plane(0, y - distance) if y - distance >= 0 else None
-            if up is None:
-                along_y = down
-            elif down is None:
-                along_y = up
+    def one_plane(centre, older_ref, potential_ref, out_ref):
+        def plane(offset, y):
+            return extended_ref[centre + offset, y].astype(jnp.float32)
+
+        for y in range(rows_y):
+            inner = plane(0, y)
+            total = 3.0 * COEF[0] * inner
+            for distance in (1, 2, 3):
+                along_z = plane(distance, y) + plane(-distance, y)
+                up = plane(0, y + distance) if y + distance < rows_y else None
+                down = plane(0, y - distance) if y - distance >= 0 else None
+                if up is None:
+                    along_y = down
+                elif down is None:
+                    along_y = up
+                else:
+                    along_y = up + down
+                ahead = jnp.where(
+                    place + distance < rows_x, pltpu.roll(inner, rows_x - distance, 0), 0.0
+                )
+                behind = jnp.where(place >= distance, pltpu.roll(inner, distance, 0), 0.0)
+                along_x = ahead + behind
+                total = total + COEF[distance] * (along_z + along_y + along_x)
+            image = potential_ref[0, y] * inner - 0.5 * total
+            if first:
+                newer = (image - CSHIFT * inner) / EWIDTH
             else:
-                along_y = up + down
-            ahead = jnp.where(place + distance < rows_x, pltpu.roll(inner, rows_x - distance, 0), 0.0)
-            behind = jnp.where(place >= distance, pltpu.roll(inner, distance, 0), 0.0)
-            along_x = ahead + behind
-            total = total + COEF[distance] * (along_z + along_y + along_x)
-        image = potential_ref[0, y] * inner - 0.5 * total
-        if first:
-            newer = (image - CSHIFT * inner) / EWIDTH
-        else:
-            newer = 2.0 / EWIDTH * (image - CSHIFT * inner) - older_ref[0, y].astype(jnp.float32)
-        out_ref[0, y] = newer.astype(out_ref.dtype)
-
-
-def chebyshev_step(extended, older, potential, first):
-    planes = older.shape[0]
-    rows_y, rows_x, bands = older.shape[1:]
+                newer = 2.0 / EWIDTH * (image - CSHIFT * inner) - older_ref[0, y].astype(
+                    jnp.float32
+                )
+            out_ref[0, y] = newer.astype(out_ref.dtype)
+
+    one_plane(z + 3, older_low_ref, low_pot_ref, low_ref)
+    one_plane(z + 3 + half, older_high_ref, high_pot_ref, high_ref)
+
+
+def chebyshev_step(extended, older_low, older_high, potential, first):
+    half = (extended.shape[0] - 6) // 2
+    rows_y, rows_x, bands = extended.shape[1:]
     lanes = 128
-    grid = (bands // lanes, planes)
+    grid = (bands // lanes, half)
+    block = (1, rows_y, rows_x, lanes)
+    high_shift = half if older_high.shape[0] == 2 * half else 0
+    piece = jax.ShapeDtypeStruct((half, rows_y, rows_x, bands), jnp.bfloat16)
     return pl.pallas_call(
         functools.partial(_step_kernel, first),
-        out_shape=jax.ShapeDtypeStruct(older.shape, jnp.bfloat16),
+        out_shape=(piece, piece),
         grid=grid,
         in_specs=[
-            pl.BlockSpec((planes + 6, rows_y, rows_x, lanes), lambda j, z: (0, 0, 0, j)),
-            pl.BlockSpec((1, rows_y, rows_x, lanes), lambda j, z: (z, 0, 0, j)),
-            pl.BlockSpec((1, rows_y, rows_x, lanes), lambda j, z: (z, 0, 0, 0)),
+            pl.BlockSpec((2 * half + 6, rows_y, rows_x, lanes), lambda j, z: (0, 0, 0, j)),
+            pl.BlockSpec(block, lambda j, z: (z, 0, 0, j)),
+            pl.BlockSpec(block, lambda j, z: (z + high_shift, 0, 0, j)),
+            pl.BlockSpec(block, lambda j, z: (z, 0, 0, 0)),
+            pl.BlockSpec(block, lambda j, z: (z + half, 0, 0, 0)),
         ],
-        out_specs=pl.BlockSpec((1, rows_y, rows_x, lanes), lambda j, z: (z, 0, 0, j)),
-    )(extended, older, potential)
+        out_specs=(
+            pl.BlockSpec(block, lambda j, z: (z, 0, 0, j)),
+            pl.BlockSpec(block, lambda j, z: (z, 0, 0, j)),
+        ),
+    )(extended, older_low, older_high, potential, potential)
 
 
 def extended_2(block, sides, width):
@@ -171,15 +189,25 @@
         ]
     )[:, None, None, None]
 
-    def rimmed(field):
-        return extended_2(field, (("gz", 0),), 3) * mask_three.astype(jnp.bfloat16)
+    forward = [(i, i + 1) for i in range(slabs - 1)]
+    backward = [(target, source) for source, target in forward]
+    bf_below = below.astype(jnp.bfloat16)
+    bf_above = above.astype(jnp.bfloat16)
+
+    def rimmed(low, high):
+        from_below = lax.ppermute(high, "gz", forward)
+        from_above = lax.ppermute(low, "gz", backward)
+        return jnp.concatenate([from_below * bf_below, low, high, from_above * bf_above], axis=0)
 
     lanes = jnp.broadcast_to(grid[..., None], grid.shape + (128,))
-    older = waves
-    current = chebyshev_step(rimmed(waves), waves, lanes, True)
+    half = planes // 2
+    low, high = chebyshev_step(rimmed(waves[:half], waves[half:]), waves, waves, lanes, True)
+    older_low, older_high = waves, waves
     for turn in range(DEGREE - 1):
-        newer = chebyshev_step(rimmed(current), older, lanes, False)
-        older, current = (current, newer)
+        newer = chebyshev_step(rimmed(low, high), older_low, older_high, lanes, False)
+        older_low, older_high = low, high
+        low, high = newer
+    current = jnp.concatenate([low, high], axis=0)
     cells = jnp.sum((domain_of == owner).astype(jnp.float32)) * (planes * NY * NX)
     rows = current.reshape(planes * NY * NX, bands)
 

time: 436 us -> 421 us (0.966)
  Pallas kernels: 247 us -> 237 us
  local copies, waits for them, and re-layouts: 12.4 us -> 7.44 us
    pallas_call x4, Pallas kernels: 46.1 us -> 35.7 us  [chebyshev_step(): pl.pallas_call(functools.partial(_step_kernel, first), out_shape=(piece,...]
    concatenate x1 -> x5, other arithmetic: 0.08 us -> 9.04 us  [the longest x4 7.53 us: rimmed(): jnp.concatenate([from_below * bf_below, low, high, from_above * bf_above]...]
    mul x4 -> x8, other arithmetic: 7.52 us -> 0.44 us  [the longest x4 0.22 us: rimmed(): from_above * bf_above]
    slice x4 -> x1, local copies, waits for them, and re-layouts: 7.78 us -> 2.81 us  [shards(): waves[half:]]
where the time goes in v5:
time: 421 us; the launch traced here: 420 us
  Pallas kernels  237 us (56%)
  starting transfers between devices  116 us (28%)
  waiting for transfers between devices  32.1 us (8%)
  other arithmetic  11.6 us (3%)
  between operations  11 us (3%)
  local copies, waits for them, and re-layouts  7.44 us (2%)
  matrix products  4.56 us (1%)
    pallas_call x2, Pallas kernels, lower_inverse(): pl.pallas_call(_lower_inverse_kernel, out_shape=jax.ShapeDtypeStruct((n,...  201 us
    ppermute x8, starting transfers between devices, domain_total(): from_low = lax.ppermute(forward, 'gz', ahead)  50.3 us
    ppermute x4, starting transfers between devices, rimmed(): from_below = lax.ppermute(high, 'gz', forward)  50.2 us
    pallas_call x4, Pallas kernels, chebyshev_step(): pl.pallas_call(functools.partial(_step_kernel, first), out_shape=(piece,...  35.7 us
    ppermute x4, waiting for transfers between devices, rimmed(): from_above = lax.ppermute(low, 'gz', backward)  14.1 us
    ppermute x8, waiting for transfers between devices, domain_total(): from_high = lax.ppermute(backward, 'gz', behind)  11.2 us
    ppermute x8, starting transfers between devices, domain_total(): from_high = lax.ppermute(backward, 'gz', behind)  10.3 us
  transfers between devices with their start and end apart: 24, of which 18 were waited for; matrix products, arithmetic and copies ran while one was open for 1% of the time, Pallas kernels for 0%

profile of v5, /device:TPU:0, one launch (start us, length us, event | category | flops | bytes accessed | tf_op | source)
XLA Modules:
  0.0 419.7 jit_solution(2643912217362416432)
XLA Ops:
  0.0 2.8 fusion.11
  2.8 2.4 collective-permute-start
  5.3 1.3 collective-permute-start.1
  6.6 0.7 fusion.12
  9.9 1.8 collective-permute-done.1
  11.8 1.9 pad_maximum_fusion.extended_ref
  13.7 1.6 broadcast_in_dim.8.low_pot_ref.high_pot_ref
  15.3 8.8 %shard_map.37 = (bf16[3,8,64,256]{3,2,1,0:T(8,128)(2,1)}, bf16[3,8,64,256]{3,2,1,0:T(8,128)(2,1)}) custom-call(bf16[12,8,64,256]{3,2,1,0:T(8,128)(2,1)} %pad_maximum_fusion.extended_ref, bf16[6,8,64,256]{3,2,1,0:T(8,128)(2,1)} %older_high_ref.3, bf16[6,8,64,256]{3,2,1,0:T(8,128)(2,1)} %older_high_ref.3, ...), custom_call_target="tpu_custom_call" | custom-call | tf_op jit(solution)/shard_map/pallas_call | solution.py:115
  24.1 15.9 %collective-permute-start.2 = (bf16[3,8,64,256]{3,2,1,0:T(8,128)(2,1)}, bf16[3,8,64,256]{3,2,1,0:T(8,128)(2,1)S(1)}, u32[]{:S(2)}, u32[]{:S(2)}) collective-permute-start(bf16[3,8,64,256]{3,2,1,0:T(8,128)(2,1)} %get-tuple-element.13.older_high_ref), channel_id=1, source_target_pairs={{0,1},{1,2},{2,3},{3,4},{4,5},{5,6},{6,7},{7,8},{8,9},{9,10},{10,1... | collective-permute-start | bytes 2359304 | tf_op jit(solution)/shard_map/ppermute | solution.py:198
  40.0 1.3 collective-permute-start.3
  41.3 0.8 collective-permute-done.2
  42.1 4.1 collective-permute-done.3
  46.3 1.9 pad_maximum_fusion.1.extended_ref
  48.2 9.0 %shard_map.38 = (bf16[3,8,64,256]{3,2,1,0:T(8,128)(2,1)}, bf16[3,8,64,256]{3,2,1,0:T(8,128)(2,1)}) custom-call(bf16[12,8,64,256]{3,2,1,0:T(8,128)(2,1)} %pad_maximum_fusion.1.extended_ref, bf16[6,8,64,256]{3,2,1,0:T(8,128)(2,1)} %older_high_ref.3, bf16[6,8,64,256]{3,2,1,0:T(8,128)(2,1)} %older_high_ref.3, ...), custom_call_target="tpu_custom_call" | custom-call | tf_op jit(solution)/shard_map/pallas_call | solution.py:115
  57.2 15.9 %collective-permute-start.4 = (bf16[3,8,64,256]{3,2,1,0:T(8,128)(2,1)}, bf16[3,8,64,256]{3,2,1,0:T(8,128)(2,1)S(1)}, u32[]{:S(2)}, u32[]{:S(2)}) collective-permute-start(bf16[3,8,64,256]{3,2,1,0:T(8,128)(2,1)} %get-tuple-element.15.older_high_ref), channel_id=1, source_target_pairs={{0,1},{1,2},{2,3},{3,4},{4,5},{5,6},{6,7},{7,8},{8,9},{9,10},{10,1... | collective-permute-start | bytes 2359304 | tf_op jit(solution)/shard_map/ppermute | solution.py:198
  73.1 1.3 collective-permute-start.5
  74.4 0.8 collective-permute-done.4
  75.2 4.1 collective-permute-done.5
  79.4 1.9 pad_maximum_fusion.2.extended_ref
  81.3 9.0 %shard_map.39 = (bf16[3,8,64,256]{3,2,1,0:T(8,128)(2,1)}, bf16[3,8,64,256]{3,2,1,0:T(8,128)(2,1)}) custom-call(bf16[12,8,64,256]{3,2,1,0:T(8,128)(2,1)} %pad_maximum_fusion.2.extended_ref, bf16[3,8,64,256]{3,2,1,0:T(8,128)(2,1)} %get-tuple-element.14.older_low_ref, bf16[3,8,64,256]{3,2,1,0:T(8,128)(2,1)} %get-tuple-element.13.older_high_ref, ...), custom_call_target="tpu_custom_call" | custom-call | tf_op jit(solution)/shard_map/pallas_call | solution.py:115
  90.3 15.9 %collective-permute-start.6 = (bf16[3,8,64,256]{3,2,1,0:T(8,128)(2,1)}, bf16[3,8,64,256]{3,2,1,0:T(8,128)(2,1)S(1)}, u32[]{:S(2)}, u32[]{:S(2)}) collective-permute-start(bf16[3,8,64,256]{3,2,1,0:T(8,128)(2,1)} %get-tuple-element.17), channel_id=1, source_target_pairs={{0,1},{1,2},{2,3},{3,4},{4,5},{5,6},{6,7},{7,8},{8,9},{9,10},{10,1... | collective-permute-start | bytes 2359304 | tf_op jit(solution)/shard_map/ppermute | solution.py:198
  106.2 1.3 collective-permute-start.7
  107.5 0.8 collective-permute-done.6
  108.3 4.1 collective-permute-done.7
  112.5 1.9 pad_maximum_fusion.3.extended_ref
  114.4 9.0 %shard_map.40 = (bf16[3,8,64,256]{3,2,1,0:T(8,128)(2,1)}, bf16[3,8,64,256]{3,2,1,0:T(8,128)(2,1)}) custom-call(bf16[12,8,64,256]{3,2,1,0:T(8,128)(2,1)} %pad_maximum_fusion.3.extended_ref, bf16[3,8,64,256]{3,2,1,0:T(8,128)(2,1)} %get-tuple-element.16.older_low_ref, bf16[3,8,64,256]{3,2,1,0:T(8,128)(2,1)} %get-tuple-element.15.older_high_ref, ...), custom_call_target="tpu_custom_call" | custom-call | tf_op jit(solution)/shard_map/pallas_call | solution.py:115
  123.4 1.5 pad_maximum_fusion.4
  124.9 0.4 fusion.2
  125.3 1.3 collective-permute-start.12
  126.6 16.4 %collective-permute-start.8 = (f32[128,256]{1,0:T(8,128)S(1)}, f32[128,256]{1,0:T(8,128)S(1)}, u32[]{:S(2)}, u32[]{:S(2)}) collective-permute-start(f32[128,256]{1,0:T(8,128)S(1)} %fusion.2), channel_id=1, source_target_pairs={{0,1},{1,2},{2,3},{3,4},{4,5},{5,6},{6,7},{7,8},{8,9},{9,10},{10,1... | collective-permute-start | bytes 393224 | tf_op jit(solution)/shard_map/ppermute | solution.py:221
  143.0 0.9 collective-permute-done.8
  144.0 7.6 %collective-permute-start.9 = (f32[128,256]{1,0:T(8,128)S(1)}, f32[128,256]{1,0:T(8,128)S(1)}, u32[]{:S(2)}, u32[]{:S(2)}) collective-permute-start(f32[128,256]{1,0:T(8,128)S(1)} %get-tuple-element.23), channel_id=1, source_target_pairs={{0,2},{1,3},{2,4},{3,5},{4,6},{5,7},{6,8},{7,9},{8,10},{9,11},{10,... | collective-permute-start | bytes 393224 | tf_op jit(solution)/shard_map/ppermute | solution.py:221
  156.5 1.3 collective-permute-start.13
  157.8 5.3 %collective-permute-start.10 = (f32[128,256]{1,0:T(8,128)S(1)}, f32[128,256]{1,0:T(8,128)S(1)}, u32[]{:S(2)}, u32[]{:S(2)}) collective-permute-start(f32[128,256]{1,0:T(8,128)S(1)} %multiply_add_fusion.4), channel_id=1, source_target_pairs={{0,4},{1,5},{2,6},{3,7},{4,8},{5,9},{6,10},{7,11},{8,12},{9,13},{1... | collective-permute-start | bytes 393224 | tf_op jit(solution)/shard_map/ppermute | solution.py:221
  163.1 0.2 collective-permute-done.13
  163.3 1.3 collective-permute-start.14
  164.6 0.9 collective-permute-done.10
  165.6 3.8 collective-permute-start.11
  169.4 0.8 collective-permute-done.14
  170.2 1.3 collective-permute-start.15
  174.0 1.2 fusion.10
  175.8 3.3 collective-permute-done.15
  179.2 0.6 slice.26.gram_ref
  179.8 100.6 %shard_map.41 = f32[128,128]{1,0:T(8,128)} custom-call(f32[128,128]{1,0:T(8,128)} %slice.26.gram_ref), custom_call_target="tpu_custom_call" | custom-call | tf_op jit(solution)/shard_map/pallas_call | solution.py:56
  280.5 1.2 convolution_convert_fusion.1
  281.7 1.3 fusion
  283.0 0.4 fusion.13
  283.4 1.3 collective-permute-start.20
  284.7 3.0 collective-permute-start.16
  287.8 0.9 collective-permute-done.16
  288.7 6.0 %collective-permute-start.17 = (f32[128,128]{1,0:T(8,128)S(1)}, f32[128,128]{1,0:T(8,128)S(1)}, u32[]{:S(2)}, u32[]{:S(2)}) collective-permute-start(f32[128,128]{1,0:T(8,128)S(1)} %get-tuple-element.25), channel_id=1, source_target_pairs={{0,2},{1,3},{2,4},{3,5},{4,6},{5,7},{6,8},{7,9},{8,10},{9,11},{10,... | collective-permute-start | bytes 196616 | tf_op jit(solution)/shard_map/ppermute | solution.py:221
  294.7 1.3 collective-permute-start.21
  296.0 1.2 collective-permute-done.17
  297.2 4.4 %collective-permute-start.18 = (f32[128,128]{1,0:T(8,128)S(1)}, f32[128,128]{1,0:T(8,128)S(1)}, u32[]{:S(2)}, u32[]{:S(2)}) collective-permute-start(f32[128,128]{1,0:T(8,128)S(1)} %multiply_add_fusion.10), channel_id=1, source_target_pairs={{0,4},{1,5},{2,6},{3,7},{4,8},{5,9},{6,10},{7,11},{8,12},{9,13},{1... | collective-permute-start | bytes 196616 | tf_op jit(solution)/shard_map/ppermute | solution.py:221
  301.6 1.3 collective-permute-start.22
  302.9 0.6 collective-permute-done.18
  303.5 3.8 collective-permute-start.19
  307.3 0.5 collective-permute-done.22
  307.8 1.3 collective-permute-start.23
  309.2 6.4 %collective-permute-done.23 = f32[128,128]{1,0:T(8,128)S(1)} collective-permute-done((f32[128,128]{1,0:T(8,128)S(1)}, f32[128,128]{1,0:T(8,128)S(1)}, u32[]{:S(2)}, u32[]{:S(2)}) %collective-permute-start.23) | collective-permute-done | bytes 65568 | tf_op jit(solution)/shard_map/ppermute | solution.py:222
  315.5 0.7 subtract_divide_fusion.1.gram_ref
  316.2 100.6 %shard_map.42 = f32[128,128]{1,0:T(8,128)} custom-call(f32[128,128]{1,0:T(8,128)} %subtract_divide_fusion.1.gram_ref), custom_call_target="tpu_custom_call" | custom-call | tf_op jit(solution)/shard_map/pallas_call | solution.py:56
  416.8 1.2 convolution_convert_fusion
  418.2 1.6 copy.5
  (46 shorter events, 1.0 us)
Async XLA Ops:
  0.0 11.8 %copy-start = (bf16[6,8,64,256]{3,2,1,0:T(8,128)(2,1)S(1)}, bf16[6,8,64,256]{3,2,1,0:T(8,128)(2,1)}, u32[]{:S(2)}) copy-start(bf16[6,8,64,256]{3,2,1,0:T(8,128)(2,1)} %older_high_ref.3) | copy-start | bytes 4718596
  0.0 6.6 %copy-start.7 = (s32[16]{0:T(128)S(1)}, s32[16]{0:T(128)}, u32[]{:S(2)}) copy-start(s32[16]{0:T(128)} %param.5) | copy-start | bytes 196
  0.0 9.8 %copy-start.8 = (f32[6,512]{1,0:T(8,128)S(1)}, f32[6,512]{1,0:T(8,128)}, u32[]{:S(2)}) copy-start(f32[6,512]{1,0:T(8,128)} %param.4) | copy-start | bytes 36868
  2.8 7.1 %collective-permute-start = (bf16[3,8,64,256]{3,2,1,0:T(8,128)(2,1)}, bf16[3,8,64,256]{3,2,1,0:T(8,128)(2,1)S(1)}, u32[]{:S(2)}, u32[]{:S(2)}) collective-permute-start(bf16[3,8,64,256]{3,2,1,0:T(8,128)(2,1)} %get-tuple-element.21), channel_id=1, source_target_pairs={{0,1},{1,2},{2,3},{3,4},{4,5},{5,6},{6,7},{7,8},{8,9},{9,10},{10,1... | collective-permute-start | bytes 2359304 | tf_op jit(solution)/shard_map/ppermute | solution.py:198
  5.3 6.5 %collective-permute-start.1 = (bf16[3,8,64,256]{3,2,1,0:T(8,128)(2,1)}, bf16[3,8,64,256]{3,2,1,0:T(8,128)(2,1)S(1)}, u32[]{:S(2)}, u32[]{:S(2)}) collective-permute-start(bf16[3,8,64,256]{3,2,1,0:T(8,128)(2,1)} %get-tuple-element.22), channel_id=1, source_target_pairs={{1,0},{2,1},{3,2},{4,3},{5,4},{6,5},{7,6},{8,7},{9,8},{10,9},{11,1... | collective-permute-start | bytes 2359304 | tf_op jit(solution)/shard_map/ppermute | solution.py:199
  24.1 22.2 %copy-start.3 = (bf16[3,8,64,256]{3,2,1,0:T(8,128)(2,1)S(1)}, bf16[3,8,64,256]{3,2,1,0:T(8,128)(2,1)}, u32[]{:S(2)}) copy-start(bf16[3,8,64,256]{3,2,1,0:T(8,128)(2,1)} %get-tuple-element.14.older_low_ref) | copy-start | bytes 2359300
  24.1 22.2 %copy-start.4 = (bf16[3,8,64,256]{3,2,1,0:T(8,128)(2,1)S(1)}, bf16[3,8,64,256]{3,2,1,0:T(8,128)(2,1)}, u32[]{:S(2)}) copy-start(bf16[3,8,64,256]{3,2,1,0:T(8,128)(2,1)} %get-tuple-element.13.older_high_ref) | copy-start | bytes 2359300
  24.1 18.0 %collective-permute-start.2 = (bf16[3,8,64,256]{3,2,1,0:T(8,128)(2,1)}, bf16[3,8,64,256]{3,2,1,0:T(8,128)(2,1)S(1)}, u32[]{:S(2)}, u32[]{:S(2)}) collective-permute-start(bf16[3,8,64,256]{3,2,1,0:T(8,128)(2,1)} %get-tuple-element.13.older_high_ref), channel_id=1, source_target_pairs={{0,1},{1,2},{2,3},{3,4},{4,5},{5,6},{6,7},{7,8},{8,9},{9,10},{10,1... | collective-permute-start | bytes 2359304 | tf_op jit(solution)/shard_map/ppermute | solution.py:198
  40.0 6.2 %collective-permute-start.3 = (bf16[3,8,64,256]{3,2,1,0:T(8,128)(2,1)}, bf16[3,8,64,256]{3,2,1,0:T(8,128)(2,1)S(1)}, u32[]{:S(2)}, u32[]{:S(2)}) collective-permute-start(bf16[3,8,64,256]{3,2,1,0:T(8,128)(2,1)} %get-tuple-element.14.older_low_ref), channel_id=1, source_target_pairs={{1,0},{2,1},{3,2},{4,3},{5,4},{6,5},{7,6},{8,7},{9,8},{10,9},{11,1... | collective-permute-start | bytes 2359304 | tf_op jit(solution)/shard_map/ppermute | solution.py:199
  57.2 22.2 %copy-start.1 = (bf16[3,8,64,256]{3,2,1,0:T(8,128)(2,1)S(1)}, bf16[3,8,64,256]{3,2,1,0:T(8,128)(2,1)}, u32[]{:S(2)}) copy-start(bf16[3,8,64,256]{3,2,1,0:T(8,128)(2,1)} %get-tuple-element.16.older_low_ref) | copy-start | bytes 2359300
  57.2 22.2 %copy-start.2 = (bf16[3,8,64,256]{3,2,1,0:T(8,128)(2,1)S(1)}, bf16[3,8,64,256]{3,2,1,0:T(8,128)(2,1)}, u32[]{:S(2)}) copy-start(bf16[3,8,64,256]{3,2,1,0:T(8,128)(2,1)} %get-tuple-element.15.older_high_ref) | copy-start | bytes 2359300
  57.2 18.0 %collective-permute-start.4 = (bf16[3,8,64,256]{3,2,1,0:T(8,128)(2,1)}, bf16[3,8,64,256]{3,2,1,0:T(8,128)(2,1)S(1)}, u32[]{:S(2)}, u32[]{:S(2)}) collective-permute-start(bf16[3,8,64,256]{3,2,1,0:T(8,128)(2,1)} %get-tuple-element.15.older_high_ref), channel_id=1, source_target_pairs={{0,1},{1,2},{2,3},{3,4},{4,5},{5,6},{6,7},{7,8},{8,9},{9,10},{10,1... | collective-permute-start | bytes 2359304 | tf_op jit(solution)/shard_map/ppermute | solution.py:198
  73.1 6.2 %collective-permute-start.5 = (bf16[3,8,64,256]{3,2,1,0:T(8,128)(2,1)}, bf16[3,8,64,256]{3,2,1,0:T(8,128)(2,1)S(1)}, u32[]{:S(2)}, u32[]{:S(2)}) collective-permute-start(bf16[3,8,64,256]{3,2,1,0:T(8,128)(2,1)} %get-tuple-element.16.older_low_ref), channel_id=1, source_target_pairs={{1,0},{2,1},{3,2},{4,3},{5,4},{6,5},{7,6},{8,7},{9,8},{10,9},{11,1... | collective-permute-start | bytes 2359304 | tf_op jit(solution)/shard_map/ppermute | solution.py:199
  90.3 22.2 %copy-start.5 = (bf16[3,8,64,256]{3,2,1,0:T(8,128)(2,1)S(1)}, bf16[3,8,64,256]{3,2,1,0:T(8,128)(2,1)}, u32[]{:S(2)}) copy-start(bf16[3,8,64,256]{3,2,1,0:T(8,128)(2,1)} %get-tuple-element.18) | copy-start | bytes 2359300
  90.3 22.2 %copy-start.6 = (bf16[3,8,64,256]{3,2,1,0:T(8,128)(2,1)S(1)}, bf16[3,8,64,256]{3,2,1,0:T(8,128)(2,1)}, u32[]{:S(2)}) copy-start(bf16[3,8,64,256]{3,2,1,0:T(8,128)(2,1)} %get-tuple-element.17) | copy-start | bytes 2359300
  90.3 18.0 %collective-permute-start.6 = (bf16[3,8,64,256]{3,2,1,0:T(8,128)(2,1)}, bf16[3,8,64,256]{3,2,1,0:T(8,128)(2,1)S(1)}, u32[]{:S(2)}, u32[]{:S(2)}) collective-permute-start(bf16[3,8,64,256]{3,2,1,0:T(8,128)(2,1)} %get-tuple-element.17), channel_id=1, source_target_pairs={{0,1},{1,2},{2,3},{3,4},{4,5},{5,6},{6,7},{7,8},{8,9},{9,10},{10,1... | collective-permute-start | bytes 2359304 | tf_op jit(solution)/shard_map/ppermute | solution.py:198
  106.2 6.2 %collective-permute-start.7 = (bf16[3,8,64,256]{3,2,1,0:T(8,128)(2,1)}, bf16[3,8,64,256]{3,2,1,0:T(8,128)(2,1)S(1)}, u32[]{:S(2)}, u32[]{:S(2)}) collective-permute-start(bf16[3,8,64,256]{3,2,1,0:T(8,128)(2,1)} %get-tuple-element.18), channel_id=1, source_target_pairs={{1,0},{2,1},{3,2},{4,3},{5,4},{6,5},{7,6},{8,7},{9,8},{10,9},{11,1... | collective-permute-start | bytes 2359304 | tf_op jit(solution)/shard_map/ppermute | solution.py:199
  125.3 17.7 %collective-permute-start.12 = (f32[128,256]{1,0:T(8,128)S(1)}, f32[128,256]{1,0:T(8,128)S(1)}, u32[]{:S(2)}, u32[]{:S(2)}) collective-permute-start(f32[128,256]{1,0:T(8,128)S(1)} %fusion.2), channel_id=1, source_target_pairs={{1,0},{2,1},{3,2},{4,3},{5,4},{6,5},{7,6},{8,7},{9,8},{10,9},{11,1... | collective-permute-start | bytes 393224 | tf_op jit(solution)/shard_map/ppermute | solution.py:222
  126.6 17.3 %collective-permute-start.8 = (f32[128,256]{1,0:T(8,128)S(1)}, f32[128,256]{1,0:T(8,128)S(1)}, u32[]{:S(2)}, u32[]{:S(2)}) collective-permute-start(f32[128,256]{1,0:T(8,128)S(1)} %fusion.2), channel_id=1, source_target_pairs={{0,1},{1,2},{2,3},{3,4},{4,5},{5,6},{6,7},{7,8},{8,9},{9,10},{10,1... | collective-permute-start | bytes 393224 | tf_op jit(solution)/shard_map/ppermute | solution.py:221
  144.0 13.8 %collective-permute-start.9 = (f32[128,256]{1,0:T(8,128)S(1)}, f32[128,256]{1,0:T(8,128)S(1)}, u32[]{:S(2)}, u32[]{:S(2)}) collective-permute-start(f32[128,256]{1,0:T(8,128)S(1)} %get-tuple-element.23), channel_id=1, source_target_pairs={{0,2},{1,3},{2,4},{3,5},{4,6},{5,7},{6,8},{7,9},{8,10},{9,11},{10,... | collective-permute-start | bytes 393224 | tf_op jit(solution)/shard_map/ppermute | solution.py:221
  156.5 6.9 %collective-permute-start.13 = (f32[128,256]{1,0:T(8,128)S(1)}, f32[128,256]{1,0:T(8,128)S(1)}, u32[]{:S(2)}, u32[]{:S(2)}) collective-permute-start(f32[128,256]{1,0:T(8,128)S(1)} %get-tuple-element.24), channel_id=1, source_target_pairs={{2,0},{3,1},{4,2},{5,3},{6,4},{7,5},{8,6},{9,7},{10,8},{11,9},{12,... | collective-permute-start | bytes 393224 | tf_op jit(solution)/shard_map/ppermute | solution.py:222
  157.8 7.8 %collective-permute-start.10 = (f32[128,256]{1,0:T(8,128)S(1)}, f32[128,256]{1,0:T(8,128)S(1)}, u32[]{:S(2)}, u32[]{:S(2)}) collective-permute-start(f32[128,256]{1,0:T(8,128)S(1)} %multiply_add_fusion.4), channel_id=1, source_target_pairs={{0,4},{1,5},{2,6},{3,7},{4,8},{5,9},{6,10},{7,11},{8,12},{9,13},{1... | collective-permute-start | bytes 393224 | tf_op jit(solution)/shard_map/ppermute | solution.py:221
  163.3 6.9 %collective-permute-start.14 = (f32[128,256]{1,0:T(8,128)S(1)}, f32[128,256]{1,0:T(8,128)S(1)}, u32[]{:S(2)}, u32[]{:S(2)}) collective-permute-start(f32[128,256]{1,0:T(8,128)S(1)} %multiply_add_fusion.1), channel_id=1, source_target_pairs={{4,0},{5,1},{6,2},{7,3},{8,4},{9,5},{10,6},{11,7},{12,8},{13,9},{1... | collective-permute-start | bytes 393224 | tf_op jit(solution)/shard_map/ppermute | solution.py:222
  165.6 10.2 %collective-permute-start.11 = (f32[128,256]{1,0:T(8,128)S(1)}, f32[128,256]{1,0:T(8,128)S(1)}, u32[]{:S(2)}, u32[]{:S(2)}) collective-permute-start(f32[128,256]{1,0:T(8,128)S(1)} %multiply_add_fusion.3), channel_id=1, source_target_pairs={{0,8},{1,9},{2,10},{3,11},{4,12},{5,13},{6,14},{7,15},{16,24},{17,... | collective-permute-start | bytes 393224 | tf_op jit(solution)/shard_map/ppermute | solution.py:221
  170.2 8.9 %collective-permute-start.15 = (f32[128,256]{1,0:T(8,128)S(1)}, f32[128,256]{1,0:T(8,128)S(1)}, u32[]{:S(2)}, u32[]{:S(2)}) collective-permute-start(f32[128,256]{1,0:T(8,128)S(1)} %multiply_add_fusion), channel_id=1, source_target_pairs={{8,0},{9,1},{10,2},{11,3},{12,4},{13,5},{14,6},{15,7},{24,16},{25,... | collective-permute-start | bytes 393224 | tf_op jit(solution)/shard_map/ppermute | solution.py:222
  283.4 4.3 %collective-permute-start.20 = (f32[128,128]{1,0:T(8,128)S(1)}, f32[128,128]{1,0:T(8,128)S(1)}, u32[]{:S(2)}, u32[]{:S(2)}) collective-permute-start(f32[128,128]{1,0:T(8,128)S(1)} %fusion.13), channel_id=1, source_target_pairs={{1,0},{2,1},{3,2},{4,3},{5,4},{6,5},{7,6},{8,7},{9,8},{10,9},{11,1... | collective-permute-start | bytes 196616 | tf_op jit(solution)/shard_map/ppermute | solution.py:222
  284.7 3.9 collective-permute-start.16
  288.7 8.5 %collective-permute-start.17 = (f32[128,128]{1,0:T(8,128)S(1)}, f32[128,128]{1,0:T(8,128)S(1)}, u32[]{:S(2)}, u32[]{:S(2)}) collective-permute-start(f32[128,128]{1,0:T(8,128)S(1)} %get-tuple-element.25), channel_id=1, source_target_pairs={{0,2},{1,3},{2,4},{3,5},{4,6},{5,7},{6,8},{7,9},{8,10},{9,11},{10,... | collective-permute-start | bytes 196616 | tf_op jit(solution)/shard_map/ppermute | solution.py:221
  294.7 6.9 %collective-permute-start.21 = (f32[128,128]{1,0:T(8,128)S(1)}, f32[128,128]{1,0:T(8,128)S(1)}, u32[]{:S(2)}, u32[]{:S(2)}) collective-permute-start(f32[128,128]{1,0:T(8,128)S(1)} %get-tuple-element.26), channel_id=1, source_target_pairs={{2,0},{3,1},{4,2},{5,3},{6,4},{7,5},{8,6},{9,7},{10,8},{11,9},{12,... | collective-permute-start | bytes 196616 | tf_op jit(solution)/shard_map/ppermute | solution.py:222
  297.2 6.3 %collective-permute-start.18 = (f32[128,128]{1,0:T(8,128)S(1)}, f32[128,128]{1,0:T(8,128)S(1)}, u32[]{:S(2)}, u32[]{:S(2)}) collective-permute-start(f32[128,128]{1,0:T(8,128)S(1)} %multiply_add_fusion.10), channel_id=1, source_target_pairs={{0,4},{1,5},{2,6},{3,7},{4,8},{5,9},{6,10},{7,11},{8,12},{9,13},{1... | collective-permute-start | bytes 196616 | tf_op jit(solution)/shard_map/ppermute | solution.py:221
  301.6 6.2 %collective-permute-start.22 = (f32[128,128]{1,0:T(8,128)S(1)}, f32[128,128]{1,0:T(8,128)S(1)}, u32[]{:S(2)}, u32[]{:S(2)}) collective-permute-start(f32[128,128]{1,0:T(8,128)S(1)} %multiply_add_fusion.7), channel_id=1, source_target_pairs={{4,0},{5,1},{6,2},{7,3},{8,4},{9,5},{10,6},{11,7},{12,8},{13,9},{1... | collective-permute-start | bytes 196616 | tf_op jit(solution)/shard_map/ppermute | solution.py:222
  303.5 5.7 %collective-permute-start.19 = (f32[128,128]{1,0:T(8,128)S(1)}, f32[128,128]{1,0:T(8,128)S(1)}, u32[]{:S(2)}, u32[]{:S(2)}) collective-permute-start(f32[128,128]{1,0:T(8,128)S(1)} %multiply_add_fusion.9), channel_id=1, source_target_pairs={{0,8},{1,9},{2,10},{3,11},{4,12},{5,13},{6,14},{7,15},{16,24},{17,... | collective-permute-start | bytes 196616 | tf_op jit(solution)/shard_map/ppermute | solution.py:221
  307.8 7.8 %collective-permute-start.23 = (f32[128,128]{1,0:T(8,128)S(1)}, f32[128,128]{1,0:T(8,128)S(1)}, u32[]{:S(2)}, u32[]{:S(2)}) collective-permute-start(f32[128,128]{1,0:T(8,128)S(1)} %multiply_add_fusion.6), channel_id=1, source_target_pairs={{8,0},{9,1},{10,2},{11,3},{12,4},{13,5},{14,6},{15,7},{24,16},{25,... | collective-permute-start | bytes 196616 | tf_op jit(solution)/shard_map/ppermute | solution.py:222

commit v6 on v5

--- a/solution.py
+++ b/solution.py
@@ -21,6 +21,8 @@
 
 def _lower_inverse_kernel(gram_ref, out_ref, work_ref):
     n = gram_ref.shape[0]
+    rows = lax.broadcasted_iota(jnp.int32, (n, 2 * n), 0)
+    lanes = lax.broadcasted_iota(jnp.int32, (n, 2 * n), 1)
     work_ref[:, :n] = gram_ref[...]
     work_ref[:, n:] = (lax.broadcasted_iota(jnp.int32, (n, n), 0) == lax.broadcasted_iota(jnp.int32, (n, n), 1)).astype(jnp.float32)
 
@@ -30,21 +32,11 @@
         pivot = jnp.sum(jnp.where(lane == k, row, 0.0), axis=1, keepdims=True)
         scale = 1.0 / jnp.sqrt(pivot)
         scaled = row * scale
-        block_rows = lax.broadcasted_iota(jnp.int32, (8, 2 * n), 0)
-        block_lanes = lax.broadcasted_iota(jnp.int32, (8, n), 1)
-        for start in range(0, n, 8):
-
-            @pl.when(start + 7 >= k)
-            def _():
-                whole = work_ref[start : start + 8, :]
-                left = whole[:, :n]
-                column = (
-                    jnp.sum(jnp.where(block_lanes == k, left, 0.0), axis=1, keepdims=True) * scale
-                )
-                place = block_rows + start
-                updated = jnp.where(place > k, whole - column * scaled, whole)
-                work_ref[start : start + 8, :] = jnp.where(place == k, scaled, updated)
-
+        whole = work_ref[...]
+        left = whole[:, :n]
+        column = jnp.sum(jnp.where(lanes[:, :n] == k, left, 0.0), axis=1, keepdims=True) * scale
+        updated = jnp.where(rows > k, whole - column * scaled, whole)
+        work_ref[...] = jnp.where(rows == k, scaled, updated)
         return carry
 
     lax.fori_loop(0, n, step, 0)

time: 421 us -> 254 us (0.60)
  Pallas kernels: 237 us -> 69.6 us
    pallas_call x2, Pallas kernels: 201 us -> 33.9 us  [lower_inverse(): pl.pallas_call(_lower_inverse_kernel, out_shape=jax.ShapeDtypeStruct((n,...]
where the time goes in v6:
time: 254 us; the launch traced here: 252 us
  starting transfers between devices  116 us (46%)
  Pallas kernels  69.6 us (27%)
  waiting for transfers between devices  32.1 us (13%)
  other arithmetic  11.6 us (5%)
  between operations  11 us (4%)
  local copies, waits for them, and re-layouts  7.44 us (3%)
  matrix products  4.57 us (2%)
    ppermute x8, starting transfers between devices, domain_total(): from_low = lax.ppermute(forward, 'gz', ahead)  50.3 us
    ppermute x4, starting transfers between devices, rimmed(): from_below = lax.ppermute(high, 'gz', forward)  50.2 us
    pallas_call x4, Pallas kernels, chebyshev_step(): pl.pallas_call(functools.partial(_step_kernel, first), out_shape=(piece,...  35.7 us
    pallas_call x2, Pallas kernels, lower_inverse(): pl.pallas_call(_lower_inverse_kernel, out_shape=jax.ShapeDtypeStruct((n,...  33.9 us
    ppermute x4, waiting for transfers between devices, rimmed(): from_above = lax.ppermute(low, 'gz', backward)  14.1 us
    ppermute x8, waiting for transfers between devices, domain_total(): from_high = lax.ppermute(backward, 'gz', behind)  11.2 us
    ppermute x8, starting transfers between devices, domain_total(): from_high = lax.ppermute(backward, 'gz', behind)  10.3 us
    concatenate x4, other arithmetic, rimmed(): jnp.concatenate([from_below * bf_below, low, high, from_above * bf_above]...  7.53 us
  transfers between devices with their start and end apart: 24, of which 18 were waited for; matrix products, arithmetic and copies ran while one was open for 1% of the time, Pallas kernels for 0%

profile of v6, /device:TPU:0, one launch (start us, length us, event | category | flops | bytes accessed | tf_op | source)
XLA Modules:
  0.0 252.3 jit_solution(10085446577154860179)
XLA Ops:
  0.0 2.8 %fusion.11 = (bf16[3,8,64,256]{3,2,1,0:T(8,128)(2,1)}, bf16[3,8,64,256]{3,2,1,0:T(8,128)(2,1)}) fusion(bf16[6,8,64,256]{3,2,1,0:T(8,128)(2,1)} %older_high_ref.3), kind=kLoop, calls=%fused_computation.42 | loop fusion | bytes 3145728 | tf_op jit(solution)/shard_map/slice | solution.py:196
  2.8 2.4 collective-permute-start
  5.3 1.3 collective-permute-start.1
  6.6 0.7 fusion.12
  9.9 1.8 collective-permute-done.1
  11.8 1.9 pad_maximum_fusion.extended_ref
  13.7 1.6 broadcast_in_dim.8.low_pot_ref.high_pot_ref
  15.3 8.8 %shard_map.37 = (bf16[3,8,64,256]{3,2,1,0:T(8,128)(2,1)}, bf16[3,8,64,256]{3,2,1,0:T(8,128)(2,1)}) custom-call(bf16[12,8,64,256]{3,2,1,0:T(8,128)(2,1)} %pad_maximum_fusion.extended_ref, bf16[6,8,64,256]{3,2,1,0:T(8,128)(2,1)} %older_high_ref.3, bf16[6,8,64,256]{3,2,1,0:T(8,128)(2,1)} %older_high_ref.3, ...), custom_call_target="tpu_custom_call" | custom-call | tf_op jit(solution)/shard_map/pallas_call | solution.py:107
  24.1 15.9 %collective-permute-start.2 = (bf16[3,8,64,256]{3,2,1,0:T(8,128)(2,1)}, bf16[3,8,64,256]{3,2,1,0:T(8,128)(2,1)S(1)}, u32[]{:S(2)}, u32[]{:S(2)}) collective-permute-start(bf16[3,8,64,256]{3,2,1,0:T(8,128)(2,1)} %get-tuple-element.13.older_high_ref), channel_id=1, source_target_pairs={{0,1},{1,2},{2,3},{3,4},{4,5},{5,6},{6,7},{7,8},{8,9},{9,10},{10,1... | collective-permute-start | bytes 2359304 | tf_op jit(solution)/shard_map/ppermute | solution.py:190
  40.0 1.3 collective-permute-start.3
  41.3 0.8 collective-permute-done.2
  42.1 4.1 %collective-permute-done.3 = bf16[3,8,64,256]{3,2,1,0:T(8,128)(2,1)S(1)} collective-permute-done((bf16[3,8,64,256]{3,2,1,0:T(8,128)(2,1)}, bf16[3,8,64,256]{3,2,1,0:T(8,128)(2,1)S(1)}, u32[]{:S(2)}, u32[]{:S(2)}) %collective-permute-start.3) | collective-permute-done | bytes 786464 | tf_op jit(solution)/shard_map/ppermute | solution.py:191
  46.3 1.9 pad_maximum_fusion.1.extended_ref
  48.2 9.0 %shard_map.38 = (bf16[3,8,64,256]{3,2,1,0:T(8,128)(2,1)}, bf16[3,8,64,256]{3,2,1,0:T(8,128)(2,1)}) custom-call(bf16[12,8,64,256]{3,2,1,0:T(8,128)(2,1)} %pad_maximum_fusion.1.extended_ref, bf16[6,8,64,256]{3,2,1,0:T(8,128)(2,1)} %older_high_ref.3, bf16[6,8,64,256]{3,2,1,0:T(8,128)(2,1)} %older_high_ref.3, ...), custom_call_target="tpu_custom_call" | custom-call | tf_op jit(solution)/shard_map/pallas_call | solution.py:107
  57.2 15.9 %collective-permute-start.4 = (bf16[3,8,64,256]{3,2,1,0:T(8,128)(2,1)}, bf16[3,8,64,256]{3,2,1,0:T(8,128)(2,1)S(1)}, u32[]{:S(2)}, u32[]{:S(2)}) collective-permute-start(bf16[3,8,64,256]{3,2,1,0:T(8,128)(2,1)} %get-tuple-element.15.older_high_ref), channel_id=1, source_target_pairs={{0,1},{1,2},{2,3},{3,4},{4,5},{5,6},{6,7},{7,8},{8,9},{9,10},{10,1... | collective-permute-start | bytes 2359304 | tf_op jit(solution)/shard_map/ppermute | solution.py:190
  73.1 1.3 collective-permute-start.5
  74.4 0.8 collective-permute-done.4
  75.2 4.1 %collective-permute-done.5 = bf16[3,8,64,256]{3,2,1,0:T(8,128)(2,1)S(1)} collective-permute-done((bf16[3,8,64,256]{3,2,1,0:T(8,128)(2,1)}, bf16[3,8,64,256]{3,2,1,0:T(8,128)(2,1)S(1)}, u32[]{:S(2)}, u32[]{:S(2)}) %collective-permute-start.5) | collective-permute-done | bytes 786464 | tf_op jit(solution)/shard_map/ppermute | solution.py:191
  79.4 1.9 pad_maximum_fusion.2.extended_ref
  81.3 9.0 %shard_map.39 = (bf16[3,8,64,256]{3,2,1,0:T(8,128)(2,1)}, bf16[3,8,64,256]{3,2,1,0:T(8,128)(2,1)}) custom-call(bf16[12,8,64,256]{3,2,1,0:T(8,128)(2,1)} %pad_maximum_fusion.2.extended_ref, bf16[3,8,64,256]{3,2,1,0:T(8,128)(2,1)} %get-tuple-element.14.older_low_ref, bf16[3,8,64,256]{3,2,1,0:T(8,128)(2,1)} %get-tuple-element.13.older_high_ref, ...), custom_call_target="tpu_custom_call" | custom-call | tf_op jit(solution)/shard_map/pallas_call | solution.py:107
  90.3 15.9 %collective-permute-start.6 = (bf16[3,8,64,256]{3,2,1,0:T(8,128)(2,1)}, bf16[3,8,64,256]{3,2,1,0:T(8,128)(2,1)S(1)}, u32[]{:S(2)}, u32[]{:S(2)}) collective-permute-start(bf16[3,8,64,256]{3,2,1,0:T(8,128)(2,1)} %get-tuple-element.17), channel_id=1, source_target_pairs={{0,1},{1,2},{2,3},{3,4},{4,5},{5,6},{6,7},{7,8},{8,9},{9,10},{10,1... | collective-permute-start | bytes 2359304 | tf_op jit(solution)/shard_map/ppermute | solution.py:190
  106.2 1.3 collective-permute-start.7
  107.5 0.8 collective-permute-done.6
  108.3 4.1 %collective-permute-done.7 = bf16[3,8,64,256]{3,2,1,0:T(8,128)(2,1)S(1)} collective-permute-done((bf16[3,8,64,256]{3,2,1,0:T(8,128)(2,1)}, bf16[3,8,64,256]{3,2,1,0:T(8,128)(2,1)S(1)}, u32[]{:S(2)}, u32[]{:S(2)}) %collective-permute-start.7) | collective-permute-done | bytes 786464 | tf_op jit(solution)/shard_map/ppermute | solution.py:191
  112.5 1.9 pad_maximum_fusion.3.extended_ref
  114.4 9.0 %shard_map.40 = (bf16[3,8,64,256]{3,2,1,0:T(8,128)(2,1)}, bf16[3,8,64,256]{3,2,1,0:T(8,128)(2,1)}) custom-call(bf16[12,8,64,256]{3,2,1,0:T(8,128)(2,1)} %pad_maximum_fusion.3.extended_ref, bf16[3,8,64,256]{3,2,1,0:T(8,128)(2,1)} %get-tuple-element.16.older_low_ref, bf16[3,8,64,256]{3,2,1,0:T(8,128)(2,1)} %get-tuple-element.15.older_high_ref, ...), custom_call_target="tpu_custom_call" | custom-call | tf_op jit(solution)/shard_map/pallas_call | solution.py:107
  123.4 1.5 pad_maximum_fusion.4
  124.9 0.4 fusion.2
  125.3 1.3 collective-permute-start.12
  126.6 16.4 %collective-permute-start.8 = (f32[128,256]{1,0:T(8,128)S(1)}, f32[128,256]{1,0:T(8,128)S(1)}, u32[]{:S(2)}, u32[]{:S(2)}) collective-permute-start(f32[128,256]{1,0:T(8,128)S(1)} %fusion.2), channel_id=1, source_target_pairs={{0,1},{1,2},{2,3},{3,4},{4,5},{5,6},{6,7},{7,8},{8,9},{9,10},{10,1... | collective-permute-start | bytes 393224 | tf_op jit(solution)/shard_map/ppermute | solution.py:213
  143.0 0.9 collective-permute-done.8
  144.0 7.6 %collective-permute-start.9 = (f32[128,256]{1,0:T(8,128)S(1)}, f32[128,256]{1,0:T(8,128)S(1)}, u32[]{:S(2)}, u32[]{:S(2)}) collective-permute-start(f32[128,256]{1,0:T(8,128)S(1)} %get-tuple-element.23), channel_id=1, source_target_pairs={{0,2},{1,3},{2,4},{3,5},{4,6},{5,7},{6,8},{7,9},{8,10},{9,11},{10,... | collective-permute-start | bytes 393224 | tf_op jit(solution)/shard_map/ppermute | solution.py:213
  156.5 1.3 collective-permute-start.13
  157.8 5.3 %collective-permute-start.10 = (f32[128,256]{1,0:T(8,128)S(1)}, f32[128,256]{1,0:T(8,128)S(1)}, u32[]{:S(2)}, u32[]{:S(2)}) collective-permute-start(f32[128,256]{1,0:T(8,128)S(1)} %multiply_add_fusion.4), channel_id=1, source_target_pairs={{0,4},{1,5},{2,6},{3,7},{4,8},{5,9},{6,10},{7,11},{8,12},{9,13},{1... | collective-permute-start | bytes 393224 | tf_op jit(solution)/shard_map/ppermute | solution.py:213
  163.1 0.2 collective-permute-done.13
  163.3 1.3 collective-permute-start.14
  164.6 0.9 collective-permute-done.10
  165.6 3.8 %collective-permute-start.11 = (f32[128,256]{1,0:T(8,128)S(1)}, f32[128,256]{1,0:T(8,128)S(1)}, u32[]{:S(2)}, u32[]{:S(2)}) collective-permute-start(f32[128,256]{1,0:T(8,128)S(1)} %multiply_add_fusion.3), channel_id=1, source_target_pairs={{0,8},{1,9},{2,10},{3,11},{4,12},{5,13},{6,14},{7,15},{16,24},{17,... | collective-permute-start | bytes 393224 | tf_op jit(solution)/shard_map/ppermute | solution.py:213
  169.4 0.8 collective-permute-done.14
  170.2 1.3 collective-permute-start.15
  174.0 1.2 fusion.10
  175.8 3.3 %collective-permute-done.15 = f32[128,256]{1,0:T(8,128)S(1)} collective-permute-done((f32[128,256]{1,0:T(8,128)S(1)}, f32[128,256]{1,0:T(8,128)S(1)}, u32[]{:S(2)}, u32[]{:S(2)}) %collective-permute-start.15) | collective-permute-done | bytes 131104 | tf_op jit(solution)/shard_map/ppermute | solution.py:214
  179.2 0.6 slice.26.gram_ref
  179.8 16.9 %shard_map.41 = f32[128,128]{1,0:T(8,128)} custom-call(f32[128,128]{1,0:T(8,128)} %slice.26.gram_ref), custom_call_target="tpu_custom_call" | custom-call | tf_op jit(solution)/shard_map/pallas_call | solution.py:48
  196.8 1.2 convolution_convert_fusion.1
  198.0 1.3 fusion
  199.3 0.4 fusion.13
  199.7 1.3 collective-permute-start.20
  201.0 3.0 %collective-permute-start.16 = (f32[128,128]{1,0:T(8,128)S(1)}, f32[128,128]{1,0:T(8,128)S(1)}, u32[]{:S(2)}, u32[]{:S(2)}) collective-permute-start(f32[128,128]{1,0:T(8,128)S(1)} %fusion.13), channel_id=1, source_target_pairs={{0,1},{1,2},{2,3},{3,4},{4,5},{5,6},{6,7},{7,8},{8,9},{9,10},{10,1... | collective-permute-start | bytes 196616 | tf_op jit(solution)/shard_map/ppermute | solution.py:213
  204.1 0.9 collective-permute-done.16
  205.0 6.0 %collective-permute-start.17 = (f32[128,128]{1,0:T(8,128)S(1)}, f32[128,128]{1,0:T(8,128)S(1)}, u32[]{:S(2)}, u32[]{:S(2)}) collective-permute-start(f32[128,128]{1,0:T(8,128)S(1)} %get-tuple-element.25), channel_id=1, source_target_pairs={{0,2},{1,3},{2,4},{3,5},{4,6},{5,7},{6,8},{7,9},{8,10},{9,11},{10,... | collective-permute-start | bytes 196616 | tf_op jit(solution)/shard_map/ppermute | solution.py:213
  211.0 1.3 collective-permute-start.21
  212.3 1.2 collective-permute-done.17
  213.5 4.4 %collective-permute-start.18 = (f32[128,128]{1,0:T(8,128)S(1)}, f32[128,128]{1,0:T(8,128)S(1)}, u32[]{:S(2)}, u32[]{:S(2)}) collective-permute-start(f32[128,128]{1,0:T(8,128)S(1)} %multiply_add_fusion.10), channel_id=1, source_target_pairs={{0,4},{1,5},{2,6},{3,7},{4,8},{5,9},{6,10},{7,11},{8,12},{9,13},{1... | collective-permute-start | bytes 196616 | tf_op jit(solution)/shard_map/ppermute | solution.py:213
  217.9 1.3 collective-permute-start.22
  219.2 0.6 collective-permute-done.18
  219.8 3.8 %collective-permute-start.19 = (f32[128,128]{1,0:T(8,128)S(1)}, f32[128,128]{1,0:T(8,128)S(1)}, u32[]{:S(2)}, u32[]{:S(2)}) collective-permute-start(f32[128,128]{1,0:T(8,128)S(1)} %multiply_add_fusion.9), channel_id=1, source_target_pairs={{0,8},{1,9},{2,10},{3,11},{4,12},{5,13},{6,14},{7,15},{16,24},{17,... | collective-permute-start | bytes 196616 | tf_op jit(solution)/shard_map/ppermute | solution.py:213
  223.6 0.5 collective-permute-done.22
  224.1 1.3 collective-permute-start.23
  225.5 6.4 %collective-permute-done.23 = f32[128,128]{1,0:T(8,128)S(1)} collective-permute-done((f32[128,128]{1,0:T(8,128)S(1)}, f32[128,128]{1,0:T(8,128)S(1)}, u32[]{:S(2)}, u32[]{:S(2)}) %collective-permute-start.23) | collective-permute-done | bytes 65568 | tf_op jit(solution)/shard_map/ppermute | solution.py:214
  231.8 0.7 subtract_divide_fusion.1.gram_ref
  232.5 16.9 %shard_map.42 = f32[128,128]{1,0:T(8,128)} custom-call(f32[128,128]{1,0:T(8,128)} %subtract_divide_fusion.1.gram_ref), custom_call_target="tpu_custom_call" | custom-call | tf_op jit(solution)/shard_map/pallas_call | solution.py:48
  249.4 1.2 convolution_convert_fusion
  250.7 1.6 copy.5
  (46 shorter events, 1.0 us)
Async XLA Ops:
  0.0 11.8 %copy-start = (bf16[6,8,64,256]{3,2,1,0:T(8,128)(2,1)S(1)}, bf16[6,8,64,256]{3,2,1,0:T(8,128)(2,1)}, u32[]{:S(2)}) copy-start(bf16[6,8,64,256]{3,2,1,0:T(8,128)(2,1)} %older_high_ref.3) | copy-start | bytes 4718596
  0.0 6.6 %copy-start.7 = (s32[16]{0:T(128)S(1)}, s32[16]{0:T(128)}, u32[]{:S(2)}) copy-start(s32[16]{0:T(128)} %param.5) | copy-start | bytes 196
  0.0 9.8 %copy-start.8 = (f32[6,512]{1,0:T(8,128)S(1)}, f32[6,512]{1,0:T(8,128)}, u32[]{:S(2)}) copy-start(f32[6,512]{1,0:T(8,128)} %param.4) | copy-start | bytes 36868
  2.8 7.1 %collective-permute-start = (bf16[3,8,64,256]{3,2,1,0:T(8,128)(2,1)}, bf16[3,8,64,256]{3,2,1,0:T(8,128)(2,1)S(1)}, u32[]{:S(2)}, u32[]{:S(2)}) collective-permute-start(bf16[3,8,64,256]{3,2,1,0:T(8,128)(2,1)} %get-tuple-element.21), channel_id=1, source_target_pairs={{0,1},{1,2},{2,3},{3,4},{4,5},{5,6},{6,7},{7,8},{8,9},{9,10},{10,1... | collective-permute-start | bytes 2359304 | tf_op jit(solution)/shard_map/ppermute | solution.py:190
  5.3 6.5 %collective-permute-start.1 = (bf16[3,8,64,256]{3,2,1,0:T(8,128)(2,1)}, bf16[3,8,64,256]{3,2,1,0:T(8,128)(2,1)S(1)}, u32[]{:S(2)}, u32[]{:S(2)}) collective-permute-start(bf16[3,8,64,256]{3,2,1,0:T(8,128)(2,1)} %get-tuple-element.22), channel_id=1, source_target_pairs={{1,0},{2,1},{3,2},{4,3},{5,4},{6,5},{7,6},{8,7},{9,8},{10,9},{11,1... | collective-permute-start | bytes 2359304 | tf_op jit(solution)/shard_map/ppermute | solution.py:191
  24.1 22.2 %copy-start.3 = (bf16[3,8,64,256]{3,2,1,0:T(8,128)(2,1)S(1)}, bf16[3,8,64,256]{3,2,1,0:T(8,128)(2,1)}, u32[]{:S(2)}) copy-start(bf16[3,8,64,256]{3,2,1,0:T(8,128)(2,1)} %get-tuple-element.14.older_low_ref) | copy-start | bytes 2359300
  24.1 22.2 %copy-start.4 = (bf16[3,8,64,256]{3,2,1,0:T(8,128)(2,1)S(1)}, bf16[3,8,64,256]{3,2,1,0:T(8,128)(2,1)}, u32[]{:S(2)}) copy-start(bf16[3,8,64,256]{3,2,1,0:T(8,128)(2,1)} %get-tuple-element.13.older_high_ref) | copy-start | bytes 2359300
  24.1 18.0 %collective-permute-start.2 = (bf16[3,8,64,256]{3,2,1,0:T(8,128)(2,1)}, bf16[3,8,64,256]{3,2,1,0:T(8,128)(2,1)S(1)}, u32[]{:S(2)}, u32[]{:S(2)}) collective-permute-start(bf16[3,8,64,256]{3,2,1,0:T(8,128)(2,1)} %get-tuple-element.13.older_high_ref), channel_id=1, source_target_pairs={{0,1},{1,2},{2,3},{3,4},{4,5},{5,6},{6,7},{7,8},{8,9},{9,10},{10,1... | collective-permute-start | bytes 2359304 | tf_op jit(solution)/shard_map/ppermute | solution.py:190
  40.0 6.2 %collective-permute-start.3 = (bf16[3,8,64,256]{3,2,1,0:T(8,128)(2,1)}, bf16[3,8,64,256]{3,2,1,0:T(8,128)(2,1)S(1)}, u32[]{:S(2)}, u32[]{:S(2)}) collective-permute-start(bf16[3,8,64,256]{3,2,1,0:T(8,128)(2,1)} %get-tuple-element.14.older_low_ref), channel_id=1, source_target_pairs={{1,0},{2,1},{3,2},{4,3},{5,4},{6,5},{7,6},{8,7},{9,8},{10,9},{11,1... | collective-permute-start | bytes 2359304 | tf_op jit(solution)/shard_map/ppermute | solution.py:191
  57.2 22.2 %copy-start.1 = (bf16[3,8,64,256]{3,2,1,0:T(8,128)(2,1)S(1)}, bf16[3,8,64,256]{3,2,1,0:T(8,128)(2,1)}, u32[]{:S(2)}) copy-start(bf16[3,8,64,256]{3,2,1,0:T(8,128)(2,1)} %get-tuple-element.16.older_low_ref) | copy-start | bytes 2359300
  57.2 22.2 %copy-start.2 = (bf16[3,8,64,256]{3,2,1,0:T(8,128)(2,1)S(1)}, bf16[3,8,64,256]{3,2,1,0:T(8,128)(2,1)}, u32[]{:S(2)}) copy-start(bf16[3,8,64,256]{3,2,1,0:T(8,128)(2,1)} %get-tuple-element.15.older_high_ref) | copy-start | bytes 2359300
  57.2 18.0 %collective-permute-start.4 = (bf16[3,8,64,256]{3,2,1,0:T(8,128)(2,1)}, bf16[3,8,64,256]{3,2,1,0:T(8,128)(2,1)S(1)}, u32[]{:S(2)}, u32[]{:S(2)}) collective-permute-start(bf16[3,8,64,256]{3,2,1,0:T(8,128)(2,1)} %get-tuple-element.15.older_high_ref), channel_id=1, source_target_pairs={{0,1},{1,2},{2,3},{3,4},{4,5},{5,6},{6,7},{7,8},{8,9},{9,10},{10,1... | collective-permute-start | bytes 2359304 | tf_op jit(solution)/shard_map/ppermute | solution.py:190
  73.1 6.2 %collective-permute-start.5 = (bf16[3,8,64,256]{3,2,1,0:T(8,128)(2,1)}, bf16[3,8,64,256]{3,2,1,0:T(8,128)(2,1)S(1)}, u32[]{:S(2)}, u32[]{:S(2)}) collective-permute-start(bf16[3,8,64,256]{3,2,1,0:T(8,128)(2,1)} %get-tuple-element.16.older_low_ref), channel_id=1, source_target_pairs={{1,0},{2,1},{3,2},{4,3},{5,4},{6,5},{7,6},{8,7},{9,8},{10,9},{11,1... | collective-permute-start | bytes 2359304 | tf_op jit(solution)/shard_map/ppermute | solution.py:191
  90.3 22.2 %copy-start.5 = (bf16[3,8,64,256]{3,2,1,0:T(8,128)(2,1)S(1)}, bf16[3,8,64,256]{3,2,1,0:T(8,128)(2,1)}, u32[]{:S(2)}) copy-start(bf16[3,8,64,256]{3,2,1,0:T(8,128)(2,1)} %get-tuple-element.18) | copy-start | bytes 2359300
  90.3 22.2 %copy-start.6 = (bf16[3,8,64,256]{3,2,1,0:T(8,128)(2,1)S(1)}, bf16[3,8,64,256]{3,2,1,0:T(8,128)(2,1)}, u32[]{:S(2)}) copy-start(bf16[3,8,64,256]{3,2,1,0:T(8,128)(2,1)} %get-tuple-element.17) | copy-start | bytes 2359300
  90.3 18.0 %collective-permute-start.6 = (bf16[3,8,64,256]{3,2,1,0:T(8,128)(2,1)}, bf16[3,8,64,256]{3,2,1,0:T(8,128)(2,1)S(1)}, u32[]{:S(2)}, u32[]{:S(2)}) collective-permute-start(bf16[3,8,64,256]{3,2,1,0:T(8,128)(2,1)} %get-tuple-element.17), channel_id=1, source_target_pairs={{0,1},{1,2},{2,3},{3,4},{4,5},{5,6},{6,7},{7,8},{8,9},{9,10},{10,1... | collective-permute-start | bytes 2359304 | tf_op jit(solution)/shard_map/ppermute | solution.py:190
  106.2 6.2 %collective-permute-start.7 = (bf16[3,8,64,256]{3,2,1,0:T(8,128)(2,1)}, bf16[3,8,64,256]{3,2,1,0:T(8,128)(2,1)S(1)}, u32[]{:S(2)}, u32[]{:S(2)}) collective-permute-start(bf16[3,8,64,256]{3,2,1,0:T(8,128)(2,1)} %get-tuple-element.18), channel_id=1, source_target_pairs={{1,0},{2,1},{3,2},{4,3},{5,4},{6,5},{7,6},{8,7},{9,8},{10,9},{11,1... | collective-permute-start | bytes 2359304 | tf_op jit(solution)/shard_map/ppermute | solution.py:191
  125.3 17.7 %collective-permute-start.12 = (f32[128,256]{1,0:T(8,128)S(1)}, f32[128,256]{1,0:T(8,128)S(1)}, u32[]{:S(2)}, u32[]{:S(2)}) collective-permute-start(f32[128,256]{1,0:T(8,128)S(1)} %fusion.2), channel_id=1, source_target_pairs={{1,0},{2,1},{3,2},{4,3},{5,4},{6,5},{7,6},{8,7},{9,8},{10,9},{11,1... | collective-permute-start | bytes 393224 | tf_op jit(solution)/shard_map/ppermute | solution.py:214
  126.6 17.3 %collective-permute-start.8 = (f32[128,256]{1,0:T(8,128)S(1)}, f32[128,256]{1,0:T(8,128)S(1)}, u32[]{:S(2)}, u32[]{:S(2)}) collective-permute-start(f32[128,256]{1,0:T(8,128)S(1)} %fusion.2), channel_id=1, source_target_pairs={{0,1},{1,2},{2,3},{3,4},{4,5},{5,6},{6,7},{7,8},{8,9},{9,10},{10,1... | collective-permute-start | bytes 393224 | tf_op jit(solution)/shard_map/ppermute | solution.py:213
  144.0 13.8 %collective-permute-start.9 = (f32[128,256]{1,0:T(8,128)S(1)}, f32[128,256]{1,0:T(8,128)S(1)}, u32[]{:S(2)}, u32[]{:S(2)}) collective-permute-start(f32[128,256]{1,0:T(8,128)S(1)} %get-tuple-element.23), channel_id=1, source_target_pairs={{0,2},{1,3},{2,4},{3,5},{4,6},{5,7},{6,8},{7,9},{8,10},{9,11},{10,... | collective-permute-start | bytes 393224 | tf_op jit(solution)/shard_map/ppermute | solution.py:213
  156.5 6.9 %collective-permute-start.13 = (f32[128,256]{1,0:T(8,128)S(1)}, f32[128,256]{1,0:T(8,128)S(1)}, u32[]{:S(2)}, u32[]{:S(2)}) collective-permute-start(f32[128,256]{1,0:T(8,128)S(1)} %get-tuple-element.24), channel_id=1, source_target_pairs={{2,0},{3,1},{4,2},{5,3},{6,4},{7,5},{8,6},{9,7},{10,8},{11,9},{12,... | collective-permute-start | bytes 393224 | tf_op jit(solution)/shard_map/ppermute | solution.py:214
  157.8 7.8 %collective-permute-start.10 = (f32[128,256]{1,0:T(8,128)S(1)}, f32[128,256]{1,0:T(8,128)S(1)}, u32[]{:S(2)}, u32[]{:S(2)}) collective-permute-start(f32[128,256]{1,0:T(8,128)S(1)} %multiply_add_fusion.4), channel_id=1, source_target_pairs={{0,4},{1,5},{2,6},{3,7},{4,8},{5,9},{6,10},{7,11},{8,12},{9,13},{1... | collective-permute-start | bytes 393224 | tf_op jit(solution)/shard_map/ppermute | solution.py:213
  163.3 6.9 %collective-permute-start.14 = (f32[128,256]{1,0:T(8,128)S(1)}, f32[128,256]{1,0:T(8,128)S(1)}, u32[]{:S(2)}, u32[]{:S(2)}) collective-permute-start(f32[128,256]{1,0:T(8,128)S(1)} %multiply_add_fusion.1), channel_id=1, source_target_pairs={{4,0},{5,1},{6,2},{7,3},{8,4},{9,5},{10,6},{11,7},{12,8},{13,9},{1... | collective-permute-start | bytes 393224 | tf_op jit(solution)/shard_map/ppermute | solution.py:214
  165.6 10.2 %collective-permute-start.11 = (f32[128,256]{1,0:T(8,128)S(1)}, f32[128,256]{1,0:T(8,128)S(1)}, u32[]{:S(2)}, u32[]{:S(2)}) collective-permute-start(f32[128,256]{1,0:T(8,128)S(1)} %multiply_add_fusion.3), channel_id=1, source_target_pairs={{0,8},{1,9},{2,10},{3,11},{4,12},{5,13},{6,14},{7,15},{16,24},{17,... | collective-permute-start | bytes 393224 | tf_op jit(solution)/shard_map/ppermute | solution.py:213
  170.2 8.9 %collective-permute-start.15 = (f32[128,256]{1,0:T(8,128)S(1)}, f32[128,256]{1,0:T(8,128)S(1)}, u32[]{:S(2)}, u32[]{:S(2)}) collective-permute-start(f32[128,256]{1,0:T(8,128)S(1)} %multiply_add_fusion), channel_id=1, source_target_pairs={{8,0},{9,1},{10,2},{11,3},{12,4},{13,5},{14,6},{15,7},{24,16},{25,... | collective-permute-start | bytes 393224 | tf_op jit(solution)/shard_map/ppermute | solution.py:214
  199.7 4.3 %collective-permute-start.20 = (f32[128,128]{1,0:T(8,128)S(1)}, f32[128,128]{1,0:T(8,128)S(1)}, u32[]{:S(2)}, u32[]{:S(2)}) collective-permute-start(f32[128,128]{1,0:T(8,128)S(1)} %fusion.13), channel_id=1, source_target_pairs={{1,0},{2,1},{3,2},{4,3},{5,4},{6,5},{7,6},{8,7},{9,8},{10,9},{11,1... | collective-permute-start | bytes 196616 | tf_op jit(solution)/shard_map/ppermute | solution.py:214
  201.0 3.9 %collective-permute-start.16 = (f32[128,128]{1,0:T(8,128)S(1)}, f32[128,128]{1,0:T(8,128)S(1)}, u32[]{:S(2)}, u32[]{:S(2)}) collective-permute-start(f32[128,128]{1,0:T(8,128)S(1)} %fusion.13), channel_id=1, source_target_pairs={{0,1},{1,2},{2,3},{3,4},{4,5},{5,6},{6,7},{7,8},{8,9},{9,10},{10,1... | collective-permute-start | bytes 196616 | tf_op jit(solution)/shard_map/ppermute | solution.py:213
  205.0 8.5 %collective-permute-start.17 = (f32[128,128]{1,0:T(8,128)S(1)}, f32[128,128]{1,0:T(8,128)S(1)}, u32[]{:S(2)}, u32[]{:S(2)}) collective-permute-start(f32[128,128]{1,0:T(8,128)S(1)} %get-tuple-element.25), channel_id=1, source_target_pairs={{0,2},{1,3},{2,4},{3,5},{4,6},{5,7},{6,8},{7,9},{8,10},{9,11},{10,... | collective-permute-start | bytes 196616 | tf_op jit(solution)/shard_map/ppermute | solution.py:213
  211.0 6.9 %collective-permute-start.21 = (f32[128,128]{1,0:T(8,128)S(1)}, f32[128,128]{1,0:T(8,128)S(1)}, u32[]{:S(2)}, u32[]{:S(2)}) collective-permute-start(f32[128,128]{1,0:T(8,128)S(1)} %get-tuple-element.26), channel_id=1, source_target_pairs={{2,0},{3,1},{4,2},{5,3},{6,4},{7,5},{8,6},{9,7},{10,8},{11,9},{12,... | collective-permute-start | bytes 196616 | tf_op jit(solution)/shard_map/ppermute | solution.py:214
  213.5 6.3 %collective-permute-start.18 = (f32[128,128]{1,0:T(8,128)S(1)}, f32[128,128]{1,0:T(8,128)S(1)}, u32[]{:S(2)}, u32[]{:S(2)}) collective-permute-start(f32[128,128]{1,0:T(8,128)S(1)} %multiply_add_fusion.10), channel_id=1, source_target_pairs={{0,4},{1,5},{2,6},{3,7},{4,8},{5,9},{6,10},{7,11},{8,12},{9,13},{1... | collective-permute-start | bytes 196616 | tf_op jit(solution)/shard_map/ppermute | solution.py:213
  217.9 6.2 %collective-permute-start.22 = (f32[128,128]{1,0:T(8,128)S(1)}, f32[128,128]{1,0:T(8,128)S(1)}, u32[]{:S(2)}, u32[]{:S(2)}) collective-permute-start(f32[128,128]{1,0:T(8,128)S(1)} %multiply_add_fusion.7), channel_id=1, source_target_pairs={{4,0},{5,1},{6,2},{7,3},{8,4},{9,5},{10,6},{11,7},{12,8},{13,9},{1... | collective-permute-start | bytes 196616 | tf_op jit(solution)/shard_map/ppermute | solution.py:214
  219.8 5.7 %collective-permute-start.19 = (f32[128,128]{1,0:T(8,128)S(1)}, f32[128,128]{1,0:T(8,128)S(1)}, u32[]{:S(2)}, u32[]{:S(2)}) collective-permute-start(f32[128,128]{1,0:T(8,128)S(1)} %multiply_add_fusion.9), channel_id=1, source_target_pairs={{0,8},{1,9},{2,10},{3,11},{4,12},{5,13},{6,14},{7,15},{16,24},{17,... | collective-permute-start | bytes 196616 | tf_op jit(solution)/shard_map/ppermute | solution.py:213
  224.1 7.8 %collective-permute-start.23 = (f32[128,128]{1,0:T(8,128)S(1)}, f32[128,128]{1,0:T(8,128)S(1)}, u32[]{:S(2)}, u32[]{:S(2)}) collective-permute-start(f32[128,128]{1,0:T(8,128)S(1)} %multiply_add_fusion.6), channel_id=1, source_target_pairs={{8,0},{9,1},{10,2},{11,3},{12,4},{13,5},{14,6},{15,7},{24,16},{25,... | collective-permute-start | bytes 196616 | tf_op jit(solution)/shard_map/ppermute | solution.py:214

commit v7 on v6

--- a/solution.py
+++ b/solution.py
@@ -164,6 +164,23 @@
     slabs = lax.axis_size("gz")
     position = lax.axis_index("gz")
     planes = waves.shape[0]
+
+    def shifted(field, distance):
+        step = abs(distance)
+        pairs = [(i, i + step) for i in range(slabs - step)]
+        if distance < 0:
+            pairs = [(target, source) for source, target in pairs]
+        first = [(s, t) for s, t in pairs if (min(s, t) // step) % 2 == 0]
+        second = [(s, t) for s, t in pairs if (min(s, t) // step) % 2 == 1]
+        got = lax.ppermute(field, "gz", first)
+        if not second:
+            return got
+        other = lax.ppermute(field, "gz", second)
+        table = [0] * slabs
+        for s, t in second:
+            table[t] = 1
+        late = jnp.asarray(table, jnp.int32)[position] == 1
+        return jnp.where(late, other, got)
     bands = waves.shape[3]
     grid = potential.reshape(planes, NY, NX)
     owner = domain_of[position]
@@ -181,14 +198,12 @@
         ]
     )[:, None, None, None]
 
-    forward = [(i, i + 1) for i in range(slabs - 1)]
-    backward = [(target, source) for source, target in forward]
     bf_below = below.astype(jnp.bfloat16)
     bf_above = above.astype(jnp.bfloat16)
 
     def rimmed(low, high):
-        from_below = lax.ppermute(high, "gz", forward)
-        from_above = lax.ppermute(low, "gz", backward)
+        from_below = shifted(high, 1)
+        from_above = shifted(low, -1)
         return jnp.concatenate([from_below * bf_below, low, high, from_above * bf_above], axis=0)
 
     lanes = jnp.broadcast_to(grid[..., None], grid.shape + (128,))
@@ -208,10 +223,8 @@
         backward = term
         distance = 1
         while distance < slabs:
-            ahead = [(i, i + distance) for i in range(slabs - distance)]
-            behind = [(i + distance, i) for i in range(slabs - distance)]
-            from_low = lax.ppermute(forward, "gz", ahead)
-            from_high = lax.ppermute(backward, "gz", behind)
+            from_low = shifted(forward, distance)
+            from_high = shifted(backward, -distance)
             low_same = jnp.where(
                 position >= distance,
                 domain_of[jnp.maximum(position - distance, 0)] == owner,

time: 254 us -> 296 us (1.17)
  starting transfers between devices: 116 us -> 155 us
  waiting for transfers between devices: 32.1 us -> 24.9 us
  between operations: 11 us -> 16.1 us
  local copies, waits for them, and re-layouts: 7.44 us -> 10.8 us
    ppermute x24 -> x44, starting transfers between devices: 116 us -> 155 us  [the longest x24 139 us: shifted(): got = lax.ppermute(field, 'gz', first)]
    ppermute x24 -> x44, waiting for transfers between devices: 32.1 us -> 24.9 us  [the longest x24 24.8 us: shifted(): got = lax.ppermute(field, 'gz', first)]
    dynamic_slice x0 -> x6, local copies, waits for them, and re-layouts: none -> 3.68 us  [shifted(): late = jnp.asarray(table, jnp.int32)[position] == 1]
  transfers between devices with their start and end apart: 24 -> 44, of which waited for: 18 -> 8; matrix products, arithmetic and copies ran while one was open for 1% -> 3% of each run, Pallas kernels for 0% -> 0%
where the time goes in v7:
time: 296 us; the launch traced here: 294 us
  starting transfers between devices  155 us (52%)
  Pallas kernels  69.6 us (24%)
  waiting for transfers between devices  24.9 us (8%)
  between operations  16.1 us (5%)
  other arithmetic  13.1 us (4%)
  local copies, waits for them, and re-layouts  10.8 us (4%)
  matrix products  4.57 us (2%)
    ppermute x24, starting transfers between devices, shifted(): got = lax.ppermute(field, 'gz', first)  139 us
    pallas_call x4, Pallas kernels, chebyshev_step(): pl.pallas_call(functools.partial(_step_kernel, first), out_shape=(piece,...  35.7 us
    pallas_call x2, Pallas kernels, lower_inverse(): pl.pallas_call(_lower_inverse_kernel, out_shape=jax.ShapeDtypeStruct((n,...  33.9 us
    ppermute x24, waiting for transfers between devices, shifted(): got = lax.ppermute(field, 'gz', first)  24.8 us
    ppermute x20, starting transfers between devices, shifted(): other = lax.ppermute(field, 'gz', second)  15.4 us
    concatenate x4, other arithmetic, rimmed(): jnp.concatenate([from_below * bf_below, low, high, from_above * bf_above]...  7.36 us
  transfers between devices with their start and end apart: 44, of which 8 were waited for; matrix products, arithmetic and copies ran while one was open for 3% of the time, Pallas kernels for 0%

profile of v7, /device:TPU:0, one launch (start us, length us, event | category | flops | bytes accessed | tf_op | source)
XLA Modules:
  0.0 293.8 jit_solution(7828457651905926453)
XLA Ops:
  0.0 2.4 fusion.11
  2.5 3.4 %collective-permute-start.1 = (bf16[3,8,64,256]{3,2,1,0:T(8,128)(2,1)}, bf16[3,8,64,256]{3,2,1,0:T(8,128)(2,1)}, u32[]{:S(2)}, u32[]{:S(2)}) collective-permute-start(bf16[3,8,64,256]{3,2,1,0:T(8,128)(2,1)} %get-tuple-element.21), channel_id=1, source_target_pairs={{0,1},{2,3},{4,5},{6,7},{8,9},{10,11},{12,13},{14,15},{16,17},{18,... | collective-permute-start | bytes 2359304 | tf_op jit(solution)/shard_map/ppermute | solution.py:175
  5.9 1.6 collective-permute-start
  7.4 1.3 collective-permute-start.3
  8.7 1.6 collective-permute-start.2
  10.3 0.7 dynamic_slice.103
  13.0 0.7 fusion.12
  16.6 1.2 select_multiply_fusion.7
  18.0 1.8 pad_maximum_fusion.extended_ref
  19.8 1.6 broadcast_in_dim.8.low_pot_ref.high_pot_ref
  21.4 8.8 %shard_map.217 = (bf16[3,8,64,256]{3,2,1,0:T(8,128)(2,1)}, bf16[3,8,64,256]{3,2,1,0:T(8,128)(2,1)}) custom-call(bf16[12,8,64,256]{3,2,1,0:T(8,128)(2,1)} %pad_maximum_fusion.extended_ref, bf16[6,8,64,256]{3,2,1,0:T(8,128)(2,1)} %older_high_ref.3, bf16[6,8,64,256]{3,2,1,0:T(8,128)(2,1)} %older_high_ref.3, ...), custom_call_target="tpu_custom_call" | custom-call | tf_op jit(solution)/shard_map/pallas_call | solution.py:107
  30.2 14.5 %collective-permute-start.5 = (bf16[3,8,64,256]{3,2,1,0:T(8,128)(2,1)}, bf16[3,8,64,256]{3,2,1,0:T(8,128)(2,1)S(1)}, u32[]{:S(2)}, u32[]{:S(2)}) collective-permute-start(bf16[3,8,64,256]{3,2,1,0:T(8,128)(2,1)} %get-tuple-element.13.older_high_ref), channel_id=1, source_target_pairs={{0,1},{2,3},{4,5},{6,7},{8,9},{10,11},{12,13},{14,15},{16,17},{18,... | collective-permute-start | bytes 2359304 | tf_op jit(solution)/shard_map/ppermute | solution.py:175
  44.7 0.7 collective-permute-start.4
  45.4 1.3 collective-permute-start.7
  46.7 0.7 collective-permute-start.6
  47.5 3.1 %collective-permute-done.7 = bf16[3,8,64,256]{3,2,1,0:T(8,128)(2,1)S(1)} collective-permute-done((bf16[3,8,64,256]{3,2,1,0:T(8,128)(2,1)}, bf16[3,8,64,256]{3,2,1,0:T(8,128)(2,1)S(1)}, u32[]{:S(2)}, u32[]{:S(2)}) %collective-permute-start.7) | collective-permute-done | bytes 786464 | tf_op jit(solution)/shard_map/ppermute | solution.py:175
  50.8 1.8 pad_maximum_fusion.1.extended_ref
  52.6 9.0 %shard_map.218 = (bf16[3,8,64,256]{3,2,1,0:T(8,128)(2,1)}, bf16[3,8,64,256]{3,2,1,0:T(8,128)(2,1)}) custom-call(bf16[12,8,64,256]{3,2,1,0:T(8,128)(2,1)} %pad_maximum_fusion.1.extended_ref, bf16[6,8,64,256]{3,2,1,0:T(8,128)(2,1)} %older_high_ref.3, bf16[6,8,64,256]{3,2,1,0:T(8,128)(2,1)} %older_high_ref.3, ...), custom_call_target="tpu_custom_call" | custom-call | tf_op jit(solution)/shard_map/pallas_call | solution.py:107
  61.6 16.5 %collective-permute-start.9 = (bf16[3,8,64,256]{3,2,1,0:T(8,128)(2,1)}, bf16[3,8,64,256]{3,2,1,0:T(8,128)(2,1)S(1)}, u32[]{:S(2)}, u32[]{:S(2)}) collective-permute-start(bf16[3,8,64,256]{3,2,1,0:T(8,128)(2,1)} %get-tuple-element.15.older_high_ref), channel_id=1, source_target_pairs={{0,1},{2,3},{4,5},{6,7},{8,9},{10,11},{12,13},{14,15},{16,17},{18,... | collective-permute-start | bytes 2359304 | tf_op jit(solution)/shard_map/ppermute | solution.py:175
  78.1 0.7 collective-permute-start.8
  78.9 1.3 collective-permute-start.11
  80.2 0.7 collective-permute-start.10
  81.0 4.1 %collective-permute-done.11 = bf16[3,8,64,256]{3,2,1,0:T(8,128)(2,1)S(1)} collective-permute-done((bf16[3,8,64,256]{3,2,1,0:T(8,128)(2,1)}, bf16[3,8,64,256]{3,2,1,0:T(8,128)(2,1)S(1)}, u32[]{:S(2)}, u32[]{:S(2)}) %collective-permute-start.11) | collective-permute-done | bytes 786464 | tf_op jit(solution)/shard_map/ppermute | solution.py:175
  85.2 1.8 pad_maximum_fusion.2.extended_ref
  87.1 9.0 %shard_map.219 = (bf16[3,8,64,256]{3,2,1,0:T(8,128)(2,1)}, bf16[3,8,64,256]{3,2,1,0:T(8,128)(2,1)}) custom-call(bf16[12,8,64,256]{3,2,1,0:T(8,128)(2,1)} %pad_maximum_fusion.2.extended_ref, bf16[3,8,64,256]{3,2,1,0:T(8,128)(2,1)} %get-tuple-element.14.older_low_ref, bf16[3,8,64,256]{3,2,1,0:T(8,128)(2,1)} %get-tuple-element.13.older_high_ref, ...), custom_call_target="tpu_custom_call" | custom-call | tf_op jit(solution)/shard_map/pallas_call | solution.py:107
  96.1 13.7 %collective-permute-start.13 = (bf16[3,8,64,256]{3,2,1,0:T(8,128)(2,1)}, bf16[3,8,64,256]{3,2,1,0:T(8,128)(2,1)S(1)}, u32[]{:S(2)}, u32[]{:S(2)}) collective-permute-start(bf16[3,8,64,256]{3,2,1,0:T(8,128)(2,1)} %get-tuple-element.17), channel_id=1, source_target_pairs={{0,1},{2,3},{4,5},{6,7},{8,9},{10,11},{12,13},{14,15},{16,17},{18,... | collective-permute-start | bytes 2359304 | tf_op jit(solution)/shard_map/ppermute | solution.py:175
  109.8 0.7 collective-permute-start.12
  110.5 1.3 collective-permute-start.15
  111.8 0.7 collective-permute-start.14
  112.6 7.3 %collective-permute-done.15 = bf16[3,8,64,256]{3,2,1,0:T(8,128)(2,1)S(1)} collective-permute-done((bf16[3,8,64,256]{3,2,1,0:T(8,128)(2,1)}, bf16[3,8,64,256]{3,2,1,0:T(8,128)(2,1)S(1)}, u32[]{:S(2)}, u32[]{:S(2)}) %collective-permute-start.15) | collective-permute-done | bytes 786464 | tf_op jit(solution)/shard_map/ppermute | solution.py:175
  120.1 1.8 pad_maximum_fusion.3.extended_ref
  121.9 9.0 %shard_map.220 = (bf16[3,8,64,256]{3,2,1,0:T(8,128)(2,1)}, bf16[3,8,64,256]{3,2,1,0:T(8,128)(2,1)}) custom-call(bf16[12,8,64,256]{3,2,1,0:T(8,128)(2,1)} %pad_maximum_fusion.3.extended_ref, bf16[3,8,64,256]{3,2,1,0:T(8,128)(2,1)} %get-tuple-element.16.older_low_ref, bf16[3,8,64,256]{3,2,1,0:T(8,128)(2,1)} %get-tuple-element.15.older_high_ref, ...), custom_call_target="tpu_custom_call" | custom-call | tf_op jit(solution)/shard_map/pallas_call | solution.py:107
  130.9 1.5 pad_maximum_fusion.4
  132.9 1.3 collective-permute-start.24
  134.2 0.7 collective-permute-start.23
  134.8 14.1 %collective-permute-start.17 = (f32[128,256]{1,0:T(8,128)S(1)}, f32[128,256]{1,0:T(8,128)S(1)}, u32[]{:S(2)}, u32[]{:S(2)}) collective-permute-start(f32[128,256]{1,0:T(8,128)S(1)} %fusion.2), channel_id=1, source_target_pairs={{0,1},{2,3},{4,5},{6,7},{8,9},{10,11},{12,13},{14,15},{16,17},{18,... | collective-permute-start | bytes 393224 | tf_op jit(solution)/shard_map/ppermute | solution.py:175
  149.0 0.7 collective-permute-start.16
  150.0 13.0 %collective-permute-start.19 = (f32[128,256]{1,0:T(8,128)S(1)}, f32[128,256]{1,0:T(8,128)S(1)}, u32[]{:S(2)}, u32[]{:S(2)}) collective-permute-start(f32[128,256]{1,0:T(8,128)S(1)} %get-tuple-element.23), channel_id=1, source_target_pairs={{0,2},{1,3},{4,6},{5,7},{8,10},{9,11},{12,14},{13,15},{16,18},{17,... | collective-permute-start | bytes 393224 | tf_op jit(solution)/shard_map/ppermute | solution.py:175
  162.9 0.7 collective-permute-start.18
  173.8 1.3 collective-permute-start.26
  175.1 0.7 collective-permute-start.25
  175.8 12.3 %collective-permute-start.21 = (f32[128,256]{1,0:T(8,128)S(1)}, f32[128,256]{1,0:T(8,128)S(1)}, u32[]{:S(2)}, u32[]{:S(2)}) collective-permute-start(f32[128,256]{1,0:T(8,128)S(1)} %multiply_add_fusion.4), channel_id=1, source_target_pairs={{0,4},{1,5},{2,6},{3,7},{8,12},{9,13},{10,14},{11,15},{16,20},{17,... | collective-permute-start | bytes 393224 | tf_op jit(solution)/shard_map/ppermute | solution.py:175
  188.2 0.7 collective-permute-start.20
  188.9 1.3 collective-permute-start.28
  190.2 0.7 collective-permute-start.27
  190.9 9.0 %collective-permute-start.22 = (f32[128,256]{1,0:T(8,128)S(1)}, f32[128,256]{1,0:T(8,128)S(1)}, u32[]{:S(2)}, u32[]{:S(2)}) collective-permute-start(f32[128,256]{1,0:T(8,128)S(1)} %multiply_add_fusion.3), channel_id=1, source_target_pairs={{0,8},{1,9},{2,10},{3,11},{4,12},{5,13},{6,14},{7,15},{16,24},{17,... | collective-permute-start | bytes 393224 | tf_op jit(solution)/shard_map/ppermute | solution.py:175
  200.0 1.3 collective-permute-start.29
  203.9 1.3 fusion.10
  205.9 3.3 %collective-permute-done.29 = f32[128,256]{1,0:T(8,128)S(1)} collective-permute-done((f32[128,256]{1,0:T(8,128)S(1)}, f32[128,256]{1,0:T(8,128)S(1)}, u32[]{:S(2)}, u32[]{:S(2)}) %collective-permute-start.29) | collective-permute-done | bytes 131104 | tf_op jit(solution)/shard_map/ppermute | solution.py:175
  209.9 16.9 %shard_map.221 = f32[128,128]{1,0:T(8,128)} custom-call(f32[128,128]{1,0:T(8,128)} %slice.26.gram_ref), custom_call_target="tpu_custom_call" | custom-call | tf_op jit(solution)/shard_map/pallas_call | solution.py:48
  226.8 1.2 convolution_convert_fusion.1
  228.0 1.3 fusion
  229.8 1.3 collective-permute-start.38
  231.8 3.7 %collective-permute-start.31 = (f32[128,128]{1,0:T(8,128)S(1)}, f32[128,128]{1,0:T(8,128)S(1)}, u32[]{:S(2)}, u32[]{:S(2)}) collective-permute-start(f32[128,128]{1,0:T(8,128)S(1)} %fusion.13), channel_id=1, source_target_pairs={{0,1},{2,3},{4,5},{6,7},{8,9},{10,11},{12,13},{14,15},{16,17},{18,... | collective-permute-start | bytes 196616 | tf_op jit(solution)/shard_map/ppermute | solution.py:175
  236.3 8.2 %collective-permute-start.33 = (f32[128,128]{1,0:T(8,128)S(1)}, f32[128,128]{1,0:T(8,128)S(1)}, u32[]{:S(2)}, u32[]{:S(2)}) collective-permute-start(f32[128,128]{1,0:T(8,128)S(1)} %get-tuple-element.25), channel_id=1, source_target_pairs={{0,2},{1,3},{4,6},{5,7},{8,10},{9,11},{12,14},{13,15},{16,18},{17,... | collective-permute-start | bytes 196616 | tf_op jit(solution)/shard_map/ppermute | solution.py:175
  245.3 1.3 collective-permute-start.40
  247.3 7.5 %collective-permute-start.35 = (f32[128,128]{1,0:T(8,128)S(1)}, f32[128,128]{1,0:T(8,128)S(1)}, u32[]{:S(2)}, u32[]{:S(2)}) collective-permute-start(f32[128,128]{1,0:T(8,128)S(1)} %multiply_add_fusion.10), channel_id=1, source_target_pairs={{0,4},{1,5},{2,6},{3,7},{8,12},{9,13},{10,14},{11,15},{16,20},{17,... | collective-permute-start | bytes 196616 | tf_op jit(solution)/shard_map/ppermute | solution.py:175
  255.5 1.3 collective-permute-start.42
  257.5 8.0 %collective-permute-start.36 = (f32[128,128]{1,0:T(8,128)S(1)}, f32[128,128]{1,0:T(8,128)S(1)}, u32[]{:S(2)}, u32[]{:S(2)}) collective-permute-start(f32[128,128]{1,0:T(8,128)S(1)} %multiply_add_fusion.9), channel_id=1, source_target_pairs={{0,8},{1,9},{2,10},{3,11},{4,12},{5,13},{6,14},{7,15},{16,24},{17,... | collective-permute-start | bytes 196616 | tf_op jit(solution)/shard_map/ppermute | solution.py:175
  265.5 1.3 collective-permute-start.43
  267.4 5.9 %collective-permute-done.43 = f32[128,128]{1,0:T(8,128)S(1)} collective-permute-done((f32[128,128]{1,0:T(8,128)S(1)}, f32[128,128]{1,0:T(8,128)S(1)}, u32[]{:S(2)}, u32[]{:S(2)}) %collective-permute-start.43) | collective-permute-done | bytes 65568 | tf_op jit(solution)/shard_map/ppermute | solution.py:175
  273.9 16.9 %shard_map.222 = f32[128,128]{1,0:T(8,128)} custom-call(f32[128,128]{1,0:T(8,128)} %subtract_divide_fusion.1.gram_ref), custom_call_target="tpu_custom_call" | custom-call | tf_op jit(solution)/shard_map/pallas_call | solution.py:48
  290.9 1.2 convolution_convert_fusion
  292.2 1.6 copy.25
  (104 shorter events, 11.3 us)
Async XLA Ops:
  0.0 10.3 %copy-start.14 = (s32[16]{0:T(128)S(1)}, s32[16]{0:T(128)}, u32[]{:S(2)}) copy-start(s32[16]{0:T(128)} %constant.70.clone) | copy-start | bytes 196
  0.0 11.0 %copy-start.13 = (s32[16]{0:T(128)S(1)}, s32[16]{0:T(128)}, u32[]{:S(2)}) copy-start(s32[16]{0:T(128)} %constant.69.clone) | copy-start | bytes 196
  0.0 13.0 %copy-start.7 = (s32[16]{0:T(128)S(1)}, s32[16]{0:T(128)}, u32[]{:S(2)}) copy-start(s32[16]{0:T(128)} %param.25) | copy-start | bytes 196
  0.0 16.5 %copy-start.8 = (f32[6,512]{1,0:T(8,128)S(1)}, f32[6,512]{1,0:T(8,128)}, u32[]{:S(2)}) copy-start(f32[6,512]{1,0:T(8,128)} %param.24) | copy-start | bytes 36868
  2.5 15.5 %copy-start = (bf16[6,8,64,256]{3,2,1,0:T(8,128)(2,1)S(1)}, bf16[6,8,64,256]{3,2,1,0:T(8,128)(2,1)}, u32[]{:S(2)}) copy-start(bf16[6,8,64,256]{3,2,1,0:T(8,128)(2,1)} %older_high_ref.3) | copy-start | bytes 4718596
  2.5 14.2 %collective-permute-start.1 = (bf16[3,8,64,256]{3,2,1,0:T(8,128)(2,1)}, bf16[3,8,64,256]{3,2,1,0:T(8,128)(2,1)}, u32[]{:S(2)}, u32[]{:S(2)}) collective-permute-start(bf16[3,8,64,256]{3,2,1,0:T(8,128)(2,1)} %get-tuple-element.21), channel_id=1, source_target_pairs={{0,1},{2,3},{4,5},{6,7},{8,9},{10,11},{12,13},{14,15},{16,17},{18,... | collective-permute-start | bytes 2359304 | tf_op jit(solution)/shard_map/ppermute | solution.py:175
  5.9 10.8 %collective-permute-start = (bf16[3,8,64,256]{3,2,1,0:T(8,128)(2,1)}, bf16[3,8,64,256]{3,2,1,0:T(8,128)(2,1)}, u32[]{:S(2)}, u32[]{:S(2)}) collective-permute-start(bf16[3,8,64,256]{3,2,1,0:T(8,128)(2,1)} %get-tuple-element.21), channel_id=1, source_target_pairs={{1,2},{3,4},{5,6},{7,8},{9,10},{11,12},{13,14},{17,18},{19,20},{21... | collective-permute-start | bytes 2359304 | tf_op jit(solution)/shard_map/ppermute | solution.py:178
  7.4 10.4 %collective-permute-start.3 = (bf16[3,8,64,256]{3,2,1,0:T(8,128)(2,1)S(1)}, bf16[3,8,64,256]{3,2,1,0:T(8,128)(2,1)S(1)}, u32[]{:S(2)}, u32[]{:S(2)}) collective-permute-start(bf16[3,8,64,256]{3,2,1,0:T(8,128)(2,1)S(1)} %get-tuple-element.22), channel_id=1, source_target_pairs={{1,0},{3,2},{5,4},{7,6},{9,8},{11,10},{13,12},{15,14},{17,16},{19,... | collective-permute-start | bytes 2359304 | tf_op jit(solution)/shard_map/ppermute | solution.py:175
  8.7 9.1 %collective-permute-start.2 = (bf16[3,8,64,256]{3,2,1,0:T(8,128)(2,1)S(1)}, bf16[3,8,64,256]{3,2,1,0:T(8,128)(2,1)}, u32[]{:S(2)}, u32[]{:S(2)}) collective-permute-start(bf16[3,8,64,256]{3,2,1,0:T(8,128)(2,1)S(1)} %get-tuple-element.22), channel_id=1, source_target_pairs={{2,1},{4,3},{6,5},{8,7},{10,9},{12,11},{14,13},{18,17},{20,19},{22... | collective-permute-start | bytes 2359304 | tf_op jit(solution)/shard_map/ppermute | solution.py:178
  30.2 20.5 %copy-start.3 = (bf16[3,8,64,256]{3,2,1,0:T(8,128)(2,1)S(1)}, bf16[3,8,64,256]{3,2,1,0:T(8,128)(2,1)}, u32[]{:S(2)}) copy-start(bf16[3,8,64,256]{3,2,1,0:T(8,128)(2,1)} %get-tuple-element.14.older_low_ref) | copy-start | bytes 2359300
  30.2 20.6 %copy-start.4 = (bf16[3,8,64,256]{3,2,1,0:T(8,128)(2,1)S(1)}, bf16[3,8,64,256]{3,2,1,0:T(8,128)(2,1)}, u32[]{:S(2)}) copy-start(bf16[3,8,64,256]{3,2,1,0:T(8,128)(2,1)} %get-tuple-element.13.older_high_ref) | copy-start | bytes 2359300
  30.2 17.2 %collective-permute-start.5 = (bf16[3,8,64,256]{3,2,1,0:T(8,128)(2,1)}, bf16[3,8,64,256]{3,2,1,0:T(8,128)(2,1)S(1)}, u32[]{:S(2)}, u32[]{:S(2)}) collective-permute-start(bf16[3,8,64,256]{3,2,1,0:T(8,128)(2,1)} %get-tuple-element.13.older_high_ref), channel_id=1, source_target_pairs={{0,1},{2,3},{4,5},{6,7},{8,9},{10,11},{12,13},{14,15},{16,17},{18,... | collective-permute-start | bytes 2359304 | tf_op jit(solution)/shard_map/ppermute | solution.py:175
  44.7 2.8 collective-permute-start.4
  45.4 5.2 %collective-permute-start.7 = (bf16[3,8,64,256]{3,2,1,0:T(8,128)(2,1)}, bf16[3,8,64,256]{3,2,1,0:T(8,128)(2,1)S(1)}, u32[]{:S(2)}, u32[]{:S(2)}) collective-permute-start(bf16[3,8,64,256]{3,2,1,0:T(8,128)(2,1)} %get-tuple-element.14.older_low_ref), channel_id=1, source_target_pairs={{1,0},{3,2},{5,4},{7,6},{9,8},{11,10},{13,12},{15,14},{17,16},{19,... | collective-permute-start | bytes 2359304 | tf_op jit(solution)/shard_map/ppermute | solution.py:175
  46.7 4.0 %collective-permute-start.6 = (bf16[3,8,64,256]{3,2,1,0:T(8,128)(2,1)}, bf16[3,8,64,256]{3,2,1,0:T(8,128)(2,1)S(1)}, u32[]{:S(2)}, u32[]{:S(2)}) collective-permute-start(bf16[3,8,64,256]{3,2,1,0:T(8,128)(2,1)} %get-tuple-element.14.older_low_ref), channel_id=1, source_target_pairs={{2,1},{4,3},{6,5},{8,7},{10,9},{12,11},{14,13},{18,17},{20,19},{22... | collective-permute-start | bytes 2359304 | tf_op jit(solution)/shard_map/ppermute | solution.py:178
  61.6 23.6 %copy-start.1 = (bf16[3,8,64,256]{3,2,1,0:T(8,128)(2,1)S(1)}, bf16[3,8,64,256]{3,2,1,0:T(8,128)(2,1)}, u32[]{:S(2)}) copy-start(bf16[3,8,64,256]{3,2,1,0:T(8,128)(2,1)} %get-tuple-element.16.older_low_ref) | copy-start | bytes 2359300
  61.6 23.6 %copy-start.2 = (bf16[3,8,64,256]{3,2,1,0:T(8,128)(2,1)S(1)}, bf16[3,8,64,256]{3,2,1,0:T(8,128)(2,1)}, u32[]{:S(2)}) copy-start(bf16[3,8,64,256]{3,2,1,0:T(8,128)(2,1)} %get-tuple-element.15.older_high_ref) | copy-start | bytes 2359300
  61.6 19.3 %collective-permute-start.9 = (bf16[3,8,64,256]{3,2,1,0:T(8,128)(2,1)}, bf16[3,8,64,256]{3,2,1,0:T(8,128)(2,1)S(1)}, u32[]{:S(2)}, u32[]{:S(2)}) collective-permute-start(bf16[3,8,64,256]{3,2,1,0:T(8,128)(2,1)} %get-tuple-element.15.older_high_ref), channel_id=1, source_target_pairs={{0,1},{2,3},{4,5},{6,7},{8,9},{10,11},{12,13},{14,15},{16,17},{18,... | collective-permute-start | bytes 2359304 | tf_op jit(solution)/shard_map/ppermute | solution.py:175
  78.1 2.8 collective-permute-start.8
  78.9 6.3 %collective-permute-start.11 = (bf16[3,8,64,256]{3,2,1,0:T(8,128)(2,1)}, bf16[3,8,64,256]{3,2,1,0:T(8,128)(2,1)S(1)}, u32[]{:S(2)}, u32[]{:S(2)}) collective-permute-start(bf16[3,8,64,256]{3,2,1,0:T(8,128)(2,1)} %get-tuple-element.16.older_low_ref), channel_id=1, source_target_pairs={{1,0},{3,2},{5,4},{7,6},{9,8},{11,10},{13,12},{15,14},{17,16},{19,... | collective-permute-start | bytes 2359304 | tf_op jit(solution)/shard_map/ppermute | solution.py:175
  80.2 5.0 %collective-permute-start.10 = (bf16[3,8,64,256]{3,2,1,0:T(8,128)(2,1)}, bf16[3,8,64,256]{3,2,1,0:T(8,128)(2,1)S(1)}, u32[]{:S(2)}, u32[]{:S(2)}) collective-permute-start(bf16[3,8,64,256]{3,2,1,0:T(8,128)(2,1)} %get-tuple-element.16.older_low_ref), channel_id=1, source_target_pairs={{2,1},{4,3},{6,5},{8,7},{10,9},{12,11},{14,13},{18,17},{20,19},{22... | collective-permute-start | bytes 2359304 | tf_op jit(solution)/shard_map/ppermute | solution.py:178
  96.1 24.0 %copy-start.5 = (bf16[3,8,64,256]{3,2,1,0:T(8,128)(2,1)S(1)}, bf16[3,8,64,256]{3,2,1,0:T(8,128)(2,1)}, u32[]{:S(2)}) copy-start(bf16[3,8,64,256]{3,2,1,0:T(8,128)(2,1)} %get-tuple-element.18) | copy-start | bytes 2359300
  96.1 24.0 %copy-start.6 = (bf16[3,8,64,256]{3,2,1,0:T(8,128)(2,1)S(1)}, bf16[3,8,64,256]{3,2,1,0:T(8,128)(2,1)}, u32[]{:S(2)}) copy-start(bf16[3,8,64,256]{3,2,1,0:T(8,128)(2,1)} %get-tuple-element.17) | copy-start | bytes 2359300
  96.1 16.4 %collective-permute-start.13 = (bf16[3,8,64,256]{3,2,1,0:T(8,128)(2,1)}, bf16[3,8,64,256]{3,2,1,0:T(8,128)(2,1)S(1)}, u32[]{:S(2)}, u32[]{:S(2)}) collective-permute-start(bf16[3,8,64,256]{3,2,1,0:T(8,128)(2,1)} %get-tuple-element.17), channel_id=1, source_target_pairs={{0,1},{2,3},{4,5},{6,7},{8,9},{10,11},{12,13},{14,15},{16,17},{18,... | collective-permute-start | bytes 2359304 | tf_op jit(solution)/shard_map/ppermute | solution.py:175
  109.8 2.8 collective-permute-start.12
  110.5 9.5 %collective-permute-start.15 = (bf16[3,8,64,256]{3,2,1,0:T(8,128)(2,1)}, bf16[3,8,64,256]{3,2,1,0:T(8,128)(2,1)S(1)}, u32[]{:S(2)}, u32[]{:S(2)}) collective-permute-start(bf16[3,8,64,256]{3,2,1,0:T(8,128)(2,1)} %get-tuple-element.18), channel_id=1, source_target_pairs={{1,0},{3,2},{5,4},{7,6},{9,8},{11,10},{13,12},{15,14},{17,16},{19,... | collective-permute-start | bytes 2359304 | tf_op jit(solution)/shard_map/ppermute | solution.py:175
  111.8 8.2 %collective-permute-start.14 = (bf16[3,8,64,256]{3,2,1,0:T(8,128)(2,1)}, bf16[3,8,64,256]{3,2,1,0:T(8,128)(2,1)S(1)}, u32[]{:S(2)}, u32[]{:S(2)}) collective-permute-start(bf16[3,8,64,256]{3,2,1,0:T(8,128)(2,1)} %get-tuple-element.18), channel_id=1, source_target_pairs={{2,1},{4,3},{6,5},{8,7},{10,9},{12,11},{14,13},{18,17},{20,19},{22... | collective-permute-start | bytes 2359304 | tf_op jit(solution)/shard_map/ppermute | solution.py:178
  130.9 32.8 %copy-start.12 = (s32[16]{0:T(128)S(1)}, s32[16]{0:T(128)}, u32[]{:S(2)}) copy-start(s32[16]{0:T(128)} %constant.74.clone) | copy-start | bytes 196
  130.9 34.0 %copy-start.11 = (s32[16]{0:T(128)S(1)}, s32[16]{0:T(128)}, u32[]{:S(2)}) copy-start(s32[16]{0:T(128)} %constant.73.clone) | copy-start | bytes 196
  130.9 35.3 %copy-start.10 = (s32[16]{0:T(128)S(1)}, s32[16]{0:T(128)}, u32[]{:S(2)}) copy-start(s32[16]{0:T(128)} %constant.72.clone) | copy-start | bytes 196
  130.9 36.5 %copy-start.9 = (s32[16]{0:T(128)S(1)}, s32[16]{0:T(128)}, u32[]{:S(2)}) copy-start(s32[16]{0:T(128)} %constant.71.clone) | copy-start | bytes 196
  132.9 16.8 %collective-permute-start.24 = (f32[128,256]{1,0:T(8,128)S(1)}, f32[128,256]{1,0:T(8,128)S(1)}, u32[]{:S(2)}, u32[]{:S(2)}) collective-permute-start(f32[128,256]{1,0:T(8,128)S(1)} %fusion.2), channel_id=1, source_target_pairs={{1,0},{3,2},{5,4},{7,6},{9,8},{11,10},{13,12},{15,14},{17,16},{19,... | collective-permute-start | bytes 393224 | tf_op jit(solution)/shard_map/ppermute | solution.py:175
  134.2 15.5 %collective-permute-start.23 = (f32[128,256]{1,0:T(8,128)S(1)}, f32[128,256]{1,0:T(8,128)S(1)}, u32[]{:S(2)}, u32[]{:S(2)}) collective-permute-start(f32[128,256]{1,0:T(8,128)S(1)} %fusion.2), channel_id=1, source_target_pairs={{2,1},{4,3},{6,5},{8,7},{10,9},{12,11},{14,13},{18,17},{20,19},{22... | collective-permute-start | bytes 393224 | tf_op jit(solution)/shard_map/ppermute | solution.py:178
  134.8 15.1 %collective-permute-start.17 = (f32[128,256]{1,0:T(8,128)S(1)}, f32[128,256]{1,0:T(8,128)S(1)}, u32[]{:S(2)}, u32[]{:S(2)}) collective-permute-start(f32[128,256]{1,0:T(8,128)S(1)} %fusion.2), channel_id=1, source_target_pairs={{0,1},{2,3},{4,5},{6,7},{8,9},{10,11},{12,13},{14,15},{16,17},{18,... | collective-permute-start | bytes 393224 | tf_op jit(solution)/shard_map/ppermute | solution.py:175
  149.0 1.0 collective-permute-start.16
  150.0 25.8 %collective-permute-start.19 = (f32[128,256]{1,0:T(8,128)S(1)}, f32[128,256]{1,0:T(8,128)S(1)}, u32[]{:S(2)}, u32[]{:S(2)}) collective-permute-start(f32[128,256]{1,0:T(8,128)S(1)} %get-tuple-element.23), channel_id=1, source_target_pairs={{0,2},{1,3},{4,6},{5,7},{8,10},{9,11},{12,14},{13,15},{16,18},{17,... | collective-permute-start | bytes 393224 | tf_op jit(solution)/shard_map/ppermute | solution.py:175
  162.9 12.8 %collective-permute-start.18 = (f32[128,256]{1,0:T(8,128)S(1)}, f32[128,256]{1,0:T(8,128)S(1)}, u32[]{:S(2)}, u32[]{:S(2)}) collective-permute-start(f32[128,256]{1,0:T(8,128)S(1)} %get-tuple-element.23), channel_id=1, source_target_pairs={{2,4},{3,5},{6,8},{7,9},{10,12},{11,13},{18,20},{19,21},{22,24},{2... | collective-permute-start | bytes 393224 | tf_op jit(solution)/shard_map/ppermute | solution.py:178
  173.8 15.1 %collective-permute-start.26 = (f32[128,256]{1,0:T(8,128)S(1)}, f32[128,256]{1,0:T(8,128)S(1)}, u32[]{:S(2)}, u32[]{:S(2)}) collective-permute-start(f32[128,256]{1,0:T(8,128)S(1)} %get-tuple-element.24), channel_id=1, source_target_pairs={{2,0},{3,1},{6,4},{7,5},{10,8},{11,9},{14,12},{15,13},{18,16},{19,... | collective-permute-start | bytes 393224 | tf_op jit(solution)/shard_map/ppermute | solution.py:175
  175.1 13.8 %collective-permute-start.25 = (f32[128,256]{1,0:T(8,128)S(1)}, f32[128,256]{1,0:T(8,128)S(1)}, u32[]{:S(2)}, u32[]{:S(2)}) collective-permute-start(f32[128,256]{1,0:T(8,128)S(1)} %get-tuple-element.24), channel_id=1, source_target_pairs={{4,2},{5,3},{8,6},{9,7},{12,10},{13,11},{20,18},{21,19},{24,22},{2... | collective-permute-start | bytes 393224 | tf_op jit(solution)/shard_map/ppermute | solution.py:178
  175.8 15.1 %collective-permute-start.21 = (f32[128,256]{1,0:T(8,128)S(1)}, f32[128,256]{1,0:T(8,128)S(1)}, u32[]{:S(2)}, u32[]{:S(2)}) collective-permute-start(f32[128,256]{1,0:T(8,128)S(1)} %multiply_add_fusion.4), channel_id=1, source_target_pairs={{0,4},{1,5},{2,6},{3,7},{8,12},{9,13},{10,14},{11,15},{16,20},{17,... | collective-permute-start | bytes 393224 | tf_op jit(solution)/shard_map/ppermute | solution.py:175
  188.2 2.7 collective-permute-start.20
  188.9 11.1 %collective-permute-start.28 = (f32[128,256]{1,0:T(8,128)S(1)}, f32[128,256]{1,0:T(8,128)S(1)}, u32[]{:S(2)}, u32[]{:S(2)}) collective-permute-start(f32[128,256]{1,0:T(8,128)S(1)} %multiply_add_fusion.1), channel_id=1, source_target_pairs={{4,0},{5,1},{6,2},{7,3},{12,8},{13,9},{14,10},{15,11},{20,16},{21,... | collective-permute-start | bytes 393224 | tf_op jit(solution)/shard_map/ppermute | solution.py:175
  190.2 9.8 %collective-permute-start.27 = (f32[128,256]{1,0:T(8,128)S(1)}, f32[128,256]{1,0:T(8,128)S(1)}, u32[]{:S(2)}, u32[]{:S(2)}) collective-permute-start(f32[128,256]{1,0:T(8,128)S(1)} %multiply_add_fusion.1), channel_id=1, source_target_pairs={{8,4},{9,5},{10,6},{11,7},{24,20},{25,21},{26,22},{27,23}} | collective-permute-start | bytes 393224 | tf_op jit(solution)/shard_map/ppermute | solution.py:178
  190.9 14.9 %collective-permute-start.22 = (f32[128,256]{1,0:T(8,128)S(1)}, f32[128,256]{1,0:T(8,128)S(1)}, u32[]{:S(2)}, u32[]{:S(2)}) collective-permute-start(f32[128,256]{1,0:T(8,128)S(1)} %multiply_add_fusion.3), channel_id=1, source_target_pairs={{0,8},{1,9},{2,10},{3,11},{4,12},{5,13},{6,14},{7,15},{16,24},{17,... | collective-permute-start | bytes 393224 | tf_op jit(solution)/shard_map/ppermute | solution.py:175
  200.0 9.2 %collective-permute-start.29 = (f32[128,256]{1,0:T(8,128)S(1)}, f32[128,256]{1,0:T(8,128)S(1)}, u32[]{:S(2)}, u32[]{:S(2)}) collective-permute-start(f32[128,256]{1,0:T(8,128)S(1)} %multiply_add_fusion), channel_id=1, source_target_pairs={{8,0},{9,1},{10,2},{11,3},{12,4},{13,5},{14,6},{15,7},{24,16},{25,... | collective-permute-start | bytes 393224 | tf_op jit(solution)/shard_map/ppermute | solution.py:175
  229.8 6.3 %collective-permute-start.38 = (f32[128,128]{1,0:T(8,128)S(1)}, f32[128,128]{1,0:T(8,128)S(1)}, u32[]{:S(2)}, u32[]{:S(2)}) collective-permute-start(f32[128,128]{1,0:T(8,128)S(1)} %fusion.13), channel_id=1, source_target_pairs={{1,0},{3,2},{5,4},{7,6},{9,8},{11,10},{13,12},{15,14},{17,16},{19,... | collective-permute-start | bytes 196616 | tf_op jit(solution)/shard_map/ppermute | solution.py:175
  231.1 5.0 %collective-permute-start.37 = (f32[128,128]{1,0:T(8,128)S(1)}, f32[128,128]{1,0:T(8,128)S(1)}, u32[]{:S(2)}, u32[]{:S(2)}) collective-permute-start(f32[128,128]{1,0:T(8,128)S(1)} %fusion.13), channel_id=1, source_target_pairs={{2,1},{4,3},{6,5},{8,7},{10,9},{12,11},{14,13},{18,17},{20,19},{22... | collective-permute-start | bytes 196616 | tf_op jit(solution)/shard_map/ppermute | solution.py:178
  231.8 4.5 %collective-permute-start.31 = (f32[128,128]{1,0:T(8,128)S(1)}, f32[128,128]{1,0:T(8,128)S(1)}, u32[]{:S(2)}, u32[]{:S(2)}) collective-permute-start(f32[128,128]{1,0:T(8,128)S(1)} %fusion.13), channel_id=1, source_target_pairs={{0,1},{2,3},{4,5},{6,7},{8,9},{10,11},{12,13},{14,15},{16,17},{18,... | collective-permute-start | bytes 196616 | tf_op jit(solution)/shard_map/ppermute | solution.py:175
  235.4 0.9 collective-permute-start.30
  236.3 10.9 %collective-permute-start.33 = (f32[128,128]{1,0:T(8,128)S(1)}, f32[128,128]{1,0:T(8,128)S(1)}, u32[]{:S(2)}, u32[]{:S(2)}) collective-permute-start(f32[128,128]{1,0:T(8,128)S(1)} %get-tuple-element.25), channel_id=1, source_target_pairs={{0,2},{1,3},{4,6},{5,7},{8,10},{9,11},{12,14},{13,15},{16,18},{17,... | collective-permute-start | bytes 196616 | tf_op jit(solution)/shard_map/ppermute | solution.py:175
  244.6 2.7 collective-permute-start.32
  245.3 10.2 %collective-permute-start.40 = (f32[128,128]{1,0:T(8,128)S(1)}, f32[128,128]{1,0:T(8,128)S(1)}, u32[]{:S(2)}, u32[]{:S(2)}) collective-permute-start(f32[128,128]{1,0:T(8,128)S(1)} %get-tuple-element.26), channel_id=1, source_target_pairs={{2,0},{3,1},{6,4},{7,5},{10,8},{11,9},{14,12},{15,13},{18,16},{19,... | collective-permute-start | bytes 196616 | tf_op jit(solution)/shard_map/ppermute | solution.py:175
  246.6 8.9 %collective-permute-start.39 = (f32[128,128]{1,0:T(8,128)S(1)}, f32[128,128]{1,0:T(8,128)S(1)}, u32[]{:S(2)}, u32[]{:S(2)}) collective-permute-start(f32[128,128]{1,0:T(8,128)S(1)} %get-tuple-element.26), channel_id=1, source_target_pairs={{4,2},{5,3},{8,6},{9,7},{12,10},{13,11},{20,18},{21,19},{24,22},{2... | collective-permute-start | bytes 196616 | tf_op jit(solution)/shard_map/ppermute | solution.py:178
  247.3 10.2 %collective-permute-start.35 = (f32[128,128]{1,0:T(8,128)S(1)}, f32[128,128]{1,0:T(8,128)S(1)}, u32[]{:S(2)}, u32[]{:S(2)}) collective-permute-start(f32[128,128]{1,0:T(8,128)S(1)} %multiply_add_fusion.10), channel_id=1, source_target_pairs={{0,4},{1,5},{2,6},{3,7},{8,12},{9,13},{10,14},{11,15},{16,20},{17,... | collective-permute-start | bytes 196616 | tf_op jit(solution)/shard_map/ppermute | solution.py:175
  254.8 2.7 collective-permute-start.34
  255.5 10.0 %collective-permute-start.42 = (f32[128,128]{1,0:T(8,128)S(1)}, f32[128,128]{1,0:T(8,128)S(1)}, u32[]{:S(2)}, u32[]{:S(2)}) collective-permute-start(f32[128,128]{1,0:T(8,128)S(1)} %multiply_add_fusion.7), channel_id=1, source_target_pairs={{4,0},{5,1},{6,2},{7,3},{12,8},{13,9},{14,10},{15,11},{20,16},{21,... | collective-permute-start | bytes 196616 | tf_op jit(solution)/shard_map/ppermute | solution.py:175
  256.8 8.7 %collective-permute-start.41 = (f32[128,128]{1,0:T(8,128)S(1)}, f32[128,128]{1,0:T(8,128)S(1)}, u32[]{:S(2)}, u32[]{:S(2)}) collective-permute-start(f32[128,128]{1,0:T(8,128)S(1)} %multiply_add_fusion.7), channel_id=1, source_target_pairs={{8,4},{9,5},{10,6},{11,7},{24,20},{25,21},{26,22},{27,23}} | collective-permute-start | bytes 196616 | tf_op jit(solution)/shard_map/ppermute | solution.py:178
  257.5 9.8 %collective-permute-start.36 = (f32[128,128]{1,0:T(8,128)S(1)}, f32[128,128]{1,0:T(8,128)S(1)}, u32[]{:S(2)}, u32[]{:S(2)}) collective-permute-start(f32[128,128]{1,0:T(8,128)S(1)} %multiply_add_fusion.9), channel_id=1, source_target_pairs={{0,8},{1,9},{2,10},{3,11},{4,12},{5,13},{6,14},{7,15},{16,24},{17,... | collective-permute-start | bytes 196616 | tf_op jit(solution)/shard_map/ppermute | solution.py:175
  265.5 7.8 %collective-permute-start.43 = (f32[128,128]{1,0:T(8,128)S(1)}, f32[128,128]{1,0:T(8,128)S(1)}, u32[]{:S(2)}, u32[]{:S(2)}) collective-permute-start(f32[128,128]{1,0:T(8,128)S(1)} %multiply_add_fusion.6), channel_id=1, source_target_pairs={{8,0},{9,1},{10,2},{11,3},{12,4},{13,5},{14,6},{15,7},{24,16},{25,... | collective-permute-start | bytes 196616 | tf_op jit(solution)/shard_map/ppermute | solution.py:175

commit v8 on v6

--- a/solution.py
+++ b/solution.py
@@ -52,25 +52,30 @@
     )(gram)
 
 
-def _step_kernel(first, extended_ref, older_low_ref, older_high_ref, low_pot_ref, high_pot_ref,
-                 low_ref, high_ref):
-    z = pl.program_id(1)
-    half = (extended_ref.shape[0] - 6) // 2
-    rows_y = extended_ref.shape[1]
-    rows_x = extended_ref.shape[2]
-    place = lax.broadcasted_iota(jnp.int32, (rows_x, extended_ref.shape[3]), 0)
-
-    def one_plane(centre, older_ref, potential_ref, out_ref):
-        def plane(offset, y):
-            return extended_ref[centre + offset, y].astype(jnp.float32)
-
+def _step_kernel(first, below_ref, low_ref, high_ref, above_ref, older_low_ref, older_high_ref,
+                 low_pot_ref, high_pot_ref, out_low_ref, out_high_ref):
+    half = low_ref.shape[0]
+    rows_y = low_ref.shape[1]
+    rows_x = low_ref.shape[2]
+    place = lax.broadcasted_iota(jnp.int32, (rows_x, low_ref.shape[3]), 0)
+    sources = (below_ref, low_ref, high_ref, above_ref)
+
+    def plane(index, y):
+        return sources[index // half][index % half, y].astype(jnp.float32)
+
+    for centre in range(half, 3 * half):
+        own = centre - half
+        older_ref = older_low_ref if own < half else older_high_ref
+        potential_ref = low_pot_ref if own < half else high_pot_ref
+        out_ref = out_low_ref if own < half else out_high_ref
+        local = own % half
         for y in range(rows_y):
-            inner = plane(0, y)
+            inner = plane(centre, y)
             total = 3.0 * COEF[0] * inner
             for distance in (1, 2, 3):
-                along_z = plane(distance, y) + plane(-distance, y)
-                up = plane(0, y + distance) if y + distance < rows_y else None
-                down = plane(0, y - distance) if y - distance >= 0 else None
+                along_z = plane(centre + distance, y) + plane(centre - distance, y)
+                up = plane(centre, y + distance) if y + distance < rows_y else None
+                down = plane(centre, y - distance) if y - distance >= 0 else None
                 if up is None:
                     along_y = down
                 elif down is None:
@@ -83,43 +88,45 @@
                 behind = jnp.where(place >= distance, pltpu.roll(inner, distance, 0), 0.0)
                 along_x = ahead + behind
                 total = total + COEF[distance] * (along_z + along_y + along_x)
-            image = potential_ref[0, y] * inner - 0.5 * total
+            image = potential_ref[local, y] * inner - 0.5 * total
             if first:
                 newer = (image - CSHIFT * inner) / EWIDTH
             else:
-                newer = 2.0 / EWIDTH * (image - CSHIFT * inner) - older_ref[0, y].astype(
+                newer = 2.0 / EWIDTH * (image - CSHIFT * inner) - older_ref[local, y].astype(
                     jnp.float32
                 )
-            out_ref[0, y] = newer.astype(out_ref.dtype)
-
-    one_plane(z + 3, older_low_ref, low_pot_ref, low_ref)
-    one_plane(z + 3 + half, older_high_ref, high_pot_ref, high_ref)
-
-
-def chebyshev_step(extended, older_low, older_high, potential, first):
-    half = (extended.shape[0] - 6) // 2
-    rows_y, rows_x, bands = extended.shape[1:]
+            out_ref[local, y] = newer.astype(out_ref.dtype)
+
+
+def chebyshev_step(below, low, high, above, older_low, older_high, potential, first):
+    half, rows_y, rows_x, bands = low.shape
     lanes = 128
-    grid = (bands // lanes, half)
-    block = (1, rows_y, rows_x, lanes)
-    high_shift = half if older_high.shape[0] == 2 * half else 0
+    block = (half, rows_y, rows_x, lanes)
+
+    def spec(array, part):
+        shift = part if array.shape[0] == 2 * half else 0
+        return pl.BlockSpec(block, lambda j: (shift, 0, 0, j))
+
     piece = jax.ShapeDtypeStruct((half, rows_y, rows_x, bands), jnp.bfloat16)
     return pl.pallas_call(
         functools.partial(_step_kernel, first),
         out_shape=(piece, piece),
-        grid=grid,
+        grid=(bands // lanes,),
         in_specs=[
-            pl.BlockSpec((2 * half + 6, rows_y, rows_x, lanes), lambda j, z: (0, 0, 0, j)),
-            pl.BlockSpec(block, lambda j, z: (z, 0, 0, j)),
-            pl.BlockSpec(block, lambda j, z: (z + high_shift, 0, 0, j)),
-            pl.BlockSpec(block, lambda j, z: (z, 0, 0, 0)),
-            pl.BlockSpec(block, lambda j, z: (z + half, 0, 0, 0)),
+            spec(below, 0),
+            spec(low, 0),
+            spec(high, 0),
+            spec(above, 0),
+            spec(older_low, 0),
+            spec(older_high, 1),
+            pl.BlockSpec(block, lambda j: (0, 0, 0, 0)),
+            pl.BlockSpec(block, lambda j: (1, 0, 0, 0)),
         ],
         out_specs=(
-            pl.BlockSpec(block, lambda j, z: (z, 0, 0, j)),
-            pl.BlockSpec(block, lambda j, z: (z, 0, 0, j)),
+            pl.BlockSpec(block, lambda j: (0, 0, 0, j)),
+            pl.BlockSpec(block, lambda j: (0, 0, 0, j)),
         ),
-    )(extended, older_low, older_high, potential, potential)
+    )(below, low, high, above, older_low, older_high, potential, potential)
 
 
 def extended_2(block, sides, width):
@@ -189,14 +196,17 @@
     def rimmed(low, high):
         from_below = lax.ppermute(high, "gz", forward)
         from_above = lax.ppermute(low, "gz", backward)
-        return jnp.concatenate([from_below * bf_below, low, high, from_above * bf_above], axis=0)
+        return from_below * bf_below, from_above * bf_above
 
     lanes = jnp.broadcast_to(grid[..., None], grid.shape + (128,))
     half = planes // 2
-    low, high = chebyshev_step(rimmed(waves[:half], waves[half:]), waves, waves, lanes, True)
+    low, high = waves[:half], waves[half:]
+    from_below, from_above = rimmed(low, high)
+    low, high = chebyshev_step(from_below, low, high, from_above, waves, waves, lanes, True)
     older_low, older_high = waves, waves
     for turn in range(DEGREE - 1):
-        newer = chebyshev_step(rimmed(low, high), older_low, older_high, lanes, False)
+        from_below, from_above = rimmed(low, high)
+        newer = chebyshev_step(from_below, low, high, from_above, older_low, older_high, lanes, False)
         older_low, older_high = low, high
         low, high = newer
     current = jnp.concatenate([low, high], axis=0)

time: 254 us -> 248 us (0.976)
  waiting for transfers between devices: 32.1 us -> 27.3 us
  starting transfers between devices: 116 us -> 120 us
    concatenate x4 -> x0, other arithmetic: 7.53 us -> none  [rimmed(): jnp.concatenate([from_below * bf_below, low, high, from_above * bf_above]...]
    mul x8, other arithmetic: 0.44 us -> 7.64 us  [rimmed(): return (from_below * bf_below, from_above * bf_above)]
    ppermute x4, waiting for transfers between devices: 14.1 us -> 9.74 us  [rimmed(): from_above = lax.ppermute(low, 'gz', backward)]
    ppermute x4, starting transfers between devices: 50.2 us -> 52.9 us  [rimmed(): from_below = lax.ppermute(high, 'gz', forward)]
  transfers between devices with their start and end apart: 24 -> 24, of which waited for: 18 -> 17; matrix products, arithmetic and copies ran while one was open for 1% -> 2% of each run, Pallas kernels for 0% -> 0%
where the time goes in v8:
time: 248 us; the launch traced here: 247 us
  starting transfers between devices  120 us (48%)
  Pallas kernels  67.9 us (27%)
  waiting for transfers between devices  27.3 us (11%)
  other arithmetic  11.3 us (5%)
  between operations  11.1 us (4%)
  local copies, waits for them, and re-layouts  6.08 us (2%)
  matrix products  3.8 us (2%)
    ppermute x4, starting transfers between devices, rimmed(): from_below = lax.ppermute(high, 'gz', forward)  52.9 us
    ppermute x8, starting transfers between devices, domain_total(): from_low = lax.ppermute(forward, 'gz', ahead)  51.1 us
    pallas_call x4, Pallas kernels, chebyshev_step(): pl.pallas_call(functools.partial(_step_kernel, first), out_shape=(piece,...  34 us
    pallas_call x2, Pallas kernels, lower_inverse(): pl.pallas_call(_lower_inverse_kernel, out_shape=jax.ShapeDtypeStruct((n,...  33.9 us
    ppermute x8, starting transfers between devices, domain_total(): from_high = lax.ppermute(backward, 'gz', behind)  10.3 us
    ppermute x8, waiting for transfers between devices, domain_total(): from_high = lax.ppermute(backward, 'gz', behind)  10.1 us
    ppermute x4, waiting for transfers between devices, rimmed(): from_above = lax.ppermute(low, 'gz', backward)  9.74 us
    mul x8, other arithmetic, rimmed(): return (from_below * bf_below, from_above * bf_above)  7.64 us
  transfers between devices with their start and end apart: 24, of which 17 were waited for; matrix products, arithmetic and copies ran while one was open for 2% of the time, Pallas kernels for 0%

profile of v8, /device:TPU:0, one launch (start us, length us, event | category | flops | bytes accessed | tf_op | source)
XLA Modules:
  0.0 247.2 jit_solution(4542674273234874053)
XLA Ops:
  0.0 1.5 fusion.11
  1.5 1.3 collective-permute-start.1
  2.8 3.1 %collective-permute-start = (bf16[3,8,64,256]{3,2,1,0:T(8,128)(2,1)S(1)}, bf16[3,8,64,256]{3,2,1,0:T(8,128)(2,1)S(1)}, u32[]{:S(2)}, u32[]{:S(2)}) collective-permute-start(bf16[3,8,64,256]{3,2,1,0:T(8,128)(2,1)S(1)} %get-tuple-element.22.high_ref), channel_id=1, source_target_pairs={{0,1},{1,2},{2,3},{3,4},{4,5},{5,6},{6,7},{7,8},{8,9},{9,10},{10,1... | collective-permute-start | bytes 2359304 | tf_op jit(solution)/shard_map/ppermute | solution.py:197
  6.0 0.7 fusion.12
  9.3 1.0 broadcast_multiply_fusion.3.above_ref
  10.2 0.9 broadcast_multiply_fusion.7.below_ref
  11.2 1.6 broadcast_in_dim.8.low_pot_ref.high_pot_ref
  12.8 8.3 %shard_map.37 = (bf16[3,8,64,256]{3,2,1,0:T(8,128)(2,1)}, bf16[3,8,64,256]{3,2,1,0:T(8,128)(2,1)}) custom-call(bf16[3,8,64,256]{3,2,1,0:T(8,128)(2,1)} %broadcast_multiply_fusion.7.below_ref, bf16[3,8,64,256]{3,2,1,0:T(8,128)(2,1)} %copy-done, bf16[3,8,64,256]{3,2,1,0:T(8,128)(2,1)} %copy-done.1, bf16[3,8,64,256]{3,2,1,0:T(8,128)(2,1)} %broadcast_multiply_fusion.3.above_ref, ...), custom_call_target="tpu_custom_call" | custom-call | tf_op jit(solution)/shard_map/pallas_call | solution.py:111
  21.1 16.5 %collective-permute-start.2 = (bf16[3,8,64,256]{3,2,1,0:T(8,128)(2,1)}, bf16[3,8,64,256]{3,2,1,0:T(8,128)(2,1)S(1)}, u32[]{:S(2)}, u32[]{:S(2)}) collective-permute-start(bf16[3,8,64,256]{3,2,1,0:T(8,128)(2,1)} %get-tuple-element.13.high_ref.older_high_ref), channel_id=1, source_target_pairs={{0,1},{1,2},{2,3},{3,4},{4,5},{5,6},{6,7},{7,8},{8,9},{9,10},{10,1... | collective-permute-start | bytes 2359304 | tf_op jit(solution)/shard_map/ppermute | solution.py:197
  37.6 1.3 collective-permute-start.3
  38.9 0.8 collective-permute-done.2
  39.7 0.9 broadcast_multiply_fusion.6.below_ref
  40.6 3.3 %collective-permute-done.3 = bf16[3,8,64,256]{3,2,1,0:T(8,128)(2,1)S(1)} collective-permute-done((bf16[3,8,64,256]{3,2,1,0:T(8,128)(2,1)}, bf16[3,8,64,256]{3,2,1,0:T(8,128)(2,1)S(1)}, u32[]{:S(2)}, u32[]{:S(2)}) %collective-permute-start.3) | collective-permute-done | bytes 786464 | tf_op jit(solution)/shard_map/ppermute | solution.py:198
  43.9 1.0 broadcast_multiply_fusion.2.above_ref
  44.9 8.6 %shard_map.38 = (bf16[3,8,64,256]{3,2,1,0:T(8,128)(2,1)}, bf16[3,8,64,256]{3,2,1,0:T(8,128)(2,1)}) custom-call(bf16[3,8,64,256]{3,2,1,0:T(8,128)(2,1)} %broadcast_multiply_fusion.6.below_ref, bf16[3,8,64,256]{3,2,1,0:T(8,128)(2,1)} %get-tuple-element.14.low_ref.older_low_ref, bf16[3,8,64,256]{3,2,1,0:T(8,128)(2,1)} %get-tuple-element.13.high_ref.older_high_ref, ...), custom_call_target="tpu_custom_call" | custom-call | tf_op jit(solution)/shard_map/pallas_call | solution.py:111
  53.4 16.6 %collective-permute-start.4 = (bf16[3,8,64,256]{3,2,1,0:T(8,128)(2,1)}, bf16[3,8,64,256]{3,2,1,0:T(8,128)(2,1)S(1)}, u32[]{:S(2)}, u32[]{:S(2)}) collective-permute-start(bf16[3,8,64,256]{3,2,1,0:T(8,128)(2,1)} %get-tuple-element.15.high_ref.older_high_ref), channel_id=1, source_target_pairs={{0,1},{1,2},{2,3},{3,4},{4,5},{5,6},{6,7},{7,8},{8,9},{9,10},{10,1... | collective-permute-start | bytes 2359304 | tf_op jit(solution)/shard_map/ppermute | solution.py:197
  70.1 1.3 collective-permute-start.5
  71.4 0.8 collective-permute-done.4
  72.2 1.0 broadcast_multiply_fusion.5.below_ref
  73.1 3.2 %collective-permute-done.5 = bf16[3,8,64,256]{3,2,1,0:T(8,128)(2,1)S(1)} collective-permute-done((bf16[3,8,64,256]{3,2,1,0:T(8,128)(2,1)}, bf16[3,8,64,256]{3,2,1,0:T(8,128)(2,1)S(1)}, u32[]{:S(2)}, u32[]{:S(2)}) %collective-permute-start.5) | collective-permute-done | bytes 786464 | tf_op jit(solution)/shard_map/ppermute | solution.py:198
  76.3 1.0 broadcast_multiply_fusion.1.above_ref
  77.3 8.6 %shard_map.39 = (bf16[3,8,64,256]{3,2,1,0:T(8,128)(2,1)}, bf16[3,8,64,256]{3,2,1,0:T(8,128)(2,1)}) custom-call(bf16[3,8,64,256]{3,2,1,0:T(8,128)(2,1)} %broadcast_multiply_fusion.5.below_ref, bf16[3,8,64,256]{3,2,1,0:T(8,128)(2,1)} %get-tuple-element.16.low_ref.older_low_ref, bf16[3,8,64,256]{3,2,1,0:T(8,128)(2,1)} %get-tuple-element.15.high_ref.older_high_ref, ...), custom_call_target="tpu_custom_call" | custom-call | tf_op jit(solution)/shard_map/pallas_call | solution.py:111
  85.8 16.7 %collective-permute-start.6 = (bf16[3,8,64,256]{3,2,1,0:T(8,128)(2,1)}, bf16[3,8,64,256]{3,2,1,0:T(8,128)(2,1)S(1)}, u32[]{:S(2)}, u32[]{:S(2)}) collective-permute-start(bf16[3,8,64,256]{3,2,1,0:T(8,128)(2,1)} %get-tuple-element.17.high_ref), channel_id=1, source_target_pairs={{0,1},{1,2},{2,3},{3,4},{4,5},{5,6},{6,7},{7,8},{8,9},{9,10},{10,1... | collective-permute-start | bytes 2359304 | tf_op jit(solution)/shard_map/ppermute | solution.py:197
  102.5 1.5 collective-permute-start.7
  104.0 0.6 collective-permute-done.6
  104.6 1.0 broadcast_multiply_fusion.4.below_ref
  105.5 3.2 %collective-permute-done.7 = bf16[3,8,64,256]{3,2,1,0:T(8,128)(2,1)S(1)} collective-permute-done((bf16[3,8,64,256]{3,2,1,0:T(8,128)(2,1)}, bf16[3,8,64,256]{3,2,1,0:T(8,128)(2,1)S(1)}, u32[]{:S(2)}, u32[]{:S(2)}) %collective-permute-start.7) | collective-permute-done | bytes 786464 | tf_op jit(solution)/shard_map/ppermute | solution.py:198
  108.8 1.0 broadcast_multiply_fusion.above_ref
  109.7 8.6 %shard_map.40 = (bf16[3,8,64,256]{3,2,1,0:T(8,128)(2,1)}, bf16[3,8,64,256]{3,2,1,0:T(8,128)(2,1)}) custom-call(bf16[3,8,64,256]{3,2,1,0:T(8,128)(2,1)} %broadcast_multiply_fusion.4.below_ref, bf16[3,8,64,256]{3,2,1,0:T(8,128)(2,1)} %get-tuple-element.18.low_ref, bf16[3,8,64,256]{3,2,1,0:T(8,128)(2,1)} %get-tuple-element.17.high_ref, ...), custom_call_target="tpu_custom_call" | custom-call | tf_op jit(solution)/shard_map/pallas_call | solution.py:111
  118.3 1.5 pad_maximum_fusion
  120.2 1.3 collective-permute-start.12
  121.5 17.3 %collective-permute-start.8 = (f32[128,256]{1,0:T(8,128)S(1)}, f32[128,256]{1,0:T(8,128)S(1)}, u32[]{:S(2)}, u32[]{:S(2)}) collective-permute-start(f32[128,256]{1,0:T(8,128)S(1)} %fusion.2), channel_id=1, source_target_pairs={{0,1},{1,2},{2,3},{3,4},{4,5},{5,6},{6,7},{7,8},{8,9},{9,10},{10,1... | collective-permute-start | bytes 393224 | tf_op jit(solution)/shard_map/ppermute | solution.py:223
  138.8 0.9 collective-permute-done.8
  139.8 7.6 %collective-permute-start.9 = (f32[128,256]{1,0:T(8,128)S(1)}, f32[128,256]{1,0:T(8,128)S(1)}, u32[]{:S(2)}, u32[]{:S(2)}) collective-permute-start(f32[128,256]{1,0:T(8,128)S(1)} %get-tuple-element.23), channel_id=1, source_target_pairs={{0,2},{1,3},{2,4},{3,5},{4,6},{5,7},{6,8},{7,9},{8,10},{9,11},{10,... | collective-permute-start | bytes 393224 | tf_op jit(solution)/shard_map/ppermute | solution.py:223
  152.4 1.3 collective-permute-start.13
  153.7 5.3 %collective-permute-start.10 = (f32[128,256]{1,0:T(8,128)S(1)}, f32[128,256]{1,0:T(8,128)S(1)}, u32[]{:S(2)}, u32[]{:S(2)}) collective-permute-start(f32[128,256]{1,0:T(8,128)S(1)} %multiply_add_fusion.4), channel_id=1, source_target_pairs={{0,4},{1,5},{2,6},{3,7},{4,8},{5,9},{6,10},{7,11},{8,12},{9,13},{1... | collective-permute-start | bytes 393224 | tf_op jit(solution)/shard_map/ppermute | solution.py:223
  159.3 1.3 collective-permute-start.14
  160.6 1.3 collective-permute-done.10
  161.9 3.6 %collective-permute-start.11 = (f32[128,256]{1,0:T(8,128)S(1)}, f32[128,256]{1,0:T(8,128)S(1)}, u32[]{:S(2)}, u32[]{:S(2)}) collective-permute-start(f32[128,256]{1,0:T(8,128)S(1)} %multiply_add_fusion.3), channel_id=1, source_target_pairs={{0,8},{1,9},{2,10},{3,11},{4,12},{5,13},{6,14},{7,15},{16,24},{17,... | collective-permute-start | bytes 393224 | tf_op jit(solution)/shard_map/ppermute | solution.py:223
  165.6 0.6 collective-permute-done.14
  166.2 1.3 collective-permute-start.15
  170.0 1.2 fusion.10
  171.9 3.2 %collective-permute-done.15 = f32[128,256]{1,0:T(8,128)S(1)} collective-permute-done((f32[128,256]{1,0:T(8,128)S(1)}, f32[128,256]{1,0:T(8,128)S(1)}, u32[]{:S(2)}, u32[]{:S(2)}) %collective-permute-start.15) | collective-permute-done | bytes 131104 | tf_op jit(solution)/shard_map/ppermute | solution.py:224
  175.1 0.6 slice.25.gram_ref
  175.8 16.9 %shard_map.41 = f32[128,128]{1,0:T(8,128)} custom-call(f32[128,128]{1,0:T(8,128)} %slice.25.gram_ref), custom_call_target="tpu_custom_call" | custom-call | tf_op jit(solution)/shard_map/pallas_call | solution.py:48
  192.7 1.3 convolution_convert_fusion.1
  194.0 0.5 fusion
  194.9 1.3 collective-permute-start.20
  196.2 3.0 %collective-permute-start.16 = (f32[128,128]{1,0:T(8,128)S(1)}, f32[128,128]{1,0:T(8,128)S(1)}, u32[]{:S(2)}, u32[]{:S(2)}) collective-permute-start(f32[128,128]{1,0:T(8,128)S(1)} %fusion.13), channel_id=1, source_target_pairs={{0,1},{1,2},{2,3},{3,4},{4,5},{5,6},{6,7},{7,8},{8,9},{9,10},{10,1... | collective-permute-start | bytes 196616 | tf_op jit(solution)/shard_map/ppermute | solution.py:223
  199.3 0.9 collective-permute-done.16
  200.2 5.7 %collective-permute-start.17 = (f32[128,128]{1,0:T(8,128)S(1)}, f32[128,128]{1,0:T(8,128)S(1)}, u32[]{:S(2)}, u32[]{:S(2)}) collective-permute-start(f32[128,128]{1,0:T(8,128)S(1)} %get-tuple-element.25), channel_id=1, source_target_pairs={{0,2},{1,3},{2,4},{3,5},{4,6},{5,7},{6,8},{7,9},{8,10},{9,11},{10,... | collective-permute-start | bytes 196616 | tf_op jit(solution)/shard_map/ppermute | solution.py:223
  205.8 1.3 collective-permute-start.21
  207.1 1.2 collective-permute-done.17
  208.3 4.4 %collective-permute-start.18 = (f32[128,128]{1,0:T(8,128)S(1)}, f32[128,128]{1,0:T(8,128)S(1)}, u32[]{:S(2)}, u32[]{:S(2)}) collective-permute-start(f32[128,128]{1,0:T(8,128)S(1)} %multiply_add_fusion.10), channel_id=1, source_target_pairs={{0,4},{1,5},{2,6},{3,7},{4,8},{5,9},{6,10},{7,11},{8,12},{9,13},{1... | collective-permute-start | bytes 196616 | tf_op jit(solution)/shard_map/ppermute | solution.py:223
  212.7 1.3 collective-permute-start.22
  214.0 0.6 collective-permute-done.18
  214.6 4.2 %collective-permute-start.19 = (f32[128,128]{1,0:T(8,128)S(1)}, f32[128,128]{1,0:T(8,128)S(1)}, u32[]{:S(2)}, u32[]{:S(2)}) collective-permute-start(f32[128,128]{1,0:T(8,128)S(1)} %multiply_add_fusion.9), channel_id=1, source_target_pairs={{0,8},{1,9},{2,10},{3,11},{4,12},{5,13},{6,14},{7,15},{16,24},{17,... | collective-permute-start | bytes 196616 | tf_op jit(solution)/shard_map/ppermute | solution.py:223
  218.9 1.3 collective-permute-start.23
  220.2 0.5 collective-permute-done.19
  220.7 6.0 %collective-permute-done.23 = f32[128,128]{1,0:T(8,128)S(1)} collective-permute-done((f32[128,128]{1,0:T(8,128)S(1)}, f32[128,128]{1,0:T(8,128)S(1)}, u32[]{:S(2)}, u32[]{:S(2)}) %collective-permute-start.23) | collective-permute-done | bytes 65568 | tf_op jit(solution)/shard_map/ppermute | solution.py:224
  226.7 0.7 subtract_divide_fusion.1.gram_ref
  227.3 16.9 %shard_map.42 = f32[128,128]{1,0:T(8,128)} custom-call(f32[128,128]{1,0:T(8,128)} %subtract_divide_fusion.1.gram_ref), custom_call_target="tpu_custom_call" | custom-call | tf_op jit(solution)/shard_map/pallas_call | solution.py:48
  244.3 1.2 convolution_convert_fusion
  245.6 1.6 copy.5
  (34 shorter events, 1.5 us)
Async XLA Ops:
  0.0 5.9 %copy-start.3 = (s32[16]{0:T(128)S(1)}, s32[16]{0:T(128)}, u32[]{:S(2)}) copy-start(s32[16]{0:T(128)} %param.5) | copy-start | bytes 196
  0.0 9.2 %copy-start.4 = (f32[6,512]{1,0:T(8,128)S(1)}, f32[6,512]{1,0:T(8,128)}, u32[]{:S(2)}) copy-start(f32[6,512]{1,0:T(8,128)} %param.4) | copy-start | bytes 36868
  1.5 9.7 %copy-start = (bf16[3,8,64,256]{3,2,1,0:T(8,128)(2,1)}, bf16[3,8,64,256]{3,2,1,0:T(8,128)(2,1)S(1)}, u32[]{:S(2)}) copy-start(bf16[3,8,64,256]{3,2,1,0:T(8,128)(2,1)S(1)} %get-tuple-element.21.low_ref) | copy-start | bytes 2359300
  1.5 9.6 %copy-start.1 = (bf16[3,8,64,256]{3,2,1,0:T(8,128)(2,1)}, bf16[3,8,64,256]{3,2,1,0:T(8,128)(2,1)S(1)}, u32[]{:S(2)}) copy-start(bf16[3,8,64,256]{3,2,1,0:T(8,128)(2,1)S(1)} %get-tuple-element.22.high_ref) | copy-start | bytes 2359300
  1.5 7.7 %collective-permute-start.1 = (bf16[3,8,64,256]{3,2,1,0:T(8,128)(2,1)S(1)}, bf16[3,8,64,256]{3,2,1,0:T(8,128)(2,1)S(1)}, u32[]{:S(2)}, u32[]{:S(2)}) collective-permute-start(bf16[3,8,64,256]{3,2,1,0:T(8,128)(2,1)S(1)} %get-tuple-element.21.low_ref), channel_id=1, source_target_pairs={{1,0},{2,1},{3,2},{4,3},{5,4},{6,5},{7,6},{8,7},{9,8},{10,9},{11,1... | collective-permute-start | bytes 2359304 | tf_op jit(solution)/shard_map/ppermute | solution.py:198
  2.8 7.4 %collective-permute-start = (bf16[3,8,64,256]{3,2,1,0:T(8,128)(2,1)S(1)}, bf16[3,8,64,256]{3,2,1,0:T(8,128)(2,1)S(1)}, u32[]{:S(2)}, u32[]{:S(2)}) collective-permute-start(bf16[3,8,64,256]{3,2,1,0:T(8,128)(2,1)S(1)} %get-tuple-element.22.high_ref), channel_id=1, source_target_pairs={{0,1},{1,2},{2,3},{3,4},{4,5},{5,6},{6,7},{7,8},{8,9},{9,10},{10,1... | collective-permute-start | bytes 2359304 | tf_op jit(solution)/shard_map/ppermute | solution.py:197
  21.1 18.6 %collective-permute-start.2 = (bf16[3,8,64,256]{3,2,1,0:T(8,128)(2,1)}, bf16[3,8,64,256]{3,2,1,0:T(8,128)(2,1)S(1)}, u32[]{:S(2)}, u32[]{:S(2)}) collective-permute-start(bf16[3,8,64,256]{3,2,1,0:T(8,128)(2,1)} %get-tuple-element.13.high_ref.older_high_ref), channel_id=1, source_target_pairs={{0,1},{1,2},{2,3},{3,4},{4,5},{5,6},{6,7},{7,8},{8,9},{9,10},{10,1... | collective-permute-start | bytes 2359304 | tf_op jit(solution)/shard_map/ppermute | solution.py:197
  37.6 6.3 %collective-permute-start.3 = (bf16[3,8,64,256]{3,2,1,0:T(8,128)(2,1)}, bf16[3,8,64,256]{3,2,1,0:T(8,128)(2,1)S(1)}, u32[]{:S(2)}, u32[]{:S(2)}) collective-permute-start(bf16[3,8,64,256]{3,2,1,0:T(8,128)(2,1)} %get-tuple-element.14.low_ref.older_low_ref), channel_id=1, source_target_pairs={{1,0},{2,1},{3,2},{4,3},{5,4},{6,5},{7,6},{8,7},{9,8},{10,9},{11,1... | collective-permute-start | bytes 2359304 | tf_op jit(solution)/shard_map/ppermute | solution.py:198
  53.4 18.7 %collective-permute-start.4 = (bf16[3,8,64,256]{3,2,1,0:T(8,128)(2,1)}, bf16[3,8,64,256]{3,2,1,0:T(8,128)(2,1)S(1)}, u32[]{:S(2)}, u32[]{:S(2)}) collective-permute-start(bf16[3,8,64,256]{3,2,1,0:T(8,128)(2,1)} %get-tuple-element.15.high_ref.older_high_ref), channel_id=1, source_target_pairs={{0,1},{1,2},{2,3},{3,4},{4,5},{5,6},{6,7},{7,8},{8,9},{9,10},{10,1... | collective-permute-start | bytes 2359304 | tf_op jit(solution)/shard_map/ppermute | solution.py:197
  70.1 6.2 %collective-permute-start.5 = (bf16[3,8,64,256]{3,2,1,0:T(8,128)(2,1)}, bf16[3,8,64,256]{3,2,1,0:T(8,128)(2,1)S(1)}, u32[]{:S(2)}, u32[]{:S(2)}) collective-permute-start(bf16[3,8,64,256]{3,2,1,0:T(8,128)(2,1)} %get-tuple-element.16.low_ref.older_low_ref), channel_id=1, source_target_pairs={{1,0},{2,1},{3,2},{4,3},{5,4},{6,5},{7,6},{8,7},{9,8},{10,9},{11,1... | collective-permute-start | bytes 2359304 | tf_op jit(solution)/shard_map/ppermute | solution.py:198
  85.8 18.7 %collective-permute-start.6 = (bf16[3,8,64,256]{3,2,1,0:T(8,128)(2,1)}, bf16[3,8,64,256]{3,2,1,0:T(8,128)(2,1)S(1)}, u32[]{:S(2)}, u32[]{:S(2)}) collective-permute-start(bf16[3,8,64,256]{3,2,1,0:T(8,128)(2,1)} %get-tuple-element.17.high_ref), channel_id=1, source_target_pairs={{0,1},{1,2},{2,3},{3,4},{4,5},{5,6},{6,7},{7,8},{8,9},{9,10},{10,1... | collective-permute-start | bytes 2359304 | tf_op jit(solution)/shard_map/ppermute | solution.py:197
  102.5 6.2 %collective-permute-start.7 = (bf16[3,8,64,256]{3,2,1,0:T(8,128)(2,1)}, bf16[3,8,64,256]{3,2,1,0:T(8,128)(2,1)S(1)}, u32[]{:S(2)}, u32[]{:S(2)}) collective-permute-start(bf16[3,8,64,256]{3,2,1,0:T(8,128)(2,1)} %get-tuple-element.18.low_ref), channel_id=1, source_target_pairs={{1,0},{2,1},{3,2},{4,3},{5,4},{6,5},{7,6},{8,7},{9,8},{10,9},{11,1... | collective-permute-start | bytes 2359304 | tf_op jit(solution)/shard_map/ppermute | solution.py:198
  120.2 18.6 %collective-permute-start.12 = (f32[128,256]{1,0:T(8,128)S(1)}, f32[128,256]{1,0:T(8,128)S(1)}, u32[]{:S(2)}, u32[]{:S(2)}) collective-permute-start(f32[128,256]{1,0:T(8,128)S(1)} %fusion.2), channel_id=1, source_target_pairs={{1,0},{2,1},{3,2},{4,3},{5,4},{6,5},{7,6},{8,7},{9,8},{10,9},{11,1... | collective-permute-start | bytes 393224 | tf_op jit(solution)/shard_map/ppermute | solution.py:224
  121.5 18.2 %collective-permute-start.8 = (f32[128,256]{1,0:T(8,128)S(1)}, f32[128,256]{1,0:T(8,128)S(1)}, u32[]{:S(2)}, u32[]{:S(2)}) collective-permute-start(f32[128,256]{1,0:T(8,128)S(1)} %fusion.2), channel_id=1, source_target_pairs={{0,1},{1,2},{2,3},{3,4},{4,5},{5,6},{6,7},{7,8},{8,9},{9,10},{10,1... | collective-permute-start | bytes 393224 | tf_op jit(solution)/shard_map/ppermute | solution.py:223
  139.8 13.9 %collective-permute-start.9 = (f32[128,256]{1,0:T(8,128)S(1)}, f32[128,256]{1,0:T(8,128)S(1)}, u32[]{:S(2)}, u32[]{:S(2)}) collective-permute-start(f32[128,256]{1,0:T(8,128)S(1)} %get-tuple-element.23), channel_id=1, source_target_pairs={{0,2},{1,3},{2,4},{3,5},{4,6},{5,7},{6,8},{7,9},{8,10},{9,11},{10,... | collective-permute-start | bytes 393224 | tf_op jit(solution)/shard_map/ppermute | solution.py:223
  152.4 6.9 %collective-permute-start.13 = (f32[128,256]{1,0:T(8,128)S(1)}, f32[128,256]{1,0:T(8,128)S(1)}, u32[]{:S(2)}, u32[]{:S(2)}) collective-permute-start(f32[128,256]{1,0:T(8,128)S(1)} %get-tuple-element.24), channel_id=1, source_target_pairs={{2,0},{3,1},{4,2},{5,3},{6,4},{7,5},{8,6},{9,7},{10,8},{11,9},{12,... | collective-permute-start | bytes 393224 | tf_op jit(solution)/shard_map/ppermute | solution.py:224
  153.7 8.2 %collective-permute-start.10 = (f32[128,256]{1,0:T(8,128)S(1)}, f32[128,256]{1,0:T(8,128)S(1)}, u32[]{:S(2)}, u32[]{:S(2)}) collective-permute-start(f32[128,256]{1,0:T(8,128)S(1)} %multiply_add_fusion.4), channel_id=1, source_target_pairs={{0,4},{1,5},{2,6},{3,7},{4,8},{5,9},{6,10},{7,11},{8,12},{9,13},{1... | collective-permute-start | bytes 393224 | tf_op jit(solution)/shard_map/ppermute | solution.py:223
  159.3 6.9 %collective-permute-start.14 = (f32[128,256]{1,0:T(8,128)S(1)}, f32[128,256]{1,0:T(8,128)S(1)}, u32[]{:S(2)}, u32[]{:S(2)}) collective-permute-start(f32[128,256]{1,0:T(8,128)S(1)} %multiply_add_fusion.1), channel_id=1, source_target_pairs={{4,0},{5,1},{6,2},{7,3},{8,4},{9,5},{10,6},{11,7},{12,8},{13,9},{1... | collective-permute-start | bytes 393224 | tf_op jit(solution)/shard_map/ppermute | solution.py:224
  161.9 9.9 %collective-permute-start.11 = (f32[128,256]{1,0:T(8,128)S(1)}, f32[128,256]{1,0:T(8,128)S(1)}, u32[]{:S(2)}, u32[]{:S(2)}) collective-permute-start(f32[128,256]{1,0:T(8,128)S(1)} %multiply_add_fusion.3), channel_id=1, source_target_pairs={{0,8},{1,9},{2,10},{3,11},{4,12},{5,13},{6,14},{7,15},{16,24},{17,... | collective-permute-start | bytes 393224 | tf_op jit(solution)/shard_map/ppermute | solution.py:223
  166.2 8.9 %collective-permute-start.15 = (f32[128,256]{1,0:T(8,128)S(1)}, f32[128,256]{1,0:T(8,128)S(1)}, u32[]{:S(2)}, u32[]{:S(2)}) collective-permute-start(f32[128,256]{1,0:T(8,128)S(1)} %multiply_add_fusion), channel_id=1, source_target_pairs={{8,0},{9,1},{10,2},{11,3},{12,4},{13,5},{14,6},{15,7},{24,16},{25,... | collective-permute-start | bytes 393224 | tf_op jit(solution)/shard_map/ppermute | solution.py:224
  192.7 1.3 copy-start.2
  194.9 4.3 %collective-permute-start.20 = (f32[128,128]{1,0:T(8,128)S(1)}, f32[128,128]{1,0:T(8,128)S(1)}, u32[]{:S(2)}, u32[]{:S(2)}) collective-permute-start(f32[128,128]{1,0:T(8,128)S(1)} %fusion.13), channel_id=1, source_target_pairs={{1,0},{2,1},{3,2},{4,3},{5,4},{6,5},{7,6},{8,7},{9,8},{10,9},{11,1... | collective-permute-start | bytes 196616 | tf_op jit(solution)/shard_map/ppermute | solution.py:224
  196.2 3.9 %collective-permute-start.16 = (f32[128,128]{1,0:T(8,128)S(1)}, f32[128,128]{1,0:T(8,128)S(1)}, u32[]{:S(2)}, u32[]{:S(2)}) collective-permute-start(f32[128,128]{1,0:T(8,128)S(1)} %fusion.13), channel_id=1, source_target_pairs={{0,1},{1,2},{2,3},{3,4},{4,5},{5,6},{6,7},{7,8},{8,9},{9,10},{10,1... | collective-permute-start | bytes 196616 | tf_op jit(solution)/shard_map/ppermute | solution.py:223
  200.2 8.2 %collective-permute-start.17 = (f32[128,128]{1,0:T(8,128)S(1)}, f32[128,128]{1,0:T(8,128)S(1)}, u32[]{:S(2)}, u32[]{:S(2)}) collective-permute-start(f32[128,128]{1,0:T(8,128)S(1)} %get-tuple-element.25), channel_id=1, source_target_pairs={{0,2},{1,3},{2,4},{3,5},{4,6},{5,7},{6,8},{7,9},{8,10},{9,11},{10,... | collective-permute-start | bytes 196616 | tf_op jit(solution)/shard_map/ppermute | solution.py:223
  205.8 6.9 %collective-permute-start.21 = (f32[128,128]{1,0:T(8,128)S(1)}, f32[128,128]{1,0:T(8,128)S(1)}, u32[]{:S(2)}, u32[]{:S(2)}) collective-permute-start(f32[128,128]{1,0:T(8,128)S(1)} %get-tuple-element.26), channel_id=1, source_target_pairs={{2,0},{3,1},{4,2},{5,3},{6,4},{7,5},{8,6},{9,7},{10,8},{11,9},{12,... | collective-permute-start | bytes 196616 | tf_op jit(solution)/shard_map/ppermute | solution.py:224
  208.3 6.3 %collective-permute-start.18 = (f32[128,128]{1,0:T(8,128)S(1)}, f32[128,128]{1,0:T(8,128)S(1)}, u32[]{:S(2)}, u32[]{:S(2)}) collective-permute-start(f32[128,128]{1,0:T(8,128)S(1)} %multiply_add_fusion.10), channel_id=1, source_target_pairs={{0,4},{1,5},{2,6},{3,7},{4,8},{5,9},{6,10},{7,11},{8,12},{9,13},{1... | collective-permute-start | bytes 196616 | tf_op jit(solution)/shard_map/ppermute | solution.py:223
  212.7 6.2 %collective-permute-start.22 = (f32[128,128]{1,0:T(8,128)S(1)}, f32[128,128]{1,0:T(8,128)S(1)}, u32[]{:S(2)}, u32[]{:S(2)}) collective-permute-start(f32[128,128]{1,0:T(8,128)S(1)} %multiply_add_fusion.7), channel_id=1, source_target_pairs={{4,0},{5,1},{6,2},{7,3},{8,4},{9,5},{10,6},{11,7},{12,8},{13,9},{1... | collective-permute-start | bytes 196616 | tf_op jit(solution)/shard_map/ppermute | solution.py:224
  214.6 6.1 %collective-permute-start.19 = (f32[128,128]{1,0:T(8,128)S(1)}, f32[128,128]{1,0:T(8,128)S(1)}, u32[]{:S(2)}, u32[]{:S(2)}) collective-permute-start(f32[128,128]{1,0:T(8,128)S(1)} %multiply_add_fusion.9), channel_id=1, source_target_pairs={{0,8},{1,9},{2,10},{3,11},{4,12},{5,13},{6,14},{7,15},{16,24},{17,... | collective-permute-start | bytes 196616 | tf_op jit(solution)/shard_map/ppermute | solution.py:223
  218.9 7.8 %collective-permute-start.23 = (f32[128,128]{1,0:T(8,128)S(1)}, f32[128,128]{1,0:T(8,128)S(1)}, u32[]{:S(2)}, u32[]{:S(2)}) collective-permute-start(f32[128,128]{1,0:T(8,128)S(1)} %multiply_add_fusion.6), channel_id=1, source_target_pairs={{8,0},{9,1},{10,2},{11,3},{12,4},{13,5},{14,6},{15,7},{24,16},{25,... | collective-permute-start | bytes 196616 | tf_op jit(solution)/shard_map/ppermute | solution.py:224

commit v9 on v8

--- a/solution.py
+++ b/solution.py
@@ -194,8 +194,12 @@
     bf_above = above.astype(jnp.bfloat16)
 
     def rimmed(low, high):
-        from_below = lax.ppermute(high, "gz", forward)
-        from_above = lax.ppermute(low, "gz", backward)
+        from_below = jnp.concatenate(
+            [lax.ppermute(high[k : k + 1], "gz", forward) for k in range(high.shape[0])], axis=0
+        )
+        from_above = jnp.concatenate(
+            [lax.ppermute(low[k : k + 1], "gz", backward) for k in range(low.shape[0])], axis=0
+        )
         return from_below * bf_below, from_above * bf_above
 
     lanes = jnp.broadcast_to(grid[..., None], grid.shape + (128,))

time: 248 us -> 254 us (1.024)
  waiting for transfers between devices: 27.3 us -> 21.2 us
  local copies, waits for them, and re-layouts: 6.08 us -> 11.5 us
  starting transfers between devices: 120 us -> 125 us
    ppermute x8 -> x24, starting transfers between devices: 58.3 us -> 66.7 us  [the longest x12 51 us: rimmed(): lax.ppermute(high[k:k + 1], 'gz', forward)]
    slice x0 -> x7, local copies, waits for them, and re-layouts: none -> 5.54 us  [the longest x3 3.75 us: rimmed(): high[k:k + 1]]
    ppermute x8 -> x24, waiting for transfers between devices: 11.8 us -> 7.04 us  [the longest x12 7.01 us: rimmed(): lax.ppermute(low[k:k + 1], 'gz', backward)]
    ppermute x8, starting transfers between devices: 51.1 us -> 48.4 us  [domain_total(): from_low = lax.ppermute(forward, 'gz', ahead)]
  transfers between devices with their start and end apart: 24 -> 40, of which waited for: 17 -> 14; matrix products, arithmetic and copies ran while one was open for 2% -> 3% of each run, Pallas kernels for 0% -> 0%
where the time goes in v9:
time: 254 us; the launch traced here: 253 us
  starting transfers between devices  125 us (49%)
  Pallas kernels  67.9 us (27%)
  waiting for transfers between devices  21.2 us (8%)
  local copies, waits for them, and re-layouts  11.5 us (5%)
  other arithmetic  11.5 us (5%)
  between operations  11.1 us (4%)
  matrix products  3.8 us (1%)
    ppermute x12, starting transfers between devices, rimmed(): lax.ppermute(high[k:k + 1], 'gz', forward)  51 us
    ppermute x8, starting transfers between devices, domain_total(): from_low = lax.ppermute(forward, 'gz', ahead)  48.4 us
    pallas_call x4, Pallas kernels, chebyshev_step(): pl.pallas_call(functools.partial(_step_kernel, first), out_shape=(piece,...  34 us
    pallas_call x2, Pallas kernels, lower_inverse(): pl.pallas_call(_lower_inverse_kernel, out_shape=jax.ShapeDtypeStruct((n,...  33.9 us
    ppermute x12, starting transfers between devices, rimmed(): lax.ppermute(low[k:k + 1], 'gz', backward)  15.7 us
    ppermute x8, starting transfers between devices, domain_total(): from_high = lax.ppermute(backward, 'gz', behind)  10.3 us
    ppermute x8, waiting for transfers between devices, domain_total(): from_high = lax.ppermute(backward, 'gz', behind)  9.56 us
    mul x8, other arithmetic, rimmed(): return (from_below * bf_below, from_above * bf_above)  7.9 us
  transfers between devices with their start and end apart: 40, of which 14 were waited for; matrix products, arithmetic and copies ran while one was open for 3% of the time, Pallas kernels for 0%

profile of v9, /device:TPU:0, one launch (start us, length us, event | category | flops | bytes accessed | tf_op | source)
XLA Modules:
  0.0 252.5 jit_solution(4070514864659054974)
XLA Ops:
  0.0 1.6 fusion.11
  1.6 1.3 collective-permute-start.3
  2.9 1.3 collective-permute-start.5
  4.2 1.3 collective-permute-start.4
  5.5 4.3 %collective-permute-start.2 = (bf16[1,8,64,256]{3,2,1,0:T(8,128)(2,1)S(1)}, bf16[1,8,64,256]{3,2,1,0:T(8,128)(2,1)S(1)}, u32[]{:S(2)}, u32[]{:S(2)}) collective-permute-start(bf16[1,8,64,256]{3,2,1,0:T(8,128)(2,1)S(1)} %get-tuple-element.24), channel_id=1, source_target_pairs={{0,1},{1,2},{2,3},{3,4},{4,5},{5,6},{6,7},{7,8},{8,9},{9,10},{10,1... | collective-permute-start | bytes 786440 | tf_op jit(solution)/shard_map/ppermute | solution.py:198
  9.8 4.5 %collective-permute-start.1 = (bf16[1,8,64,256]{3,2,1,0:T(8,128)(2,1)S(1)}, bf16[1,8,64,256]{3,2,1,0:T(8,128)(2,1)S(1)}, u32[]{:S(2)}, u32[]{:S(2)}) collective-permute-start(bf16[1,8,64,256]{3,2,1,0:T(8,128)(2,1)S(1)} %get-tuple-element.25), channel_id=1, source_target_pairs={{0,1},{1,2},{2,3},{3,4},{4,5},{5,6},{6,7},{7,8},{8,9},{9,10},{10,1... | collective-permute-start | bytes 786440 | tf_op jit(solution)/shard_map/ppermute | solution.py:198
  14.4 2.4 collective-permute-start
  16.8 1.3 fusion.12
  23.4 1.6 broadcast_in_dim.8.low_pot_ref.high_pot_ref
  25.0 8.3 %shard_map.37 = (bf16[3,8,64,256]{3,2,1,0:T(8,128)(2,1)}, bf16[3,8,64,256]{3,2,1,0:T(8,128)(2,1)}) custom-call(bf16[3,8,64,256]{3,2,1,0:T(8,128)(2,1)} %maximum_multiply_fusion.below_ref, bf16[3,8,64,256]{3,2,1,0:T(8,128)(2,1)} %get-tuple-element.28.low_ref, bf16[3,8,64,256]{3,2,1,0:T(8,128)(2,1)} %get-tuple-element.27.high_ref, ...), custom_call_target="tpu_custom_call" | custom-call | tf_op jit(solution)/shard_map/pallas_call | solution.py:111
  33.3 1.2 fusion.18
  34.6 4.5 %collective-permute-start.6 = (bf16[1,8,64,256]{3,2,1,0:T(8,128)(2,1)S(1)}, bf16[1,8,64,256]{3,2,1,0:T(8,128)(2,1)S(1)}, u32[]{:S(2)}, u32[]{:S(2)}) collective-permute-start(bf16[1,8,64,256]{3,2,1,0:T(8,128)(2,1)S(1)} %get-tuple-element.44), channel_id=1, source_target_pairs={{0,1},{1,2},{2,3},{3,4},{4,5},{5,6},{6,7},{7,8},{8,9},{9,10},{10,1... | collective-permute-start | bytes 786440 | tf_op jit(solution)/shard_map/ppermute | solution.py:198
  39.1 4.2 %collective-permute-start.8 = (bf16[1,8,64,256]{3,2,1,0:T(8,128)(2,1)S(1)}, bf16[1,8,64,256]{3,2,1,0:T(8,128)(2,1)S(1)}, u32[]{:S(2)}, u32[]{:S(2)}) collective-permute-start(bf16[1,8,64,256]{3,2,1,0:T(8,128)(2,1)S(1)} %get-tuple-element.45), channel_id=1, source_target_pairs={{0,1},{1,2},{2,3},{3,4},{4,5},{5,6},{6,7},{7,8},{8,9},{9,10},{10,1... | collective-permute-start | bytes 786440 | tf_op jit(solution)/shard_map/ppermute | solution.py:198
  43.4 1.9 collective-permute-start.7
  45.4 1.3 collective-permute-start.9
  46.7 1.3 collective-permute-start.11
  48.0 1.3 collective-permute-start.10
  50.8 1.9 collective-permute-done.10
  53.7 8.5 %shard_map.38 = (bf16[3,8,64,256]{3,2,1,0:T(8,128)(2,1)}, bf16[3,8,64,256]{3,2,1,0:T(8,128)(2,1)}) custom-call(bf16[3,8,64,256]{3,2,1,0:T(8,128)(2,1)} %maximum_multiply_fusion.2.below_ref, bf16[3,8,64,256]{3,2,1,0:T(8,128)(2,1)} %get-tuple-element.14.low_ref.older_low_ref, bf16[3,8,64,256]{3,2,1,0:T(8,128)(2,1)} %get-tuple-element.13.high_ref.older_high_ref, ...), custom_call_target="tpu_custom_call" | custom-call | tf_op jit(solution)/shard_map/pallas_call | solution.py:111
  62.3 1.2 fusion.16
  63.5 8.4 %collective-permute-start.12 = (bf16[1,8,64,256]{3,2,1,0:T(8,128)(2,1)S(1)}, bf16[1,8,64,256]{3,2,1,0:T(8,128)(2,1)S(1)}, u32[]{:S(2)}, u32[]{:S(2)}) collective-permute-start(bf16[1,8,64,256]{3,2,1,0:T(8,128)(2,1)S(1)} %get-tuple-element.38), channel_id=1, source_target_pairs={{0,1},{1,2},{2,3},{3,4},{4,5},{5,6},{6,7},{7,8},{8,9},{9,10},{10,1... | collective-permute-start | bytes 786440 | tf_op jit(solution)/shard_map/ppermute | solution.py:198
  72.0 1.9 collective-permute-start.14
  73.9 5.5 %collective-permute-start.13 = (bf16[1,8,64,256]{3,2,1,0:T(8,128)(2,1)S(1)}, bf16[1,8,64,256]{3,2,1,0:T(8,128)(2,1)S(1)}, u32[]{:S(2)}, u32[]{:S(2)}) collective-permute-start(bf16[1,8,64,256]{3,2,1,0:T(8,128)(2,1)S(1)} %get-tuple-element.40), channel_id=1, source_target_pairs={{0,1},{1,2},{2,3},{3,4},{4,5},{5,6},{6,7},{7,8},{8,9},{9,10},{10,1... | collective-permute-start | bytes 786440 | tf_op jit(solution)/shard_map/ppermute | solution.py:198
  79.5 1.3 collective-permute-start.15
  80.8 1.3 collective-permute-start.17
  82.1 1.5 collective-permute-start.16
  84.8 1.9 collective-permute-done.16
  87.8 8.6 %shard_map.39 = (bf16[3,8,64,256]{3,2,1,0:T(8,128)(2,1)}, bf16[3,8,64,256]{3,2,1,0:T(8,128)(2,1)}) custom-call(bf16[3,8,64,256]{3,2,1,0:T(8,128)(2,1)} %maximum_multiply_fusion.4.below_ref, bf16[3,8,64,256]{3,2,1,0:T(8,128)(2,1)} %get-tuple-element.16.low_ref.older_low_ref, bf16[3,8,64,256]{3,2,1,0:T(8,128)(2,1)} %get-tuple-element.15.high_ref.older_high_ref, ...), custom_call_target="tpu_custom_call" | custom-call | tf_op jit(solution)/shard_map/pallas_call | solution.py:111
  96.4 1.2 fusion.14
  97.6 7.9 %collective-permute-start.18 = (bf16[1,8,64,256]{3,2,1,0:T(8,128)(2,1)S(1)}, bf16[1,8,64,256]{3,2,1,0:T(8,128)(2,1)S(1)}, u32[]{:S(2)}, u32[]{:S(2)}) collective-permute-start(bf16[1,8,64,256]{3,2,1,0:T(8,128)(2,1)S(1)} %get-tuple-element.32), channel_id=1, source_target_pairs={{0,1},{1,2},{2,3},{3,4},{4,5},{5,6},{6,7},{7,8},{8,9},{9,10},{10,1... | collective-permute-start | bytes 786440 | tf_op jit(solution)/shard_map/ppermute | solution.py:198
  105.6 1.9 collective-permute-start.20
  107.5 3.4 %collective-permute-start.19 = (bf16[1,8,64,256]{3,2,1,0:T(8,128)(2,1)S(1)}, bf16[1,8,64,256]{3,2,1,0:T(8,128)(2,1)S(1)}, u32[]{:S(2)}, u32[]{:S(2)}) collective-permute-start(bf16[1,8,64,256]{3,2,1,0:T(8,128)(2,1)S(1)} %get-tuple-element.34), channel_id=1, source_target_pairs={{0,1},{1,2},{2,3},{3,4},{4,5},{5,6},{6,7},{7,8},{8,9},{9,10},{10,1... | collective-permute-start | bytes 786440 | tf_op jit(solution)/shard_map/ppermute | solution.py:198
  111.0 1.3 collective-permute-start.21
  112.3 1.3 collective-permute-start.23
  113.6 1.3 collective-permute-start.22
  114.9 1.0 maximum_multiply_fusion.6.below_ref
  116.4 1.9 collective-permute-done.22
  119.3 8.5 %shard_map.40 = (bf16[3,8,64,256]{3,2,1,0:T(8,128)(2,1)}, bf16[3,8,64,256]{3,2,1,0:T(8,128)(2,1)}) custom-call(bf16[3,8,64,256]{3,2,1,0:T(8,128)(2,1)} %maximum_multiply_fusion.6.below_ref, bf16[3,8,64,256]{3,2,1,0:T(8,128)(2,1)} %get-tuple-element.18.low_ref, bf16[3,8,64,256]{3,2,1,0:T(8,128)(2,1)} %get-tuple-element.17.high_ref, ...), custom_call_target="tpu_custom_call" | custom-call | tf_op jit(solution)/shard_map/pallas_call | solution.py:111
  127.8 1.5 pad_maximum_fusion
  129.7 1.3 collective-permute-start.28
  131.0 8.6 %collective-permute-start.24 = (f32[128,256]{1,0:T(8,128)S(1)}, f32[128,256]{1,0:T(8,128)S(1)}, u32[]{:S(2)}, u32[]{:S(2)}) collective-permute-start(f32[128,256]{1,0:T(8,128)S(1)} %fusion.2), channel_id=1, source_target_pairs={{0,1},{1,2},{2,3},{3,4},{4,5},{5,6},{6,7},{7,8},{8,9},{9,10},{10,1... | collective-permute-start | bytes 393224 | tf_op jit(solution)/shard_map/ppermute | solution.py:227
  140.6 8.3 %collective-permute-start.25 = (f32[128,256]{1,0:T(8,128)S(1)}, f32[128,256]{1,0:T(8,128)S(1)}, u32[]{:S(2)}, u32[]{:S(2)}) collective-permute-start(f32[128,256]{1,0:T(8,128)S(1)} %get-tuple-element.47), channel_id=1, source_target_pairs={{0,2},{1,3},{2,4},{3,5},{4,6},{5,7},{6,8},{7,9},{8,10},{9,11},{10,... | collective-permute-start | bytes 393224 | tf_op jit(solution)/shard_map/ppermute | solution.py:227
  153.8 1.3 collective-permute-start.29
  155.2 6.9 %collective-permute-start.26 = (f32[128,256]{1,0:T(8,128)S(1)}, f32[128,256]{1,0:T(8,128)S(1)}, u32[]{:S(2)}, u32[]{:S(2)}) collective-permute-start(f32[128,256]{1,0:T(8,128)S(1)} %multiply_add_fusion.4), channel_id=1, source_target_pairs={{0,4},{1,5},{2,6},{3,7},{4,8},{5,9},{6,10},{7,11},{8,12},{9,13},{1... | collective-permute-start | bytes 393224 | tf_op jit(solution)/shard_map/ppermute | solution.py:227
  162.1 1.3 collective-permute-start.30
  163.4 1.2 collective-permute-done.26
  164.6 5.4 %collective-permute-start.27 = (f32[128,256]{1,0:T(8,128)S(1)}, f32[128,256]{1,0:T(8,128)S(1)}, u32[]{:S(2)}, u32[]{:S(2)}) collective-permute-start(f32[128,256]{1,0:T(8,128)S(1)} %multiply_add_fusion.3), channel_id=1, source_target_pairs={{0,8},{1,9},{2,10},{3,11},{4,12},{5,13},{6,14},{7,15},{16,24},{17,... | collective-permute-start | bytes 393224 | tf_op jit(solution)/shard_map/ppermute | solution.py:227
  170.0 1.3 collective-permute-start.31
  173.7 1.2 fusion.10
  175.5 3.6 %collective-permute-done.31 = f32[128,256]{1,0:T(8,128)S(1)} collective-permute-done((f32[128,256]{1,0:T(8,128)S(1)}, f32[128,256]{1,0:T(8,128)S(1)}, u32[]{:S(2)}, u32[]{:S(2)}) %collective-permute-start.31) | collective-permute-done | bytes 131104 | tf_op jit(solution)/shard_map/ppermute | solution.py:228
  179.9 16.9 %shard_map.41 = f32[128,128]{1,0:T(8,128)} custom-call(f32[128,128]{1,0:T(8,128)} %slice.127.gram_ref), custom_call_target="tpu_custom_call" | custom-call | tf_op jit(solution)/shard_map/pallas_call | solution.py:48
  196.8 1.3 convolution_convert_fusion.1
  199.0 1.3 collective-permute-start.36
  200.3 3.0 %collective-permute-start.32 = (f32[128,128]{1,0:T(8,128)S(1)}, f32[128,128]{1,0:T(8,128)S(1)}, u32[]{:S(2)}, u32[]{:S(2)}) collective-permute-start(f32[128,128]{1,0:T(8,128)S(1)} %fusion.20), channel_id=1, source_target_pairs={{0,1},{1,2},{2,3},{3,4},{4,5},{5,6},{6,7},{7,8},{8,9},{9,10},{10,1... | collective-permute-start | bytes 196616 | tf_op jit(solution)/shard_map/ppermute | solution.py:227
  204.3 4.6 %collective-permute-start.33 = (f32[128,128]{1,0:T(8,128)S(1)}, f32[128,128]{1,0:T(8,128)S(1)}, u32[]{:S(2)}, u32[]{:S(2)}) collective-permute-start(f32[128,128]{1,0:T(8,128)S(1)} %get-tuple-element.49), channel_id=1, source_target_pairs={{0,2},{1,3},{2,4},{3,5},{4,6},{5,7},{6,8},{7,9},{8,10},{9,11},{10,... | collective-permute-start | bytes 196616 | tf_op jit(solution)/shard_map/ppermute | solution.py:227
  208.9 1.3 collective-permute-start.37
  210.8 5.5 %collective-permute-start.34 = (f32[128,128]{1,0:T(8,128)S(1)}, f32[128,128]{1,0:T(8,128)S(1)}, u32[]{:S(2)}, u32[]{:S(2)}) collective-permute-start(f32[128,128]{1,0:T(8,128)S(1)} %multiply_add_fusion.10), channel_id=1, source_target_pairs={{0,4},{1,5},{2,6},{3,7},{4,8},{5,9},{6,10},{7,11},{8,12},{9,13},{1... | collective-permute-start | bytes 196616 | tf_op jit(solution)/shard_map/ppermute | solution.py:227
  216.3 1.3 collective-permute-start.38
  218.2 6.0 %collective-permute-start.35 = (f32[128,128]{1,0:T(8,128)S(1)}, f32[128,128]{1,0:T(8,128)S(1)}, u32[]{:S(2)}, u32[]{:S(2)}) collective-permute-start(f32[128,128]{1,0:T(8,128)S(1)} %multiply_add_fusion.9), channel_id=1, source_target_pairs={{0,8},{1,9},{2,10},{3,11},{4,12},{5,13},{6,14},{7,15},{16,24},{17,... | collective-permute-start | bytes 196616 | tf_op jit(solution)/shard_map/ppermute | solution.py:227
  224.3 1.3 collective-permute-start.39
  226.1 5.9 %collective-permute-done.39 = f32[128,128]{1,0:T(8,128)S(1)} collective-permute-done((f32[128,128]{1,0:T(8,128)S(1)}, f32[128,128]{1,0:T(8,128)S(1)}, u32[]{:S(2)}, u32[]{:S(2)}) %collective-permute-start.39) | collective-permute-done | bytes 65568 | tf_op jit(solution)/shard_map/ppermute | solution.py:228
  232.7 16.9 %shard_map.42 = f32[128,128]{1,0:T(8,128)} custom-call(f32[128,128]{1,0:T(8,128)} %subtract_divide_fusion.1.gram_ref), custom_call_target="tpu_custom_call" | custom-call | tf_op jit(solution)/shard_map/pallas_call | solution.py:48
  249.6 1.2 convolution_convert_fusion
  250.9 1.6 copy.5
  (77 shorter events, 15.6 us)
Async XLA Ops:
  0.0 16.8 %copy-start = (bf16[6,8,64,256]{3,2,1,0:T(8,128)(2,1)S(1)}, bf16[6,8,64,256]{3,2,1,0:T(8,128)(2,1)}, u32[]{:S(2)}) copy-start(bf16[6,8,64,256]{3,2,1,0:T(8,128)(2,1)} %older_high_ref.3) | copy-start | bytes 4718596
  1.6 12.7 %collective-permute-start.3 = (bf16[1,8,64,256]{3,2,1,0:T(8,128)(2,1)S(1)}, bf16[1,8,64,256]{3,2,1,0:T(8,128)(2,1)S(1)}, u32[]{:S(2)}, u32[]{:S(2)}) collective-permute-start(bf16[1,8,64,256]{3,2,1,0:T(8,128)(2,1)S(1)} %get-tuple-element.21), channel_id=1, source_target_pairs={{1,0},{2,1},{3,2},{4,3},{5,4},{6,5},{7,6},{8,7},{9,8},{10,9},{11,1... | collective-permute-start | bytes 786440 | tf_op jit(solution)/shard_map/ppermute | solution.py:201
  2.9 18.5 %collective-permute-start.5 = (bf16[1,8,64,256]{3,2,1,0:T(8,128)(2,1)S(1)}, bf16[1,8,64,256]{3,2,1,0:T(8,128)(2,1)S(1)}, u32[]{:S(2)}, u32[]{:S(2)}) collective-permute-start(bf16[1,8,64,256]{3,2,1,0:T(8,128)(2,1)S(1)} %get-tuple-element.22), channel_id=1, source_target_pairs={{1,0},{2,1},{3,2},{4,3},{5,4},{6,5},{7,6},{8,7},{9,8},{10,9},{11,1... | collective-permute-start | bytes 786440 | tf_op jit(solution)/shard_map/ppermute | solution.py:201
  4.2 17.2 %collective-permute-start.4 = (bf16[1,8,64,256]{3,2,1,0:T(8,128)(2,1)S(1)}, bf16[1,8,64,256]{3,2,1,0:T(8,128)(2,1)S(1)}, u32[]{:S(2)}, u32[]{:S(2)}) collective-permute-start(bf16[1,8,64,256]{3,2,1,0:T(8,128)(2,1)S(1)} %get-tuple-element.23), channel_id=1, source_target_pairs={{1,0},{2,1},{3,2},{4,3},{5,4},{6,5},{7,6},{8,7},{9,8},{10,9},{11,1... | collective-permute-start | bytes 786440 | tf_op jit(solution)/shard_map/ppermute | solution.py:201
  5.5 16.9 %collective-permute-start.2 = (bf16[1,8,64,256]{3,2,1,0:T(8,128)(2,1)S(1)}, bf16[1,8,64,256]{3,2,1,0:T(8,128)(2,1)S(1)}, u32[]{:S(2)}, u32[]{:S(2)}) collective-permute-start(bf16[1,8,64,256]{3,2,1,0:T(8,128)(2,1)S(1)} %get-tuple-element.24), channel_id=1, source_target_pairs={{0,1},{1,2},{2,3},{3,4},{4,5},{5,6},{6,7},{7,8},{8,9},{9,10},{10,1... | collective-permute-start | bytes 786440 | tf_op jit(solution)/shard_map/ppermute | solution.py:198
  9.8 12.6 %collective-permute-start.1 = (bf16[1,8,64,256]{3,2,1,0:T(8,128)(2,1)S(1)}, bf16[1,8,64,256]{3,2,1,0:T(8,128)(2,1)S(1)}, u32[]{:S(2)}, u32[]{:S(2)}) collective-permute-start(bf16[1,8,64,256]{3,2,1,0:T(8,128)(2,1)S(1)} %get-tuple-element.25), channel_id=1, source_target_pairs={{0,1},{1,2},{2,3},{3,4},{4,5},{5,6},{6,7},{7,8},{8,9},{9,10},{10,1... | collective-permute-start | bytes 786440 | tf_op jit(solution)/shard_map/ppermute | solution.py:198
  14.3 3.8 %copy-start.5 = (s32[16]{0:T(128)S(1)}, s32[16]{0:T(128)}, u32[]{:S(2)}) copy-start(s32[16]{0:T(128)} %param.5) | copy-start | bytes 196
  14.4 6.9 %copy-start.6 = (f32[6,512]{1,0:T(8,128)S(1)}, f32[6,512]{1,0:T(8,128)}, u32[]{:S(2)}) copy-start(f32[6,512]{1,0:T(8,128)} %param.4) | copy-start | bytes 36868
  14.4 8.0 %collective-permute-start = (bf16[1,8,64,256]{3,2,1,0:T(8,128)(2,1)S(1)}, bf16[1,8,64,256]{3,2,1,0:T(8,128)(2,1)S(1)}, u32[]{:S(2)}, u32[]{:S(2)}) collective-permute-start(bf16[1,8,64,256]{3,2,1,0:T(8,128)(2,1)S(1)} %get-tuple-element.26), channel_id=1, source_target_pairs={{0,1},{1,2},{2,3},{3,4},{4,5},{5,6},{6,7},{7,8},{8,9},{9,10},{10,1... | collective-permute-start | bytes 786440 | tf_op jit(solution)/shard_map/ppermute | solution.py:198
  33.3 12.0 %copy-start.1 = (bf16[3,8,64,256]{3,2,1,0:T(8,128)(2,1)S(1)}, bf16[3,8,64,256]{3,2,1,0:T(8,128)(2,1)}, u32[]{:S(2)}) copy-start(bf16[3,8,64,256]{3,2,1,0:T(8,128)(2,1)} %get-tuple-element.14.low_ref.older_low_ref) | copy-start | bytes 2359300
  34.6 13.4 %collective-permute-start.6 = (bf16[1,8,64,256]{3,2,1,0:T(8,128)(2,1)S(1)}, bf16[1,8,64,256]{3,2,1,0:T(8,128)(2,1)S(1)}, u32[]{:S(2)}, u32[]{:S(2)}) collective-permute-start(bf16[1,8,64,256]{3,2,1,0:T(8,128)(2,1)S(1)} %get-tuple-element.44), channel_id=1, source_target_pairs={{0,1},{1,2},{2,3},{3,4},{4,5},{5,6},{6,7},{7,8},{8,9},{9,10},{10,1... | collective-permute-start | bytes 786440 | tf_op jit(solution)/shard_map/ppermute | solution.py:198
  39.1 10.2 %collective-permute-start.8 = (bf16[1,8,64,256]{3,2,1,0:T(8,128)(2,1)S(1)}, bf16[1,8,64,256]{3,2,1,0:T(8,128)(2,1)S(1)}, u32[]{:S(2)}, u32[]{:S(2)}) collective-permute-start(bf16[1,8,64,256]{3,2,1,0:T(8,128)(2,1)S(1)} %get-tuple-element.45), channel_id=1, source_target_pairs={{0,1},{1,2},{2,3},{3,4},{4,5},{5,6},{6,7},{7,8},{8,9},{9,10},{10,1... | collective-permute-start | bytes 786440 | tf_op jit(solution)/shard_map/ppermute | solution.py:198
  43.4 5.9 %collective-permute-start.7 = (bf16[1,8,64,256]{3,2,1,0:T(8,128)(2,1)S(1)}, bf16[1,8,64,256]{3,2,1,0:T(8,128)(2,1)S(1)}, u32[]{:S(2)}, u32[]{:S(2)}) collective-permute-start(bf16[1,8,64,256]{3,2,1,0:T(8,128)(2,1)S(1)} %get-tuple-element.46), channel_id=1, source_target_pairs={{0,1},{1,2},{2,3},{3,4},{4,5},{5,6},{6,7},{7,8},{8,9},{9,10},{10,1... | collective-permute-start | bytes 786440 | tf_op jit(solution)/shard_map/ppermute | solution.py:198
  45.4 4.9 %collective-permute-start.9 = (bf16[1,8,64,256]{3,2,1,0:T(8,128)(2,1)S(1)}, bf16[1,8,64,256]{3,2,1,0:T(8,128)(2,1)S(1)}, u32[]{:S(2)}, u32[]{:S(2)}) collective-permute-start(bf16[1,8,64,256]{3,2,1,0:T(8,128)(2,1)S(1)} %get-tuple-element.41), channel_id=1, source_target_pairs={{1,0},{2,1},{3,2},{4,3},{5,4},{6,5},{7,6},{8,7},{9,8},{10,9},{11,1... | collective-permute-start | bytes 786440 | tf_op jit(solution)/shard_map/ppermute | solution.py:201
  46.7 4.1 %collective-permute-start.11 = (bf16[1,8,64,256]{3,2,1,0:T(8,128)(2,1)S(1)}, bf16[1,8,64,256]{3,2,1,0:T(8,128)(2,1)S(1)}, u32[]{:S(2)}, u32[]{:S(2)}) collective-permute-start(bf16[1,8,64,256]{3,2,1,0:T(8,128)(2,1)S(1)} %get-tuple-element.42), channel_id=1, source_target_pairs={{1,0},{2,1},{3,2},{4,3},{5,4},{6,5},{7,6},{8,7},{9,8},{10,9},{11,1... | collective-permute-start | bytes 786440 | tf_op jit(solution)/shard_map/ppermute | solution.py:201
  48.0 4.7 %collective-permute-start.10 = (bf16[1,8,64,256]{3,2,1,0:T(8,128)(2,1)S(1)}, bf16[1,8,64,256]{3,2,1,0:T(8,128)(2,1)S(1)}, u32[]{:S(2)}, u32[]{:S(2)}) collective-permute-start(bf16[1,8,64,256]{3,2,1,0:T(8,128)(2,1)S(1)} %get-tuple-element.43), channel_id=1, source_target_pairs={{1,0},{2,1},{3,2},{4,3},{5,4},{6,5},{7,6},{8,7},{9,8},{10,9},{11,1... | collective-permute-start | bytes 786440 | tf_op jit(solution)/shard_map/ppermute | solution.py:201
  62.3 17.1 %copy-start.2 = (bf16[3,8,64,256]{3,2,1,0:T(8,128)(2,1)S(1)}, bf16[3,8,64,256]{3,2,1,0:T(8,128)(2,1)}, u32[]{:S(2)}) copy-start(bf16[3,8,64,256]{3,2,1,0:T(8,128)(2,1)} %get-tuple-element.16.low_ref.older_low_ref) | copy-start | bytes 2359300
  63.5 18.6 %collective-permute-start.12 = (bf16[1,8,64,256]{3,2,1,0:T(8,128)(2,1)S(1)}, bf16[1,8,64,256]{3,2,1,0:T(8,128)(2,1)S(1)}, u32[]{:S(2)}, u32[]{:S(2)}) collective-permute-start(bf16[1,8,64,256]{3,2,1,0:T(8,128)(2,1)S(1)} %get-tuple-element.38), channel_id=1, source_target_pairs={{0,1},{1,2},{2,3},{3,4},{4,5},{5,6},{6,7},{7,8},{8,9},{9,10},{10,1... | collective-permute-start | bytes 786440 | tf_op jit(solution)/shard_map/ppermute | solution.py:198
  72.0 11.6 %collective-permute-start.14 = (bf16[1,8,64,256]{3,2,1,0:T(8,128)(2,1)S(1)}, bf16[1,8,64,256]{3,2,1,0:T(8,128)(2,1)S(1)}, u32[]{:S(2)}, u32[]{:S(2)}) collective-permute-start(bf16[1,8,64,256]{3,2,1,0:T(8,128)(2,1)S(1)} %get-tuple-element.39), channel_id=1, source_target_pairs={{0,1},{1,2},{2,3},{3,4},{4,5},{5,6},{6,7},{7,8},{8,9},{9,10},{10,1... | collective-permute-start | bytes 786440 | tf_op jit(solution)/shard_map/ppermute | solution.py:198
  73.9 9.7 %collective-permute-start.13 = (bf16[1,8,64,256]{3,2,1,0:T(8,128)(2,1)S(1)}, bf16[1,8,64,256]{3,2,1,0:T(8,128)(2,1)S(1)}, u32[]{:S(2)}, u32[]{:S(2)}) collective-permute-start(bf16[1,8,64,256]{3,2,1,0:T(8,128)(2,1)S(1)} %get-tuple-element.40), channel_id=1, source_target_pairs={{0,1},{1,2},{2,3},{3,4},{4,5},{5,6},{6,7},{7,8},{8,9},{9,10},{10,1... | collective-permute-start | bytes 786440 | tf_op jit(solution)/shard_map/ppermute | solution.py:198
  79.5 5.1 %collective-permute-start.15 = (bf16[1,8,64,256]{3,2,1,0:T(8,128)(2,1)S(1)}, bf16[1,8,64,256]{3,2,1,0:T(8,128)(2,1)S(1)}, u32[]{:S(2)}, u32[]{:S(2)}) collective-permute-start(bf16[1,8,64,256]{3,2,1,0:T(8,128)(2,1)S(1)} %get-tuple-element.35), channel_id=1, source_target_pairs={{1,0},{2,1},{3,2},{4,3},{5,4},{6,5},{7,6},{8,7},{9,8},{10,9},{11,1... | collective-permute-start | bytes 786440 | tf_op jit(solution)/shard_map/ppermute | solution.py:201
  80.8 4.1 %collective-permute-start.17 = (bf16[1,8,64,256]{3,2,1,0:T(8,128)(2,1)S(1)}, bf16[1,8,64,256]{3,2,1,0:T(8,128)(2,1)S(1)}, u32[]{:S(2)}, u32[]{:S(2)}) collective-permute-start(bf16[1,8,64,256]{3,2,1,0:T(8,128)(2,1)S(1)} %get-tuple-element.36), channel_id=1, source_target_pairs={{1,0},{2,1},{3,2},{4,3},{5,4},{6,5},{7,6},{8,7},{9,8},{10,9},{11,1... | collective-permute-start | bytes 786440 | tf_op jit(solution)/shard_map/ppermute | solution.py:201
  82.1 4.7 %collective-permute-start.16 = (bf16[1,8,64,256]{3,2,1,0:T(8,128)(2,1)S(1)}, bf16[1,8,64,256]{3,2,1,0:T(8,128)(2,1)S(1)}, u32[]{:S(2)}, u32[]{:S(2)}) collective-permute-start(bf16[1,8,64,256]{3,2,1,0:T(8,128)(2,1)S(1)} %get-tuple-element.37), channel_id=1, source_target_pairs={{1,0},{2,1},{3,2},{4,3},{5,4},{6,5},{7,6},{8,7},{9,8},{10,9},{11,1... | collective-permute-start | bytes 786440 | tf_op jit(solution)/shard_map/ppermute | solution.py:201
  96.4 14.6 %copy-start.3 = (bf16[3,8,64,256]{3,2,1,0:T(8,128)(2,1)S(1)}, bf16[3,8,64,256]{3,2,1,0:T(8,128)(2,1)}, u32[]{:S(2)}) copy-start(bf16[3,8,64,256]{3,2,1,0:T(8,128)(2,1)} %get-tuple-element.18.low_ref) | copy-start | bytes 2359300
  97.6 16.0 %collective-permute-start.18 = (bf16[1,8,64,256]{3,2,1,0:T(8,128)(2,1)S(1)}, bf16[1,8,64,256]{3,2,1,0:T(8,128)(2,1)S(1)}, u32[]{:S(2)}, u32[]{:S(2)}) collective-permute-start(bf16[1,8,64,256]{3,2,1,0:T(8,128)(2,1)S(1)} %get-tuple-element.32), channel_id=1, source_target_pairs={{0,1},{1,2},{2,3},{3,4},{4,5},{5,6},{6,7},{7,8},{8,9},{9,10},{10,1... | collective-permute-start | bytes 786440 | tf_op jit(solution)/shard_map/ppermute | solution.py:198
  105.6 9.4 %collective-permute-start.20 = (bf16[1,8,64,256]{3,2,1,0:T(8,128)(2,1)S(1)}, bf16[1,8,64,256]{3,2,1,0:T(8,128)(2,1)S(1)}, u32[]{:S(2)}, u32[]{:S(2)}) collective-permute-start(bf16[1,8,64,256]{3,2,1,0:T(8,128)(2,1)S(1)} %get-tuple-element.33), channel_id=1, source_target_pairs={{0,1},{1,2},{2,3},{3,4},{4,5},{5,6},{6,7},{7,8},{8,9},{9,10},{10,1... | collective-permute-start | bytes 786440 | tf_op jit(solution)/shard_map/ppermute | solution.py:198
  107.5 7.4 %collective-permute-start.19 = (bf16[1,8,64,256]{3,2,1,0:T(8,128)(2,1)S(1)}, bf16[1,8,64,256]{3,2,1,0:T(8,128)(2,1)S(1)}, u32[]{:S(2)}, u32[]{:S(2)}) collective-permute-start(bf16[1,8,64,256]{3,2,1,0:T(8,128)(2,1)S(1)} %get-tuple-element.34), channel_id=1, source_target_pairs={{0,1},{1,2},{2,3},{3,4},{4,5},{5,6},{6,7},{7,8},{8,9},{9,10},{10,1... | collective-permute-start | bytes 786440 | tf_op jit(solution)/shard_map/ppermute | solution.py:198
  111.0 4.9 %collective-permute-start.21 = (bf16[1,8,64,256]{3,2,1,0:T(8,128)(2,1)S(1)}, bf16[1,8,64,256]{3,2,1,0:T(8,128)(2,1)S(1)}, u32[]{:S(2)}, u32[]{:S(2)}) collective-permute-start(bf16[1,8,64,256]{3,2,1,0:T(8,128)(2,1)S(1)} %get-tuple-element.29), channel_id=1, source_target_pairs={{1,0},{2,1},{3,2},{4,3},{5,4},{6,5},{7,6},{8,7},{9,8},{10,9},{11,1... | collective-permute-start | bytes 786440 | tf_op jit(solution)/shard_map/ppermute | solution.py:201
  112.3 4.1 %collective-permute-start.23 = (bf16[1,8,64,256]{3,2,1,0:T(8,128)(2,1)S(1)}, bf16[1,8,64,256]{3,2,1,0:T(8,128)(2,1)S(1)}, u32[]{:S(2)}, u32[]{:S(2)}) collective-permute-start(bf16[1,8,64,256]{3,2,1,0:T(8,128)(2,1)S(1)} %get-tuple-element.30), channel_id=1, source_target_pairs={{1,0},{2,1},{3,2},{4,3},{5,4},{6,5},{7,6},{8,7},{9,8},{10,9},{11,1... | collective-permute-start | bytes 786440 | tf_op jit(solution)/shard_map/ppermute | solution.py:201
  113.6 4.7 %collective-permute-start.22 = (bf16[1,8,64,256]{3,2,1,0:T(8,128)(2,1)S(1)}, bf16[1,8,64,256]{3,2,1,0:T(8,128)(2,1)S(1)}, u32[]{:S(2)}, u32[]{:S(2)}) collective-permute-start(bf16[1,8,64,256]{3,2,1,0:T(8,128)(2,1)S(1)} %get-tuple-element.31), channel_id=1, source_target_pairs={{1,0},{2,1},{3,2},{4,3},{5,4},{6,5},{7,6},{8,7},{9,8},{10,9},{11,1... | collective-permute-start | bytes 786440 | tf_op jit(solution)/shard_map/ppermute | solution.py:201
  129.7 9.9 %collective-permute-start.28 = (f32[128,256]{1,0:T(8,128)S(1)}, f32[128,256]{1,0:T(8,128)S(1)}, u32[]{:S(2)}, u32[]{:S(2)}) collective-permute-start(f32[128,256]{1,0:T(8,128)S(1)} %fusion.2), channel_id=1, source_target_pairs={{1,0},{2,1},{3,2},{4,3},{5,4},{6,5},{7,6},{8,7},{9,8},{10,9},{11,1... | collective-permute-start | bytes 393224 | tf_op jit(solution)/shard_map/ppermute | solution.py:228
  131.0 9.6 %collective-permute-start.24 = (f32[128,256]{1,0:T(8,128)S(1)}, f32[128,256]{1,0:T(8,128)S(1)}, u32[]{:S(2)}, u32[]{:S(2)}) collective-permute-start(f32[128,256]{1,0:T(8,128)S(1)} %fusion.2), channel_id=1, source_target_pairs={{0,1},{1,2},{2,3},{3,4},{4,5},{5,6},{6,7},{7,8},{8,9},{9,10},{10,1... | collective-permute-start | bytes 393224 | tf_op jit(solution)/shard_map/ppermute | solution.py:227
  140.6 14.5 %collective-permute-start.25 = (f32[128,256]{1,0:T(8,128)S(1)}, f32[128,256]{1,0:T(8,128)S(1)}, u32[]{:S(2)}, u32[]{:S(2)}) collective-permute-start(f32[128,256]{1,0:T(8,128)S(1)} %get-tuple-element.47), channel_id=1, source_target_pairs={{0,2},{1,3},{2,4},{3,5},{4,6},{5,7},{6,8},{7,9},{8,10},{9,11},{10,... | collective-permute-start | bytes 393224 | tf_op jit(solution)/shard_map/ppermute | solution.py:227
  153.8 8.3 %collective-permute-start.29 = (f32[128,256]{1,0:T(8,128)S(1)}, f32[128,256]{1,0:T(8,128)S(1)}, u32[]{:S(2)}, u32[]{:S(2)}) collective-permute-start(f32[128,256]{1,0:T(8,128)S(1)} %get-tuple-element.48), channel_id=1, source_target_pairs={{2,0},{3,1},{4,2},{5,3},{6,4},{7,5},{8,6},{9,7},{10,8},{11,9},{12,... | collective-permute-start | bytes 393224 | tf_op jit(solution)/shard_map/ppermute | solution.py:228
  155.2 9.4 %collective-permute-start.26 = (f32[128,256]{1,0:T(8,128)S(1)}, f32[128,256]{1,0:T(8,128)S(1)}, u32[]{:S(2)}, u32[]{:S(2)}) collective-permute-start(f32[128,256]{1,0:T(8,128)S(1)} %multiply_add_fusion.4), channel_id=1, source_target_pairs={{0,4},{1,5},{2,6},{3,7},{4,8},{5,9},{6,10},{7,11},{8,12},{9,13},{1... | collective-permute-start | bytes 393224 | tf_op jit(solution)/shard_map/ppermute | solution.py:227
  162.1 7.9 %collective-permute-start.30 = (f32[128,256]{1,0:T(8,128)S(1)}, f32[128,256]{1,0:T(8,128)S(1)}, u32[]{:S(2)}, u32[]{:S(2)}) collective-permute-start(f32[128,256]{1,0:T(8,128)S(1)} %multiply_add_fusion.1), channel_id=1, source_target_pairs={{4,0},{5,1},{6,2},{7,3},{8,4},{9,5},{10,6},{11,7},{12,8},{13,9},{1... | collective-permute-start | bytes 393224 | tf_op jit(solution)/shard_map/ppermute | solution.py:228
  164.6 10.9 %collective-permute-start.27 = (f32[128,256]{1,0:T(8,128)S(1)}, f32[128,256]{1,0:T(8,128)S(1)}, u32[]{:S(2)}, u32[]{:S(2)}) collective-permute-start(f32[128,256]{1,0:T(8,128)S(1)} %multiply_add_fusion.3), channel_id=1, source_target_pairs={{0,8},{1,9},{2,10},{3,11},{4,12},{5,13},{6,14},{7,15},{16,24},{17,... | collective-permute-start | bytes 393224 | tf_op jit(solution)/shard_map/ppermute | solution.py:227
  170.0 9.2 %collective-permute-start.31 = (f32[128,256]{1,0:T(8,128)S(1)}, f32[128,256]{1,0:T(8,128)S(1)}, u32[]{:S(2)}, u32[]{:S(2)}) collective-permute-start(f32[128,256]{1,0:T(8,128)S(1)} %multiply_add_fusion), channel_id=1, source_target_pairs={{8,0},{9,1},{10,2},{11,3},{12,4},{13,5},{14,6},{15,7},{24,16},{25,... | collective-permute-start | bytes 393224 | tf_op jit(solution)/shard_map/ppermute | solution.py:228
  196.8 1.3 copy-start.4
  199.0 4.3 %collective-permute-start.36 = (f32[128,128]{1,0:T(8,128)S(1)}, f32[128,128]{1,0:T(8,128)S(1)}, u32[]{:S(2)}, u32[]{:S(2)}) collective-permute-start(f32[128,128]{1,0:T(8,128)S(1)} %fusion.20), channel_id=1, source_target_pairs={{1,0},{2,1},{3,2},{4,3},{5,4},{6,5},{7,6},{8,7},{9,8},{10,9},{11,1... | collective-permute-start | bytes 196616 | tf_op jit(solution)/shard_map/ppermute | solution.py:228
  200.3 3.9 %collective-permute-start.32 = (f32[128,128]{1,0:T(8,128)S(1)}, f32[128,128]{1,0:T(8,128)S(1)}, u32[]{:S(2)}, u32[]{:S(2)}) collective-permute-start(f32[128,128]{1,0:T(8,128)S(1)} %fusion.20), channel_id=1, source_target_pairs={{0,1},{1,2},{2,3},{3,4},{4,5},{5,6},{6,7},{7,8},{8,9},{9,10},{10,1... | collective-permute-start | bytes 196616 | tf_op jit(solution)/shard_map/ppermute | solution.py:227
  204.3 6.5 %collective-permute-start.33 = (f32[128,128]{1,0:T(8,128)S(1)}, f32[128,128]{1,0:T(8,128)S(1)}, u32[]{:S(2)}, u32[]{:S(2)}) collective-permute-start(f32[128,128]{1,0:T(8,128)S(1)} %get-tuple-element.49), channel_id=1, source_target_pairs={{0,2},{1,3},{2,4},{3,5},{4,6},{5,7},{6,8},{7,9},{8,10},{9,11},{10,... | collective-permute-start | bytes 196616 | tf_op jit(solution)/shard_map/ppermute | solution.py:227
  208.9 7.4 %collective-permute-start.37 = (f32[128,128]{1,0:T(8,128)S(1)}, f32[128,128]{1,0:T(8,128)S(1)}, u32[]{:S(2)}, u32[]{:S(2)}) collective-permute-start(f32[128,128]{1,0:T(8,128)S(1)} %get-tuple-element.50), channel_id=1, source_target_pairs={{2,0},{3,1},{4,2},{5,3},{6,4},{7,5},{8,6},{9,7},{10,8},{11,9},{12,... | collective-permute-start | bytes 196616 | tf_op jit(solution)/shard_map/ppermute | solution.py:228
  210.8 7.4 %collective-permute-start.34 = (f32[128,128]{1,0:T(8,128)S(1)}, f32[128,128]{1,0:T(8,128)S(1)}, u32[]{:S(2)}, u32[]{:S(2)}) collective-permute-start(f32[128,128]{1,0:T(8,128)S(1)} %multiply_add_fusion.10), channel_id=1, source_target_pairs={{0,4},{1,5},{2,6},{3,7},{4,8},{5,9},{6,10},{7,11},{8,12},{9,13},{1... | collective-permute-start | bytes 196616 | tf_op jit(solution)/shard_map/ppermute | solution.py:227
  216.3 7.9 %collective-permute-start.38 = (f32[128,128]{1,0:T(8,128)S(1)}, f32[128,128]{1,0:T(8,128)S(1)}, u32[]{:S(2)}, u32[]{:S(2)}) collective-permute-start(f32[128,128]{1,0:T(8,128)S(1)} %multiply_add_fusion.7), channel_id=1, source_target_pairs={{4,0},{5,1},{6,2},{7,3},{8,4},{9,5},{10,6},{11,7},{12,8},{13,9},{1... | collective-permute-start | bytes 196616 | tf_op jit(solution)/shard_map/ppermute | solution.py:228
  218.2 7.9 %collective-permute-start.35 = (f32[128,128]{1,0:T(8,128)S(1)}, f32[128,128]{1,0:T(8,128)S(1)}, u32[]{:S(2)}, u32[]{:S(2)}) collective-permute-start(f32[128,128]{1,0:T(8,128)S(1)} %multiply_add_fusion.9), channel_id=1, source_target_pairs={{0,8},{1,9},{2,10},{3,11},{4,12},{5,13},{6,14},{7,15},{16,24},{17,... | collective-permute-start | bytes 196616 | tf_op jit(solution)/shard_map/ppermute | solution.py:227
  224.3 7.8 %collective-permute-start.39 = (f32[128,128]{1,0:T(8,128)S(1)}, f32[128,128]{1,0:T(8,128)S(1)}, u32[]{:S(2)}, u32[]{:S(2)}) collective-permute-start(f32[128,128]{1,0:T(8,128)S(1)} %multiply_add_fusion.6), channel_id=1, source_target_pairs={{8,0},{9,1},{10,2},{11,3},{12,4},{13,5},{14,6},{15,7},{24,16},{25,... | collective-permute-start | bytes 196616 | tf_op jit(solution)/shard_map/ppermute | solution.py:228

commit v10 on v8

--- a/solution.py
+++ b/solution.py
@@ -39,7 +39,7 @@
         work_ref[...] = jnp.where(rows == k, scaled, updated)
         return carry
 
-    lax.fori_loop(0, n, step, 0)
+    lax.fori_loop(0, n, step, 0, unroll=4)
     out_ref[...] = work_ref[:, n:]
 
 

time: 248 us -> 249 us (level)
  no operation moved by 1% of the time
where the time goes in v10:
time: 249 us; the launch traced here: 248 us
  starting transfers between devices  120 us (48%)
  Pallas kernels  68.4 us (27%)
  waiting for transfers between devices  27.3 us (11%)
  other arithmetic  11.3 us (5%)
  between operations  11.1 us (4%)
  local copies, waits for them, and re-layouts  6.08 us (2%)
  matrix products  3.8 us (2%)
    ppermute x4, starting transfers between devices, rimmed(): from_below = lax.ppermute(high, 'gz', forward)  52.9 us
    ppermute x8, starting transfers between devices, domain_total(): from_low = lax.ppermute(forward, 'gz', ahead)  51.1 us
    pallas_call x2, Pallas kernels, lower_inverse(): pl.pallas_call(_lower_inverse_kernel, out_shape=jax.ShapeDtypeStruct((n,...  34.3 us
    pallas_call x4, Pallas kernels, chebyshev_step(): pl.pallas_call(functools.partial(_step_kernel, first), out_shape=(piece,...  34 us
    ppermute x8, starting transfers between devices, domain_total(): from_high = lax.ppermute(backward, 'gz', behind)  10.3 us
    ppermute x8, waiting for transfers between devices, domain_total(): from_high = lax.ppermute(backward, 'gz', behind)  10.1 us
    ppermute x4, waiting for transfers between devices, rimmed(): from_above = lax.ppermute(low, 'gz', backward)  9.74 us
    mul x8, other arithmetic, rimmed(): return (from_below * bf_below, from_above * bf_above)  7.64 us
  transfers between devices with their start and end apart: 24, of which 17 were waited for; matrix products, arithmetic and copies ran while one was open for 2% of the time, Pallas kernels for 0%

profile of v10, /device:TPU:0, one launch (start us, length us, event | category | flops | bytes accessed | tf_op | source)
XLA Modules:
  0.0 247.6 jit_solution(13326735149332821358)
XLA Ops:
  0.0 1.5 fusion.11
  1.5 1.3 collective-permute-start.1
  2.8 3.1 %collective-permute-start = (bf16[3,8,64,256]{3,2,1,0:T(8,128)(2,1)S(1)}, bf16[3,8,64,256]{3,2,1,0:T(8,128)(2,1)S(1)}, u32[]{:S(2)}, u32[]{:S(2)}) collective-permute-start(bf16[3,8,64,256]{3,2,1,0:T(8,128)(2,1)S(1)} %get-tuple-element.22.high_ref), channel_id=1, source_target_pairs={{0,1},{1,2},{2,3},{3,4},{4,5},{5,6},{6,7},{7,8},{8,9},{9,10},{10,1... | collective-permute-start | bytes 2359304 | tf_op jit(solution)/shard_map/ppermute | solution.py:197
  6.0 0.7 fusion.12
  9.3 1.0 broadcast_multiply_fusion.3.above_ref
  10.2 0.9 broadcast_multiply_fusion.7.below_ref
  11.2 1.6 broadcast_in_dim.8.low_pot_ref.high_pot_ref
  12.8 8.3 %shard_map.37 = (bf16[3,8,64,256]{3,2,1,0:T(8,128)(2,1)}, bf16[3,8,64,256]{3,2,1,0:T(8,128)(2,1)}) custom-call(bf16[3,8,64,256]{3,2,1,0:T(8,128)(2,1)} %broadcast_multiply_fusion.7.below_ref, bf16[3,8,64,256]{3,2,1,0:T(8,128)(2,1)} %copy-done, bf16[3,8,64,256]{3,2,1,0:T(8,128)(2,1)} %copy-done.1, bf16[3,8,64,256]{3,2,1,0:T(8,128)(2,1)} %broadcast_multiply_fusion.3.above_ref, ...), custom_call_target="tpu_custom_call" | custom-call | tf_op jit(solution)/shard_map/pallas_call | solution.py:111
  21.1 16.5 %collective-permute-start.2 = (bf16[3,8,64,256]{3,2,1,0:T(8,128)(2,1)}, bf16[3,8,64,256]{3,2,1,0:T(8,128)(2,1)S(1)}, u32[]{:S(2)}, u32[]{:S(2)}) collective-permute-start(bf16[3,8,64,256]{3,2,1,0:T(8,128)(2,1)} %get-tuple-element.13.high_ref.older_high_ref), channel_id=1, source_target_pairs={{0,1},{1,2},{2,3},{3,4},{4,5},{5,6},{6,7},{7,8},{8,9},{9,10},{10,1... | collective-permute-start | bytes 2359304 | tf_op jit(solution)/shard_map/ppermute | solution.py:197
  37.6 1.3 collective-permute-start.3
  38.9 0.8 collective-permute-done.2
  39.7 0.9 broadcast_multiply_fusion.6.below_ref
  40.6 3.3 %collective-permute-done.3 = bf16[3,8,64,256]{3,2,1,0:T(8,128)(2,1)S(1)} collective-permute-done((bf16[3,8,64,256]{3,2,1,0:T(8,128)(2,1)}, bf16[3,8,64,256]{3,2,1,0:T(8,128)(2,1)S(1)}, u32[]{:S(2)}, u32[]{:S(2)}) %collective-permute-start.3) | collective-permute-done | bytes 786464 | tf_op jit(solution)/shard_map/ppermute | solution.py:198
  43.9 1.0 broadcast_multiply_fusion.2.above_ref
  44.9 8.6 %shard_map.38 = (bf16[3,8,64,256]{3,2,1,0:T(8,128)(2,1)}, bf16[3,8,64,256]{3,2,1,0:T(8,128)(2,1)}) custom-call(bf16[3,8,64,256]{3,2,1,0:T(8,128)(2,1)} %broadcast_multiply_fusion.6.below_ref, bf16[3,8,64,256]{3,2,1,0:T(8,128)(2,1)} %get-tuple-element.14.low_ref.older_low_ref, bf16[3,8,64,256]{3,2,1,0:T(8,128)(2,1)} %get-tuple-element.13.high_ref.older_high_ref, ...), custom_call_target="tpu_custom_call" | custom-call | tf_op jit(solution)/shard_map/pallas_call | solution.py:111
  53.4 16.6 %collective-permute-start.4 = (bf16[3,8,64,256]{3,2,1,0:T(8,128)(2,1)}, bf16[3,8,64,256]{3,2,1,0:T(8,128)(2,1)S(1)}, u32[]{:S(2)}, u32[]{:S(2)}) collective-permute-start(bf16[3,8,64,256]{3,2,1,0:T(8,128)(2,1)} %get-tuple-element.15.high_ref.older_high_ref), channel_id=1, source_target_pairs={{0,1},{1,2},{2,3},{3,4},{4,5},{5,6},{6,7},{7,8},{8,9},{9,10},{10,1... | collective-permute-start | bytes 2359304 | tf_op jit(solution)/shard_map/ppermute | solution.py:197
  70.1 1.3 collective-permute-start.5
  71.4 0.8 collective-permute-done.4
  72.2 1.0 broadcast_multiply_fusion.5.below_ref
  73.1 3.2 %collective-permute-done.5 = bf16[3,8,64,256]{3,2,1,0:T(8,128)(2,1)S(1)} collective-permute-done((bf16[3,8,64,256]{3,2,1,0:T(8,128)(2,1)}, bf16[3,8,64,256]{3,2,1,0:T(8,128)(2,1)S(1)}, u32[]{:S(2)}, u32[]{:S(2)}) %collective-permute-start.5) | collective-permute-done | bytes 786464 | tf_op jit(solution)/shard_map/ppermute | solution.py:198
  76.3 1.0 broadcast_multiply_fusion.1.above_ref
  77.3 8.6 %shard_map.39 = (bf16[3,8,64,256]{3,2,1,0:T(8,128)(2,1)}, bf16[3,8,64,256]{3,2,1,0:T(8,128)(2,1)}) custom-call(bf16[3,8,64,256]{3,2,1,0:T(8,128)(2,1)} %broadcast_multiply_fusion.5.below_ref, bf16[3,8,64,256]{3,2,1,0:T(8,128)(2,1)} %get-tuple-element.16.low_ref.older_low_ref, bf16[3,8,64,256]{3,2,1,0:T(8,128)(2,1)} %get-tuple-element.15.high_ref.older_high_ref, ...), custom_call_target="tpu_custom_call" | custom-call | tf_op jit(solution)/shard_map/pallas_call | solution.py:111
  85.8 16.7 %collective-permute-start.6 = (bf16[3,8,64,256]{3,2,1,0:T(8,128)(2,1)}, bf16[3,8,64,256]{3,2,1,0:T(8,128)(2,1)S(1)}, u32[]{:S(2)}, u32[]{:S(2)}) collective-permute-start(bf16[3,8,64,256]{3,2,1,0:T(8,128)(2,1)} %get-tuple-element.17.high_ref), channel_id=1, source_target_pairs={{0,1},{1,2},{2,3},{3,4},{4,5},{5,6},{6,7},{7,8},{8,9},{9,10},{10,1... | collective-permute-start | bytes 2359304 | tf_op jit(solution)/shard_map/ppermute | solution.py:197
  102.5 1.5 collective-permute-start.7
  104.0 0.6 collective-permute-done.6
  104.6 1.0 broadcast_multiply_fusion.4.below_ref
  105.5 3.2 %collective-permute-done.7 = bf16[3,8,64,256]{3,2,1,0:T(8,128)(2,1)S(1)} collective-permute-done((bf16[3,8,64,256]{3,2,1,0:T(8,128)(2,1)}, bf16[3,8,64,256]{3,2,1,0:T(8,128)(2,1)S(1)}, u32[]{:S(2)}, u32[]{:S(2)}) %collective-permute-start.7) | collective-permute-done | bytes 786464 | tf_op jit(solution)/shard_map/ppermute | solution.py:198
  108.8 1.0 broadcast_multiply_fusion.above_ref
  109.7 8.6 %shard_map.40 = (bf16[3,8,64,256]{3,2,1,0:T(8,128)(2,1)}, bf16[3,8,64,256]{3,2,1,0:T(8,128)(2,1)}) custom-call(bf16[3,8,64,256]{3,2,1,0:T(8,128)(2,1)} %broadcast_multiply_fusion.4.below_ref, bf16[3,8,64,256]{3,2,1,0:T(8,128)(2,1)} %get-tuple-element.18.low_ref, bf16[3,8,64,256]{3,2,1,0:T(8,128)(2,1)} %get-tuple-element.17.high_ref, ...), custom_call_target="tpu_custom_call" | custom-call | tf_op jit(solution)/shard_map/pallas_call | solution.py:111
  118.3 1.5 pad_maximum_fusion
  120.2 1.3 collective-permute-start.12
  121.5 17.3 %collective-permute-start.8 = (f32[128,256]{1,0:T(8,128)S(1)}, f32[128,256]{1,0:T(8,128)S(1)}, u32[]{:S(2)}, u32[]{:S(2)}) collective-permute-start(f32[128,256]{1,0:T(8,128)S(1)} %fusion.2), channel_id=1, source_target_pairs={{0,1},{1,2},{2,3},{3,4},{4,5},{5,6},{6,7},{7,8},{8,9},{9,10},{10,1... | collective-permute-start | bytes 393224 | tf_op jit(solution)/shard_map/ppermute | solution.py:223
  138.8 0.9 collective-permute-done.8
  139.8 7.6 %collective-permute-start.9 = (f32[128,256]{1,0:T(8,128)S(1)}, f32[128,256]{1,0:T(8,128)S(1)}, u32[]{:S(2)}, u32[]{:S(2)}) collective-permute-start(f32[128,256]{1,0:T(8,128)S(1)} %get-tuple-element.23), channel_id=1, source_target_pairs={{0,2},{1,3},{2,4},{3,5},{4,6},{5,7},{6,8},{7,9},{8,10},{9,11},{10,... | collective-permute-start | bytes 393224 | tf_op jit(solution)/shard_map/ppermute | solution.py:223
  152.4 1.3 collective-permute-start.13
  153.7 5.3 %collective-permute-start.10 = (f32[128,256]{1,0:T(8,128)S(1)}, f32[128,256]{1,0:T(8,128)S(1)}, u32[]{:S(2)}, u32[]{:S(2)}) collective-permute-start(f32[128,256]{1,0:T(8,128)S(1)} %multiply_add_fusion.4), channel_id=1, source_target_pairs={{0,4},{1,5},{2,6},{3,7},{4,8},{5,9},{6,10},{7,11},{8,12},{9,13},{1... | collective-permute-start | bytes 393224 | tf_op jit(solution)/shard_map/ppermute | solution.py:223
  159.3 1.3 collective-permute-start.14
  160.6 1.3 collective-permute-done.10
  161.9 3.6 %collective-permute-start.11 = (f32[128,256]{1,0:T(8,128)S(1)}, f32[128,256]{1,0:T(8,128)S(1)}, u32[]{:S(2)}, u32[]{:S(2)}) collective-permute-start(f32[128,256]{1,0:T(8,128)S(1)} %multiply_add_fusion.3), channel_id=1, source_target_pairs={{0,8},{1,9},{2,10},{3,11},{4,12},{5,13},{6,14},{7,15},{16,24},{17,... | collective-permute-start | bytes 393224 | tf_op jit(solution)/shard_map/ppermute | solution.py:223
  165.6 0.6 collective-permute-done.14
  166.2 1.3 collective-permute-start.15
  170.0 1.2 fusion.10
  171.9 3.2 %collective-permute-done.15 = f32[128,256]{1,0:T(8,128)S(1)} collective-permute-done((f32[128,256]{1,0:T(8,128)S(1)}, f32[128,256]{1,0:T(8,128)S(1)}, u32[]{:S(2)}, u32[]{:S(2)}) %collective-permute-start.15) | collective-permute-done | bytes 131104 | tf_op jit(solution)/shard_map/ppermute | solution.py:224
  175.1 0.6 slice.25.gram_ref
  175.8 17.2 %shard_map.41 = f32[128,128]{1,0:T(8,128)} custom-call(f32[128,128]{1,0:T(8,128)} %slice.25.gram_ref), custom_call_target="tpu_custom_call" | custom-call | tf_op jit(solution)/shard_map/pallas_call | solution.py:48
  192.9 1.3 convolution_convert_fusion.1
  194.2 0.5 fusion
  195.1 1.3 collective-permute-start.20
  196.4 3.0 %collective-permute-start.16 = (f32[128,128]{1,0:T(8,128)S(1)}, f32[128,128]{1,0:T(8,128)S(1)}, u32[]{:S(2)}, u32[]{:S(2)}) collective-permute-start(f32[128,128]{1,0:T(8,128)S(1)} %fusion.13), channel_id=1, source_target_pairs={{0,1},{1,2},{2,3},{3,4},{4,5},{5,6},{6,7},{7,8},{8,9},{9,10},{10,1... | collective-permute-start | bytes 196616 | tf_op jit(solution)/shard_map/ppermute | solution.py:223
  199.5 0.9 collective-permute-done.16
  200.4 5.7 %collective-permute-start.17 = (f32[128,128]{1,0:T(8,128)S(1)}, f32[128,128]{1,0:T(8,128)S(1)}, u32[]{:S(2)}, u32[]{:S(2)}) collective-permute-start(f32[128,128]{1,0:T(8,128)S(1)} %get-tuple-element.25), channel_id=1, source_target_pairs={{0,2},{1,3},{2,4},{3,5},{4,6},{5,7},{6,8},{7,9},{8,10},{9,11},{10,... | collective-permute-start | bytes 196616 | tf_op jit(solution)/shard_map/ppermute | solution.py:223
  206.1 1.3 collective-permute-start.21
  207.4 1.2 collective-permute-done.17
  208.6 4.4 %collective-permute-start.18 = (f32[128,128]{1,0:T(8,128)S(1)}, f32[128,128]{1,0:T(8,128)S(1)}, u32[]{:S(2)}, u32[]{:S(2)}) collective-permute-start(f32[128,128]{1,0:T(8,128)S(1)} %multiply_add_fusion.10), channel_id=1, source_target_pairs={{0,4},{1,5},{2,6},{3,7},{4,8},{5,9},{6,10},{7,11},{8,12},{9,13},{1... | collective-permute-start | bytes 196616 | tf_op jit(solution)/shard_map/ppermute | solution.py:223
  213.0 1.3 collective-permute-start.22
  214.3 0.6 collective-permute-done.18
  214.9 4.2 %collective-permute-start.19 = (f32[128,128]{1,0:T(8,128)S(1)}, f32[128,128]{1,0:T(8,128)S(1)}, u32[]{:S(2)}, u32[]{:S(2)}) collective-permute-start(f32[128,128]{1,0:T(8,128)S(1)} %multiply_add_fusion.9), channel_id=1, source_target_pairs={{0,8},{1,9},{2,10},{3,11},{4,12},{5,13},{6,14},{7,15},{16,24},{17,... | collective-permute-start | bytes 196616 | tf_op jit(solution)/shard_map/ppermute | solution.py:223
  219.2 1.3 collective-permute-start.23
  220.5 0.5 collective-permute-done.19
  221.0 6.0 %collective-permute-done.23 = f32[128,128]{1,0:T(8,128)S(1)} collective-permute-done((f32[128,128]{1,0:T(8,128)S(1)}, f32[128,128]{1,0:T(8,128)S(1)}, u32[]{:S(2)}, u32[]{:S(2)}) %collective-permute-start.23) | collective-permute-done | bytes 65568 | tf_op jit(solution)/shard_map/ppermute | solution.py:224
  226.9 0.7 subtract_divide_fusion.1.gram_ref
  227.6 17.2 %shard_map.42 = f32[128,128]{1,0:T(8,128)} custom-call(f32[128,128]{1,0:T(8,128)} %subtract_divide_fusion.1.gram_ref), custom_call_target="tpu_custom_call" | custom-call | tf_op jit(solution)/shard_map/pallas_call | solution.py:48
  244.8 1.2 convolution_convert_fusion
  246.1 1.6 copy.5
  (34 shorter events, 1.5 us)
Async XLA Ops:
  0.0 5.9 %copy-start.3 = (s32[16]{0:T(128)S(1)}, s32[16]{0:T(128)}, u32[]{:S(2)}) copy-start(s32[16]{0:T(128)} %param.5) | copy-start | bytes 196
  0.0 9.2 %copy-start.4 = (f32[6,512]{1,0:T(8,128)S(1)}, f32[6,512]{1,0:T(8,128)}, u32[]{:S(2)}) copy-start(f32[6,512]{1,0:T(8,128)} %param.4) | copy-start | bytes 36868
  1.5 9.7 %copy-start = (bf16[3,8,64,256]{3,2,1,0:T(8,128)(2,1)}, bf16[3,8,64,256]{3,2,1,0:T(8,128)(2,1)S(1)}, u32[]{:S(2)}) copy-start(bf16[3,8,64,256]{3,2,1,0:T(8,128)(2,1)S(1)} %get-tuple-element.21.low_ref) | copy-start | bytes 2359300
  1.5 9.6 %copy-start.1 = (bf16[3,8,64,256]{3,2,1,0:T(8,128)(2,1)}, bf16[3,8,64,256]{3,2,1,0:T(8,128)(2,1)S(1)}, u32[]{:S(2)}) copy-start(bf16[3,8,64,256]{3,2,1,0:T(8,128)(2,1)S(1)} %get-tuple-element.22.high_ref) | copy-start | bytes 2359300
  1.5 7.7 %collective-permute-start.1 = (bf16[3,8,64,256]{3,2,1,0:T(8,128)(2,1)S(1)}, bf16[3,8,64,256]{3,2,1,0:T(8,128)(2,1)S(1)}, u32[]{:S(2)}, u32[]{:S(2)}) collective-permute-start(bf16[3,8,64,256]{3,2,1,0:T(8,128)(2,1)S(1)} %get-tuple-element.21.low_ref), channel_id=1, source_target_pairs={{1,0},{2,1},{3,2},{4,3},{5,4},{6,5},{7,6},{8,7},{9,8},{10,9},{11,1... | collective-permute-start | bytes 2359304 | tf_op jit(solution)/shard_map/ppermute | solution.py:198
  2.8 7.4 %collective-permute-start = (bf16[3,8,64,256]{3,2,1,0:T(8,128)(2,1)S(1)}, bf16[3,8,64,256]{3,2,1,0:T(8,128)(2,1)S(1)}, u32[]{:S(2)}, u32[]{:S(2)}) collective-permute-start(bf16[3,8,64,256]{3,2,1,0:T(8,128)(2,1)S(1)} %get-tuple-element.22.high_ref), channel_id=1, source_target_pairs={{0,1},{1,2},{2,3},{3,4},{4,5},{5,6},{6,7},{7,8},{8,9},{9,10},{10,1... | collective-permute-start | bytes 2359304 | tf_op jit(solution)/shard_map/ppermute | solution.py:197
  21.1 18.6 %collective-permute-start.2 = (bf16[3,8,64,256]{3,2,1,0:T(8,128)(2,1)}, bf16[3,8,64,256]{3,2,1,0:T(8,128)(2,1)S(1)}, u32[]{:S(2)}, u32[]{:S(2)}) collective-permute-start(bf16[3,8,64,256]{3,2,1,0:T(8,128)(2,1)} %get-tuple-element.13.high_ref.older_high_ref), channel_id=1, source_target_pairs={{0,1},{1,2},{2,3},{3,4},{4,5},{5,6},{6,7},{7,8},{8,9},{9,10},{10,1... | collective-permute-start | bytes 2359304 | tf_op jit(solution)/shard_map/ppermute | solution.py:197
  37.6 6.3 %collective-permute-start.3 = (bf16[3,8,64,256]{3,2,1,0:T(8,128)(2,1)}, bf16[3,8,64,256]{3,2,1,0:T(8,128)(2,1)S(1)}, u32[]{:S(2)}, u32[]{:S(2)}) collective-permute-start(bf16[3,8,64,256]{3,2,1,0:T(8,128)(2,1)} %get-tuple-element.14.low_ref.older_low_ref), channel_id=1, source_target_pairs={{1,0},{2,1},{3,2},{4,3},{5,4},{6,5},{7,6},{8,7},{9,8},{10,9},{11,1... | collective-permute-start | bytes 2359304 | tf_op jit(solution)/shard_map/ppermute | solution.py:198
  53.4 18.7 %collective-permute-start.4 = (bf16[3,8,64,256]{3,2,1,0:T(8,128)(2,1)}, bf16[3,8,64,256]{3,2,1,0:T(8,128)(2,1)S(1)}, u32[]{:S(2)}, u32[]{:S(2)}) collective-permute-start(bf16[3,8,64,256]{3,2,1,0:T(8,128)(2,1)} %get-tuple-element.15.high_ref.older_high_ref), channel_id=1, source_target_pairs={{0,1},{1,2},{2,3},{3,4},{4,5},{5,6},{6,7},{7,8},{8,9},{9,10},{10,1... | collective-permute-start | bytes 2359304 | tf_op jit(solution)/shard_map/ppermute | solution.py:197
  70.1 6.2 %collective-permute-start.5 = (bf16[3,8,64,256]{3,2,1,0:T(8,128)(2,1)}, bf16[3,8,64,256]{3,2,1,0:T(8,128)(2,1)S(1)}, u32[]{:S(2)}, u32[]{:S(2)}) collective-permute-start(bf16[3,8,64,256]{3,2,1,0:T(8,128)(2,1)} %get-tuple-element.16.low_ref.older_low_ref), channel_id=1, source_target_pairs={{1,0},{2,1},{3,2},{4,3},{5,4},{6,5},{7,6},{8,7},{9,8},{10,9},{11,1... | collective-permute-start | bytes 2359304 | tf_op jit(solution)/shard_map/ppermute | solution.py:198
  85.8 18.7 %collective-permute-start.6 = (bf16[3,8,64,256]{3,2,1,0:T(8,128)(2,1)}, bf16[3,8,64,256]{3,2,1,0:T(8,128)(2,1)S(1)}, u32[]{:S(2)}, u32[]{:S(2)}) collective-permute-start(bf16[3,8,64,256]{3,2,1,0:T(8,128)(2,1)} %get-tuple-element.17.high_ref), channel_id=1, source_target_pairs={{0,1},{1,2},{2,3},{3,4},{4,5},{5,6},{6,7},{7,8},{8,9},{9,10},{10,1... | collective-permute-start | bytes 2359304 | tf_op jit(solution)/shard_map/ppermute | solution.py:197
  102.5 6.2 %collective-permute-start.7 = (bf16[3,8,64,256]{3,2,1,0:T(8,128)(2,1)}, bf16[3,8,64,256]{3,2,1,0:T(8,128)(2,1)S(1)}, u32[]{:S(2)}, u32[]{:S(2)}) collective-permute-start(bf16[3,8,64,256]{3,2,1,0:T(8,128)(2,1)} %get-tuple-element.18.low_ref), channel_id=1, source_target_pairs={{1,0},{2,1},{3,2},{4,3},{5,4},{6,5},{7,6},{8,7},{9,8},{10,9},{11,1... | collective-permute-start | bytes 2359304 | tf_op jit(solution)/shard_map/ppermute | solution.py:198
  120.2 18.6 %collective-permute-start.12 = (f32[128,256]{1,0:T(8,128)S(1)}, f32[128,256]{1,0:T(8,128)S(1)}, u32[]{:S(2)}, u32[]{:S(2)}) collective-permute-start(f32[128,256]{1,0:T(8,128)S(1)} %fusion.2), channel_id=1, source_target_pairs={{1,0},{2,1},{3,2},{4,3},{5,4},{6,5},{7,6},{8,7},{9,8},{10,9},{11,1... | collective-permute-start | bytes 393224 | tf_op jit(solution)/shard_map/ppermute | solution.py:224
  121.5 18.2 %collective-permute-start.8 = (f32[128,256]{1,0:T(8,128)S(1)}, f32[128,256]{1,0:T(8,128)S(1)}, u32[]{:S(2)}, u32[]{:S(2)}) collective-permute-start(f32[128,256]{1,0:T(8,128)S(1)} %fusion.2), channel_id=1, source_target_pairs={{0,1},{1,2},{2,3},{3,4},{4,5},{5,6},{6,7},{7,8},{8,9},{9,10},{10,1... | collective-permute-start | bytes 393224 | tf_op jit(solution)/shard_map/ppermute | solution.py:223
  139.8 13.9 %collective-permute-start.9 = (f32[128,256]{1,0:T(8,128)S(1)}, f32[128,256]{1,0:T(8,128)S(1)}, u32[]{:S(2)}, u32[]{:S(2)}) collective-permute-start(f32[128,256]{1,0:T(8,128)S(1)} %get-tuple-element.23), channel_id=1, source_target_pairs={{0,2},{1,3},{2,4},{3,5},{4,6},{5,7},{6,8},{7,9},{8,10},{9,11},{10,... | collective-permute-start | bytes 393224 | tf_op jit(solution)/shard_map/ppermute | solution.py:223
  152.4 6.9 %collective-permute-start.13 = (f32[128,256]{1,0:T(8,128)S(1)}, f32[128,256]{1,0:T(8,128)S(1)}, u32[]{:S(2)}, u32[]{:S(2)}) collective-permute-start(f32[128,256]{1,0:T(8,128)S(1)} %get-tuple-element.24), channel_id=1, source_target_pairs={{2,0},{3,1},{4,2},{5,3},{6,4},{7,5},{8,6},{9,7},{10,8},{11,9},{12,... | collective-permute-start | bytes 393224 | tf_op jit(solution)/shard_map/ppermute | solution.py:224
  153.7 8.2 %collective-permute-start.10 = (f32[128,256]{1,0:T(8,128)S(1)}, f32[128,256]{1,0:T(8,128)S(1)}, u32[]{:S(2)}, u32[]{:S(2)}) collective-permute-start(f32[128,256]{1,0:T(8,128)S(1)} %multiply_add_fusion.4), channel_id=1, source_target_pairs={{0,4},{1,5},{2,6},{3,7},{4,8},{5,9},{6,10},{7,11},{8,12},{9,13},{1... | collective-permute-start | bytes 393224 | tf_op jit(solution)/shard_map/ppermute | solution.py:223
  159.3 6.9 %collective-permute-start.14 = (f32[128,256]{1,0:T(8,128)S(1)}, f32[128,256]{1,0:T(8,128)S(1)}, u32[]{:S(2)}, u32[]{:S(2)}) collective-permute-start(f32[128,256]{1,0:T(8,128)S(1)} %multiply_add_fusion.1), channel_id=1, source_target_pairs={{4,0},{5,1},{6,2},{7,3},{8,4},{9,5},{10,6},{11,7},{12,8},{13,9},{1... | collective-permute-start | bytes 393224 | tf_op jit(solution)/shard_map/ppermute | solution.py:224
  161.9 9.9 %collective-permute-start.11 = (f32[128,256]{1,0:T(8,128)S(1)}, f32[128,256]{1,0:T(8,128)S(1)}, u32[]{:S(2)}, u32[]{:S(2)}) collective-permute-start(f32[128,256]{1,0:T(8,128)S(1)} %multiply_add_fusion.3), channel_id=1, source_target_pairs={{0,8},{1,9},{2,10},{3,11},{4,12},{5,13},{6,14},{7,15},{16,24},{17,... | collective-permute-start | bytes 393224 | tf_op jit(solution)/shard_map/ppermute | solution.py:223
  166.2 8.9 %collective-permute-start.15 = (f32[128,256]{1,0:T(8,128)S(1)}, f32[128,256]{1,0:T(8,128)S(1)}, u32[]{:S(2)}, u32[]{:S(2)}) collective-permute-start(f32[128,256]{1,0:T(8,128)S(1)} %multiply_add_fusion), channel_id=1, source_target_pairs={{8,0},{9,1},{10,2},{11,3},{12,4},{13,5},{14,6},{15,7},{24,16},{25,... | collective-permute-start | bytes 393224 | tf_op jit(solution)/shard_map/ppermute | solution.py:224
  192.9 1.3 copy-start.2
  195.1 4.3 %collective-permute-start.20 = (f32[128,128]{1,0:T(8,128)S(1)}, f32[128,128]{1,0:T(8,128)S(1)}, u32[]{:S(2)}, u32[]{:S(2)}) collective-permute-start(f32[128,128]{1,0:T(8,128)S(1)} %fusion.13), channel_id=1, source_target_pairs={{1,0},{2,1},{3,2},{4,3},{5,4},{6,5},{7,6},{8,7},{9,8},{10,9},{11,1... | collective-permute-start | bytes 196616 | tf_op jit(solution)/shard_map/ppermute | solution.py:224
  196.4 3.9 %collective-permute-start.16 = (f32[128,128]{1,0:T(8,128)S(1)}, f32[128,128]{1,0:T(8,128)S(1)}, u32[]{:S(2)}, u32[]{:S(2)}) collective-permute-start(f32[128,128]{1,0:T(8,128)S(1)} %fusion.13), channel_id=1, source_target_pairs={{0,1},{1,2},{2,3},{3,4},{4,5},{5,6},{6,7},{7,8},{8,9},{9,10},{10,1... | collective-permute-start | bytes 196616 | tf_op jit(solution)/shard_map/ppermute | solution.py:223
  200.4 8.2 %collective-permute-start.17 = (f32[128,128]{1,0:T(8,128)S(1)}, f32[128,128]{1,0:T(8,128)S(1)}, u32[]{:S(2)}, u32[]{:S(2)}) collective-permute-start(f32[128,128]{1,0:T(8,128)S(1)} %get-tuple-element.25), channel_id=1, source_target_pairs={{0,2},{1,3},{2,4},{3,5},{4,6},{5,7},{6,8},{7,9},{8,10},{9,11},{10,... | collective-permute-start | bytes 196616 | tf_op jit(solution)/shard_map/ppermute | solution.py:223
  206.1 6.9 %collective-permute-start.21 = (f32[128,128]{1,0:T(8,128)S(1)}, f32[128,128]{1,0:T(8,128)S(1)}, u32[]{:S(2)}, u32[]{:S(2)}) collective-permute-start(f32[128,128]{1,0:T(8,128)S(1)} %get-tuple-element.26), channel_id=1, source_target_pairs={{2,0},{3,1},{4,2},{5,3},{6,4},{7,5},{8,6},{9,7},{10,8},{11,9},{12,... | collective-permute-start | bytes 196616 | tf_op jit(solution)/shard_map/ppermute | solution.py:224
  208.6 6.3 %collective-permute-start.18 = (f32[128,128]{1,0:T(8,128)S(1)}, f32[128,128]{1,0:T(8,128)S(1)}, u32[]{:S(2)}, u32[]{:S(2)}) collective-permute-start(f32[128,128]{1,0:T(8,128)S(1)} %multiply_add_fusion.10), channel_id=1, source_target_pairs={{0,4},{1,5},{2,6},{3,7},{4,8},{5,9},{6,10},{7,11},{8,12},{9,13},{1... | collective-permute-start | bytes 196616 | tf_op jit(solution)/shard_map/ppermute | solution.py:223
  213.0 6.2 %collective-permute-start.22 = (f32[128,128]{1,0:T(8,128)S(1)}, f32[128,128]{1,0:T(8,128)S(1)}, u32[]{:S(2)}, u32[]{:S(2)}) collective-permute-start(f32[128,128]{1,0:T(8,128)S(1)} %multiply_add_fusion.7), channel_id=1, source_target_pairs={{4,0},{5,1},{6,2},{7,3},{8,4},{9,5},{10,6},{11,7},{12,8},{13,9},{1... | collective-permute-start | bytes 196616 | tf_op jit(solution)/shard_map/ppermute | solution.py:224
  214.9 6.1 %collective-permute-start.19 = (f32[128,128]{1,0:T(8,128)S(1)}, f32[128,128]{1,0:T(8,128)S(1)}, u32[]{:S(2)}, u32[]{:S(2)}) collective-permute-start(f32[128,128]{1,0:T(8,128)S(1)} %multiply_add_fusion.9), channel_id=1, source_target_pairs={{0,8},{1,9},{2,10},{3,11},{4,12},{5,13},{6,14},{7,15},{16,24},{17,... | collective-permute-start | bytes 196616 | tf_op jit(solution)/shard_map/ppermute | solution.py:223
  219.2 7.8 %collective-permute-start.23 = (f32[128,128]{1,0:T(8,128)S(1)}, f32[128,128]{1,0:T(8,128)S(1)}, u32[]{:S(2)}, u32[]{:S(2)}) collective-permute-start(f32[128,128]{1,0:T(8,128)S(1)} %multiply_add_fusion.6), channel_id=1, source_target_pairs={{8,0},{9,1},{10,2},{11,3},{12,4},{13,5},{14,6},{15,7},{24,16},{25,... | collective-permute-start | bytes 196616 | tf_op jit(solution)/shard_map/ppermute | solution.py:224

commit v11 on v8

--- a/solution.py
+++ b/solution.py
@@ -52,8 +52,8 @@
     )(gram)
 
 
-def _step_kernel(first, below_ref, low_ref, high_ref, above_ref, older_low_ref, older_high_ref,
-                 low_pot_ref, high_pot_ref, out_low_ref, out_high_ref):
+def _step_kernel(first, rim_ref, below_ref, low_ref, high_ref, above_ref, older_low_ref,
+                 older_high_ref, low_pot_ref, high_pot_ref, out_low_ref, out_high_ref):
     half = low_ref.shape[0]
     rows_y = low_ref.shape[1]
     rows_x = low_ref.shape[2]
@@ -61,7 +61,12 @@
     sources = (below_ref, low_ref, high_ref, above_ref)
 
     def plane(index, y):
-        return sources[index // half][index % half, y].astype(jnp.float32)
+        value = sources[index // half][index % half, y].astype(jnp.float32)
+        if index < half:
+            return value * rim_ref[0]
+        if index >= 3 * half:
+            return value * rim_ref[1]
+        return value
 
     for centre in range(half, 3 * half):
         own = centre - half
@@ -98,7 +103,7 @@
             out_ref[local, y] = newer.astype(out_ref.dtype)
 
 
-def chebyshev_step(below, low, high, above, older_low, older_high, potential, first):
+def chebyshev_step(rim, below, low, high, above, older_low, older_high, potential, first):
     half, rows_y, rows_x, bands = low.shape
     lanes = 128
     block = (half, rows_y, rows_x, lanes)
@@ -113,6 +118,7 @@
         out_shape=(piece, piece),
         grid=(bands // lanes,),
         in_specs=[
+            pl.BlockSpec(memory_space=pltpu.SMEM),
             spec(below, 0),
             spec(low, 0),
             spec(high, 0),
@@ -126,7 +132,7 @@
             pl.BlockSpec(block, lambda j: (0, 0, 0, j)),
             pl.BlockSpec(block, lambda j: (0, 0, 0, j)),
         ),
-    )(below, low, high, above, older_low, older_high, potential, potential)
+    )(rim, below, low, high, above, older_low, older_high, potential, potential)
 
 
 def extended_2(block, sides, width):
@@ -190,23 +196,24 @@
 
     forward = [(i, i + 1) for i in range(slabs - 1)]
     backward = [(target, source) for source, target in forward]
-    bf_below = below.astype(jnp.bfloat16)
-    bf_above = above.astype(jnp.bfloat16)
+    rim = jnp.stack([below, above])
 
     def rimmed(low, high):
         from_below = lax.ppermute(high, "gz", forward)
         from_above = lax.ppermute(low, "gz", backward)
-        return from_below * bf_below, from_above * bf_above
+        return from_below, from_above
 
     lanes = jnp.broadcast_to(grid[..., None], grid.shape + (128,))
     half = planes // 2
     low, high = waves[:half], waves[half:]
     from_below, from_above = rimmed(low, high)
-    low, high = chebyshev_step(from_below, low, high, from_above, waves, waves, lanes, True)
+    low, high = chebyshev_step(rim, from_below, low, high, from_above, waves, waves, lanes, True)
     older_low, older_high = waves, waves
     for turn in range(DEGREE - 1):
         from_below, from_above = rimmed(low, high)
-        newer = chebyshev_step(from_below, low, high, from_above, older_low, older_high, lanes, False)
+        newer = chebyshev_step(
+            rim, from_below, low, high, from_above, older_low, older_high, lanes, False
+        )
         older_low, older_high = low, high
         low, high = newer
     current = jnp.concatenate([low, high], axis=0)

time: 248 us -> 248 us (level)
  other arithmetic: 11.3 us -> 4.28 us
  waiting for transfers between devices: 27.3 us -> 30.1 us
  local copies, waits for them, and re-layouts: 6.08 us -> 8.82 us
    mul x8 -> x0, other arithmetic: 7.64 us -> none  [rimmed(): return (from_below * bf_below, from_above * bf_above)]
    ppermute x4, waiting for transfers between devices: 9.74 us -> 12.6 us  [rimmed(): from_above = lax.ppermute(low, 'gz', backward)]
    unnamed x10 -> x26, local copies, waits for them, and re-layouts: 0.02 us -> 2.7 us
  transfers between devices with their start and end apart: 24 -> 24, of which waited for: 17 -> 16; matrix products, arithmetic and copies ran while one was open for 2% -> 1% of each run, Pallas kernels for 0% -> 0%
where the time goes in v11:
time: 248 us; the launch traced here: 247 us
  starting transfers between devices  120 us (48%)
  Pallas kernels  68.8 us (28%)
  waiting for transfers between devices  30.1 us (12%)
  between operations  11.3 us (5%)
  local copies, waits for them, and re-layouts  8.82 us (4%)
  other arithmetic  4.28 us (2%)
  matrix products  3.8 us (2%)
    ppermute x4, starting transfers between devices, rimmed(): from_below = lax.ppermute(high, 'gz', forward)  53 us
    ppermute x8, starting transfers between devices, domain_total(): from_low = lax.ppermute(forward, 'gz', ahead)  51 us
    pallas_call x4, Pallas kernels, chebyshev_step(): pl.pallas_call(functools.partial(_step_kernel, first), out_shape=(piece,...  34.9 us
    pallas_call x2, Pallas kernels, lower_inverse(): pl.pallas_call(_lower_inverse_kernel, out_shape=jax.ShapeDtypeStruct((n,...  33.9 us
    ppermute x4, waiting for transfers between devices, rimmed(): from_above = lax.ppermute(low, 'gz', backward)  12.6 us
    ppermute x8, starting transfers between devices, domain_total(): from_high = lax.ppermute(backward, 'gz', behind)  10.3 us
    ppermute x8, waiting for transfers between devices, domain_total(): from_high = lax.ppermute(backward, 'gz', behind)  10 us
    ppermute x8, waiting for transfers between devices, domain_total(): from_low = lax.ppermute(forward, 'gz', ahead)  5.39 us
  transfers between devices with their start and end apart: 24, of which 16 were waited for; matrix products, arithmetic and copies ran while one was open for 1% of the time, Pallas kernels for 0%

profile of v11, /device:TPU:0, one launch (start us, length us, event | category | flops | bytes accessed | tf_op | source)
XLA Modules:
  0.0 246.7 jit_solution(12588829265600528566)
XLA Ops:
  0.0 1.5 fusion.11
  1.5 1.3 collective-permute-start.1
  2.8 3.1 %collective-permute-start = (bf16[3,8,64,256]{3,2,1,0:T(8,128)(2,1)S(1)}, bf16[3,8,64,256]{3,2,1,0:T(8,128)(2,1)S(1)}, u32[]{:S(2)}, u32[]{:S(2)}) collective-permute-start(bf16[3,8,64,256]{3,2,1,0:T(8,128)(2,1)S(1)} %get-tuple-element.22.high_ref), channel_id=1, source_target_pairs={{0,1},{1,2},{2,3},{3,4},{4,5},{5,6},{6,7},{7,8},{8,9},{9,10},{10,1... | collective-permute-start | bytes 2359304 | tf_op jit(solution)/shard_map/ppermute | solution.py:202
  6.0 0.7 fusion.12
  9.3 0.6 add_convert_fusion.rim_ref
  9.9 1.6 broadcast_in_dim.8.low_pot_ref.high_pot_ref
  11.6 8.6 %shard_map.37 = (bf16[3,8,64,256]{3,2,1,0:T(8,128)(2,1)}, bf16[3,8,64,256]{3,2,1,0:T(8,128)(2,1)}) custom-call(f32[2]{0:T(128)} %add_convert_fusion.rim_ref, bf16[3,8,64,256]{3,2,1,0:T(8,128)(2,1)} %copy-done.3, bf16[3,8,64,256]{3,2,1,0:T(8,128)(2,1)} %copy-done, bf16[3,8,64,256]{3,2,1,0:T(8,128)(2,1)} %copy-done.1, bf16[3,8,64,256]{3,2,1,0:T(8,128)(2,1)} %copy-done.2, ...), custom_call_target="tpu_custom_call" | custom-call | tf_op jit(solution)/shard_map/pallas_call | solution.py:116
  20.2 16.8 %collective-permute-start.2 = (bf16[3,8,64,256]{3,2,1,0:T(8,128)(2,1)}, bf16[3,8,64,256]{3,2,1,0:T(8,128)(2,1)S(1)}, u32[]{:S(2)}, u32[]{:S(2)}) collective-permute-start(bf16[3,8,64,256]{3,2,1,0:T(8,128)(2,1)} %get-tuple-element.13.high_ref.older_high_ref), channel_id=1, source_target_pairs={{0,1},{1,2},{2,3},{3,4},{4,5},{5,6},{6,7},{7,8},{8,9},{9,10},{10,1... | collective-permute-start | bytes 2359304 | tf_op jit(solution)/shard_map/ppermute | solution.py:202
  36.9 1.3 collective-permute-start.3
  38.2 0.8 collective-permute-done.2.below_ref
  39.0 4.3 %collective-permute-done.3.above_ref = bf16[3,8,64,256]{3,2,1,0:T(8,128)(2,1)S(1)} collective-permute-done((bf16[3,8,64,256]{3,2,1,0:T(8,128)(2,1)}, bf16[3,8,64,256]{3,2,1,0:T(8,128)(2,1)S(1)}, u32[]{:S(2)}, u32[]{:S(2)}) %collective-permute-start.3) | collective-permute-done | bytes 786464 | tf_op jit(solution)/shard_map/ppermute | solution.py:203
  43.3 0.9 copy-done.5
  44.1 8.8 %shard_map.38 = (bf16[3,8,64,256]{3,2,1,0:T(8,128)(2,1)}, bf16[3,8,64,256]{3,2,1,0:T(8,128)(2,1)}) custom-call(f32[2]{0:T(128)} %add_convert_fusion.rim_ref, bf16[3,8,64,256]{3,2,1,0:T(8,128)(2,1)} %copy-done.4, bf16[3,8,64,256]{3,2,1,0:T(8,128)(2,1)} %get-tuple-element.14.low_ref.older_low_ref, ...), custom_call_target="tpu_custom_call" | custom-call | tf_op jit(solution)/shard_map/pallas_call | solution.py:116
  52.9 16.6 %collective-permute-start.4 = (bf16[3,8,64,256]{3,2,1,0:T(8,128)(2,1)}, bf16[3,8,64,256]{3,2,1,0:T(8,128)(2,1)S(1)}, u32[]{:S(2)}, u32[]{:S(2)}) collective-permute-start(bf16[3,8,64,256]{3,2,1,0:T(8,128)(2,1)} %get-tuple-element.15.high_ref.older_high_ref), channel_id=1, source_target_pairs={{0,1},{1,2},{2,3},{3,4},{4,5},{5,6},{6,7},{7,8},{8,9},{9,10},{10,1... | collective-permute-start | bytes 2359304 | tf_op jit(solution)/shard_map/ppermute | solution.py:202
  69.5 1.3 collective-permute-start.5
  70.8 0.8 collective-permute-done.4.below_ref
  71.6 4.2 %collective-permute-done.5.above_ref = bf16[3,8,64,256]{3,2,1,0:T(8,128)(2,1)S(1)} collective-permute-done((bf16[3,8,64,256]{3,2,1,0:T(8,128)(2,1)}, bf16[3,8,64,256]{3,2,1,0:T(8,128)(2,1)S(1)}, u32[]{:S(2)}, u32[]{:S(2)}) %collective-permute-start.5) | collective-permute-done | bytes 786464 | tf_op jit(solution)/shard_map/ppermute | solution.py:203
  75.7 0.9 copy-done.9
  76.6 8.8 %shard_map.39 = (bf16[3,8,64,256]{3,2,1,0:T(8,128)(2,1)}, bf16[3,8,64,256]{3,2,1,0:T(8,128)(2,1)}) custom-call(f32[2]{0:T(128)} %add_convert_fusion.rim_ref, bf16[3,8,64,256]{3,2,1,0:T(8,128)(2,1)} %copy-done.7, bf16[3,8,64,256]{3,2,1,0:T(8,128)(2,1)} %get-tuple-element.16.low_ref.older_low_ref, ...), custom_call_target="tpu_custom_call" | custom-call | tf_op jit(solution)/shard_map/pallas_call | solution.py:116
  85.4 16.6 %collective-permute-start.6 = (bf16[3,8,64,256]{3,2,1,0:T(8,128)(2,1)}, bf16[3,8,64,256]{3,2,1,0:T(8,128)(2,1)S(1)}, u32[]{:S(2)}, u32[]{:S(2)}) collective-permute-start(bf16[3,8,64,256]{3,2,1,0:T(8,128)(2,1)} %get-tuple-element.17.high_ref), channel_id=1, source_target_pairs={{0,1},{1,2},{2,3},{3,4},{4,5},{5,6},{6,7},{7,8},{8,9},{9,10},{10,1... | collective-permute-start | bytes 2359304 | tf_op jit(solution)/shard_map/ppermute | solution.py:202
  102.0 1.5 collective-permute-start.7
  103.5 0.6 collective-permute-done.6.below_ref
  104.1 4.2 %collective-permute-done.7.above_ref = bf16[3,8,64,256]{3,2,1,0:T(8,128)(2,1)S(1)} collective-permute-done((bf16[3,8,64,256]{3,2,1,0:T(8,128)(2,1)}, bf16[3,8,64,256]{3,2,1,0:T(8,128)(2,1)S(1)}, u32[]{:S(2)}, u32[]{:S(2)}) %collective-permute-start.7) | collective-permute-done | bytes 786464 | tf_op jit(solution)/shard_map/ppermute | solution.py:203
  108.3 0.9 copy-done.8
  109.2 8.8 %shard_map.40 = (bf16[3,8,64,256]{3,2,1,0:T(8,128)(2,1)}, bf16[3,8,64,256]{3,2,1,0:T(8,128)(2,1)}) custom-call(f32[2]{0:T(128)} %add_convert_fusion.rim_ref, bf16[3,8,64,256]{3,2,1,0:T(8,128)(2,1)} %copy-done.6, bf16[3,8,64,256]{3,2,1,0:T(8,128)(2,1)} %get-tuple-element.18.low_ref, bf16[3,8,64,256]{3,2,1,0:T(8,128)(2,1)} %get-tuple-element.17.high_ref, ...), custom_call_target="tpu_custom_call" | custom-call | tf_op jit(solution)/shard_map/pallas_call | solution.py:116
  117.9 1.5 pad_maximum_fusion
  119.4 0.4 fusion.2
  119.8 1.3 collective-permute-start.12
  121.1 17.2 %collective-permute-start.8 = (f32[128,256]{1,0:T(8,128)S(1)}, f32[128,256]{1,0:T(8,128)S(1)}, u32[]{:S(2)}, u32[]{:S(2)}) collective-permute-start(f32[128,256]{1,0:T(8,128)S(1)} %fusion.2), channel_id=1, source_target_pairs={{0,1},{1,2},{2,3},{3,4},{4,5},{5,6},{6,7},{7,8},{8,9},{9,10},{10,1... | collective-permute-start | bytes 393224 | tf_op jit(solution)/shard_map/ppermute | solution.py:230
  138.4 0.9 collective-permute-done.8
  139.3 7.6 %collective-permute-start.9 = (f32[128,256]{1,0:T(8,128)S(1)}, f32[128,256]{1,0:T(8,128)S(1)}, u32[]{:S(2)}, u32[]{:S(2)}) collective-permute-start(f32[128,256]{1,0:T(8,128)S(1)} %get-tuple-element.23), channel_id=1, source_target_pairs={{0,2},{1,3},{2,4},{3,5},{4,6},{5,7},{6,8},{7,9},{8,10},{9,11},{10,... | collective-permute-start | bytes 393224 | tf_op jit(solution)/shard_map/ppermute | solution.py:230
  152.0 1.3 collective-permute-start.13
  153.3 5.3 %collective-permute-start.10 = (f32[128,256]{1,0:T(8,128)S(1)}, f32[128,256]{1,0:T(8,128)S(1)}, u32[]{:S(2)}, u32[]{:S(2)}) collective-permute-start(f32[128,256]{1,0:T(8,128)S(1)} %multiply_add_fusion.4), channel_id=1, source_target_pairs={{0,4},{1,5},{2,6},{3,7},{4,8},{5,9},{6,10},{7,11},{8,12},{9,13},{1... | collective-permute-start | bytes 393224 | tf_op jit(solution)/shard_map/ppermute | solution.py:230
  158.6 0.2 collective-permute-done.13
  158.8 1.3 collective-permute-start.14
  160.1 1.3 collective-permute-done.10
  161.5 3.6 %collective-permute-start.11 = (f32[128,256]{1,0:T(8,128)S(1)}, f32[128,256]{1,0:T(8,128)S(1)}, u32[]{:S(2)}, u32[]{:S(2)}) collective-permute-start(f32[128,256]{1,0:T(8,128)S(1)} %multiply_add_fusion.3), channel_id=1, source_target_pairs={{0,8},{1,9},{2,10},{3,11},{4,12},{5,13},{6,14},{7,15},{16,24},{17,... | collective-permute-start | bytes 393224 | tf_op jit(solution)/shard_map/ppermute | solution.py:230
  165.1 0.6 collective-permute-done.14
  165.7 1.3 collective-permute-start.15
  169.5 1.2 fusion.10
  171.4 3.2 %collective-permute-done.15 = f32[128,256]{1,0:T(8,128)S(1)} collective-permute-done((f32[128,256]{1,0:T(8,128)S(1)}, f32[128,256]{1,0:T(8,128)S(1)}, u32[]{:S(2)}, u32[]{:S(2)}) %collective-permute-start.15) | collective-permute-done | bytes 131104 | tf_op jit(solution)/shard_map/ppermute | solution.py:231
  174.7 0.6 slice.25.gram_ref
  175.3 16.9 %shard_map.41 = f32[128,128]{1,0:T(8,128)} custom-call(f32[128,128]{1,0:T(8,128)} %slice.25.gram_ref), custom_call_target="tpu_custom_call" | custom-call | tf_op jit(solution)/shard_map/pallas_call | solution.py:48
  192.3 1.3 convolution_convert_fusion.1
  193.5 0.5 fusion
  194.1 0.4 fusion.13
  194.5 1.3 collective-permute-start.20
  195.8 3.0 %collective-permute-start.16 = (f32[128,128]{1,0:T(8,128)S(1)}, f32[128,128]{1,0:T(8,128)S(1)}, u32[]{:S(2)}, u32[]{:S(2)}) collective-permute-start(f32[128,128]{1,0:T(8,128)S(1)} %fusion.13), channel_id=1, source_target_pairs={{0,1},{1,2},{2,3},{3,4},{4,5},{5,6},{6,7},{7,8},{8,9},{9,10},{10,1... | collective-permute-start | bytes 196616 | tf_op jit(solution)/shard_map/ppermute | solution.py:230
  198.8 0.9 collective-permute-done.16
  199.7 5.7 %collective-permute-start.17 = (f32[128,128]{1,0:T(8,128)S(1)}, f32[128,128]{1,0:T(8,128)S(1)}, u32[]{:S(2)}, u32[]{:S(2)}) collective-permute-start(f32[128,128]{1,0:T(8,128)S(1)} %get-tuple-element.25), channel_id=1, source_target_pairs={{0,2},{1,3},{2,4},{3,5},{4,6},{5,7},{6,8},{7,9},{8,10},{9,11},{10,... | collective-permute-start | bytes 196616 | tf_op jit(solution)/shard_map/ppermute | solution.py:230
  205.4 1.3 collective-permute-start.21
  206.7 1.2 collective-permute-done.17
  207.9 4.4 %collective-permute-start.18 = (f32[128,128]{1,0:T(8,128)S(1)}, f32[128,128]{1,0:T(8,128)S(1)}, u32[]{:S(2)}, u32[]{:S(2)}) collective-permute-start(f32[128,128]{1,0:T(8,128)S(1)} %multiply_add_fusion.10), channel_id=1, source_target_pairs={{0,4},{1,5},{2,6},{3,7},{4,8},{5,9},{6,10},{7,11},{8,12},{9,13},{1... | collective-permute-start | bytes 196616 | tf_op jit(solution)/shard_map/ppermute | solution.py:230
  212.3 1.3 collective-permute-start.22
  213.6 0.6 collective-permute-done.18
  214.2 4.2 %collective-permute-start.19 = (f32[128,128]{1,0:T(8,128)S(1)}, f32[128,128]{1,0:T(8,128)S(1)}, u32[]{:S(2)}, u32[]{:S(2)}) collective-permute-start(f32[128,128]{1,0:T(8,128)S(1)} %multiply_add_fusion.9), channel_id=1, source_target_pairs={{0,8},{1,9},{2,10},{3,11},{4,12},{5,13},{6,14},{7,15},{16,24},{17,... | collective-permute-start | bytes 196616 | tf_op jit(solution)/shard_map/ppermute | solution.py:230
  218.5 1.3 collective-permute-start.23
  219.8 0.5 collective-permute-done.19
  220.3 5.9 %collective-permute-done.23 = f32[128,128]{1,0:T(8,128)S(1)} collective-permute-done((f32[128,128]{1,0:T(8,128)S(1)}, f32[128,128]{1,0:T(8,128)S(1)}, u32[]{:S(2)}, u32[]{:S(2)}) %collective-permute-start.23) | collective-permute-done | bytes 65568 | tf_op jit(solution)/shard_map/ppermute | solution.py:231
  226.2 0.7 subtract_divide_fusion.1.gram_ref
  226.9 16.9 %shard_map.42 = f32[128,128]{1,0:T(8,128)} custom-call(f32[128,128]{1,0:T(8,128)} %subtract_divide_fusion.1.gram_ref), custom_call_target="tpu_custom_call" | custom-call | tf_op jit(solution)/shard_map/pallas_call | solution.py:48
  243.8 1.2 convolution_convert_fusion
  245.0 0.1 pad_maximum_fusion.1
  245.2 1.6 copy.5
  (43 shorter events, 0.4 us)
Async XLA Ops:
  0.0 5.9 %copy-start.11 = (s32[16]{0:T(128)S(1)}, s32[16]{0:T(128)}, u32[]{:S(2)}) copy-start(s32[16]{0:T(128)} %param.5) | copy-start | bytes 196
  0.0 9.3 %copy-start.12 = (f32[6,512]{1,0:T(8,128)S(1)}, f32[6,512]{1,0:T(8,128)}, u32[]{:S(2)}) copy-start(f32[6,512]{1,0:T(8,128)} %param.4) | copy-start | bytes 36868
  1.5 10.1 %copy-start = (bf16[3,8,64,256]{3,2,1,0:T(8,128)(2,1)}, bf16[3,8,64,256]{3,2,1,0:T(8,128)(2,1)S(1)}, u32[]{:S(2)}) copy-start(bf16[3,8,64,256]{3,2,1,0:T(8,128)(2,1)S(1)} %get-tuple-element.21.low_ref) | copy-start | bytes 2359300
  1.5 10.1 %copy-start.1 = (bf16[3,8,64,256]{3,2,1,0:T(8,128)(2,1)}, bf16[3,8,64,256]{3,2,1,0:T(8,128)(2,1)S(1)}, u32[]{:S(2)}) copy-start(bf16[3,8,64,256]{3,2,1,0:T(8,128)(2,1)S(1)} %get-tuple-element.22.high_ref) | copy-start | bytes 2359300
  1.5 8.4 %collective-permute-start.1 = (bf16[3,8,64,256]{3,2,1,0:T(8,128)(2,1)S(1)}, bf16[3,8,64,256]{3,2,1,0:T(8,128)(2,1)S(1)}, u32[]{:S(2)}, u32[]{:S(2)}) collective-permute-start(bf16[3,8,64,256]{3,2,1,0:T(8,128)(2,1)S(1)} %get-tuple-element.21.low_ref), channel_id=1, source_target_pairs={{1,0},{2,1},{3,2},{4,3},{5,4},{6,5},{7,6},{8,7},{9,8},{10,9},{11,1... | collective-permute-start | bytes 2359304 | tf_op jit(solution)/shard_map/ppermute | solution.py:203
  2.8 7.1 %collective-permute-start = (bf16[3,8,64,256]{3,2,1,0:T(8,128)(2,1)S(1)}, bf16[3,8,64,256]{3,2,1,0:T(8,128)(2,1)S(1)}, u32[]{:S(2)}, u32[]{:S(2)}) collective-permute-start(bf16[3,8,64,256]{3,2,1,0:T(8,128)(2,1)S(1)} %get-tuple-element.22.high_ref), channel_id=1, source_target_pairs={{0,1},{1,2},{2,3},{3,4},{4,5},{5,6},{6,7},{7,8},{8,9},{9,10},{10,1... | collective-permute-start | bytes 2359304 | tf_op jit(solution)/shard_map/ppermute | solution.py:202
  9.9 1.7 copy-start.2
  9.9 1.7 copy-start.3
  20.2 18.8 %collective-permute-start.2 = (bf16[3,8,64,256]{3,2,1,0:T(8,128)(2,1)}, bf16[3,8,64,256]{3,2,1,0:T(8,128)(2,1)S(1)}, u32[]{:S(2)}, u32[]{:S(2)}) collective-permute-start(bf16[3,8,64,256]{3,2,1,0:T(8,128)(2,1)} %get-tuple-element.13.high_ref.older_high_ref), channel_id=1, source_target_pairs={{0,1},{1,2},{2,3},{3,4},{4,5},{5,6},{6,7},{7,8},{8,9},{9,10},{10,1... | collective-permute-start | bytes 2359304 | tf_op jit(solution)/shard_map/ppermute | solution.py:202
  36.9 6.3 %collective-permute-start.3 = (bf16[3,8,64,256]{3,2,1,0:T(8,128)(2,1)}, bf16[3,8,64,256]{3,2,1,0:T(8,128)(2,1)S(1)}, u32[]{:S(2)}, u32[]{:S(2)}) collective-permute-start(bf16[3,8,64,256]{3,2,1,0:T(8,128)(2,1)} %get-tuple-element.14.low_ref.older_low_ref), channel_id=1, source_target_pairs={{1,0},{2,1},{3,2},{4,3},{5,4},{6,5},{7,6},{8,7},{9,8},{10,9},{11,1... | collective-permute-start | bytes 2359304 | tf_op jit(solution)/shard_map/ppermute | solution.py:203
  39.0 4.3 %copy-start.4 = (bf16[3,8,64,256]{3,2,1,0:T(8,128)(2,1)}, bf16[3,8,64,256]{3,2,1,0:T(8,128)(2,1)S(1)}, u32[]{:S(2)}) copy-start(bf16[3,8,64,256]{3,2,1,0:T(8,128)(2,1)S(1)} %collective-permute-done.2.below_ref) | copy-start | bytes 2359300
  43.3 0.9 copy-start.5
  52.9 18.6 %collective-permute-start.4 = (bf16[3,8,64,256]{3,2,1,0:T(8,128)(2,1)}, bf16[3,8,64,256]{3,2,1,0:T(8,128)(2,1)S(1)}, u32[]{:S(2)}, u32[]{:S(2)}) collective-permute-start(bf16[3,8,64,256]{3,2,1,0:T(8,128)(2,1)} %get-tuple-element.15.high_ref.older_high_ref), channel_id=1, source_target_pairs={{0,1},{1,2},{2,3},{3,4},{4,5},{5,6},{6,7},{7,8},{8,9},{9,10},{10,1... | collective-permute-start | bytes 2359304 | tf_op jit(solution)/shard_map/ppermute | solution.py:202
  69.5 6.2 %collective-permute-start.5 = (bf16[3,8,64,256]{3,2,1,0:T(8,128)(2,1)}, bf16[3,8,64,256]{3,2,1,0:T(8,128)(2,1)S(1)}, u32[]{:S(2)}, u32[]{:S(2)}) collective-permute-start(bf16[3,8,64,256]{3,2,1,0:T(8,128)(2,1)} %get-tuple-element.16.low_ref.older_low_ref), channel_id=1, source_target_pairs={{1,0},{2,1},{3,2},{4,3},{5,4},{6,5},{7,6},{8,7},{9,8},{10,9},{11,1... | collective-permute-start | bytes 2359304 | tf_op jit(solution)/shard_map/ppermute | solution.py:203
  71.6 4.2 %copy-start.7 = (bf16[3,8,64,256]{3,2,1,0:T(8,128)(2,1)}, bf16[3,8,64,256]{3,2,1,0:T(8,128)(2,1)S(1)}, u32[]{:S(2)}) copy-start(bf16[3,8,64,256]{3,2,1,0:T(8,128)(2,1)S(1)} %collective-permute-done.4.below_ref) | copy-start | bytes 2359300
  75.7 0.9 copy-start.9
  85.4 18.7 %collective-permute-start.6 = (bf16[3,8,64,256]{3,2,1,0:T(8,128)(2,1)}, bf16[3,8,64,256]{3,2,1,0:T(8,128)(2,1)S(1)}, u32[]{:S(2)}, u32[]{:S(2)}) collective-permute-start(bf16[3,8,64,256]{3,2,1,0:T(8,128)(2,1)} %get-tuple-element.17.high_ref), channel_id=1, source_target_pairs={{0,1},{1,2},{2,3},{3,4},{4,5},{5,6},{6,7},{7,8},{8,9},{9,10},{10,1... | collective-permute-start | bytes 2359304 | tf_op jit(solution)/shard_map/ppermute | solution.py:202
  102.0 6.2 %collective-permute-start.7 = (bf16[3,8,64,256]{3,2,1,0:T(8,128)(2,1)}, bf16[3,8,64,256]{3,2,1,0:T(8,128)(2,1)S(1)}, u32[]{:S(2)}, u32[]{:S(2)}) collective-permute-start(bf16[3,8,64,256]{3,2,1,0:T(8,128)(2,1)} %get-tuple-element.18.low_ref), channel_id=1, source_target_pairs={{1,0},{2,1},{3,2},{4,3},{5,4},{6,5},{7,6},{8,7},{9,8},{10,9},{11,1... | collective-permute-start | bytes 2359304 | tf_op jit(solution)/shard_map/ppermute | solution.py:203
  104.1 4.2 %copy-start.6 = (bf16[3,8,64,256]{3,2,1,0:T(8,128)(2,1)}, bf16[3,8,64,256]{3,2,1,0:T(8,128)(2,1)S(1)}, u32[]{:S(2)}) copy-start(bf16[3,8,64,256]{3,2,1,0:T(8,128)(2,1)S(1)} %collective-permute-done.6.below_ref) | copy-start | bytes 2359300
  108.3 0.9 copy-start.8
  119.8 18.5 %collective-permute-start.12 = (f32[128,256]{1,0:T(8,128)S(1)}, f32[128,256]{1,0:T(8,128)S(1)}, u32[]{:S(2)}, u32[]{:S(2)}) collective-permute-start(f32[128,256]{1,0:T(8,128)S(1)} %fusion.2), channel_id=1, source_target_pairs={{1,0},{2,1},{3,2},{4,3},{5,4},{6,5},{7,6},{8,7},{9,8},{10,9},{11,1... | collective-permute-start | bytes 393224 | tf_op jit(solution)/shard_map/ppermute | solution.py:231
  121.1 18.2 %collective-permute-start.8 = (f32[128,256]{1,0:T(8,128)S(1)}, f32[128,256]{1,0:T(8,128)S(1)}, u32[]{:S(2)}, u32[]{:S(2)}) collective-permute-start(f32[128,256]{1,0:T(8,128)S(1)} %fusion.2), channel_id=1, source_target_pairs={{0,1},{1,2},{2,3},{3,4},{4,5},{5,6},{6,7},{7,8},{8,9},{9,10},{10,1... | collective-permute-start | bytes 393224 | tf_op jit(solution)/shard_map/ppermute | solution.py:230
  139.3 13.9 %collective-permute-start.9 = (f32[128,256]{1,0:T(8,128)S(1)}, f32[128,256]{1,0:T(8,128)S(1)}, u32[]{:S(2)}, u32[]{:S(2)}) collective-permute-start(f32[128,256]{1,0:T(8,128)S(1)} %get-tuple-element.23), channel_id=1, source_target_pairs={{0,2},{1,3},{2,4},{3,5},{4,6},{5,7},{6,8},{7,9},{8,10},{9,11},{10,... | collective-permute-start | bytes 393224 | tf_op jit(solution)/shard_map/ppermute | solution.py:230
  152.0 6.9 %collective-permute-start.13 = (f32[128,256]{1,0:T(8,128)S(1)}, f32[128,256]{1,0:T(8,128)S(1)}, u32[]{:S(2)}, u32[]{:S(2)}) collective-permute-start(f32[128,256]{1,0:T(8,128)S(1)} %get-tuple-element.24), channel_id=1, source_target_pairs={{2,0},{3,1},{4,2},{5,3},{6,4},{7,5},{8,6},{9,7},{10,8},{11,9},{12,... | collective-permute-start | bytes 393224 | tf_op jit(solution)/shard_map/ppermute | solution.py:231
  153.3 8.2 %collective-permute-start.10 = (f32[128,256]{1,0:T(8,128)S(1)}, f32[128,256]{1,0:T(8,128)S(1)}, u32[]{:S(2)}, u32[]{:S(2)}) collective-permute-start(f32[128,256]{1,0:T(8,128)S(1)} %multiply_add_fusion.4), channel_id=1, source_target_pairs={{0,4},{1,5},{2,6},{3,7},{4,8},{5,9},{6,10},{7,11},{8,12},{9,13},{1... | collective-permute-start | bytes 393224 | tf_op jit(solution)/shard_map/ppermute | solution.py:230
  158.8 6.9 %collective-permute-start.14 = (f32[128,256]{1,0:T(8,128)S(1)}, f32[128,256]{1,0:T(8,128)S(1)}, u32[]{:S(2)}, u32[]{:S(2)}) collective-permute-start(f32[128,256]{1,0:T(8,128)S(1)} %multiply_add_fusion.1), channel_id=1, source_target_pairs={{4,0},{5,1},{6,2},{7,3},{8,4},{9,5},{10,6},{11,7},{12,8},{13,9},{1... | collective-permute-start | bytes 393224 | tf_op jit(solution)/shard_map/ppermute | solution.py:231
  161.5 10.0 %collective-permute-start.11 = (f32[128,256]{1,0:T(8,128)S(1)}, f32[128,256]{1,0:T(8,128)S(1)}, u32[]{:S(2)}, u32[]{:S(2)}) collective-permute-start(f32[128,256]{1,0:T(8,128)S(1)} %multiply_add_fusion.3), channel_id=1, source_target_pairs={{0,8},{1,9},{2,10},{3,11},{4,12},{5,13},{6,14},{7,15},{16,24},{17,... | collective-permute-start | bytes 393224 | tf_op jit(solution)/shard_map/ppermute | solution.py:230
  165.7 8.9 %collective-permute-start.15 = (f32[128,256]{1,0:T(8,128)S(1)}, f32[128,256]{1,0:T(8,128)S(1)}, u32[]{:S(2)}, u32[]{:S(2)}) collective-permute-start(f32[128,256]{1,0:T(8,128)S(1)} %multiply_add_fusion), channel_id=1, source_target_pairs={{8,0},{9,1},{10,2},{11,3},{12,4},{13,5},{14,6},{15,7},{24,16},{25,... | collective-permute-start | bytes 393224 | tf_op jit(solution)/shard_map/ppermute | solution.py:231
  192.2 1.3 copy-start.10
  194.5 4.3 %collective-permute-start.20 = (f32[128,128]{1,0:T(8,128)S(1)}, f32[128,128]{1,0:T(8,128)S(1)}, u32[]{:S(2)}, u32[]{:S(2)}) collective-permute-start(f32[128,128]{1,0:T(8,128)S(1)} %fusion.13), channel_id=1, source_target_pairs={{1,0},{2,1},{3,2},{4,3},{5,4},{6,5},{7,6},{8,7},{9,8},{10,9},{11,1... | collective-permute-start | bytes 196616 | tf_op jit(solution)/shard_map/ppermute | solution.py:231
  195.8 3.9 %collective-permute-start.16 = (f32[128,128]{1,0:T(8,128)S(1)}, f32[128,128]{1,0:T(8,128)S(1)}, u32[]{:S(2)}, u32[]{:S(2)}) collective-permute-start(f32[128,128]{1,0:T(8,128)S(1)} %fusion.13), channel_id=1, source_target_pairs={{0,1},{1,2},{2,3},{3,4},{4,5},{5,6},{6,7},{7,8},{8,9},{9,10},{10,1... | collective-permute-start | bytes 196616 | tf_op jit(solution)/shard_map/ppermute | solution.py:230
  199.7 8.2 %collective-permute-start.17 = (f32[128,128]{1,0:T(8,128)S(1)}, f32[128,128]{1,0:T(8,128)S(1)}, u32[]{:S(2)}, u32[]{:S(2)}) collective-permute-start(f32[128,128]{1,0:T(8,128)S(1)} %get-tuple-element.25), channel_id=1, source_target_pairs={{0,2},{1,3},{2,4},{3,5},{4,6},{5,7},{6,8},{7,9},{8,10},{9,11},{10,... | collective-permute-start | bytes 196616 | tf_op jit(solution)/shard_map/ppermute | solution.py:230
  205.4 6.9 %collective-permute-start.21 = (f32[128,128]{1,0:T(8,128)S(1)}, f32[128,128]{1,0:T(8,128)S(1)}, u32[]{:S(2)}, u32[]{:S(2)}) collective-permute-start(f32[128,128]{1,0:T(8,128)S(1)} %get-tuple-element.26), channel_id=1, source_target_pairs={{2,0},{3,1},{4,2},{5,3},{6,4},{7,5},{8,6},{9,7},{10,8},{11,9},{12,... | collective-permute-start | bytes 196616 | tf_op jit(solution)/shard_map/ppermute | solution.py:231
  207.9 6.3 %collective-permute-start.18 = (f32[128,128]{1,0:T(8,128)S(1)}, f32[128,128]{1,0:T(8,128)S(1)}, u32[]{:S(2)}, u32[]{:S(2)}) collective-permute-start(f32[128,128]{1,0:T(8,128)S(1)} %multiply_add_fusion.10), channel_id=1, source_target_pairs={{0,4},{1,5},{2,6},{3,7},{4,8},{5,9},{6,10},{7,11},{8,12},{9,13},{1... | collective-permute-start | bytes 196616 | tf_op jit(solution)/shard_map/ppermute | solution.py:230
  212.3 6.2 %collective-permute-start.22 = (f32[128,128]{1,0:T(8,128)S(1)}, f32[128,128]{1,0:T(8,128)S(1)}, u32[]{:S(2)}, u32[]{:S(2)}) collective-permute-start(f32[128,128]{1,0:T(8,128)S(1)} %multiply_add_fusion.7), channel_id=1, source_target_pairs={{4,0},{5,1},{6,2},{7,3},{8,4},{9,5},{10,6},{11,7},{12,8},{13,9},{1... | collective-permute-start | bytes 196616 | tf_op jit(solution)/shard_map/ppermute | solution.py:231
  214.2 6.1 %collective-permute-start.19 = (f32[128,128]{1,0:T(8,128)S(1)}, f32[128,128]{1,0:T(8,128)S(1)}, u32[]{:S(2)}, u32[]{:S(2)}) collective-permute-start(f32[128,128]{1,0:T(8,128)S(1)} %multiply_add_fusion.9), channel_id=1, source_target_pairs={{0,8},{1,9},{2,10},{3,11},{4,12},{5,13},{6,14},{7,15},{16,24},{17,... | collective-permute-start | bytes 196616 | tf_op jit(solution)/shard_map/ppermute | solution.py:230
  218.5 7.8 %collective-permute-start.23 = (f32[128,128]{1,0:T(8,128)S(1)}, f32[128,128]{1,0:T(8,128)S(1)}, u32[]{:S(2)}, u32[]{:S(2)}) collective-permute-start(f32[128,128]{1,0:T(8,128)S(1)} %multiply_add_fusion.6), channel_id=1, source_target_pairs={{8,0},{9,1},{10,2},{11,3},{12,4},{13,5},{14,6},{15,7},{24,16},{25,... | collective-permute-start | bytes 196616 | tf_op jit(solution)/shard_map/ppermute | solution.py:231

commit v12 on v11

--- a/solution.py
+++ b/solution.py
@@ -21,25 +21,37 @@
 
 def _lower_inverse_kernel(gram_ref, out_ref, work_ref):
     n = gram_ref.shape[0]
-    rows = lax.broadcasted_iota(jnp.int32, (n, 2 * n), 0)
-    lanes = lax.broadcasted_iota(jnp.int32, (n, 2 * n), 1)
     work_ref[:, :n] = gram_ref[...]
     work_ref[:, n:] = (lax.broadcasted_iota(jnp.int32, (n, n), 0) == lax.broadcasted_iota(jnp.int32, (n, n), 1)).astype(jnp.float32)
 
-    def step(k, carry):
-        row = work_ref[pl.ds(k, 1), :]
-        lane = lax.broadcasted_iota(jnp.int32, (1, 2 * n), 1)
-        pivot = jnp.sum(jnp.where(lane == k, row, 0.0), axis=1, keepdims=True)
-        scale = 1.0 / jnp.sqrt(pivot)
-        scaled = row * scale
+    rows = lax.broadcasted_iota(jnp.int32, (n, 2 * n), 0)
+    left_lanes = lax.broadcasted_iota(jnp.int32, (n, n), 1)
+    lane = lax.broadcasted_iota(jnp.int32, (1, 2 * n), 1)
+
+    def pick(vector, index):
+        return jnp.sum(jnp.where(lane == index, vector, 0.0), axis=1, keepdims=True)
+
+    def step(pair, carry):
+        k = 2 * pair
+        row_a = work_ref[pl.ds(k, 1), :]
+        row_b = work_ref[pl.ds(k + 1, 1), :]
+        scale_a = 1.0 / jnp.sqrt(pick(row_a, k))
+        scaled_a = row_a * scale_a
+        row_b = row_b - (pick(row_b, k) * scale_a) * scaled_a
+        scale_b = 1.0 / jnp.sqrt(pick(row_b, k + 1))
+        scaled_b = row_b * scale_b
         whole = work_ref[...]
         left = whole[:, :n]
-        column = jnp.sum(jnp.where(lanes[:, :n] == k, left, 0.0), axis=1, keepdims=True) * scale
-        updated = jnp.where(rows > k, whole - column * scaled, whole)
-        work_ref[...] = jnp.where(rows == k, scaled, updated)
+        column_a = jnp.sum(jnp.where(left_lanes == k, left, 0.0), axis=1, keepdims=True) * scale_a
+        next_column = jnp.sum(jnp.where(left_lanes == k + 1, left, 0.0), axis=1, keepdims=True)
+        column_b = (next_column - column_a * pick(scaled_a, k + 1)) * scale_b
+        updated = (whole - column_a * scaled_a) - column_b * scaled_b
+        updated = jnp.where(rows > k + 1, updated, whole)
+        updated = jnp.where(rows == k, scaled_a, updated)
+        work_ref[...] = jnp.where(rows == k + 1, scaled_b, updated)
         return carry
 
-    lax.fori_loop(0, n, step, 0)
+    lax.fori_loop(0, n // 2, step, 0)
     out_ref[...] = work_ref[:, n:]
 
 

time: 248 us -> 247 us (level)
  no operation moved by 1% of the time
where the time goes in v12:
time: 247 us; the launch traced here: 246 us
  starting transfers between devices  120 us (49%)
  Pallas kernels  68.2 us (28%)
  waiting for transfers between devices  30.1 us (12%)
  between operations  11.3 us (5%)
  local copies, waits for them, and re-layouts  8.82 us (4%)
  other arithmetic  4.28 us (2%)
  matrix products  3.8 us (2%)
    ppermute x4, starting transfers between devices, rimmed(): from_below = lax.ppermute(high, 'gz', forward)  53 us
    ppermute x8, starting transfers between devices, domain_total(): from_low = lax.ppermute(forward, 'gz', ahead)  51 us
    pallas_call x4, Pallas kernels, chebyshev_step(): pl.pallas_call(functools.partial(_step_kernel, first), out_shape=(piece,...  34.9 us
    pallas_call x2, Pallas kernels, lower_inverse(): pl.pallas_call(_lower_inverse_kernel, out_shape=jax.ShapeDtypeStruct((n,...  33.3 us
    ppermute x4, waiting for transfers between devices, rimmed(): from_above = lax.ppermute(low, 'gz', backward)  12.6 us
    ppermute x8, starting transfers between devices, domain_total(): from_high = lax.ppermute(backward, 'gz', behind)  10.3 us
    ppermute x8, waiting for transfers between devices, domain_total(): from_high = lax.ppermute(backward, 'gz', behind)  10 us
    ppermute x8, waiting for transfers between devices, domain_total(): from_low = lax.ppermute(forward, 'gz', ahead)  5.39 us
  transfers between devices with their start and end apart: 24, of which 16 were waited for; matrix products, arithmetic and copies ran while one was open for 1% of the time, Pallas kernels for 0%

profile of v12, /device:TPU:0, one launch (start us, length us, event | category | flops | bytes accessed | tf_op | source)
XLA Modules:
  0.0 246.1 jit_solution(14954279565727791106)
XLA Ops:
  0.0 1.5 fusion.11
  1.5 1.3 collective-permute-start.1
  2.8 3.1 %collective-permute-start = (bf16[3,8,64,256]{3,2,1,0:T(8,128)(2,1)S(1)}, bf16[3,8,64,256]{3,2,1,0:T(8,128)(2,1)S(1)}, u32[]{:S(2)}, u32[]{:S(2)}) collective-permute-start(bf16[3,8,64,256]{3,2,1,0:T(8,128)(2,1)S(1)} %get-tuple-element.22.high_ref), channel_id=1, source_target_pairs={{0,1},{1,2},{2,3},{3,4},{4,5},{5,6},{6,7},{7,8},{8,9},{9,10},{10,1... | collective-permute-start | bytes 2359304 | tf_op jit(solution)/shard_map/ppermute | solution.py:214
  6.0 0.7 fusion.12
  9.3 0.6 add_convert_fusion.rim_ref
  9.9 1.6 broadcast_in_dim.8.low_pot_ref.high_pot_ref
  11.6 8.6 %shard_map.37 = (bf16[3,8,64,256]{3,2,1,0:T(8,128)(2,1)}, bf16[3,8,64,256]{3,2,1,0:T(8,128)(2,1)}) custom-call(f32[2]{0:T(128)} %add_convert_fusion.rim_ref, bf16[3,8,64,256]{3,2,1,0:T(8,128)(2,1)} %copy-done.3, bf16[3,8,64,256]{3,2,1,0:T(8,128)(2,1)} %copy-done, bf16[3,8,64,256]{3,2,1,0:T(8,128)(2,1)} %copy-done.1, bf16[3,8,64,256]{3,2,1,0:T(8,128)(2,1)} %copy-done.2, ...), custom_call_target="tpu_custom_call" | custom-call | tf_op jit(solution)/shard_map/pallas_call | solution.py:128
  20.2 16.8 %collective-permute-start.2 = (bf16[3,8,64,256]{3,2,1,0:T(8,128)(2,1)}, bf16[3,8,64,256]{3,2,1,0:T(8,128)(2,1)S(1)}, u32[]{:S(2)}, u32[]{:S(2)}) collective-permute-start(bf16[3,8,64,256]{3,2,1,0:T(8,128)(2,1)} %get-tuple-element.13.high_ref.older_high_ref), channel_id=1, source_target_pairs={{0,1},{1,2},{2,3},{3,4},{4,5},{5,6},{6,7},{7,8},{8,9},{9,10},{10,1... | collective-permute-start | bytes 2359304 | tf_op jit(solution)/shard_map/ppermute | solution.py:214
  36.9 1.3 collective-permute-start.3
  38.2 0.8 collective-permute-done.2.below_ref
  39.0 4.3 %collective-permute-done.3.above_ref = bf16[3,8,64,256]{3,2,1,0:T(8,128)(2,1)S(1)} collective-permute-done((bf16[3,8,64,256]{3,2,1,0:T(8,128)(2,1)}, bf16[3,8,64,256]{3,2,1,0:T(8,128)(2,1)S(1)}, u32[]{:S(2)}, u32[]{:S(2)}) %collective-permute-start.3) | collective-permute-done | bytes 786464 | tf_op jit(solution)/shard_map/ppermute | solution.py:215
  43.3 0.9 copy-done.5
  44.1 8.8 %shard_map.38 = (bf16[3,8,64,256]{3,2,1,0:T(8,128)(2,1)}, bf16[3,8,64,256]{3,2,1,0:T(8,128)(2,1)}) custom-call(f32[2]{0:T(128)} %add_convert_fusion.rim_ref, bf16[3,8,64,256]{3,2,1,0:T(8,128)(2,1)} %copy-done.4, bf16[3,8,64,256]{3,2,1,0:T(8,128)(2,1)} %get-tuple-element.14.low_ref.older_low_ref, ...), custom_call_target="tpu_custom_call" | custom-call | tf_op jit(solution)/shard_map/pallas_call | solution.py:128
  52.9 16.6 %collective-permute-start.4 = (bf16[3,8,64,256]{3,2,1,0:T(8,128)(2,1)}, bf16[3,8,64,256]{3,2,1,0:T(8,128)(2,1)S(1)}, u32[]{:S(2)}, u32[]{:S(2)}) collective-permute-start(bf16[3,8,64,256]{3,2,1,0:T(8,128)(2,1)} %get-tuple-element.15.high_ref.older_high_ref), channel_id=1, source_target_pairs={{0,1},{1,2},{2,3},{3,4},{4,5},{5,6},{6,7},{7,8},{8,9},{9,10},{10,1... | collective-permute-start | bytes 2359304 | tf_op jit(solution)/shard_map/ppermute | solution.py:214
  69.5 1.3 collective-permute-start.5
  70.8 0.8 collective-permute-done.4.below_ref
  71.6 4.2 %collective-permute-done.5.above_ref = bf16[3,8,64,256]{3,2,1,0:T(8,128)(2,1)S(1)} collective-permute-done((bf16[3,8,64,256]{3,2,1,0:T(8,128)(2,1)}, bf16[3,8,64,256]{3,2,1,0:T(8,128)(2,1)S(1)}, u32[]{:S(2)}, u32[]{:S(2)}) %collective-permute-start.5) | collective-permute-done | bytes 786464 | tf_op jit(solution)/shard_map/ppermute | solution.py:215
  75.7 0.9 copy-done.9
  76.6 8.8 %shard_map.39 = (bf16[3,8,64,256]{3,2,1,0:T(8,128)(2,1)}, bf16[3,8,64,256]{3,2,1,0:T(8,128)(2,1)}) custom-call(f32[2]{0:T(128)} %add_convert_fusion.rim_ref, bf16[3,8,64,256]{3,2,1,0:T(8,128)(2,1)} %copy-done.7, bf16[3,8,64,256]{3,2,1,0:T(8,128)(2,1)} %get-tuple-element.16.low_ref.older_low_ref, ...), custom_call_target="tpu_custom_call" | custom-call | tf_op jit(solution)/shard_map/pallas_call | solution.py:128
  85.4 16.6 %collective-permute-start.6 = (bf16[3,8,64,256]{3,2,1,0:T(8,128)(2,1)}, bf16[3,8,64,256]{3,2,1,0:T(8,128)(2,1)S(1)}, u32[]{:S(2)}, u32[]{:S(2)}) collective-permute-start(bf16[3,8,64,256]{3,2,1,0:T(8,128)(2,1)} %get-tuple-element.17.high_ref), channel_id=1, source_target_pairs={{0,1},{1,2},{2,3},{3,4},{4,5},{5,6},{6,7},{7,8},{8,9},{9,10},{10,1... | collective-permute-start | bytes 2359304 | tf_op jit(solution)/shard_map/ppermute | solution.py:214
  102.0 1.5 collective-permute-start.7
  103.5 0.6 collective-permute-done.6.below_ref
  104.1 4.2 %collective-permute-done.7.above_ref = bf16[3,8,64,256]{3,2,1,0:T(8,128)(2,1)S(1)} collective-permute-done((bf16[3,8,64,256]{3,2,1,0:T(8,128)(2,1)}, bf16[3,8,64,256]{3,2,1,0:T(8,128)(2,1)S(1)}, u32[]{:S(2)}, u32[]{:S(2)}) %collective-permute-start.7) | collective-permute-done | bytes 786464 | tf_op jit(solution)/shard_map/ppermute | solution.py:215
  108.3 0.9 copy-done.8
  109.2 8.8 %shard_map.40 = (bf16[3,8,64,256]{3,2,1,0:T(8,128)(2,1)}, bf16[3,8,64,256]{3,2,1,0:T(8,128)(2,1)}) custom-call(f32[2]{0:T(128)} %add_convert_fusion.rim_ref, bf16[3,8,64,256]{3,2,1,0:T(8,128)(2,1)} %copy-done.6, bf16[3,8,64,256]{3,2,1,0:T(8,128)(2,1)} %get-tuple-element.18.low_ref, bf16[3,8,64,256]{3,2,1,0:T(8,128)(2,1)} %get-tuple-element.17.high_ref, ...), custom_call_target="tpu_custom_call" | custom-call | tf_op jit(solution)/shard_map/pallas_call | solution.py:128
  117.9 1.5 pad_maximum_fusion
  119.4 0.4 fusion.2
  119.8 1.3 collective-permute-start.12
  121.1 17.2 %collective-permute-start.8 = (f32[128,256]{1,0:T(8,128)S(1)}, f32[128,256]{1,0:T(8,128)S(1)}, u32[]{:S(2)}, u32[]{:S(2)}) collective-permute-start(f32[128,256]{1,0:T(8,128)S(1)} %fusion.2), channel_id=1, source_target_pairs={{0,1},{1,2},{2,3},{3,4},{4,5},{5,6},{6,7},{7,8},{8,9},{9,10},{10,1... | collective-permute-start | bytes 393224 | tf_op jit(solution)/shard_map/ppermute | solution.py:242
  138.4 0.9 collective-permute-done.8
  139.3 7.6 %collective-permute-start.9 = (f32[128,256]{1,0:T(8,128)S(1)}, f32[128,256]{1,0:T(8,128)S(1)}, u32[]{:S(2)}, u32[]{:S(2)}) collective-permute-start(f32[128,256]{1,0:T(8,128)S(1)} %get-tuple-element.23), channel_id=1, source_target_pairs={{0,2},{1,3},{2,4},{3,5},{4,6},{5,7},{6,8},{7,9},{8,10},{9,11},{10,... | collective-permute-start | bytes 393224 | tf_op jit(solution)/shard_map/ppermute | solution.py:242
  152.0 1.3 collective-permute-start.13
  153.3 5.3 %collective-permute-start.10 = (f32[128,256]{1,0:T(8,128)S(1)}, f32[128,256]{1,0:T(8,128)S(1)}, u32[]{:S(2)}, u32[]{:S(2)}) collective-permute-start(f32[128,256]{1,0:T(8,128)S(1)} %multiply_add_fusion.4), channel_id=1, source_target_pairs={{0,4},{1,5},{2,6},{3,7},{4,8},{5,9},{6,10},{7,11},{8,12},{9,13},{1... | collective-permute-start | bytes 393224 | tf_op jit(solution)/shard_map/ppermute | solution.py:242
  158.6 0.2 collective-permute-done.13
  158.8 1.3 collective-permute-start.14
  160.1 1.3 collective-permute-done.10
  161.5 3.6 %collective-permute-start.11 = (f32[128,256]{1,0:T(8,128)S(1)}, f32[128,256]{1,0:T(8,128)S(1)}, u32[]{:S(2)}, u32[]{:S(2)}) collective-permute-start(f32[128,256]{1,0:T(8,128)S(1)} %multiply_add_fusion.3), channel_id=1, source_target_pairs={{0,8},{1,9},{2,10},{3,11},{4,12},{5,13},{6,14},{7,15},{16,24},{17,... | collective-permute-start | bytes 393224 | tf_op jit(solution)/shard_map/ppermute | solution.py:242
  165.1 0.6 collective-permute-done.14
  165.7 1.3 collective-permute-start.15
  169.5 1.2 fusion.10
  171.4 3.2 %collective-permute-done.15 = f32[128,256]{1,0:T(8,128)S(1)} collective-permute-done((f32[128,256]{1,0:T(8,128)S(1)}, f32[128,256]{1,0:T(8,128)S(1)}, u32[]{:S(2)}, u32[]{:S(2)}) %collective-permute-start.15) | collective-permute-done | bytes 131104 | tf_op jit(solution)/shard_map/ppermute | solution.py:243
  174.7 0.6 slice.25.gram_ref
  175.3 16.6 %shard_map.41 = f32[128,128]{1,0:T(8,128)} custom-call(f32[128,128]{1,0:T(8,128)} %slice.25.gram_ref), custom_call_target="tpu_custom_call" | custom-call | tf_op jit(solution)/shard_map/pallas_call | solution.py:60
  192.0 1.3 convolution_convert_fusion.1
  193.3 0.5 fusion
  193.8 0.4 fusion.13
  194.2 1.3 collective-permute-start.20
  195.5 3.0 %collective-permute-start.16 = (f32[128,128]{1,0:T(8,128)S(1)}, f32[128,128]{1,0:T(8,128)S(1)}, u32[]{:S(2)}, u32[]{:S(2)}) collective-permute-start(f32[128,128]{1,0:T(8,128)S(1)} %fusion.13), channel_id=1, source_target_pairs={{0,1},{1,2},{2,3},{3,4},{4,5},{5,6},{6,7},{7,8},{8,9},{9,10},{10,1... | collective-permute-start | bytes 196616 | tf_op jit(solution)/shard_map/ppermute | solution.py:242
  198.5 0.9 collective-permute-done.16
  199.4 5.7 %collective-permute-start.17 = (f32[128,128]{1,0:T(8,128)S(1)}, f32[128,128]{1,0:T(8,128)S(1)}, u32[]{:S(2)}, u32[]{:S(2)}) collective-permute-start(f32[128,128]{1,0:T(8,128)S(1)} %get-tuple-element.25), channel_id=1, source_target_pairs={{0,2},{1,3},{2,4},{3,5},{4,6},{5,7},{6,8},{7,9},{8,10},{9,11},{10,... | collective-permute-start | bytes 196616 | tf_op jit(solution)/shard_map/ppermute | solution.py:242
  205.1 1.3 collective-permute-start.21
  206.4 1.2 collective-permute-done.17
  207.6 4.4 %collective-permute-start.18 = (f32[128,128]{1,0:T(8,128)S(1)}, f32[128,128]{1,0:T(8,128)S(1)}, u32[]{:S(2)}, u32[]{:S(2)}) collective-permute-start(f32[128,128]{1,0:T(8,128)S(1)} %multiply_add_fusion.10), channel_id=1, source_target_pairs={{0,4},{1,5},{2,6},{3,7},{4,8},{5,9},{6,10},{7,11},{8,12},{9,13},{1... | collective-permute-start | bytes 196616 | tf_op jit(solution)/shard_map/ppermute | solution.py:242
  212.0 1.3 collective-permute-start.22
  213.3 0.6 collective-permute-done.18
  213.9 4.2 %collective-permute-start.19 = (f32[128,128]{1,0:T(8,128)S(1)}, f32[128,128]{1,0:T(8,128)S(1)}, u32[]{:S(2)}, u32[]{:S(2)}) collective-permute-start(f32[128,128]{1,0:T(8,128)S(1)} %multiply_add_fusion.9), channel_id=1, source_target_pairs={{0,8},{1,9},{2,10},{3,11},{4,12},{5,13},{6,14},{7,15},{16,24},{17,... | collective-permute-start | bytes 196616 | tf_op jit(solution)/shard_map/ppermute | solution.py:242
  218.2 1.3 collective-permute-start.23
  219.5 0.5 collective-permute-done.19
  220.0 5.9 %collective-permute-done.23 = f32[128,128]{1,0:T(8,128)S(1)} collective-permute-done((f32[128,128]{1,0:T(8,128)S(1)}, f32[128,128]{1,0:T(8,128)S(1)}, u32[]{:S(2)}, u32[]{:S(2)}) %collective-permute-start.23) | collective-permute-done | bytes 65568 | tf_op jit(solution)/shard_map/ppermute | solution.py:243
  226.0 0.7 subtract_divide_fusion.1.gram_ref
  226.6 16.6 %shard_map.42 = f32[128,128]{1,0:T(8,128)} custom-call(f32[128,128]{1,0:T(8,128)} %subtract_divide_fusion.1.gram_ref), custom_call_target="tpu_custom_call" | custom-call | tf_op jit(solution)/shard_map/pallas_call | solution.py:60
  243.3 1.2 convolution_convert_fusion
  244.5 0.1 pad_maximum_fusion.1
  244.6 1.6 copy.5
  (43 shorter events, 0.4 us)
Async XLA Ops:
  0.0 5.9 %copy-start.11 = (s32[16]{0:T(128)S(1)}, s32[16]{0:T(128)}, u32[]{:S(2)}) copy-start(s32[16]{0:T(128)} %param.5) | copy-start | bytes 196
  0.0 9.3 %copy-start.12 = (f32[6,512]{1,0:T(8,128)S(1)}, f32[6,512]{1,0:T(8,128)}, u32[]{:S(2)}) copy-start(f32[6,512]{1,0:T(8,128)} %param.4) | copy-start | bytes 36868
  1.5 10.1 %copy-start = (bf16[3,8,64,256]{3,2,1,0:T(8,128)(2,1)}, bf16[3,8,64,256]{3,2,1,0:T(8,128)(2,1)S(1)}, u32[]{:S(2)}) copy-start(bf16[3,8,64,256]{3,2,1,0:T(8,128)(2,1)S(1)} %get-tuple-element.21.low_ref) | copy-start | bytes 2359300
  1.5 10.1 %copy-start.1 = (bf16[3,8,64,256]{3,2,1,0:T(8,128)(2,1)}, bf16[3,8,64,256]{3,2,1,0:T(8,128)(2,1)S(1)}, u32[]{:S(2)}) copy-start(bf16[3,8,64,256]{3,2,1,0:T(8,128)(2,1)S(1)} %get-tuple-element.22.high_ref) | copy-start | bytes 2359300
  1.5 8.4 %collective-permute-start.1 = (bf16[3,8,64,256]{3,2,1,0:T(8,128)(2,1)S(1)}, bf16[3,8,64,256]{3,2,1,0:T(8,128)(2,1)S(1)}, u32[]{:S(2)}, u32[]{:S(2)}) collective-permute-start(bf16[3,8,64,256]{3,2,1,0:T(8,128)(2,1)S(1)} %get-tuple-element.21.low_ref), channel_id=1, source_target_pairs={{1,0},{2,1},{3,2},{4,3},{5,4},{6,5},{7,6},{8,7},{9,8},{10,9},{11,1... | collective-permute-start | bytes 2359304 | tf_op jit(solution)/shard_map/ppermute | solution.py:215
  2.8 7.1 %collective-permute-start = (bf16[3,8,64,256]{3,2,1,0:T(8,128)(2,1)S(1)}, bf16[3,8,64,256]{3,2,1,0:T(8,128)(2,1)S(1)}, u32[]{:S(2)}, u32[]{:S(2)}) collective-permute-start(bf16[3,8,64,256]{3,2,1,0:T(8,128)(2,1)S(1)} %get-tuple-element.22.high_ref), channel_id=1, source_target_pairs={{0,1},{1,2},{2,3},{3,4},{4,5},{5,6},{6,7},{7,8},{8,9},{9,10},{10,1... | collective-permute-start | bytes 2359304 | tf_op jit(solution)/shard_map/ppermute | solution.py:214
  9.9 1.7 copy-start.2
  9.9 1.7 copy-start.3
  20.2 18.8 %collective-permute-start.2 = (bf16[3,8,64,256]{3,2,1,0:T(8,128)(2,1)}, bf16[3,8,64,256]{3,2,1,0:T(8,128)(2,1)S(1)}, u32[]{:S(2)}, u32[]{:S(2)}) collective-permute-start(bf16[3,8,64,256]{3,2,1,0:T(8,128)(2,1)} %get-tuple-element.13.high_ref.older_high_ref), channel_id=1, source_target_pairs={{0,1},{1,2},{2,3},{3,4},{4,5},{5,6},{6,7},{7,8},{8,9},{9,10},{10,1... | collective-permute-start | bytes 2359304 | tf_op jit(solution)/shard_map/ppermute | solution.py:214
  36.9 6.3 %collective-permute-start.3 = (bf16[3,8,64,256]{3,2,1,0:T(8,128)(2,1)}, bf16[3,8,64,256]{3,2,1,0:T(8,128)(2,1)S(1)}, u32[]{:S(2)}, u32[]{:S(2)}) collective-permute-start(bf16[3,8,64,256]{3,2,1,0:T(8,128)(2,1)} %get-tuple-element.14.low_ref.older_low_ref), channel_id=1, source_target_pairs={{1,0},{2,1},{3,2},{4,3},{5,4},{6,5},{7,6},{8,7},{9,8},{10,9},{11,1... | collective-permute-start | bytes 2359304 | tf_op jit(solution)/shard_map/ppermute | solution.py:215
  39.0 4.3 %copy-start.4 = (bf16[3,8,64,256]{3,2,1,0:T(8,128)(2,1)}, bf16[3,8,64,256]{3,2,1,0:T(8,128)(2,1)S(1)}, u32[]{:S(2)}) copy-start(bf16[3,8,64,256]{3,2,1,0:T(8,128)(2,1)S(1)} %collective-permute-done.2.below_ref) | copy-start | bytes 2359300
  43.3 0.9 copy-start.5
  52.9 18.6 %collective-permute-start.4 = (bf16[3,8,64,256]{3,2,1,0:T(8,128)(2,1)}, bf16[3,8,64,256]{3,2,1,0:T(8,128)(2,1)S(1)}, u32[]{:S(2)}, u32[]{:S(2)}) collective-permute-start(bf16[3,8,64,256]{3,2,1,0:T(8,128)(2,1)} %get-tuple-element.15.high_ref.older_high_ref), channel_id=1, source_target_pairs={{0,1},{1,2},{2,3},{3,4},{4,5},{5,6},{6,7},{7,8},{8,9},{9,10},{10,1... | collective-permute-start | bytes 2359304 | tf_op jit(solution)/shard_map/ppermute | solution.py:214
  69.5 6.2 %collective-permute-start.5 = (bf16[3,8,64,256]{3,2,1,0:T(8,128)(2,1)}, bf16[3,8,64,256]{3,2,1,0:T(8,128)(2,1)S(1)}, u32[]{:S(2)}, u32[]{:S(2)}) collective-permute-start(bf16[3,8,64,256]{3,2,1,0:T(8,128)(2,1)} %get-tuple-element.16.low_ref.older_low_ref), channel_id=1, source_target_pairs={{1,0},{2,1},{3,2},{4,3},{5,4},{6,5},{7,6},{8,7},{9,8},{10,9},{11,1... | collective-permute-start | bytes 2359304 | tf_op jit(solution)/shard_map/ppermute | solution.py:215
  71.6 4.2 %copy-start.7 = (bf16[3,8,64,256]{3,2,1,0:T(8,128)(2,1)}, bf16[3,8,64,256]{3,2,1,0:T(8,128)(2,1)S(1)}, u32[]{:S(2)}) copy-start(bf16[3,8,64,256]{3,2,1,0:T(8,128)(2,1)S(1)} %collective-permute-done.4.below_ref) | copy-start | bytes 2359300
  75.7 0.9 copy-start.9
  85.4 18.7 %collective-permute-start.6 = (bf16[3,8,64,256]{3,2,1,0:T(8,128)(2,1)}, bf16[3,8,64,256]{3,2,1,0:T(8,128)(2,1)S(1)}, u32[]{:S(2)}, u32[]{:S(2)}) collective-permute-start(bf16[3,8,64,256]{3,2,1,0:T(8,128)(2,1)} %get-tuple-element.17.high_ref), channel_id=1, source_target_pairs={{0,1},{1,2},{2,3},{3,4},{4,5},{5,6},{6,7},{7,8},{8,9},{9,10},{10,1... | collective-permute-start | bytes 2359304 | tf_op jit(solution)/shard_map/ppermute | solution.py:214
  102.0 6.2 %collective-permute-start.7 = (bf16[3,8,64,256]{3,2,1,0:T(8,128)(2,1)}, bf16[3,8,64,256]{3,2,1,0:T(8,128)(2,1)S(1)}, u32[]{:S(2)}, u32[]{:S(2)}) collective-permute-start(bf16[3,8,64,256]{3,2,1,0:T(8,128)(2,1)} %get-tuple-element.18.low_ref), channel_id=1, source_target_pairs={{1,0},{2,1},{3,2},{4,3},{5,4},{6,5},{7,6},{8,7},{9,8},{10,9},{11,1... | collective-permute-start | bytes 2359304 | tf_op jit(solution)/shard_map/ppermute | solution.py:215
  104.1 4.2 %copy-start.6 = (bf16[3,8,64,256]{3,2,1,0:T(8,128)(2,1)}, bf16[3,8,64,256]{3,2,1,0:T(8,128)(2,1)S(1)}, u32[]{:S(2)}) copy-start(bf16[3,8,64,256]{3,2,1,0:T(8,128)(2,1)S(1)} %collective-permute-done.6.below_ref) | copy-start | bytes 2359300
  108.3 0.9 copy-start.8
  119.8 18.5 %collective-permute-start.12 = (f32[128,256]{1,0:T(8,128)S(1)}, f32[128,256]{1,0:T(8,128)S(1)}, u32[]{:S(2)}, u32[]{:S(2)}) collective-permute-start(f32[128,256]{1,0:T(8,128)S(1)} %fusion.2), channel_id=1, source_target_pairs={{1,0},{2,1},{3,2},{4,3},{5,4},{6,5},{7,6},{8,7},{9,8},{10,9},{11,1... | collective-permute-start | bytes 393224 | tf_op jit(solution)/shard_map/ppermute | solution.py:243
  121.1 18.2 %collective-permute-start.8 = (f32[128,256]{1,0:T(8,128)S(1)}, f32[128,256]{1,0:T(8,128)S(1)}, u32[]{:S(2)}, u32[]{:S(2)}) collective-permute-start(f32[128,256]{1,0:T(8,128)S(1)} %fusion.2), channel_id=1, source_target_pairs={{0,1},{1,2},{2,3},{3,4},{4,5},{5,6},{6,7},{7,8},{8,9},{9,10},{10,1... | collective-permute-start | bytes 393224 | tf_op jit(solution)/shard_map/ppermute | solution.py:242
  139.3 13.9 %collective-permute-start.9 = (f32[128,256]{1,0:T(8,128)S(1)}, f32[128,256]{1,0:T(8,128)S(1)}, u32[]{:S(2)}, u32[]{:S(2)}) collective-permute-start(f32[128,256]{1,0:T(8,128)S(1)} %get-tuple-element.23), channel_id=1, source_target_pairs={{0,2},{1,3},{2,4},{3,5},{4,6},{5,7},{6,8},{7,9},{8,10},{9,11},{10,... | collective-permute-start | bytes 393224 | tf_op jit(solution)/shard_map/ppermute | solution.py:242
  152.0 6.9 %collective-permute-start.13 = (f32[128,256]{1,0:T(8,128)S(1)}, f32[128,256]{1,0:T(8,128)S(1)}, u32[]{:S(2)}, u32[]{:S(2)}) collective-permute-start(f32[128,256]{1,0:T(8,128)S(1)} %get-tuple-element.24), channel_id=1, source_target_pairs={{2,0},{3,1},{4,2},{5,3},{6,4},{7,5},{8,6},{9,7},{10,8},{11,9},{12,... | collective-permute-start | bytes 393224 | tf_op jit(solution)/shard_map/ppermute | solution.py:243
  153.3 8.2 %collective-permute-start.10 = (f32[128,256]{1,0:T(8,128)S(1)}, f32[128,256]{1,0:T(8,128)S(1)}, u32[]{:S(2)}, u32[]{:S(2)}) collective-permute-start(f32[128,256]{1,0:T(8,128)S(1)} %multiply_add_fusion.4), channel_id=1, source_target_pairs={{0,4},{1,5},{2,6},{3,7},{4,8},{5,9},{6,10},{7,11},{8,12},{9,13},{1... | collective-permute-start | bytes 393224 | tf_op jit(solution)/shard_map/ppermute | solution.py:242
  158.8 6.9 %collective-permute-start.14 = (f32[128,256]{1,0:T(8,128)S(1)}, f32[128,256]{1,0:T(8,128)S(1)}, u32[]{:S(2)}, u32[]{:S(2)}) collective-permute-start(f32[128,256]{1,0:T(8,128)S(1)} %multiply_add_fusion.1), channel_id=1, source_target_pairs={{4,0},{5,1},{6,2},{7,3},{8,4},{9,5},{10,6},{11,7},{12,8},{13,9},{1... | collective-permute-start | bytes 393224 | tf_op jit(solution)/shard_map/ppermute | solution.py:243
  161.5 10.0 %collective-permute-start.11 = (f32[128,256]{1,0:T(8,128)S(1)}, f32[128,256]{1,0:T(8,128)S(1)}, u32[]{:S(2)}, u32[]{:S(2)}) collective-permute-start(f32[128,256]{1,0:T(8,128)S(1)} %multiply_add_fusion.3), channel_id=1, source_target_pairs={{0,8},{1,9},{2,10},{3,11},{4,12},{5,13},{6,14},{7,15},{16,24},{17,... | collective-permute-start | bytes 393224 | tf_op jit(solution)/shard_map/ppermute | solution.py:242
  165.7 8.9 %collective-permute-start.15 = (f32[128,256]{1,0:T(8,128)S(1)}, f32[128,256]{1,0:T(8,128)S(1)}, u32[]{:S(2)}, u32[]{:S(2)}) collective-permute-start(f32[128,256]{1,0:T(8,128)S(1)} %multiply_add_fusion), channel_id=1, source_target_pairs={{8,0},{9,1},{10,2},{11,3},{12,4},{13,5},{14,6},{15,7},{24,16},{25,... | collective-permute-start | bytes 393224 | tf_op jit(solution)/shard_map/ppermute | solution.py:243
  192.0 1.3 copy-start.10
  194.2 4.3 %collective-permute-start.20 = (f32[128,128]{1,0:T(8,128)S(1)}, f32[128,128]{1,0:T(8,128)S(1)}, u32[]{:S(2)}, u32[]{:S(2)}) collective-permute-start(f32[128,128]{1,0:T(8,128)S(1)} %fusion.13), channel_id=1, source_target_pairs={{1,0},{2,1},{3,2},{4,3},{5,4},{6,5},{7,6},{8,7},{9,8},{10,9},{11,1... | collective-permute-start | bytes 196616 | tf_op jit(solution)/shard_map/ppermute | solution.py:243
  195.5 3.9 %collective-permute-start.16 = (f32[128,128]{1,0:T(8,128)S(1)}, f32[128,128]{1,0:T(8,128)S(1)}, u32[]{:S(2)}, u32[]{:S(2)}) collective-permute-start(f32[128,128]{1,0:T(8,128)S(1)} %fusion.13), channel_id=1, source_target_pairs={{0,1},{1,2},{2,3},{3,4},{4,5},{5,6},{6,7},{7,8},{8,9},{9,10},{10,1... | collective-permute-start | bytes 196616 | tf_op jit(solution)/shard_map/ppermute | solution.py:242
  199.4 8.2 %collective-permute-start.17 = (f32[128,128]{1,0:T(8,128)S(1)}, f32[128,128]{1,0:T(8,128)S(1)}, u32[]{:S(2)}, u32[]{:S(2)}) collective-permute-start(f32[128,128]{1,0:T(8,128)S(1)} %get-tuple-element.25), channel_id=1, source_target_pairs={{0,2},{1,3},{2,4},{3,5},{4,6},{5,7},{6,8},{7,9},{8,10},{9,11},{10,... | collective-permute-start | bytes 196616 | tf_op jit(solution)/shard_map/ppermute | solution.py:242
  205.1 6.9 %collective-permute-start.21 = (f32[128,128]{1,0:T(8,128)S(1)}, f32[128,128]{1,0:T(8,128)S(1)}, u32[]{:S(2)}, u32[]{:S(2)}) collective-permute-start(f32[128,128]{1,0:T(8,128)S(1)} %get-tuple-element.26), channel_id=1, source_target_pairs={{2,0},{3,1},{4,2},{5,3},{6,4},{7,5},{8,6},{9,7},{10,8},{11,9},{12,... | collective-permute-start | bytes 196616 | tf_op jit(solution)/shard_map/ppermute | solution.py:243
  207.6 6.3 %collective-permute-start.18 = (f32[128,128]{1,0:T(8,128)S(1)}, f32[128,128]{1,0:T(8,128)S(1)}, u32[]{:S(2)}, u32[]{:S(2)}) collective-permute-start(f32[128,128]{1,0:T(8,128)S(1)} %multiply_add_fusion.10), channel_id=1, source_target_pairs={{0,4},{1,5},{2,6},{3,7},{4,8},{5,9},{6,10},{7,11},{8,12},{9,13},{1... | collective-permute-start | bytes 196616 | tf_op jit(solution)/shard_map/ppermute | solution.py:242
  212.0 6.2 %collective-permute-start.22 = (f32[128,128]{1,0:T(8,128)S(1)}, f32[128,128]{1,0:T(8,128)S(1)}, u32[]{:S(2)}, u32[]{:S(2)}) collective-permute-start(f32[128,128]{1,0:T(8,128)S(1)} %multiply_add_fusion.7), channel_id=1, source_target_pairs={{4,0},{5,1},{6,2},{7,3},{8,4},{9,5},{10,6},{11,7},{12,8},{13,9},{1... | collective-permute-start | bytes 196616 | tf_op jit(solution)/shard_map/ppermute | solution.py:243
  213.9 6.1 %collective-permute-start.19 = (f32[128,128]{1,0:T(8,128)S(1)}, f32[128,128]{1,0:T(8,128)S(1)}, u32[]{:S(2)}, u32[]{:S(2)}) collective-permute-start(f32[128,128]{1,0:T(8,128)S(1)} %multiply_add_fusion.9), channel_id=1, source_target_pairs={{0,8},{1,9},{2,10},{3,11},{4,12},{5,13},{6,14},{7,15},{16,24},{17,... | collective-permute-start | bytes 196616 | tf_op jit(solution)/shard_map/ppermute | solution.py:242
  218.2 7.8 %collective-permute-start.23 = (f32[128,128]{1,0:T(8,128)S(1)}, f32[128,128]{1,0:T(8,128)S(1)}, u32[]{:S(2)}, u32[]{:S(2)}) collective-permute-start(f32[128,128]{1,0:T(8,128)S(1)} %multiply_add_fusion.6), channel_id=1, source_target_pairs={{8,0},{9,1},{10,2},{11,3},{12,4},{13,5},{14,6},{15,7},{24,16},{25,... | collective-permute-start | bytes 196616 | tf_op jit(solution)/shard_map/ppermute | solution.py:243

commit v13 on v12

--- a/solution.py
+++ b/solution.py
@@ -25,7 +25,6 @@
     work_ref[:, n:] = (lax.broadcasted_iota(jnp.int32, (n, n), 0) == lax.broadcasted_iota(jnp.int32, (n, n), 1)).astype(jnp.float32)
 
     rows = lax.broadcasted_iota(jnp.int32, (n, 2 * n), 0)
-    left_lanes = lax.broadcasted_iota(jnp.int32, (n, n), 1)
     lane = lax.broadcasted_iota(jnp.int32, (1, 2 * n), 1)
 
     def pick(vector, index):
@@ -35,15 +34,18 @@
         k = 2 * pair
         row_a = work_ref[pl.ds(k, 1), :]
         row_b = work_ref[pl.ds(k + 1, 1), :]
+        first_row, second_row = row_a, row_b
         scale_a = 1.0 / jnp.sqrt(pick(row_a, k))
         scaled_a = row_a * scale_a
         row_b = row_b - (pick(row_b, k) * scale_a) * scaled_a
         scale_b = 1.0 / jnp.sqrt(pick(row_b, k + 1))
         scaled_b = row_b * scale_b
         whole = work_ref[...]
-        left = whole[:, :n]
-        column_a = jnp.sum(jnp.where(left_lanes == k, left, 0.0), axis=1, keepdims=True) * scale_a
-        next_column = jnp.sum(jnp.where(left_lanes == k + 1, left, 0.0), axis=1, keepdims=True)
+        sub = lax.broadcasted_iota(jnp.int32, (n, n), 0)
+        pivots = jnp.where(sub == 0, first_row[:, :n], jnp.where(sub == 1, second_row[:, :n], 0.0))
+        columns = pivots.T
+        column_a = columns[:, 0:1] * scale_a
+        next_column = columns[:, 1:2]
         column_b = (next_column - column_a * pick(scaled_a, k + 1)) * scale_b
         updated = (whole - column_a * scaled_a) - column_b * scaled_b
         updated = jnp.where(rows > k + 1, updated, whole)

time: 247 us -> 266 us (1.077)
  Pallas kernels: 68.2 us -> 86.5 us
    pallas_call x2, Pallas kernels: 33.3 us -> 51.6 us  [lower_inverse(): pl.pallas_call(_lower_inverse_kernel, out_shape=jax.ShapeDtypeStruct((n,...]
where the time goes in v13:
time: 266 us; the launch traced here: 264 us
  starting transfers between devices  120 us (45%)
  Pallas kernels  86.5 us (33%)
  waiting for transfers between devices  30.1 us (11%)
  between operations  11.3 us (4%)
  local copies, waits for them, and re-layouts  8.82 us (3%)
  other arithmetic  4.28 us (2%)
  matrix products  3.8 us (1%)
    ppermute x4, starting transfers between devices, rimmed(): from_below = lax.ppermute(high, 'gz', forward)  53 us
    pallas_call x2, Pallas kernels, lower_inverse(): pl.pallas_call(_lower_inverse_kernel, out_shape=jax.ShapeDtypeStruct((n,...  51.6 us
    ppermute x8, starting transfers between devices, domain_total(): from_low = lax.ppermute(forward, 'gz', ahead)  51 us
    pallas_call x4, Pallas kernels, chebyshev_step(): pl.pallas_call(functools.partial(_step_kernel, first), out_shape=(piece,...  34.9 us
    ppermute x4, waiting for transfers between devices, rimmed(): from_above = lax.ppermute(low, 'gz', backward)  12.6 us
    ppermute x8, starting transfers between devices, domain_total(): from_high = lax.ppermute(backward, 'gz', behind)  10.3 us
    ppermute x8, waiting for transfers between devices, domain_total(): from_high = lax.ppermute(backward, 'gz', behind)  10 us
    ppermute x8, waiting for transfers between devices, domain_total(): from_low = lax.ppermute(forward, 'gz', ahead)  5.39 us
  transfers between devices with their start and end apart: 24, of which 16 were waited for; matrix products, arithmetic and copies ran while one was open for 1% of the time, Pallas kernels for 0%

profile of v13, /device:TPU:0, one launch (start us, length us, event | category | flops | bytes accessed | tf_op | source)
XLA Modules:
  0.0 264.5 jit_solution(8309185177946090016)
XLA Ops:
  0.0 1.5 fusion.11
  1.5 1.3 collective-permute-start.1
  2.8 3.1 %collective-permute-start = (bf16[3,8,64,256]{3,2,1,0:T(8,128)(2,1)S(1)}, bf16[3,8,64,256]{3,2,1,0:T(8,128)(2,1)S(1)}, u32[]{:S(2)}, u32[]{:S(2)}) collective-permute-start(bf16[3,8,64,256]{3,2,1,0:T(8,128)(2,1)S(1)} %get-tuple-element.22.high_ref), channel_id=1, source_target_pairs={{0,1},{1,2},{2,3},{3,4},{4,5},{5,6},{6,7},{7,8},{8,9},{9,10},{10,1... | collective-permute-start | bytes 2359304 | tf_op jit(solution)/shard_map/ppermute | solution.py:216
  6.0 0.7 fusion.12
  9.3 0.6 add_convert_fusion.rim_ref
  9.9 1.6 broadcast_in_dim.8.low_pot_ref.high_pot_ref
  11.6 8.6 %shard_map.37 = (bf16[3,8,64,256]{3,2,1,0:T(8,128)(2,1)}, bf16[3,8,64,256]{3,2,1,0:T(8,128)(2,1)}) custom-call(f32[2]{0:T(128)} %add_convert_fusion.rim_ref, bf16[3,8,64,256]{3,2,1,0:T(8,128)(2,1)} %copy-done.3, bf16[3,8,64,256]{3,2,1,0:T(8,128)(2,1)} %copy-done, bf16[3,8,64,256]{3,2,1,0:T(8,128)(2,1)} %copy-done.1, bf16[3,8,64,256]{3,2,1,0:T(8,128)(2,1)} %copy-done.2, ...), custom_call_target="tpu_custom_call" | custom-call | tf_op jit(solution)/shard_map/pallas_call | solution.py:130
  20.2 16.8 %collective-permute-start.2 = (bf16[3,8,64,256]{3,2,1,0:T(8,128)(2,1)}, bf16[3,8,64,256]{3,2,1,0:T(8,128)(2,1)S(1)}, u32[]{:S(2)}, u32[]{:S(2)}) collective-permute-start(bf16[3,8,64,256]{3,2,1,0:T(8,128)(2,1)} %get-tuple-element.13.high_ref.older_high_ref), channel_id=1, source_target_pairs={{0,1},{1,2},{2,3},{3,4},{4,5},{5,6},{6,7},{7,8},{8,9},{9,10},{10,1... | collective-permute-start | bytes 2359304 | tf_op jit(solution)/shard_map/ppermute | solution.py:216
  36.9 1.3 collective-permute-start.3
  38.2 0.8 collective-permute-done.2.below_ref
  39.0 4.3 %collective-permute-done.3.above_ref = bf16[3,8,64,256]{3,2,1,0:T(8,128)(2,1)S(1)} collective-permute-done((bf16[3,8,64,256]{3,2,1,0:T(8,128)(2,1)}, bf16[3,8,64,256]{3,2,1,0:T(8,128)(2,1)S(1)}, u32[]{:S(2)}, u32[]{:S(2)}) %collective-permute-start.3) | collective-permute-done | bytes 786464 | tf_op jit(solution)/shard_map/ppermute | solution.py:217
  43.3 0.9 copy-done.5
  44.1 8.8 %shard_map.38 = (bf16[3,8,64,256]{3,2,1,0:T(8,128)(2,1)}, bf16[3,8,64,256]{3,2,1,0:T(8,128)(2,1)}) custom-call(f32[2]{0:T(128)} %add_convert_fusion.rim_ref, bf16[3,8,64,256]{3,2,1,0:T(8,128)(2,1)} %copy-done.4, bf16[3,8,64,256]{3,2,1,0:T(8,128)(2,1)} %get-tuple-element.14.low_ref.older_low_ref, ...), custom_call_target="tpu_custom_call" | custom-call | tf_op jit(solution)/shard_map/pallas_call | solution.py:130
  52.9 16.6 %collective-permute-start.4 = (bf16[3,8,64,256]{3,2,1,0:T(8,128)(2,1)}, bf16[3,8,64,256]{3,2,1,0:T(8,128)(2,1)S(1)}, u32[]{:S(2)}, u32[]{:S(2)}) collective-permute-start(bf16[3,8,64,256]{3,2,1,0:T(8,128)(2,1)} %get-tuple-element.15.high_ref.older_high_ref), channel_id=1, source_target_pairs={{0,1},{1,2},{2,3},{3,4},{4,5},{5,6},{6,7},{7,8},{8,9},{9,10},{10,1... | collective-permute-start | bytes 2359304 | tf_op jit(solution)/shard_map/ppermute | solution.py:216
  69.5 1.3 collective-permute-start.5
  70.8 0.8 collective-permute-done.4.below_ref
  71.6 4.2 %collective-permute-done.5.above_ref = bf16[3,8,64,256]{3,2,1,0:T(8,128)(2,1)S(1)} collective-permute-done((bf16[3,8,64,256]{3,2,1,0:T(8,128)(2,1)}, bf16[3,8,64,256]{3,2,1,0:T(8,128)(2,1)S(1)}, u32[]{:S(2)}, u32[]{:S(2)}) %collective-permute-start.5) | collective-permute-done | bytes 786464 | tf_op jit(solution)/shard_map/ppermute | solution.py:217
  75.7 0.9 copy-done.9
  76.6 8.8 %shard_map.39 = (bf16[3,8,64,256]{3,2,1,0:T(8,128)(2,1)}, bf16[3,8,64,256]{3,2,1,0:T(8,128)(2,1)}) custom-call(f32[2]{0:T(128)} %add_convert_fusion.rim_ref, bf16[3,8,64,256]{3,2,1,0:T(8,128)(2,1)} %copy-done.7, bf16[3,8,64,256]{3,2,1,0:T(8,128)(2,1)} %get-tuple-element.16.low_ref.older_low_ref, ...), custom_call_target="tpu_custom_call" | custom-call | tf_op jit(solution)/shard_map/pallas_call | solution.py:130
  85.4 16.6 %collective-permute-start.6 = (bf16[3,8,64,256]{3,2,1,0:T(8,128)(2,1)}, bf16[3,8,64,256]{3,2,1,0:T(8,128)(2,1)S(1)}, u32[]{:S(2)}, u32[]{:S(2)}) collective-permute-start(bf16[3,8,64,256]{3,2,1,0:T(8,128)(2,1)} %get-tuple-element.17.high_ref), channel_id=1, source_target_pairs={{0,1},{1,2},{2,3},{3,4},{4,5},{5,6},{6,7},{7,8},{8,9},{9,10},{10,1... | collective-permute-start | bytes 2359304 | tf_op jit(solution)/shard_map/ppermute | solution.py:216
  102.0 1.5 collective-permute-start.7
  103.5 0.6 collective-permute-done.6.below_ref
  104.1 4.2 %collective-permute-done.7.above_ref = bf16[3,8,64,256]{3,2,1,0:T(8,128)(2,1)S(1)} collective-permute-done((bf16[3,8,64,256]{3,2,1,0:T(8,128)(2,1)}, bf16[3,8,64,256]{3,2,1,0:T(8,128)(2,1)S(1)}, u32[]{:S(2)}, u32[]{:S(2)}) %collective-permute-start.7) | collective-permute-done | bytes 786464 | tf_op jit(solution)/shard_map/ppermute | solution.py:217
  108.3 0.9 copy-done.8
  109.2 8.8 %shard_map.40 = (bf16[3,8,64,256]{3,2,1,0:T(8,128)(2,1)}, bf16[3,8,64,256]{3,2,1,0:T(8,128)(2,1)}) custom-call(f32[2]{0:T(128)} %add_convert_fusion.rim_ref, bf16[3,8,64,256]{3,2,1,0:T(8,128)(2,1)} %copy-done.6, bf16[3,8,64,256]{3,2,1,0:T(8,128)(2,1)} %get-tuple-element.18.low_ref, bf16[3,8,64,256]{3,2,1,0:T(8,128)(2,1)} %get-tuple-element.17.high_ref, ...), custom_call_target="tpu_custom_call" | custom-call | tf_op jit(solution)/shard_map/pallas_call | solution.py:130
  117.9 1.5 pad_maximum_fusion
  119.4 0.4 fusion.2
  119.8 1.3 collective-permute-start.12
  121.1 17.2 %collective-permute-start.8 = (f32[128,256]{1,0:T(8,128)S(1)}, f32[128,256]{1,0:T(8,128)S(1)}, u32[]{:S(2)}, u32[]{:S(2)}) collective-permute-start(f32[128,256]{1,0:T(8,128)S(1)} %fusion.2), channel_id=1, source_target_pairs={{0,1},{1,2},{2,3},{3,4},{4,5},{5,6},{6,7},{7,8},{8,9},{9,10},{10,1... | collective-permute-start | bytes 393224 | tf_op jit(solution)/shard_map/ppermute | solution.py:244
  138.4 0.9 collective-permute-done.8
  139.3 7.6 %collective-permute-start.9 = (f32[128,256]{1,0:T(8,128)S(1)}, f32[128,256]{1,0:T(8,128)S(1)}, u32[]{:S(2)}, u32[]{:S(2)}) collective-permute-start(f32[128,256]{1,0:T(8,128)S(1)} %get-tuple-element.23), channel_id=1, source_target_pairs={{0,2},{1,3},{2,4},{3,5},{4,6},{5,7},{6,8},{7,9},{8,10},{9,11},{10,... | collective-permute-start | bytes 393224 | tf_op jit(solution)/shard_map/ppermute | solution.py:244
  152.0 1.3 collective-permute-start.13
  153.3 5.3 %collective-permute-start.10 = (f32[128,256]{1,0:T(8,128)S(1)}, f32[128,256]{1,0:T(8,128)S(1)}, u32[]{:S(2)}, u32[]{:S(2)}) collective-permute-start(f32[128,256]{1,0:T(8,128)S(1)} %multiply_add_fusion.4), channel_id=1, source_target_pairs={{0,4},{1,5},{2,6},{3,7},{4,8},{5,9},{6,10},{7,11},{8,12},{9,13},{1... | collective-permute-start | bytes 393224 | tf_op jit(solution)/shard_map/ppermute | solution.py:244
  158.6 0.2 collective-permute-done.13
  158.8 1.3 collective-permute-start.14
  160.1 1.3 collective-permute-done.10
  161.5 3.6 %collective-permute-start.11 = (f32[128,256]{1,0:T(8,128)S(1)}, f32[128,256]{1,0:T(8,128)S(1)}, u32[]{:S(2)}, u32[]{:S(2)}) collective-permute-start(f32[128,256]{1,0:T(8,128)S(1)} %multiply_add_fusion.3), channel_id=1, source_target_pairs={{0,8},{1,9},{2,10},{3,11},{4,12},{5,13},{6,14},{7,15},{16,24},{17,... | collective-permute-start | bytes 393224 | tf_op jit(solution)/shard_map/ppermute | solution.py:244
  165.1 0.6 collective-permute-done.14
  165.7 1.3 collective-permute-start.15
  169.5 1.2 fusion.10
  171.4 3.2 %collective-permute-done.15 = f32[128,256]{1,0:T(8,128)S(1)} collective-permute-done((f32[128,256]{1,0:T(8,128)S(1)}, f32[128,256]{1,0:T(8,128)S(1)}, u32[]{:S(2)}, u32[]{:S(2)}) %collective-permute-start.15) | collective-permute-done | bytes 131104 | tf_op jit(solution)/shard_map/ppermute | solution.py:245
  174.7 0.6 slice.25.gram_ref
  175.3 25.8 %shard_map.41 = f32[128,128]{1,0:T(8,128)} custom-call(f32[128,128]{1,0:T(8,128)} %slice.25.gram_ref), custom_call_target="tpu_custom_call" | custom-call | tf_op jit(solution)/shard_map/pallas_call | solution.py:62
  201.1 1.3 convolution_convert_fusion.1
  202.4 0.5 fusion
  202.9 0.4 fusion.13
  203.3 1.3 collective-permute-start.20
  204.6 3.0 %collective-permute-start.16 = (f32[128,128]{1,0:T(8,128)S(1)}, f32[128,128]{1,0:T(8,128)S(1)}, u32[]{:S(2)}, u32[]{:S(2)}) collective-permute-start(f32[128,128]{1,0:T(8,128)S(1)} %fusion.13), channel_id=1, source_target_pairs={{0,1},{1,2},{2,3},{3,4},{4,5},{5,6},{6,7},{7,8},{8,9},{9,10},{10,1... | collective-permute-start | bytes 196616 | tf_op jit(solution)/shard_map/ppermute | solution.py:244
  207.7 0.9 collective-permute-done.16
  208.6 5.7 %collective-permute-start.17 = (f32[128,128]{1,0:T(8,128)S(1)}, f32[128,128]{1,0:T(8,128)S(1)}, u32[]{:S(2)}, u32[]{:S(2)}) collective-permute-start(f32[128,128]{1,0:T(8,128)S(1)} %get-tuple-element.25), channel_id=1, source_target_pairs={{0,2},{1,3},{2,4},{3,5},{4,6},{5,7},{6,8},{7,9},{8,10},{9,11},{10,... | collective-permute-start | bytes 196616 | tf_op jit(solution)/shard_map/ppermute | solution.py:244
  214.3 1.3 collective-permute-start.21
  215.6 1.2 collective-permute-done.17
  216.8 4.4 %collective-permute-start.18 = (f32[128,128]{1,0:T(8,128)S(1)}, f32[128,128]{1,0:T(8,128)S(1)}, u32[]{:S(2)}, u32[]{:S(2)}) collective-permute-start(f32[128,128]{1,0:T(8,128)S(1)} %multiply_add_fusion.10), channel_id=1, source_target_pairs={{0,4},{1,5},{2,6},{3,7},{4,8},{5,9},{6,10},{7,11},{8,12},{9,13},{1... | collective-permute-start | bytes 196616 | tf_op jit(solution)/shard_map/ppermute | solution.py:244
  221.2 1.3 collective-permute-start.22
  222.5 0.6 collective-permute-done.18
  223.1 4.2 %collective-permute-start.19 = (f32[128,128]{1,0:T(8,128)S(1)}, f32[128,128]{1,0:T(8,128)S(1)}, u32[]{:S(2)}, u32[]{:S(2)}) collective-permute-start(f32[128,128]{1,0:T(8,128)S(1)} %multiply_add_fusion.9), channel_id=1, source_target_pairs={{0,8},{1,9},{2,10},{3,11},{4,12},{5,13},{6,14},{7,15},{16,24},{17,... | collective-permute-start | bytes 196616 | tf_op jit(solution)/shard_map/ppermute | solution.py:244
  227.4 1.3 collective-permute-start.23
  228.7 0.5 collective-permute-done.19
  229.2 5.9 %collective-permute-done.23 = f32[128,128]{1,0:T(8,128)S(1)} collective-permute-done((f32[128,128]{1,0:T(8,128)S(1)}, f32[128,128]{1,0:T(8,128)S(1)}, u32[]{:S(2)}, u32[]{:S(2)}) %collective-permute-start.23) | collective-permute-done | bytes 65568 | tf_op jit(solution)/shard_map/ppermute | solution.py:245
  235.1 0.7 subtract_divide_fusion.1.gram_ref
  235.8 25.8 %shard_map.42 = f32[128,128]{1,0:T(8,128)} custom-call(f32[128,128]{1,0:T(8,128)} %subtract_divide_fusion.1.gram_ref), custom_call_target="tpu_custom_call" | custom-call | tf_op jit(solution)/shard_map/pallas_call | solution.py:62
  261.6 1.2 convolution_convert_fusion
  262.8 0.1 pad_maximum_fusion.1
  262.9 1.6 copy.5
  (43 shorter events, 0.4 us)
Async XLA Ops:
  0.0 5.9 %copy-start.11 = (s32[16]{0:T(128)S(1)}, s32[16]{0:T(128)}, u32[]{:S(2)}) copy-start(s32[16]{0:T(128)} %param.5) | copy-start | bytes 196
  0.0 9.3 %copy-start.12 = (f32[6,512]{1,0:T(8,128)S(1)}, f32[6,512]{1,0:T(8,128)}, u32[]{:S(2)}) copy-start(f32[6,512]{1,0:T(8,128)} %param.4) | copy-start | bytes 36868
  1.5 10.1 %copy-start = (bf16[3,8,64,256]{3,2,1,0:T(8,128)(2,1)}, bf16[3,8,64,256]{3,2,1,0:T(8,128)(2,1)S(1)}, u32[]{:S(2)}) copy-start(bf16[3,8,64,256]{3,2,1,0:T(8,128)(2,1)S(1)} %get-tuple-element.21.low_ref) | copy-start | bytes 2359300
  1.5 10.1 %copy-start.1 = (bf16[3,8,64,256]{3,2,1,0:T(8,128)(2,1)}, bf16[3,8,64,256]{3,2,1,0:T(8,128)(2,1)S(1)}, u32[]{:S(2)}) copy-start(bf16[3,8,64,256]{3,2,1,0:T(8,128)(2,1)S(1)} %get-tuple-element.22.high_ref) | copy-start | bytes 2359300
  1.5 8.4 %collective-permute-start.1 = (bf16[3,8,64,256]{3,2,1,0:T(8,128)(2,1)S(1)}, bf16[3,8,64,256]{3,2,1,0:T(8,128)(2,1)S(1)}, u32[]{:S(2)}, u32[]{:S(2)}) collective-permute-start(bf16[3,8,64,256]{3,2,1,0:T(8,128)(2,1)S(1)} %get-tuple-element.21.low_ref), channel_id=1, source_target_pairs={{1,0},{2,1},{3,2},{4,3},{5,4},{6,5},{7,6},{8,7},{9,8},{10,9},{11,1... | collective-permute-start | bytes 2359304 | tf_op jit(solution)/shard_map/ppermute | solution.py:217
  2.8 7.1 %collective-permute-start = (bf16[3,8,64,256]{3,2,1,0:T(8,128)(2,1)S(1)}, bf16[3,8,64,256]{3,2,1,0:T(8,128)(2,1)S(1)}, u32[]{:S(2)}, u32[]{:S(2)}) collective-permute-start(bf16[3,8,64,256]{3,2,1,0:T(8,128)(2,1)S(1)} %get-tuple-element.22.high_ref), channel_id=1, source_target_pairs={{0,1},{1,2},{2,3},{3,4},{4,5},{5,6},{6,7},{7,8},{8,9},{9,10},{10,1... | collective-permute-start | bytes 2359304 | tf_op jit(solution)/shard_map/ppermute | solution.py:216
  9.9 1.7 copy-start.2
  9.9 1.7 copy-start.3
  20.2 18.8 %collective-permute-start.2 = (bf16[3,8,64,256]{3,2,1,0:T(8,128)(2,1)}, bf16[3,8,64,256]{3,2,1,0:T(8,128)(2,1)S(1)}, u32[]{:S(2)}, u32[]{:S(2)}) collective-permute-start(bf16[3,8,64,256]{3,2,1,0:T(8,128)(2,1)} %get-tuple-element.13.high_ref.older_high_ref), channel_id=1, source_target_pairs={{0,1},{1,2},{2,3},{3,4},{4,5},{5,6},{6,7},{7,8},{8,9},{9,10},{10,1... | collective-permute-start | bytes 2359304 | tf_op jit(solution)/shard_map/ppermute | solution.py:216
  36.9 6.3 %collective-permute-start.3 = (bf16[3,8,64,256]{3,2,1,0:T(8,128)(2,1)}, bf16[3,8,64,256]{3,2,1,0:T(8,128)(2,1)S(1)}, u32[]{:S(2)}, u32[]{:S(2)}) collective-permute-start(bf16[3,8,64,256]{3,2,1,0:T(8,128)(2,1)} %get-tuple-element.14.low_ref.older_low_ref), channel_id=1, source_target_pairs={{1,0},{2,1},{3,2},{4,3},{5,4},{6,5},{7,6},{8,7},{9,8},{10,9},{11,1... | collective-permute-start | bytes 2359304 | tf_op jit(solution)/shard_map/ppermute | solution.py:217
  39.0 4.3 %copy-start.4 = (bf16[3,8,64,256]{3,2,1,0:T(8,128)(2,1)}, bf16[3,8,64,256]{3,2,1,0:T(8,128)(2,1)S(1)}, u32[]{:S(2)}) copy-start(bf16[3,8,64,256]{3,2,1,0:T(8,128)(2,1)S(1)} %collective-permute-done.2.below_ref) | copy-start | bytes 2359300
  43.3 0.9 copy-start.5
  52.9 18.6 %collective-permute-start.4 = (bf16[3,8,64,256]{3,2,1,0:T(8,128)(2,1)}, bf16[3,8,64,256]{3,2,1,0:T(8,128)(2,1)S(1)}, u32[]{:S(2)}, u32[]{:S(2)}) collective-permute-start(bf16[3,8,64,256]{3,2,1,0:T(8,128)(2,1)} %get-tuple-element.15.high_ref.older_high_ref), channel_id=1, source_target_pairs={{0,1},{1,2},{2,3},{3,4},{4,5},{5,6},{6,7},{7,8},{8,9},{9,10},{10,1... | collective-permute-start | bytes 2359304 | tf_op jit(solution)/shard_map/ppermute | solution.py:216
  69.5 6.2 %collective-permute-start.5 = (bf16[3,8,64,256]{3,2,1,0:T(8,128)(2,1)}, bf16[3,8,64,256]{3,2,1,0:T(8,128)(2,1)S(1)}, u32[]{:S(2)}, u32[]{:S(2)}) collective-permute-start(bf16[3,8,64,256]{3,2,1,0:T(8,128)(2,1)} %get-tuple-element.16.low_ref.older_low_ref), channel_id=1, source_target_pairs={{1,0},{2,1},{3,2},{4,3},{5,4},{6,5},{7,6},{8,7},{9,8},{10,9},{11,1... | collective-permute-start | bytes 2359304 | tf_op jit(solution)/shard_map/ppermute | solution.py:217
  71.6 4.2 %copy-start.7 = (bf16[3,8,64,256]{3,2,1,0:T(8,128)(2,1)}, bf16[3,8,64,256]{3,2,1,0:T(8,128)(2,1)S(1)}, u32[]{:S(2)}) copy-start(bf16[3,8,64,256]{3,2,1,0:T(8,128)(2,1)S(1)} %collective-permute-done.4.below_ref) | copy-start | bytes 2359300
  75.7 0.9 copy-start.9
  85.4 18.7 %collective-permute-start.6 = (bf16[3,8,64,256]{3,2,1,0:T(8,128)(2,1)}, bf16[3,8,64,256]{3,2,1,0:T(8,128)(2,1)S(1)}, u32[]{:S(2)}, u32[]{:S(2)}) collective-permute-start(bf16[3,8,64,256]{3,2,1,0:T(8,128)(2,1)} %get-tuple-element.17.high_ref), channel_id=1, source_target_pairs={{0,1},{1,2},{2,3},{3,4},{4,5},{5,6},{6,7},{7,8},{8,9},{9,10},{10,1... | collective-permute-start | bytes 2359304 | tf_op jit(solution)/shard_map/ppermute | solution.py:216
  102.0 6.2 %collective-permute-start.7 = (bf16[3,8,64,256]{3,2,1,0:T(8,128)(2,1)}, bf16[3,8,64,256]{3,2,1,0:T(8,128)(2,1)S(1)}, u32[]{:S(2)}, u32[]{:S(2)}) collective-permute-start(bf16[3,8,64,256]{3,2,1,0:T(8,128)(2,1)} %get-tuple-element.18.low_ref), channel_id=1, source_target_pairs={{1,0},{2,1},{3,2},{4,3},{5,4},{6,5},{7,6},{8,7},{9,8},{10,9},{11,1... | collective-permute-start | bytes 2359304 | tf_op jit(solution)/shard_map/ppermute | solution.py:217
  104.1 4.2 %copy-start.6 = (bf16[3,8,64,256]{3,2,1,0:T(8,128)(2,1)}, bf16[3,8,64,256]{3,2,1,0:T(8,128)(2,1)S(1)}, u32[]{:S(2)}) copy-start(bf16[3,8,64,256]{3,2,1,0:T(8,128)(2,1)S(1)} %collective-permute-done.6.below_ref) | copy-start | bytes 2359300
  108.3 0.9 copy-start.8
  119.8 18.5 %collective-permute-start.12 = (f32[128,256]{1,0:T(8,128)S(1)}, f32[128,256]{1,0:T(8,128)S(1)}, u32[]{:S(2)}, u32[]{:S(2)}) collective-permute-start(f32[128,256]{1,0:T(8,128)S(1)} %fusion.2), channel_id=1, source_target_pairs={{1,0},{2,1},{3,2},{4,3},{5,4},{6,5},{7,6},{8,7},{9,8},{10,9},{11,1... | collective-permute-start | bytes 393224 | tf_op jit(solution)/shard_map/ppermute | solution.py:245
  121.1 18.2 %collective-permute-start.8 = (f32[128,256]{1,0:T(8,128)S(1)}, f32[128,256]{1,0:T(8,128)S(1)}, u32[]{:S(2)}, u32[]{:S(2)}) collective-permute-start(f32[128,256]{1,0:T(8,128)S(1)} %fusion.2), channel_id=1, source_target_pairs={{0,1},{1,2},{2,3},{3,4},{4,5},{5,6},{6,7},{7,8},{8,9},{9,10},{10,1... | collective-permute-start | bytes 393224 | tf_op jit(solution)/shard_map/ppermute | solution.py:244
  139.3 13.9 %collective-permute-start.9 = (f32[128,256]{1,0:T(8,128)S(1)}, f32[128,256]{1,0:T(8,128)S(1)}, u32[]{:S(2)}, u32[]{:S(2)}) collective-permute-start(f32[128,256]{1,0:T(8,128)S(1)} %get-tuple-element.23), channel_id=1, source_target_pairs={{0,2},{1,3},{2,4},{3,5},{4,6},{5,7},{6,8},{7,9},{8,10},{9,11},{10,... | collective-permute-start | bytes 393224 | tf_op jit(solution)/shard_map/ppermute | solution.py:244
  152.0 6.9 %collective-permute-start.13 = (f32[128,256]{1,0:T(8,128)S(1)}, f32[128,256]{1,0:T(8,128)S(1)}, u32[]{:S(2)}, u32[]{:S(2)}) collective-permute-start(f32[128,256]{1,0:T(8,128)S(1)} %get-tuple-element.24), channel_id=1, source_target_pairs={{2,0},{3,1},{4,2},{5,3},{6,4},{7,5},{8,6},{9,7},{10,8},{11,9},{12,... | collective-permute-start | bytes 393224 | tf_op jit(solution)/shard_map/ppermute | solution.py:245
  153.3 8.2 %collective-permute-start.10 = (f32[128,256]{1,0:T(8,128)S(1)}, f32[128,256]{1,0:T(8,128)S(1)}, u32[]{:S(2)}, u32[]{:S(2)}) collective-permute-start(f32[128,256]{1,0:T(8,128)S(1)} %multiply_add_fusion.4), channel_id=1, source_target_pairs={{0,4},{1,5},{2,6},{3,7},{4,8},{5,9},{6,10},{7,11},{8,12},{9,13},{1... | collective-permute-start | bytes 393224 | tf_op jit(solution)/shard_map/ppermute | solution.py:244
  158.8 6.9 %collective-permute-start.14 = (f32[128,256]{1,0:T(8,128)S(1)}, f32[128,256]{1,0:T(8,128)S(1)}, u32[]{:S(2)}, u32[]{:S(2)}) collective-permute-start(f32[128,256]{1,0:T(8,128)S(1)} %multiply_add_fusion.1), channel_id=1, source_target_pairs={{4,0},{5,1},{6,2},{7,3},{8,4},{9,5},{10,6},{11,7},{12,8},{13,9},{1... | collective-permute-start | bytes 393224 | tf_op jit(solution)/shard_map/ppermute | solution.py:245
  161.5 10.0 %collective-permute-start.11 = (f32[128,256]{1,0:T(8,128)S(1)}, f32[128,256]{1,0:T(8,128)S(1)}, u32[]{:S(2)}, u32[]{:S(2)}) collective-permute-start(f32[128,256]{1,0:T(8,128)S(1)} %multiply_add_fusion.3), channel_id=1, source_target_pairs={{0,8},{1,9},{2,10},{3,11},{4,12},{5,13},{6,14},{7,15},{16,24},{17,... | collective-permute-start | bytes 393224 | tf_op jit(solution)/shard_map/ppermute | solution.py:244
  165.7 8.9 %collective-permute-start.15 = (f32[128,256]{1,0:T(8,128)S(1)}, f32[128,256]{1,0:T(8,128)S(1)}, u32[]{:S(2)}, u32[]{:S(2)}) collective-permute-start(f32[128,256]{1,0:T(8,128)S(1)} %multiply_add_fusion), channel_id=1, source_target_pairs={{8,0},{9,1},{10,2},{11,3},{12,4},{13,5},{14,6},{15,7},{24,16},{25,... | collective-permute-start | bytes 393224 | tf_op jit(solution)/shard_map/ppermute | solution.py:245
  201.1 1.3 copy-start.10
  203.3 4.3 %collective-permute-start.20 = (f32[128,128]{1,0:T(8,128)S(1)}, f32[128,128]{1,0:T(8,128)S(1)}, u32[]{:S(2)}, u32[]{:S(2)}) collective-permute-start(f32[128,128]{1,0:T(8,128)S(1)} %fusion.13), channel_id=1, source_target_pairs={{1,0},{2,1},{3,2},{4,3},{5,4},{6,5},{7,6},{8,7},{9,8},{10,9},{11,1... | collective-permute-start | bytes 196616 | tf_op jit(solution)/shard_map/ppermute | solution.py:245
  204.6 3.9 %collective-permute-start.16 = (f32[128,128]{1,0:T(8,128)S(1)}, f32[128,128]{1,0:T(8,128)S(1)}, u32[]{:S(2)}, u32[]{:S(2)}) collective-permute-start(f32[128,128]{1,0:T(8,128)S(1)} %fusion.13), channel_id=1, source_target_pairs={{0,1},{1,2},{2,3},{3,4},{4,5},{5,6},{6,7},{7,8},{8,9},{9,10},{10,1... | collective-permute-start | bytes 196616 | tf_op jit(solution)/shard_map/ppermute | solution.py:244
  208.6 8.2 %collective-permute-start.17 = (f32[128,128]{1,0:T(8,128)S(1)}, f32[128,128]{1,0:T(8,128)S(1)}, u32[]{:S(2)}, u32[]{:S(2)}) collective-permute-start(f32[128,128]{1,0:T(8,128)S(1)} %get-tuple-element.25), channel_id=1, source_target_pairs={{0,2},{1,3},{2,4},{3,5},{4,6},{5,7},{6,8},{7,9},{8,10},{9,11},{10,... | collective-permute-start | bytes 196616 | tf_op jit(solution)/shard_map/ppermute | solution.py:244
  214.3 6.9 %collective-permute-start.21 = (f32[128,128]{1,0:T(8,128)S(1)}, f32[128,128]{1,0:T(8,128)S(1)}, u32[]{:S(2)}, u32[]{:S(2)}) collective-permute-start(f32[128,128]{1,0:T(8,128)S(1)} %get-tuple-element.26), channel_id=1, source_target_pairs={{2,0},{3,1},{4,2},{5,3},{6,4},{7,5},{8,6},{9,7},{10,8},{11,9},{12,... | collective-permute-start | bytes 196616 | tf_op jit(solution)/shard_map/ppermute | solution.py:245
  216.8 6.3 %collective-permute-start.18 = (f32[128,128]{1,0:T(8,128)S(1)}, f32[128,128]{1,0:T(8,128)S(1)}, u32[]{:S(2)}, u32[]{:S(2)}) collective-permute-start(f32[128,128]{1,0:T(8,128)S(1)} %multiply_add_fusion.10), channel_id=1, source_target_pairs={{0,4},{1,5},{2,6},{3,7},{4,8},{5,9},{6,10},{7,11},{8,12},{9,13},{1... | collective-permute-start | bytes 196616 | tf_op jit(solution)/shard_map/ppermute | solution.py:244
  221.2 6.2 %collective-permute-start.22 = (f32[128,128]{1,0:T(8,128)S(1)}, f32[128,128]{1,0:T(8,128)S(1)}, u32[]{:S(2)}, u32[]{:S(2)}) collective-permute-start(f32[128,128]{1,0:T(8,128)S(1)} %multiply_add_fusion.7), channel_id=1, source_target_pairs={{4,0},{5,1},{6,2},{7,3},{8,4},{9,5},{10,6},{11,7},{12,8},{13,9},{1... | collective-permute-start | bytes 196616 | tf_op jit(solution)/shard_map/ppermute | solution.py:245
  223.1 6.1 %collective-permute-start.19 = (f32[128,128]{1,0:T(8,128)S(1)}, f32[128,128]{1,0:T(8,128)S(1)}, u32[]{:S(2)}, u32[]{:S(2)}) collective-permute-start(f32[128,128]{1,0:T(8,128)S(1)} %multiply_add_fusion.9), channel_id=1, source_target_pairs={{0,8},{1,9},{2,10},{3,11},{4,12},{5,13},{6,14},{7,15},{16,24},{17,... | collective-permute-start | bytes 196616 | tf_op jit(solution)/shard_map/ppermute | solution.py:244
  227.4 7.8 %collective-permute-start.23 = (f32[128,128]{1,0:T(8,128)S(1)}, f32[128,128]{1,0:T(8,128)S(1)}, u32[]{:S(2)}, u32[]{:S(2)}) collective-permute-start(f32[128,128]{1,0:T(8,128)S(1)} %multiply_add_fusion.6), channel_id=1, source_target_pairs={{8,0},{9,1},{10,2},{11,3},{12,4},{13,5},{14,6},{15,7},{24,16},{25,... | collective-permute-start | bytes 196616 | tf_op jit(solution)/shard_map/ppermute | solution.py:245

commit v14 on v12

--- a/solution.py
+++ b/solution.py
@@ -65,20 +65,23 @@
 
 
 def _step_kernel(first, rim_ref, below_ref, low_ref, high_ref, above_ref, older_low_ref,
-                 older_high_ref, low_pot_ref, high_pot_ref, out_low_ref, out_high_ref):
+                 older_high_ref, low_pot_ref, high_pot_ref, out_low_ref, out_high_ref, wide_ref):
     half = low_ref.shape[0]
     rows_y = low_ref.shape[1]
     rows_x = low_ref.shape[2]
     place = lax.broadcasted_iota(jnp.int32, (rows_x, low_ref.shape[3]), 0)
     sources = (below_ref, low_ref, high_ref, above_ref)
 
+    for index in range(4 * half):
+        value = sources[index // half][index % half].astype(jnp.float32)
+        if index < half:
+            value = value * rim_ref[0]
+        elif index >= 3 * half:
+            value = value * rim_ref[1]
+        wide_ref[index] = value
+
     def plane(index, y):
-        value = sources[index // half][index % half, y].astype(jnp.float32)
-        if index < half:
-            return value * rim_ref[0]
-        if index >= 3 * half:
-            return value * rim_ref[1]
-        return value
+        return wide_ref[index, y]
 
     for centre in range(half, 3 * half):
         own = centre - half
@@ -144,6 +147,7 @@
             pl.BlockSpec(block, lambda j: (0, 0, 0, j)),
             pl.BlockSpec(block, lambda j: (0, 0, 0, j)),
         ),
+        scratch_shapes=[pltpu.VMEM((4 * half, rows_y, rows_x, lanes), jnp.float32)],
     )(rim, below, low, high, above, older_low, older_high, potential, potential)
 
 

time: 247 us -> 244 us (0.988)
  Pallas kernels: 68.2 us -> 65.2 us
    pallas_call x4, Pallas kernels: 34.9 us -> 31.9 us  [chebyshev_step(): pl.pallas_call(functools.partial(_step_kernel, first), out_shape=(piece,...]
where the time goes in v14:
time: 244 us; the launch traced here: 243 us
  starting transfers between devices  120 us (49%)
  Pallas kernels  65.2 us (27%)
  waiting for transfers between devices  30.1 us (12%)
  between operations  11.3 us (5%)
  local copies, waits for them, and re-layouts  8.82 us (4%)
  other arithmetic  4.28 us (2%)
  matrix products  3.8 us (2%)
    ppermute x4, starting transfers between devices, rimmed(): from_below = lax.ppermute(high, 'gz', forward)  53 us
    ppermute x8, starting transfers between devices, domain_total(): from_low = lax.ppermute(forward, 'gz', ahead)  51 us
    pallas_call x2, Pallas kernels, lower_inverse(): pl.pallas_call(_lower_inverse_kernel, out_shape=jax.ShapeDtypeStruct((n,...  33.3 us
    pallas_call x4, Pallas kernels, chebyshev_step(): pl.pallas_call(functools.partial(_step_kernel, first), out_shape=(piece,...  31.9 us
    ppermute x4, waiting for transfers between devices, rimmed(): from_above = lax.ppermute(low, 'gz', backward)  12.6 us
    ppermute x8, starting transfers between devices, domain_total(): from_high = lax.ppermute(backward, 'gz', behind)  10.3 us
    ppermute x8, waiting for transfers between devices, domain_total(): from_high = lax.ppermute(backward, 'gz', behind)  10 us
    ppermute x8, waiting for transfers between devices, domain_total(): from_low = lax.ppermute(forward, 'gz', ahead)  5.39 us
  transfers between devices with their start and end apart: 24, of which 16 were waited for; matrix products, arithmetic and copies ran while one was open for 1% of the time, Pallas kernels for 0%

profile of v14, /device:TPU:0, one launch (start us, length us, event | category | flops | bytes accessed | tf_op | source)
XLA Modules:
  0.0 243.2 jit_solution(11885220441492548770)
XLA Ops:
  0.0 1.5 fusion.11
  1.5 1.3 collective-permute-start.1
  2.8 3.1 %collective-permute-start = (bf16[3,8,64,256]{3,2,1,0:T(8,128)(2,1)S(1)}, bf16[3,8,64,256]{3,2,1,0:T(8,128)(2,1)S(1)}, u32[]{:S(2)}, u32[]{:S(2)}) collective-permute-start(bf16[3,8,64,256]{3,2,1,0:T(8,128)(2,1)S(1)} %get-tuple-element.22.high_ref), channel_id=1, source_target_pairs={{0,1},{1,2},{2,3},{3,4},{4,5},{5,6},{6,7},{7,8},{8,9},{9,10},{10,1... | collective-permute-start | bytes 2359304 | tf_op jit(solution)/shard_map/ppermute | solution.py:218
  6.0 0.7 fusion.12
  9.3 0.6 add_convert_fusion.rim_ref
  9.9 1.6 broadcast_in_dim.8.low_pot_ref.high_pot_ref
  11.6 7.8 %shard_map.37 = (bf16[3,8,64,256]{3,2,1,0:T(8,128)(2,1)}, bf16[3,8,64,256]{3,2,1,0:T(8,128)(2,1)}) custom-call(f32[2]{0:T(128)} %add_convert_fusion.rim_ref, bf16[3,8,64,256]{3,2,1,0:T(8,128)(2,1)} %copy-done.3, bf16[3,8,64,256]{3,2,1,0:T(8,128)(2,1)} %copy-done, bf16[3,8,64,256]{3,2,1,0:T(8,128)(2,1)} %copy-done.1, bf16[3,8,64,256]{3,2,1,0:T(8,128)(2,1)} %copy-done.2, ...), custom_call_target="tpu_custom_call" | custom-call | tf_op jit(solution)/shard_map/pallas_call | solution.py:131
  19.4 16.8 %collective-permute-start.2 = (bf16[3,8,64,256]{3,2,1,0:T(8,128)(2,1)}, bf16[3,8,64,256]{3,2,1,0:T(8,128)(2,1)S(1)}, u32[]{:S(2)}, u32[]{:S(2)}) collective-permute-start(bf16[3,8,64,256]{3,2,1,0:T(8,128)(2,1)} %get-tuple-element.13.high_ref.older_high_ref), channel_id=1, source_target_pairs={{0,1},{1,2},{2,3},{3,4},{4,5},{5,6},{6,7},{7,8},{8,9},{9,10},{10,1... | collective-permute-start | bytes 2359304 | tf_op jit(solution)/shard_map/ppermute | solution.py:218
  36.2 1.3 collective-permute-start.3
  37.5 0.8 collective-permute-done.2.below_ref
  38.3 4.3 %collective-permute-done.3.above_ref = bf16[3,8,64,256]{3,2,1,0:T(8,128)(2,1)S(1)} collective-permute-done((bf16[3,8,64,256]{3,2,1,0:T(8,128)(2,1)}, bf16[3,8,64,256]{3,2,1,0:T(8,128)(2,1)S(1)}, u32[]{:S(2)}, u32[]{:S(2)}) %collective-permute-start.3) | collective-permute-done | bytes 786464 | tf_op jit(solution)/shard_map/ppermute | solution.py:219
  42.5 0.9 copy-done.5
  43.4 8.0 %shard_map.38 = (bf16[3,8,64,256]{3,2,1,0:T(8,128)(2,1)}, bf16[3,8,64,256]{3,2,1,0:T(8,128)(2,1)}) custom-call(f32[2]{0:T(128)} %add_convert_fusion.rim_ref, bf16[3,8,64,256]{3,2,1,0:T(8,128)(2,1)} %copy-done.4, bf16[3,8,64,256]{3,2,1,0:T(8,128)(2,1)} %get-tuple-element.14.low_ref.older_low_ref, ...), custom_call_target="tpu_custom_call" | custom-call | tf_op jit(solution)/shard_map/pallas_call | solution.py:131
  51.5 16.6 %collective-permute-start.4 = (bf16[3,8,64,256]{3,2,1,0:T(8,128)(2,1)}, bf16[3,8,64,256]{3,2,1,0:T(8,128)(2,1)S(1)}, u32[]{:S(2)}, u32[]{:S(2)}) collective-permute-start(bf16[3,8,64,256]{3,2,1,0:T(8,128)(2,1)} %get-tuple-element.15.high_ref.older_high_ref), channel_id=1, source_target_pairs={{0,1},{1,2},{2,3},{3,4},{4,5},{5,6},{6,7},{7,8},{8,9},{9,10},{10,1... | collective-permute-start | bytes 2359304 | tf_op jit(solution)/shard_map/ppermute | solution.py:218
  68.0 1.3 collective-permute-start.5
  69.3 0.8 collective-permute-done.4.below_ref
  70.1 4.2 %collective-permute-done.5.above_ref = bf16[3,8,64,256]{3,2,1,0:T(8,128)(2,1)S(1)} collective-permute-done((bf16[3,8,64,256]{3,2,1,0:T(8,128)(2,1)}, bf16[3,8,64,256]{3,2,1,0:T(8,128)(2,1)S(1)}, u32[]{:S(2)}, u32[]{:S(2)}) %collective-permute-start.5) | collective-permute-done | bytes 786464 | tf_op jit(solution)/shard_map/ppermute | solution.py:219
  74.3 0.9 copy-done.9
  75.2 8.0 %shard_map.39 = (bf16[3,8,64,256]{3,2,1,0:T(8,128)(2,1)}, bf16[3,8,64,256]{3,2,1,0:T(8,128)(2,1)}) custom-call(f32[2]{0:T(128)} %add_convert_fusion.rim_ref, bf16[3,8,64,256]{3,2,1,0:T(8,128)(2,1)} %copy-done.7, bf16[3,8,64,256]{3,2,1,0:T(8,128)(2,1)} %get-tuple-element.16.low_ref.older_low_ref, ...), custom_call_target="tpu_custom_call" | custom-call | tf_op jit(solution)/shard_map/pallas_call | solution.py:131
  83.2 16.6 %collective-permute-start.6 = (bf16[3,8,64,256]{3,2,1,0:T(8,128)(2,1)}, bf16[3,8,64,256]{3,2,1,0:T(8,128)(2,1)S(1)}, u32[]{:S(2)}, u32[]{:S(2)}) collective-permute-start(bf16[3,8,64,256]{3,2,1,0:T(8,128)(2,1)} %get-tuple-element.17.high_ref), channel_id=1, source_target_pairs={{0,1},{1,2},{2,3},{3,4},{4,5},{5,6},{6,7},{7,8},{8,9},{9,10},{10,1... | collective-permute-start | bytes 2359304 | tf_op jit(solution)/shard_map/ppermute | solution.py:218
  99.8 1.5 collective-permute-start.7
  101.3 0.6 collective-permute-done.6.below_ref
  101.9 4.2 %collective-permute-done.7.above_ref = bf16[3,8,64,256]{3,2,1,0:T(8,128)(2,1)S(1)} collective-permute-done((bf16[3,8,64,256]{3,2,1,0:T(8,128)(2,1)}, bf16[3,8,64,256]{3,2,1,0:T(8,128)(2,1)S(1)}, u32[]{:S(2)}, u32[]{:S(2)}) %collective-permute-start.7) | collective-permute-done | bytes 786464 | tf_op jit(solution)/shard_map/ppermute | solution.py:219
  106.0 0.9 copy-done.8
  106.9 8.0 %shard_map.40 = (bf16[3,8,64,256]{3,2,1,0:T(8,128)(2,1)}, bf16[3,8,64,256]{3,2,1,0:T(8,128)(2,1)}) custom-call(f32[2]{0:T(128)} %add_convert_fusion.rim_ref, bf16[3,8,64,256]{3,2,1,0:T(8,128)(2,1)} %copy-done.6, bf16[3,8,64,256]{3,2,1,0:T(8,128)(2,1)} %get-tuple-element.18.low_ref, bf16[3,8,64,256]{3,2,1,0:T(8,128)(2,1)} %get-tuple-element.17.high_ref, ...), custom_call_target="tpu_custom_call" | custom-call | tf_op jit(solution)/shard_map/pallas_call | solution.py:131
  114.9 1.5 pad_maximum_fusion
  116.5 0.4 fusion.2
  116.9 1.3 collective-permute-start.12
  118.2 17.2 %collective-permute-start.8 = (f32[128,256]{1,0:T(8,128)S(1)}, f32[128,256]{1,0:T(8,128)S(1)}, u32[]{:S(2)}, u32[]{:S(2)}) collective-permute-start(f32[128,256]{1,0:T(8,128)S(1)} %fusion.2), channel_id=1, source_target_pairs={{0,1},{1,2},{2,3},{3,4},{4,5},{5,6},{6,7},{7,8},{8,9},{9,10},{10,1... | collective-permute-start | bytes 393224 | tf_op jit(solution)/shard_map/ppermute | solution.py:246
  135.4 0.9 collective-permute-done.8
  136.4 7.6 %collective-permute-start.9 = (f32[128,256]{1,0:T(8,128)S(1)}, f32[128,256]{1,0:T(8,128)S(1)}, u32[]{:S(2)}, u32[]{:S(2)}) collective-permute-start(f32[128,256]{1,0:T(8,128)S(1)} %get-tuple-element.23), channel_id=1, source_target_pairs={{0,2},{1,3},{2,4},{3,5},{4,6},{5,7},{6,8},{7,9},{8,10},{9,11},{10,... | collective-permute-start | bytes 393224 | tf_op jit(solution)/shard_map/ppermute | solution.py:246
  149.0 1.3 collective-permute-start.13
  150.3 5.3 %collective-permute-start.10 = (f32[128,256]{1,0:T(8,128)S(1)}, f32[128,256]{1,0:T(8,128)S(1)}, u32[]{:S(2)}, u32[]{:S(2)}) collective-permute-start(f32[128,256]{1,0:T(8,128)S(1)} %multiply_add_fusion.4), channel_id=1, source_target_pairs={{0,4},{1,5},{2,6},{3,7},{4,8},{5,9},{6,10},{7,11},{8,12},{9,13},{1... | collective-permute-start | bytes 393224 | tf_op jit(solution)/shard_map/ppermute | solution.py:246
  155.6 0.2 collective-permute-done.13
  155.9 1.3 collective-permute-start.14
  157.2 1.3 collective-permute-done.10
  158.5 3.6 %collective-permute-start.11 = (f32[128,256]{1,0:T(8,128)S(1)}, f32[128,256]{1,0:T(8,128)S(1)}, u32[]{:S(2)}, u32[]{:S(2)}) collective-permute-start(f32[128,256]{1,0:T(8,128)S(1)} %multiply_add_fusion.3), channel_id=1, source_target_pairs={{0,8},{1,9},{2,10},{3,11},{4,12},{5,13},{6,14},{7,15},{16,24},{17,... | collective-permute-start | bytes 393224 | tf_op jit(solution)/shard_map/ppermute | solution.py:246
  162.2 0.6 collective-permute-done.14
  162.8 1.3 collective-permute-start.15
  166.6 1.2 fusion.10
  168.5 3.2 %collective-permute-done.15 = f32[128,256]{1,0:T(8,128)S(1)} collective-permute-done((f32[128,256]{1,0:T(8,128)S(1)}, f32[128,256]{1,0:T(8,128)S(1)}, u32[]{:S(2)}, u32[]{:S(2)}) %collective-permute-start.15) | collective-permute-done | bytes 131104 | tf_op jit(solution)/shard_map/ppermute | solution.py:247
  171.7 0.6 slice.25.gram_ref
  172.3 16.6 %shard_map.41 = f32[128,128]{1,0:T(8,128)} custom-call(f32[128,128]{1,0:T(8,128)} %slice.25.gram_ref), custom_call_target="tpu_custom_call" | custom-call | tf_op jit(solution)/shard_map/pallas_call | solution.py:60
  189.0 1.3 convolution_convert_fusion.1
  190.3 0.5 fusion
  190.8 0.4 fusion.13
  191.2 1.3 collective-permute-start.20
  192.5 3.0 %collective-permute-start.16 = (f32[128,128]{1,0:T(8,128)S(1)}, f32[128,128]{1,0:T(8,128)S(1)}, u32[]{:S(2)}, u32[]{:S(2)}) collective-permute-start(f32[128,128]{1,0:T(8,128)S(1)} %fusion.13), channel_id=1, source_target_pairs={{0,1},{1,2},{2,3},{3,4},{4,5},{5,6},{6,7},{7,8},{8,9},{9,10},{10,1... | collective-permute-start | bytes 196616 | tf_op jit(solution)/shard_map/ppermute | solution.py:246
  195.6 0.9 collective-permute-done.16
  196.4 5.7 %collective-permute-start.17 = (f32[128,128]{1,0:T(8,128)S(1)}, f32[128,128]{1,0:T(8,128)S(1)}, u32[]{:S(2)}, u32[]{:S(2)}) collective-permute-start(f32[128,128]{1,0:T(8,128)S(1)} %get-tuple-element.25), channel_id=1, source_target_pairs={{0,2},{1,3},{2,4},{3,5},{4,6},{5,7},{6,8},{7,9},{8,10},{9,11},{10,... | collective-permute-start | bytes 196616 | tf_op jit(solution)/shard_map/ppermute | solution.py:246
  202.1 1.3 collective-permute-start.21
  203.4 1.2 collective-permute-done.17
  204.6 4.4 %collective-permute-start.18 = (f32[128,128]{1,0:T(8,128)S(1)}, f32[128,128]{1,0:T(8,128)S(1)}, u32[]{:S(2)}, u32[]{:S(2)}) collective-permute-start(f32[128,128]{1,0:T(8,128)S(1)} %multiply_add_fusion.10), channel_id=1, source_target_pairs={{0,4},{1,5},{2,6},{3,7},{4,8},{5,9},{6,10},{7,11},{8,12},{9,13},{1... | collective-permute-start | bytes 196616 | tf_op jit(solution)/shard_map/ppermute | solution.py:246
  209.1 1.3 collective-permute-start.22
  210.4 0.6 collective-permute-done.18
  210.9 4.2 %collective-permute-start.19 = (f32[128,128]{1,0:T(8,128)S(1)}, f32[128,128]{1,0:T(8,128)S(1)}, u32[]{:S(2)}, u32[]{:S(2)}) collective-permute-start(f32[128,128]{1,0:T(8,128)S(1)} %multiply_add_fusion.9), channel_id=1, source_target_pairs={{0,8},{1,9},{2,10},{3,11},{4,12},{5,13},{6,14},{7,15},{16,24},{17,... | collective-permute-start | bytes 196616 | tf_op jit(solution)/shard_map/ppermute | solution.py:246
  215.2 1.3 collective-permute-start.23
  216.5 0.5 collective-permute-done.19
  217.1 5.9 %collective-permute-done.23 = f32[128,128]{1,0:T(8,128)S(1)} collective-permute-done((f32[128,128]{1,0:T(8,128)S(1)}, f32[128,128]{1,0:T(8,128)S(1)}, u32[]{:S(2)}, u32[]{:S(2)}) %collective-permute-start.23) | collective-permute-done | bytes 65568 | tf_op jit(solution)/shard_map/ppermute | solution.py:247
  223.0 0.7 subtract_divide_fusion.1.gram_ref
  223.6 16.6 %shard_map.42 = f32[128,128]{1,0:T(8,128)} custom-call(f32[128,128]{1,0:T(8,128)} %subtract_divide_fusion.1.gram_ref), custom_call_target="tpu_custom_call" | custom-call | tf_op jit(solution)/shard_map/pallas_call | solution.py:60
  240.3 1.2 convolution_convert_fusion
  241.5 0.1 pad_maximum_fusion.1
  241.6 1.6 copy.5
  (43 shorter events, 0.4 us)
Async XLA Ops:
  0.0 5.9 %copy-start.11 = (s32[16]{0:T(128)S(1)}, s32[16]{0:T(128)}, u32[]{:S(2)}) copy-start(s32[16]{0:T(128)} %param.5) | copy-start | bytes 196
  0.0 9.3 %copy-start.12 = (f32[6,512]{1,0:T(8,128)S(1)}, f32[6,512]{1,0:T(8,128)}, u32[]{:S(2)}) copy-start(f32[6,512]{1,0:T(8,128)} %param.4) | copy-start | bytes 36868
  1.5 10.1 %copy-start = (bf16[3,8,64,256]{3,2,1,0:T(8,128)(2,1)}, bf16[3,8,64,256]{3,2,1,0:T(8,128)(2,1)S(1)}, u32[]{:S(2)}) copy-start(bf16[3,8,64,256]{3,2,1,0:T(8,128)(2,1)S(1)} %get-tuple-element.21.low_ref) | copy-start | bytes 2359300
  1.5 10.1 %copy-start.1 = (bf16[3,8,64,256]{3,2,1,0:T(8,128)(2,1)}, bf16[3,8,64,256]{3,2,1,0:T(8,128)(2,1)S(1)}, u32[]{:S(2)}) copy-start(bf16[3,8,64,256]{3,2,1,0:T(8,128)(2,1)S(1)} %get-tuple-element.22.high_ref) | copy-start | bytes 2359300
  1.5 8.4 %collective-permute-start.1 = (bf16[3,8,64,256]{3,2,1,0:T(8,128)(2,1)S(1)}, bf16[3,8,64,256]{3,2,1,0:T(8,128)(2,1)S(1)}, u32[]{:S(2)}, u32[]{:S(2)}) collective-permute-start(bf16[3,8,64,256]{3,2,1,0:T(8,128)(2,1)S(1)} %get-tuple-element.21.low_ref), channel_id=1, source_target_pairs={{1,0},{2,1},{3,2},{4,3},{5,4},{6,5},{7,6},{8,7},{9,8},{10,9},{11,1... | collective-permute-start | bytes 2359304 | tf_op jit(solution)/shard_map/ppermute | solution.py:219
  2.8 7.1 %collective-permute-start = (bf16[3,8,64,256]{3,2,1,0:T(8,128)(2,1)S(1)}, bf16[3,8,64,256]{3,2,1,0:T(8,128)(2,1)S(1)}, u32[]{:S(2)}, u32[]{:S(2)}) collective-permute-start(bf16[3,8,64,256]{3,2,1,0:T(8,128)(2,1)S(1)} %get-tuple-element.22.high_ref), channel_id=1, source_target_pairs={{0,1},{1,2},{2,3},{3,4},{4,5},{5,6},{6,7},{7,8},{8,9},{9,10},{10,1... | collective-permute-start | bytes 2359304 | tf_op jit(solution)/shard_map/ppermute | solution.py:218
  9.9 1.7 copy-start.2
  9.9 1.7 copy-start.3
  19.4 18.8 %collective-permute-start.2 = (bf16[3,8,64,256]{3,2,1,0:T(8,128)(2,1)}, bf16[3,8,64,256]{3,2,1,0:T(8,128)(2,1)S(1)}, u32[]{:S(2)}, u32[]{:S(2)}) collective-permute-start(bf16[3,8,64,256]{3,2,1,0:T(8,128)(2,1)} %get-tuple-element.13.high_ref.older_high_ref), channel_id=1, source_target_pairs={{0,1},{1,2},{2,3},{3,4},{4,5},{5,6},{6,7},{7,8},{8,9},{9,10},{10,1... | collective-permute-start | bytes 2359304 | tf_op jit(solution)/shard_map/ppermute | solution.py:218
  36.2 6.3 %collective-permute-start.3 = (bf16[3,8,64,256]{3,2,1,0:T(8,128)(2,1)}, bf16[3,8,64,256]{3,2,1,0:T(8,128)(2,1)S(1)}, u32[]{:S(2)}, u32[]{:S(2)}) collective-permute-start(bf16[3,8,64,256]{3,2,1,0:T(8,128)(2,1)} %get-tuple-element.14.low_ref.older_low_ref), channel_id=1, source_target_pairs={{1,0},{2,1},{3,2},{4,3},{5,4},{6,5},{7,6},{8,7},{9,8},{10,9},{11,1... | collective-permute-start | bytes 2359304 | tf_op jit(solution)/shard_map/ppermute | solution.py:219
  38.3 4.3 %copy-start.4 = (bf16[3,8,64,256]{3,2,1,0:T(8,128)(2,1)}, bf16[3,8,64,256]{3,2,1,0:T(8,128)(2,1)S(1)}, u32[]{:S(2)}) copy-start(bf16[3,8,64,256]{3,2,1,0:T(8,128)(2,1)S(1)} %collective-permute-done.2.below_ref) | copy-start | bytes 2359300
  42.5 0.9 copy-start.5
  51.5 18.6 %collective-permute-start.4 = (bf16[3,8,64,256]{3,2,1,0:T(8,128)(2,1)}, bf16[3,8,64,256]{3,2,1,0:T(8,128)(2,1)S(1)}, u32[]{:S(2)}, u32[]{:S(2)}) collective-permute-start(bf16[3,8,64,256]{3,2,1,0:T(8,128)(2,1)} %get-tuple-element.15.high_ref.older_high_ref), channel_id=1, source_target_pairs={{0,1},{1,2},{2,3},{3,4},{4,5},{5,6},{6,7},{7,8},{8,9},{9,10},{10,1... | collective-permute-start | bytes 2359304 | tf_op jit(solution)/shard_map/ppermute | solution.py:218
  68.0 6.2 %collective-permute-start.5 = (bf16[3,8,64,256]{3,2,1,0:T(8,128)(2,1)}, bf16[3,8,64,256]{3,2,1,0:T(8,128)(2,1)S(1)}, u32[]{:S(2)}, u32[]{:S(2)}) collective-permute-start(bf16[3,8,64,256]{3,2,1,0:T(8,128)(2,1)} %get-tuple-element.16.low_ref.older_low_ref), channel_id=1, source_target_pairs={{1,0},{2,1},{3,2},{4,3},{5,4},{6,5},{7,6},{8,7},{9,8},{10,9},{11,1... | collective-permute-start | bytes 2359304 | tf_op jit(solution)/shard_map/ppermute | solution.py:219
  70.1 4.2 %copy-start.7 = (bf16[3,8,64,256]{3,2,1,0:T(8,128)(2,1)}, bf16[3,8,64,256]{3,2,1,0:T(8,128)(2,1)S(1)}, u32[]{:S(2)}) copy-start(bf16[3,8,64,256]{3,2,1,0:T(8,128)(2,1)S(1)} %collective-permute-done.4.below_ref) | copy-start | bytes 2359300
  74.3 0.9 copy-start.9
  83.2 18.7 %collective-permute-start.6 = (bf16[3,8,64,256]{3,2,1,0:T(8,128)(2,1)}, bf16[3,8,64,256]{3,2,1,0:T(8,128)(2,1)S(1)}, u32[]{:S(2)}, u32[]{:S(2)}) collective-permute-start(bf16[3,8,64,256]{3,2,1,0:T(8,128)(2,1)} %get-tuple-element.17.high_ref), channel_id=1, source_target_pairs={{0,1},{1,2},{2,3},{3,4},{4,5},{5,6},{6,7},{7,8},{8,9},{9,10},{10,1... | collective-permute-start | bytes 2359304 | tf_op jit(solution)/shard_map/ppermute | solution.py:218
  99.8 6.2 %collective-permute-start.7 = (bf16[3,8,64,256]{3,2,1,0:T(8,128)(2,1)}, bf16[3,8,64,256]{3,2,1,0:T(8,128)(2,1)S(1)}, u32[]{:S(2)}, u32[]{:S(2)}) collective-permute-start(bf16[3,8,64,256]{3,2,1,0:T(8,128)(2,1)} %get-tuple-element.18.low_ref), channel_id=1, source_target_pairs={{1,0},{2,1},{3,2},{4,3},{5,4},{6,5},{7,6},{8,7},{9,8},{10,9},{11,1... | collective-permute-start | bytes 2359304 | tf_op jit(solution)/shard_map/ppermute | solution.py:219
  101.9 4.2 %copy-start.6 = (bf16[3,8,64,256]{3,2,1,0:T(8,128)(2,1)}, bf16[3,8,64,256]{3,2,1,0:T(8,128)(2,1)S(1)}, u32[]{:S(2)}) copy-start(bf16[3,8,64,256]{3,2,1,0:T(8,128)(2,1)S(1)} %collective-permute-done.6.below_ref) | copy-start | bytes 2359300
  106.0 0.9 copy-start.8
  116.9 18.5 %collective-permute-start.12 = (f32[128,256]{1,0:T(8,128)S(1)}, f32[128,256]{1,0:T(8,128)S(1)}, u32[]{:S(2)}, u32[]{:S(2)}) collective-permute-start(f32[128,256]{1,0:T(8,128)S(1)} %fusion.2), channel_id=1, source_target_pairs={{1,0},{2,1},{3,2},{4,3},{5,4},{6,5},{7,6},{8,7},{9,8},{10,9},{11,1... | collective-permute-start | bytes 393224 | tf_op jit(solution)/shard_map/ppermute | solution.py:247
  118.2 18.2 %collective-permute-start.8 = (f32[128,256]{1,0:T(8,128)S(1)}, f32[128,256]{1,0:T(8,128)S(1)}, u32[]{:S(2)}, u32[]{:S(2)}) collective-permute-start(f32[128,256]{1,0:T(8,128)S(1)} %fusion.2), channel_id=1, source_target_pairs={{0,1},{1,2},{2,3},{3,4},{4,5},{5,6},{6,7},{7,8},{8,9},{9,10},{10,1... | collective-permute-start | bytes 393224 | tf_op jit(solution)/shard_map/ppermute | solution.py:246
  136.4 13.9 %collective-permute-start.9 = (f32[128,256]{1,0:T(8,128)S(1)}, f32[128,256]{1,0:T(8,128)S(1)}, u32[]{:S(2)}, u32[]{:S(2)}) collective-permute-start(f32[128,256]{1,0:T(8,128)S(1)} %get-tuple-element.23), channel_id=1, source_target_pairs={{0,2},{1,3},{2,4},{3,5},{4,6},{5,7},{6,8},{7,9},{8,10},{9,11},{10,... | collective-permute-start | bytes 393224 | tf_op jit(solution)/shard_map/ppermute | solution.py:246
  149.0 6.9 %collective-permute-start.13 = (f32[128,256]{1,0:T(8,128)S(1)}, f32[128,256]{1,0:T(8,128)S(1)}, u32[]{:S(2)}, u32[]{:S(2)}) collective-permute-start(f32[128,256]{1,0:T(8,128)S(1)} %get-tuple-element.24), channel_id=1, source_target_pairs={{2,0},{3,1},{4,2},{5,3},{6,4},{7,5},{8,6},{9,7},{10,8},{11,9},{12,... | collective-permute-start | bytes 393224 | tf_op jit(solution)/shard_map/ppermute | solution.py:247
  150.3 8.2 %collective-permute-start.10 = (f32[128,256]{1,0:T(8,128)S(1)}, f32[128,256]{1,0:T(8,128)S(1)}, u32[]{:S(2)}, u32[]{:S(2)}) collective-permute-start(f32[128,256]{1,0:T(8,128)S(1)} %multiply_add_fusion.4), channel_id=1, source_target_pairs={{0,4},{1,5},{2,6},{3,7},{4,8},{5,9},{6,10},{7,11},{8,12},{9,13},{1... | collective-permute-start | bytes 393224 | tf_op jit(solution)/shard_map/ppermute | solution.py:246
  155.9 6.9 %collective-permute-start.14 = (f32[128,256]{1,0:T(8,128)S(1)}, f32[128,256]{1,0:T(8,128)S(1)}, u32[]{:S(2)}, u32[]{:S(2)}) collective-permute-start(f32[128,256]{1,0:T(8,128)S(1)} %multiply_add_fusion.1), channel_id=1, source_target_pairs={{4,0},{5,1},{6,2},{7,3},{8,4},{9,5},{10,6},{11,7},{12,8},{13,9},{1... | collective-permute-start | bytes 393224 | tf_op jit(solution)/shard_map/ppermute | solution.py:247
  158.5 10.0 %collective-permute-start.11 = (f32[128,256]{1,0:T(8,128)S(1)}, f32[128,256]{1,0:T(8,128)S(1)}, u32[]{:S(2)}, u32[]{:S(2)}) collective-permute-start(f32[128,256]{1,0:T(8,128)S(1)} %multiply_add_fusion.3), channel_id=1, source_target_pairs={{0,8},{1,9},{2,10},{3,11},{4,12},{5,13},{6,14},{7,15},{16,24},{17,... | collective-permute-start | bytes 393224 | tf_op jit(solution)/shard_map/ppermute | solution.py:246
  162.8 8.9 %collective-permute-start.15 = (f32[128,256]{1,0:T(8,128)S(1)}, f32[128,256]{1,0:T(8,128)S(1)}, u32[]{:S(2)}, u32[]{:S(2)}) collective-permute-start(f32[128,256]{1,0:T(8,128)S(1)} %multiply_add_fusion), channel_id=1, source_target_pairs={{8,0},{9,1},{10,2},{11,3},{12,4},{13,5},{14,6},{15,7},{24,16},{25,... | collective-permute-start | bytes 393224 | tf_op jit(solution)/shard_map/ppermute | solution.py:247
  189.0 1.3 copy-start.10
  191.2 4.3 %collective-permute-start.20 = (f32[128,128]{1,0:T(8,128)S(1)}, f32[128,128]{1,0:T(8,128)S(1)}, u32[]{:S(2)}, u32[]{:S(2)}) collective-permute-start(f32[128,128]{1,0:T(8,128)S(1)} %fusion.13), channel_id=1, source_target_pairs={{1,0},{2,1},{3,2},{4,3},{5,4},{6,5},{7,6},{8,7},{9,8},{10,9},{11,1... | collective-permute-start | bytes 196616 | tf_op jit(solution)/shard_map/ppermute | solution.py:247
  192.5 3.9 %collective-permute-start.16 = (f32[128,128]{1,0:T(8,128)S(1)}, f32[128,128]{1,0:T(8,128)S(1)}, u32[]{:S(2)}, u32[]{:S(2)}) collective-permute-start(f32[128,128]{1,0:T(8,128)S(1)} %fusion.13), channel_id=1, source_target_pairs={{0,1},{1,2},{2,3},{3,4},{4,5},{5,6},{6,7},{7,8},{8,9},{9,10},{10,1... | collective-permute-start | bytes 196616 | tf_op jit(solution)/shard_map/ppermute | solution.py:246
  196.4 8.2 %collective-permute-start.17 = (f32[128,128]{1,0:T(8,128)S(1)}, f32[128,128]{1,0:T(8,128)S(1)}, u32[]{:S(2)}, u32[]{:S(2)}) collective-permute-start(f32[128,128]{1,0:T(8,128)S(1)} %get-tuple-element.25), channel_id=1, source_target_pairs={{0,2},{1,3},{2,4},{3,5},{4,6},{5,7},{6,8},{7,9},{8,10},{9,11},{10,... | collective-permute-start | bytes 196616 | tf_op jit(solution)/shard_map/ppermute | solution.py:246
  202.1 6.9 %collective-permute-start.21 = (f32[128,128]{1,0:T(8,128)S(1)}, f32[128,128]{1,0:T(8,128)S(1)}, u32[]{:S(2)}, u32[]{:S(2)}) collective-permute-start(f32[128,128]{1,0:T(8,128)S(1)} %get-tuple-element.26), channel_id=1, source_target_pairs={{2,0},{3,1},{4,2},{5,3},{6,4},{7,5},{8,6},{9,7},{10,8},{11,9},{12,... | collective-permute-start | bytes 196616 | tf_op jit(solution)/shard_map/ppermute | solution.py:247
  204.6 6.3 %collective-permute-start.18 = (f32[128,128]{1,0:T(8,128)S(1)}, f32[128,128]{1,0:T(8,128)S(1)}, u32[]{:S(2)}, u32[]{:S(2)}) collective-permute-start(f32[128,128]{1,0:T(8,128)S(1)} %multiply_add_fusion.10), channel_id=1, source_target_pairs={{0,4},{1,5},{2,6},{3,7},{4,8},{5,9},{6,10},{7,11},{8,12},{9,13},{1... | collective-permute-start | bytes 196616 | tf_op jit(solution)/shard_map/ppermute | solution.py:246
  209.1 6.2 %collective-permute-start.22 = (f32[128,128]{1,0:T(8,128)S(1)}, f32[128,128]{1,0:T(8,128)S(1)}, u32[]{:S(2)}, u32[]{:S(2)}) collective-permute-start(f32[128,128]{1,0:T(8,128)S(1)} %multiply_add_fusion.7), channel_id=1, source_target_pairs={{4,0},{5,1},{6,2},{7,3},{8,4},{9,5},{10,6},{11,7},{12,8},{13,9},{1... | collective-permute-start | bytes 196616 | tf_op jit(solution)/shard_map/ppermute | solution.py:247
  210.9 6.1 %collective-permute-start.19 = (f32[128,128]{1,0:T(8,128)S(1)}, f32[128,128]{1,0:T(8,128)S(1)}, u32[]{:S(2)}, u32[]{:S(2)}) collective-permute-start(f32[128,128]{1,0:T(8,128)S(1)} %multiply_add_fusion.9), channel_id=1, source_target_pairs={{0,8},{1,9},{2,10},{3,11},{4,12},{5,13},{6,14},{7,15},{16,24},{17,... | collective-permute-start | bytes 196616 | tf_op jit(solution)/shard_map/ppermute | solution.py:246
  215.2 7.8 %collective-permute-start.23 = (f32[128,128]{1,0:T(8,128)S(1)}, f32[128,128]{1,0:T(8,128)S(1)}, u32[]{:S(2)}, u32[]{:S(2)}) collective-permute-start(f32[128,128]{1,0:T(8,128)S(1)} %multiply_add_fusion.6), channel_id=1, source_target_pairs={{8,0},{9,1},{10,2},{11,3},{12,4},{13,5},{14,6},{15,7},{24,16},{25,... | collective-permute-start | bytes 196616 | tf_op jit(solution)/shard_map/ppermute | solution.py:247

commit v15 on v14

--- a/solution.py
+++ b/solution.py
@@ -69,7 +69,6 @@
     half = low_ref.shape[0]
     rows_y = low_ref.shape[1]
     rows_x = low_ref.shape[2]
-    place = lax.broadcasted_iota(jnp.int32, (rows_x, low_ref.shape[3]), 0)
     sources = (below_ref, low_ref, high_ref, above_ref)
 
     for index in range(4 * half):
@@ -78,10 +77,15 @@
             value = value * rim_ref[0]
         elif index >= 3 * half:
             value = value * rim_ref[1]
-        wide_ref[index] = value
+        wide_ref[index, :, 8 : 8 + rows_x] = value
+        if half <= index < 3 * half:
+            wide_ref[index, :, 0:8] = jnp.zeros((rows_y, 8, value.shape[-1]), jnp.float32)
+            wide_ref[index, :, 8 + rows_x : 16 + rows_x] = jnp.zeros(
+                (rows_y, 8, value.shape[-1]), jnp.float32
+            )
 
     def plane(index, y):
-        return wide_ref[index, y]
+        return wide_ref[index, y, 8 : 8 + rows_x]
 
     for centre in range(half, 3 * half):
         own = centre - half
@@ -102,10 +106,8 @@
                     along_y = up
                 else:
                     along_y = up + down
-                ahead = jnp.where(
-                    place + distance < rows_x, pltpu.roll(inner, rows_x - distance, 0), 0.0
-                )
-                behind = jnp.where(place >= distance, pltpu.roll(inner, distance, 0), 0.0)
+                ahead = wide_ref[centre, y, 8 + distance : 8 + distance + rows_x]
+                behind = wide_ref[centre, y, 8 - distance : 8 - distance + rows_x]
                 along_x = ahead + behind
                 total = total + COEF[distance] * (along_z + along_y + along_x)
             image = potential_ref[local, y] * inner - 0.5 * total
@@ -147,7 +149,7 @@
             pl.BlockSpec(block, lambda j: (0, 0, 0, j)),
             pl.BlockSpec(block, lambda j: (0, 0, 0, j)),
         ),
-        scratch_shapes=[pltpu.VMEM((4 * half, rows_y, rows_x, lanes), jnp.float32)],
+        scratch_shapes=[pltpu.VMEM((4 * half, rows_y, rows_x + 16, lanes), jnp.float32)],
     )(rim, below, low, high, above, older_low, older_high, potential, potential)
 
 

time: 244 us -> 240 us (0.984)
  Pallas kernels: 65.2 us -> 60.3 us
    pallas_call x4, Pallas kernels: 31.9 us -> 27 us  [chebyshev_step(): pl.pallas_call(functools.partial(_step_kernel, first), out_shape=(piece,...]
where the time goes in v15:
time: 240 us; the launch traced here: 238 us
  starting transfers between devices  120 us (50%)
  Pallas kernels  60.3 us (25%)
  waiting for transfers between devices  30 us (12%)
  between operations  11.3 us (5%)
  local copies, waits for them, and re-layouts  8.82 us (4%)
  other arithmetic  4.29 us (2%)
  matrix products  3.8 us (2%)
    ppermute x4, starting transfers between devices, rimmed(): from_below = lax.ppermute(high, 'gz', forward)  53 us
    ppermute x8, starting transfers between devices, domain_total(): from_low = lax.ppermute(forward, 'gz', ahead)  51.2 us
    pallas_call x2, Pallas kernels, lower_inverse(): pl.pallas_call(_lower_inverse_kernel, out_shape=jax.ShapeDtypeStruct((n,...  33.3 us
    pallas_call x4, Pallas kernels, chebyshev_step(): pl.pallas_call(functools.partial(_step_kernel, first), out_shape=(piece,...  27 us
    ppermute x4, waiting for transfers between devices, rimmed(): from_above = lax.ppermute(low, 'gz', backward)  12.6 us
    ppermute x8, starting transfers between devices, domain_total(): from_high = lax.ppermute(backward, 'gz', behind)  10.5 us
    ppermute x8, waiting for transfers between devices, domain_total(): from_high = lax.ppermute(backward, 'gz', behind)  9.75 us
    ppermute x8, waiting for transfers between devices, domain_total(): from_low = lax.ppermute(forward, 'gz', ahead)  5.42 us
  transfers between devices with their start and end apart: 24, of which 16 were waited for; matrix products, arithmetic and copies ran while one was open for 1% of the time, Pallas kernels for 0%

profile of v15, /device:TPU:0, one launch (start us, length us, event | category | flops | bytes accessed | tf_op | source)
XLA Modules:
  0.0 238.5 jit_solution(136271829378086684)
XLA Ops:
  0.0 1.5 fusion.11
  1.5 1.3 collective-permute-start.1
  2.8 3.1 %collective-permute-start = (bf16[3,8,64,256]{3,2,1,0:T(8,128)(2,1)S(1)}, bf16[3,8,64,256]{3,2,1,0:T(8,128)(2,1)S(1)}, u32[]{:S(2)}, u32[]{:S(2)}) collective-permute-start(bf16[3,8,64,256]{3,2,1,0:T(8,128)(2,1)S(1)} %get-tuple-element.22.high_ref), channel_id=1, source_target_pairs={{0,1},{1,2},{2,3},{3,4},{4,5},{5,6},{6,7},{7,8},{8,9},{9,10},{10,1... | collective-permute-start | bytes 2359304 | tf_op jit(solution)/shard_map/ppermute | solution.py:220
  6.0 0.7 fusion.12
  9.3 0.6 add_convert_fusion.rim_ref
  9.9 1.6 broadcast_in_dim.8.low_pot_ref.high_pot_ref
  11.6 6.6 %shard_map.37 = (bf16[3,8,64,256]{3,2,1,0:T(8,128)(2,1)}, bf16[3,8,64,256]{3,2,1,0:T(8,128)(2,1)}) custom-call(f32[2]{0:T(128)} %add_convert_fusion.rim_ref, bf16[3,8,64,256]{3,2,1,0:T(8,128)(2,1)} %copy-done.3, bf16[3,8,64,256]{3,2,1,0:T(8,128)(2,1)} %copy-done, bf16[3,8,64,256]{3,2,1,0:T(8,128)(2,1)} %copy-done.1, bf16[3,8,64,256]{3,2,1,0:T(8,128)(2,1)} %copy-done.2, ...), custom_call_target="tpu_custom_call" | custom-call | tf_op jit(solution)/shard_map/pallas_call | solution.py:133
  18.2 16.8 %collective-permute-start.2 = (bf16[3,8,64,256]{3,2,1,0:T(8,128)(2,1)}, bf16[3,8,64,256]{3,2,1,0:T(8,128)(2,1)S(1)}, u32[]{:S(2)}, u32[]{:S(2)}) collective-permute-start(bf16[3,8,64,256]{3,2,1,0:T(8,128)(2,1)} %get-tuple-element.13.high_ref.older_high_ref), channel_id=1, source_target_pairs={{0,1},{1,2},{2,3},{3,4},{4,5},{5,6},{6,7},{7,8},{8,9},{9,10},{10,1... | collective-permute-start | bytes 2359304 | tf_op jit(solution)/shard_map/ppermute | solution.py:220
  35.0 1.3 collective-permute-start.3
  36.3 0.8 collective-permute-done.2.below_ref
  37.1 4.3 %collective-permute-done.3.above_ref = bf16[3,8,64,256]{3,2,1,0:T(8,128)(2,1)S(1)} collective-permute-done((bf16[3,8,64,256]{3,2,1,0:T(8,128)(2,1)}, bf16[3,8,64,256]{3,2,1,0:T(8,128)(2,1)S(1)}, u32[]{:S(2)}, u32[]{:S(2)}) %collective-permute-start.3) | collective-permute-done | bytes 786464 | tf_op jit(solution)/shard_map/ppermute | solution.py:221
  41.4 0.9 copy-done.5
  42.2 6.8 %shard_map.38 = (bf16[3,8,64,256]{3,2,1,0:T(8,128)(2,1)}, bf16[3,8,64,256]{3,2,1,0:T(8,128)(2,1)}) custom-call(f32[2]{0:T(128)} %add_convert_fusion.rim_ref, bf16[3,8,64,256]{3,2,1,0:T(8,128)(2,1)} %copy-done.4, bf16[3,8,64,256]{3,2,1,0:T(8,128)(2,1)} %get-tuple-element.14.low_ref.older_low_ref, ...), custom_call_target="tpu_custom_call" | custom-call | tf_op jit(solution)/shard_map/pallas_call | solution.py:133
  49.0 16.6 %collective-permute-start.4 = (bf16[3,8,64,256]{3,2,1,0:T(8,128)(2,1)}, bf16[3,8,64,256]{3,2,1,0:T(8,128)(2,1)S(1)}, u32[]{:S(2)}, u32[]{:S(2)}) collective-permute-start(bf16[3,8,64,256]{3,2,1,0:T(8,128)(2,1)} %get-tuple-element.15.high_ref.older_high_ref), channel_id=1, source_target_pairs={{0,1},{1,2},{2,3},{3,4},{4,5},{5,6},{6,7},{7,8},{8,9},{9,10},{10,1... | collective-permute-start | bytes 2359304 | tf_op jit(solution)/shard_map/ppermute | solution.py:220
  65.6 1.3 collective-permute-start.5
  66.9 0.8 collective-permute-done.4.below_ref
  67.7 4.2 %collective-permute-done.5.above_ref = bf16[3,8,64,256]{3,2,1,0:T(8,128)(2,1)S(1)} collective-permute-done((bf16[3,8,64,256]{3,2,1,0:T(8,128)(2,1)}, bf16[3,8,64,256]{3,2,1,0:T(8,128)(2,1)S(1)}, u32[]{:S(2)}, u32[]{:S(2)}) %collective-permute-start.5) | collective-permute-done | bytes 786464 | tf_op jit(solution)/shard_map/ppermute | solution.py:221
  71.8 0.9 copy-done.9
  72.7 6.8 %shard_map.39 = (bf16[3,8,64,256]{3,2,1,0:T(8,128)(2,1)}, bf16[3,8,64,256]{3,2,1,0:T(8,128)(2,1)}) custom-call(f32[2]{0:T(128)} %add_convert_fusion.rim_ref, bf16[3,8,64,256]{3,2,1,0:T(8,128)(2,1)} %copy-done.7, bf16[3,8,64,256]{3,2,1,0:T(8,128)(2,1)} %get-tuple-element.16.low_ref.older_low_ref, ...), custom_call_target="tpu_custom_call" | custom-call | tf_op jit(solution)/shard_map/pallas_call | solution.py:133
  79.5 16.6 %collective-permute-start.6 = (bf16[3,8,64,256]{3,2,1,0:T(8,128)(2,1)}, bf16[3,8,64,256]{3,2,1,0:T(8,128)(2,1)S(1)}, u32[]{:S(2)}, u32[]{:S(2)}) collective-permute-start(bf16[3,8,64,256]{3,2,1,0:T(8,128)(2,1)} %get-tuple-element.17.high_ref), channel_id=1, source_target_pairs={{0,1},{1,2},{2,3},{3,4},{4,5},{5,6},{6,7},{7,8},{8,9},{9,10},{10,1... | collective-permute-start | bytes 2359304 | tf_op jit(solution)/shard_map/ppermute | solution.py:220
  96.2 1.3 collective-permute-start.7
  97.5 0.8 collective-permute-done.6.below_ref
  98.2 4.2 %collective-permute-done.7.above_ref = bf16[3,8,64,256]{3,2,1,0:T(8,128)(2,1)S(1)} collective-permute-done((bf16[3,8,64,256]{3,2,1,0:T(8,128)(2,1)}, bf16[3,8,64,256]{3,2,1,0:T(8,128)(2,1)S(1)}, u32[]{:S(2)}, u32[]{:S(2)}) %collective-permute-start.7) | collective-permute-done | bytes 786464 | tf_op jit(solution)/shard_map/ppermute | solution.py:221
  102.4 0.9 copy-done.8
  103.3 6.8 %shard_map.40 = (bf16[3,8,64,256]{3,2,1,0:T(8,128)(2,1)}, bf16[3,8,64,256]{3,2,1,0:T(8,128)(2,1)}) custom-call(f32[2]{0:T(128)} %add_convert_fusion.rim_ref, bf16[3,8,64,256]{3,2,1,0:T(8,128)(2,1)} %copy-done.6, bf16[3,8,64,256]{3,2,1,0:T(8,128)(2,1)} %get-tuple-element.18.low_ref, bf16[3,8,64,256]{3,2,1,0:T(8,128)(2,1)} %get-tuple-element.17.high_ref, ...), custom_call_target="tpu_custom_call" | custom-call | tf_op jit(solution)/shard_map/pallas_call | solution.py:133
  110.1 1.5 pad_maximum_fusion
  111.6 0.4 fusion.2
  112.0 1.3 collective-permute-start.12
  113.3 17.2 %collective-permute-start.8 = (f32[128,256]{1,0:T(8,128)S(1)}, f32[128,256]{1,0:T(8,128)S(1)}, u32[]{:S(2)}, u32[]{:S(2)}) collective-permute-start(f32[128,256]{1,0:T(8,128)S(1)} %fusion.2), channel_id=1, source_target_pairs={{0,1},{1,2},{2,3},{3,4},{4,5},{5,6},{6,7},{7,8},{8,9},{9,10},{10,1... | collective-permute-start | bytes 393224 | tf_op jit(solution)/shard_map/ppermute | solution.py:248
  130.5 0.9 collective-permute-done.8
  131.5 7.6 %collective-permute-start.9 = (f32[128,256]{1,0:T(8,128)S(1)}, f32[128,256]{1,0:T(8,128)S(1)}, u32[]{:S(2)}, u32[]{:S(2)}) collective-permute-start(f32[128,256]{1,0:T(8,128)S(1)} %get-tuple-element.23), channel_id=1, source_target_pairs={{0,2},{1,3},{2,4},{3,5},{4,6},{5,7},{6,8},{7,9},{8,10},{9,11},{10,... | collective-permute-start | bytes 393224 | tf_op jit(solution)/shard_map/ppermute | solution.py:248
  144.1 1.3 collective-permute-start.13
  145.5 5.3 %collective-permute-start.10 = (f32[128,256]{1,0:T(8,128)S(1)}, f32[128,256]{1,0:T(8,128)S(1)}, u32[]{:S(2)}, u32[]{:S(2)}) collective-permute-start(f32[128,256]{1,0:T(8,128)S(1)} %multiply_add_fusion.4), channel_id=1, source_target_pairs={{0,4},{1,5},{2,6},{3,7},{4,8},{5,9},{6,10},{7,11},{8,12},{9,13},{1... | collective-permute-start | bytes 393224 | tf_op jit(solution)/shard_map/ppermute | solution.py:248
  150.7 0.2 collective-permute-done.13
  151.0 1.3 collective-permute-start.14
  152.3 1.3 collective-permute-done.10
  153.6 3.6 %collective-permute-start.11 = (f32[128,256]{1,0:T(8,128)S(1)}, f32[128,256]{1,0:T(8,128)S(1)}, u32[]{:S(2)}, u32[]{:S(2)}) collective-permute-start(f32[128,256]{1,0:T(8,128)S(1)} %multiply_add_fusion.3), channel_id=1, source_target_pairs={{0,8},{1,9},{2,10},{3,11},{4,12},{5,13},{6,14},{7,15},{16,24},{17,... | collective-permute-start | bytes 393224 | tf_op jit(solution)/shard_map/ppermute | solution.py:248
  157.3 0.6 collective-permute-done.14
  157.9 1.5 collective-permute-start.15
  161.9 1.2 fusion.10
  163.8 3.0 %collective-permute-done.15 = f32[128,256]{1,0:T(8,128)S(1)} collective-permute-done((f32[128,256]{1,0:T(8,128)S(1)}, f32[128,256]{1,0:T(8,128)S(1)}, u32[]{:S(2)}, u32[]{:S(2)}) %collective-permute-start.15) | collective-permute-done | bytes 131104 | tf_op jit(solution)/shard_map/ppermute | solution.py:249
  166.8 0.6 slice.25.gram_ref
  167.5 16.6 %shard_map.41 = f32[128,128]{1,0:T(8,128)} custom-call(f32[128,128]{1,0:T(8,128)} %slice.25.gram_ref), custom_call_target="tpu_custom_call" | custom-call | tf_op jit(solution)/shard_map/pallas_call | solution.py:60
  184.1 1.3 convolution_convert_fusion.1
  185.4 0.5 fusion
  185.9 0.4 fusion.13
  186.3 1.3 collective-permute-start.20
  187.6 3.0 %collective-permute-start.16 = (f32[128,128]{1,0:T(8,128)S(1)}, f32[128,128]{1,0:T(8,128)S(1)}, u32[]{:S(2)}, u32[]{:S(2)}) collective-permute-start(f32[128,128]{1,0:T(8,128)S(1)} %fusion.13), channel_id=1, source_target_pairs={{0,1},{1,2},{2,3},{3,4},{4,5},{5,6},{6,7},{7,8},{8,9},{9,10},{10,1... | collective-permute-start | bytes 196616 | tf_op jit(solution)/shard_map/ppermute | solution.py:248
  190.7 0.9 collective-permute-done.16
  191.6 5.7 %collective-permute-start.17 = (f32[128,128]{1,0:T(8,128)S(1)}, f32[128,128]{1,0:T(8,128)S(1)}, u32[]{:S(2)}, u32[]{:S(2)}) collective-permute-start(f32[128,128]{1,0:T(8,128)S(1)} %get-tuple-element.25), channel_id=1, source_target_pairs={{0,2},{1,3},{2,4},{3,5},{4,6},{5,7},{6,8},{7,9},{8,10},{9,11},{10,... | collective-permute-start | bytes 196616 | tf_op jit(solution)/shard_map/ppermute | solution.py:248
  197.3 1.3 collective-permute-start.21
  198.6 1.2 collective-permute-done.17
  199.8 4.4 %collective-permute-start.18 = (f32[128,128]{1,0:T(8,128)S(1)}, f32[128,128]{1,0:T(8,128)S(1)}, u32[]{:S(2)}, u32[]{:S(2)}) collective-permute-start(f32[128,128]{1,0:T(8,128)S(1)} %multiply_add_fusion.10), channel_id=1, source_target_pairs={{0,4},{1,5},{2,6},{3,7},{4,8},{5,9},{6,10},{7,11},{8,12},{9,13},{1... | collective-permute-start | bytes 196616 | tf_op jit(solution)/shard_map/ppermute | solution.py:248
  204.2 1.3 collective-permute-start.22
  205.5 0.6 collective-permute-done.18
  206.1 4.4 %collective-permute-start.19 = (f32[128,128]{1,0:T(8,128)S(1)}, f32[128,128]{1,0:T(8,128)S(1)}, u32[]{:S(2)}, u32[]{:S(2)}) collective-permute-start(f32[128,128]{1,0:T(8,128)S(1)} %multiply_add_fusion.9), channel_id=1, source_target_pairs={{0,8},{1,9},{2,10},{3,11},{4,12},{5,13},{6,14},{7,15},{16,24},{17,... | collective-permute-start | bytes 196616 | tf_op jit(solution)/shard_map/ppermute | solution.py:248
  210.5 1.3 collective-permute-start.23
  211.8 0.6 collective-permute-done.19
  212.4 5.9 %collective-permute-done.23 = f32[128,128]{1,0:T(8,128)S(1)} collective-permute-done((f32[128,128]{1,0:T(8,128)S(1)}, f32[128,128]{1,0:T(8,128)S(1)}, u32[]{:S(2)}, u32[]{:S(2)}) %collective-permute-start.23) | collective-permute-done | bytes 65568 | tf_op jit(solution)/shard_map/ppermute | solution.py:249
  218.3 0.7 subtract_divide_fusion.1.gram_ref
  218.9 16.6 %shard_map.42 = f32[128,128]{1,0:T(8,128)} custom-call(f32[128,128]{1,0:T(8,128)} %subtract_divide_fusion.1.gram_ref), custom_call_target="tpu_custom_call" | custom-call | tf_op jit(solution)/shard_map/pallas_call | solution.py:60
  235.6 1.2 convolution_convert_fusion
  236.8 0.1 pad_maximum_fusion.1
  236.9 1.6 copy.5
  (43 shorter events, 0.3 us)
Async XLA Ops:
  0.0 5.9 %copy-start.11 = (s32[16]{0:T(128)S(1)}, s32[16]{0:T(128)}, u32[]{:S(2)}) copy-start(s32[16]{0:T(128)} %param.5) | copy-start | bytes 196
  0.0 9.3 %copy-start.12 = (f32[6,512]{1,0:T(8,128)S(1)}, f32[6,512]{1,0:T(8,128)}, u32[]{:S(2)}) copy-start(f32[6,512]{1,0:T(8,128)} %param.4) | copy-start | bytes 36868
  1.5 10.1 %copy-start = (bf16[3,8,64,256]{3,2,1,0:T(8,128)(2,1)}, bf16[3,8,64,256]{3,2,1,0:T(8,128)(2,1)S(1)}, u32[]{:S(2)}) copy-start(bf16[3,8,64,256]{3,2,1,0:T(8,128)(2,1)S(1)} %get-tuple-element.21.low_ref) | copy-start | bytes 2359300
  1.5 10.1 %copy-start.1 = (bf16[3,8,64,256]{3,2,1,0:T(8,128)(2,1)}, bf16[3,8,64,256]{3,2,1,0:T(8,128)(2,1)S(1)}, u32[]{:S(2)}) copy-start(bf16[3,8,64,256]{3,2,1,0:T(8,128)(2,1)S(1)} %get-tuple-element.22.high_ref) | copy-start | bytes 2359300
  1.5 8.4 %collective-permute-start.1 = (bf16[3,8,64,256]{3,2,1,0:T(8,128)(2,1)S(1)}, bf16[3,8,64,256]{3,2,1,0:T(8,128)(2,1)S(1)}, u32[]{:S(2)}, u32[]{:S(2)}) collective-permute-start(bf16[3,8,64,256]{3,2,1,0:T(8,128)(2,1)S(1)} %get-tuple-element.21.low_ref), channel_id=1, source_target_pairs={{1,0},{2,1},{3,2},{4,3},{5,4},{6,5},{7,6},{8,7},{9,8},{10,9},{11,1... | collective-permute-start | bytes 2359304 | tf_op jit(solution)/shard_map/ppermute | solution.py:221
  2.8 7.1 %collective-permute-start = (bf16[3,8,64,256]{3,2,1,0:T(8,128)(2,1)S(1)}, bf16[3,8,64,256]{3,2,1,0:T(8,128)(2,1)S(1)}, u32[]{:S(2)}, u32[]{:S(2)}) collective-permute-start(bf16[3,8,64,256]{3,2,1,0:T(8,128)(2,1)S(1)} %get-tuple-element.22.high_ref), channel_id=1, source_target_pairs={{0,1},{1,2},{2,3},{3,4},{4,5},{5,6},{6,7},{7,8},{8,9},{9,10},{10,1... | collective-permute-start | bytes 2359304 | tf_op jit(solution)/shard_map/ppermute | solution.py:220
  9.9 1.7 copy-start.2
  9.9 1.7 copy-start.3
  18.2 18.8 %collective-permute-start.2 = (bf16[3,8,64,256]{3,2,1,0:T(8,128)(2,1)}, bf16[3,8,64,256]{3,2,1,0:T(8,128)(2,1)S(1)}, u32[]{:S(2)}, u32[]{:S(2)}) collective-permute-start(bf16[3,8,64,256]{3,2,1,0:T(8,128)(2,1)} %get-tuple-element.13.high_ref.older_high_ref), channel_id=1, source_target_pairs={{0,1},{1,2},{2,3},{3,4},{4,5},{5,6},{6,7},{7,8},{8,9},{9,10},{10,1... | collective-permute-start | bytes 2359304 | tf_op jit(solution)/shard_map/ppermute | solution.py:220
  35.0 6.3 %collective-permute-start.3 = (bf16[3,8,64,256]{3,2,1,0:T(8,128)(2,1)}, bf16[3,8,64,256]{3,2,1,0:T(8,128)(2,1)S(1)}, u32[]{:S(2)}, u32[]{:S(2)}) collective-permute-start(bf16[3,8,64,256]{3,2,1,0:T(8,128)(2,1)} %get-tuple-element.14.low_ref.older_low_ref), channel_id=1, source_target_pairs={{1,0},{2,1},{3,2},{4,3},{5,4},{6,5},{7,6},{8,7},{9,8},{10,9},{11,1... | collective-permute-start | bytes 2359304 | tf_op jit(solution)/shard_map/ppermute | solution.py:221
  37.1 4.3 %copy-start.4 = (bf16[3,8,64,256]{3,2,1,0:T(8,128)(2,1)}, bf16[3,8,64,256]{3,2,1,0:T(8,128)(2,1)S(1)}, u32[]{:S(2)}) copy-start(bf16[3,8,64,256]{3,2,1,0:T(8,128)(2,1)S(1)} %collective-permute-done.2.below_ref) | copy-start | bytes 2359300
  41.3 0.9 copy-start.5
  49.0 18.6 %collective-permute-start.4 = (bf16[3,8,64,256]{3,2,1,0:T(8,128)(2,1)}, bf16[3,8,64,256]{3,2,1,0:T(8,128)(2,1)S(1)}, u32[]{:S(2)}, u32[]{:S(2)}) collective-permute-start(bf16[3,8,64,256]{3,2,1,0:T(8,128)(2,1)} %get-tuple-element.15.high_ref.older_high_ref), channel_id=1, source_target_pairs={{0,1},{1,2},{2,3},{3,4},{4,5},{5,6},{6,7},{7,8},{8,9},{9,10},{10,1... | collective-permute-start | bytes 2359304 | tf_op jit(solution)/shard_map/ppermute | solution.py:220
  65.6 6.2 %collective-permute-start.5 = (bf16[3,8,64,256]{3,2,1,0:T(8,128)(2,1)}, bf16[3,8,64,256]{3,2,1,0:T(8,128)(2,1)S(1)}, u32[]{:S(2)}, u32[]{:S(2)}) collective-permute-start(bf16[3,8,64,256]{3,2,1,0:T(8,128)(2,1)} %get-tuple-element.16.low_ref.older_low_ref), channel_id=1, source_target_pairs={{1,0},{2,1},{3,2},{4,3},{5,4},{6,5},{7,6},{8,7},{9,8},{10,9},{11,1... | collective-permute-start | bytes 2359304 | tf_op jit(solution)/shard_map/ppermute | solution.py:221
  67.7 4.2 %copy-start.7 = (bf16[3,8,64,256]{3,2,1,0:T(8,128)(2,1)}, bf16[3,8,64,256]{3,2,1,0:T(8,128)(2,1)S(1)}, u32[]{:S(2)}) copy-start(bf16[3,8,64,256]{3,2,1,0:T(8,128)(2,1)S(1)} %collective-permute-done.4.below_ref) | copy-start | bytes 2359300
  71.8 0.9 copy-start.9
  79.5 18.7 %collective-permute-start.6 = (bf16[3,8,64,256]{3,2,1,0:T(8,128)(2,1)}, bf16[3,8,64,256]{3,2,1,0:T(8,128)(2,1)S(1)}, u32[]{:S(2)}, u32[]{:S(2)}) collective-permute-start(bf16[3,8,64,256]{3,2,1,0:T(8,128)(2,1)} %get-tuple-element.17.high_ref), channel_id=1, source_target_pairs={{0,1},{1,2},{2,3},{3,4},{4,5},{5,6},{6,7},{7,8},{8,9},{9,10},{10,1... | collective-permute-start | bytes 2359304 | tf_op jit(solution)/shard_map/ppermute | solution.py:220
  96.2 6.2 %collective-permute-start.7 = (bf16[3,8,64,256]{3,2,1,0:T(8,128)(2,1)}, bf16[3,8,64,256]{3,2,1,0:T(8,128)(2,1)S(1)}, u32[]{:S(2)}, u32[]{:S(2)}) collective-permute-start(bf16[3,8,64,256]{3,2,1,0:T(8,128)(2,1)} %get-tuple-element.18.low_ref), channel_id=1, source_target_pairs={{1,0},{2,1},{3,2},{4,3},{5,4},{6,5},{7,6},{8,7},{9,8},{10,9},{11,1... | collective-permute-start | bytes 2359304 | tf_op jit(solution)/shard_map/ppermute | solution.py:221
  98.2 4.2 %copy-start.6 = (bf16[3,8,64,256]{3,2,1,0:T(8,128)(2,1)}, bf16[3,8,64,256]{3,2,1,0:T(8,128)(2,1)S(1)}, u32[]{:S(2)}) copy-start(bf16[3,8,64,256]{3,2,1,0:T(8,128)(2,1)S(1)} %collective-permute-done.6.below_ref) | copy-start | bytes 2359300
  102.4 0.9 copy-start.8
  112.0 18.5 %collective-permute-start.12 = (f32[128,256]{1,0:T(8,128)S(1)}, f32[128,256]{1,0:T(8,128)S(1)}, u32[]{:S(2)}, u32[]{:S(2)}) collective-permute-start(f32[128,256]{1,0:T(8,128)S(1)} %fusion.2), channel_id=1, source_target_pairs={{1,0},{2,1},{3,2},{4,3},{5,4},{6,5},{7,6},{8,7},{9,8},{10,9},{11,1... | collective-permute-start | bytes 393224 | tf_op jit(solution)/shard_map/ppermute | solution.py:249
  113.3 18.1 %collective-permute-start.8 = (f32[128,256]{1,0:T(8,128)S(1)}, f32[128,256]{1,0:T(8,128)S(1)}, u32[]{:S(2)}, u32[]{:S(2)}) collective-permute-start(f32[128,256]{1,0:T(8,128)S(1)} %fusion.2), channel_id=1, source_target_pairs={{0,1},{1,2},{2,3},{3,4},{4,5},{5,6},{6,7},{7,8},{8,9},{9,10},{10,1... | collective-permute-start | bytes 393224 | tf_op jit(solution)/shard_map/ppermute | solution.py:248
  131.5 13.9 %collective-permute-start.9 = (f32[128,256]{1,0:T(8,128)S(1)}, f32[128,256]{1,0:T(8,128)S(1)}, u32[]{:S(2)}, u32[]{:S(2)}) collective-permute-start(f32[128,256]{1,0:T(8,128)S(1)} %get-tuple-element.23), channel_id=1, source_target_pairs={{0,2},{1,3},{2,4},{3,5},{4,6},{5,7},{6,8},{7,9},{8,10},{9,11},{10,... | collective-permute-start | bytes 393224 | tf_op jit(solution)/shard_map/ppermute | solution.py:248
  144.1 6.9 %collective-permute-start.13 = (f32[128,256]{1,0:T(8,128)S(1)}, f32[128,256]{1,0:T(8,128)S(1)}, u32[]{:S(2)}, u32[]{:S(2)}) collective-permute-start(f32[128,256]{1,0:T(8,128)S(1)} %get-tuple-element.24), channel_id=1, source_target_pairs={{2,0},{3,1},{4,2},{5,3},{6,4},{7,5},{8,6},{9,7},{10,8},{11,9},{12,... | collective-permute-start | bytes 393224 | tf_op jit(solution)/shard_map/ppermute | solution.py:249
  145.5 8.2 %collective-permute-start.10 = (f32[128,256]{1,0:T(8,128)S(1)}, f32[128,256]{1,0:T(8,128)S(1)}, u32[]{:S(2)}, u32[]{:S(2)}) collective-permute-start(f32[128,256]{1,0:T(8,128)S(1)} %multiply_add_fusion.4), channel_id=1, source_target_pairs={{0,4},{1,5},{2,6},{3,7},{4,8},{5,9},{6,10},{7,11},{8,12},{9,13},{1... | collective-permute-start | bytes 393224 | tf_op jit(solution)/shard_map/ppermute | solution.py:248
  151.0 6.9 %collective-permute-start.14 = (f32[128,256]{1,0:T(8,128)S(1)}, f32[128,256]{1,0:T(8,128)S(1)}, u32[]{:S(2)}, u32[]{:S(2)}) collective-permute-start(f32[128,256]{1,0:T(8,128)S(1)} %multiply_add_fusion.1), channel_id=1, source_target_pairs={{4,0},{5,1},{6,2},{7,3},{8,4},{9,5},{10,6},{11,7},{12,8},{13,9},{1... | collective-permute-start | bytes 393224 | tf_op jit(solution)/shard_map/ppermute | solution.py:249
  153.6 10.1 %collective-permute-start.11 = (f32[128,256]{1,0:T(8,128)S(1)}, f32[128,256]{1,0:T(8,128)S(1)}, u32[]{:S(2)}, u32[]{:S(2)}) collective-permute-start(f32[128,256]{1,0:T(8,128)S(1)} %multiply_add_fusion.3), channel_id=1, source_target_pairs={{0,8},{1,9},{2,10},{3,11},{4,12},{5,13},{6,14},{7,15},{16,24},{17,... | collective-permute-start | bytes 393224 | tf_op jit(solution)/shard_map/ppermute | solution.py:248
  157.9 8.9 %collective-permute-start.15 = (f32[128,256]{1,0:T(8,128)S(1)}, f32[128,256]{1,0:T(8,128)S(1)}, u32[]{:S(2)}, u32[]{:S(2)}) collective-permute-start(f32[128,256]{1,0:T(8,128)S(1)} %multiply_add_fusion), channel_id=1, source_target_pairs={{8,0},{9,1},{10,2},{11,3},{12,4},{13,5},{14,6},{15,7},{24,16},{25,... | collective-permute-start | bytes 393224 | tf_op jit(solution)/shard_map/ppermute | solution.py:249
  184.1 1.3 copy-start.10
  186.3 4.3 %collective-permute-start.20 = (f32[128,128]{1,0:T(8,128)S(1)}, f32[128,128]{1,0:T(8,128)S(1)}, u32[]{:S(2)}, u32[]{:S(2)}) collective-permute-start(f32[128,128]{1,0:T(8,128)S(1)} %fusion.13), channel_id=1, source_target_pairs={{1,0},{2,1},{3,2},{4,3},{5,4},{6,5},{7,6},{8,7},{9,8},{10,9},{11,1... | collective-permute-start | bytes 196616 | tf_op jit(solution)/shard_map/ppermute | solution.py:249
  187.6 3.9 %collective-permute-start.16 = (f32[128,128]{1,0:T(8,128)S(1)}, f32[128,128]{1,0:T(8,128)S(1)}, u32[]{:S(2)}, u32[]{:S(2)}) collective-permute-start(f32[128,128]{1,0:T(8,128)S(1)} %fusion.13), channel_id=1, source_target_pairs={{0,1},{1,2},{2,3},{3,4},{4,5},{5,6},{6,7},{7,8},{8,9},{9,10},{10,1... | collective-permute-start | bytes 196616 | tf_op jit(solution)/shard_map/ppermute | solution.py:248
  191.6 8.2 %collective-permute-start.17 = (f32[128,128]{1,0:T(8,128)S(1)}, f32[128,128]{1,0:T(8,128)S(1)}, u32[]{:S(2)}, u32[]{:S(2)}) collective-permute-start(f32[128,128]{1,0:T(8,128)S(1)} %get-tuple-element.25), channel_id=1, source_target_pairs={{0,2},{1,3},{2,4},{3,5},{4,6},{5,7},{6,8},{7,9},{8,10},{9,11},{10,... | collective-permute-start | bytes 196616 | tf_op jit(solution)/shard_map/ppermute | solution.py:248
  197.3 6.9 %collective-permute-start.21 = (f32[128,128]{1,0:T(8,128)S(1)}, f32[128,128]{1,0:T(8,128)S(1)}, u32[]{:S(2)}, u32[]{:S(2)}) collective-permute-start(f32[128,128]{1,0:T(8,128)S(1)} %get-tuple-element.26), channel_id=1, source_target_pairs={{2,0},{3,1},{4,2},{5,3},{6,4},{7,5},{8,6},{9,7},{10,8},{11,9},{12,... | collective-permute-start | bytes 196616 | tf_op jit(solution)/shard_map/ppermute | solution.py:249
  199.8 6.3 %collective-permute-start.18 = (f32[128,128]{1,0:T(8,128)S(1)}, f32[128,128]{1,0:T(8,128)S(1)}, u32[]{:S(2)}, u32[]{:S(2)}) collective-permute-start(f32[128,128]{1,0:T(8,128)S(1)} %multiply_add_fusion.10), channel_id=1, source_target_pairs={{0,4},{1,5},{2,6},{3,7},{4,8},{5,9},{6,10},{7,11},{8,12},{9,13},{1... | collective-permute-start | bytes 196616 | tf_op jit(solution)/shard_map/ppermute | solution.py:248
  204.2 6.3 %collective-permute-start.22 = (f32[128,128]{1,0:T(8,128)S(1)}, f32[128,128]{1,0:T(8,128)S(1)}, u32[]{:S(2)}, u32[]{:S(2)}) collective-permute-start(f32[128,128]{1,0:T(8,128)S(1)} %multiply_add_fusion.7), channel_id=1, source_target_pairs={{4,0},{5,1},{6,2},{7,3},{8,4},{9,5},{10,6},{11,7},{12,8},{13,9},{1... | collective-permute-start | bytes 196616 | tf_op jit(solution)/shard_map/ppermute | solution.py:249
  206.1 6.3 %collective-permute-start.19 = (f32[128,128]{1,0:T(8,128)S(1)}, f32[128,128]{1,0:T(8,128)S(1)}, u32[]{:S(2)}, u32[]{:S(2)}) collective-permute-start(f32[128,128]{1,0:T(8,128)S(1)} %multiply_add_fusion.9), channel_id=1, source_target_pairs={{0,8},{1,9},{2,10},{3,11},{4,12},{5,13},{6,14},{7,15},{16,24},{17,... | collective-permute-start | bytes 196616 | tf_op jit(solution)/shard_map/ppermute | solution.py:248
  210.5 7.8 %collective-permute-start.23 = (f32[128,128]{1,0:T(8,128)S(1)}, f32[128,128]{1,0:T(8,128)S(1)}, u32[]{:S(2)}, u32[]{:S(2)}) collective-permute-start(f32[128,128]{1,0:T(8,128)S(1)} %multiply_add_fusion.6), channel_id=1, source_target_pairs={{8,0},{9,1},{10,2},{11,3},{12,4},{13,5},{14,6},{15,7},{24,16},{25,... | collective-permute-start | bytes 196616 | tf_op jit(solution)/shard_map/ppermute | solution.py:249

commit v16 on v15

--- a/solution.py
+++ b/solution.py
@@ -35,10 +35,10 @@
         k = 2 * pair
         row_a = work_ref[pl.ds(k, 1), :]
         row_b = work_ref[pl.ds(k + 1, 1), :]
-        scale_a = 1.0 / jnp.sqrt(pick(row_a, k))
+        scale_a = lax.rsqrt(pick(row_a, k))
         scaled_a = row_a * scale_a
         row_b = row_b - (pick(row_b, k) * scale_a) * scaled_a
-        scale_b = 1.0 / jnp.sqrt(pick(row_b, k + 1))
+        scale_b = lax.rsqrt(pick(row_b, k + 1))
         scaled_b = row_b * scale_b
         whole = work_ref[...]
         left = whole[:, :n]

time: 240 us -> 238 us (level)
  no operation moved by 1% of the time
where the time goes in v16:
time: 238 us; the launch traced here: 236 us
  starting transfers between devices  120 us (50%)
  Pallas kernels  58.3 us (24%)
  waiting for transfers between devices  30 us (13%)
  between operations  11.3 us (5%)
  local copies, waits for them, and re-layouts  8.82 us (4%)
  other arithmetic  4.29 us (2%)
  matrix products  3.8 us (2%)
    ppermute x4, starting transfers between devices, rimmed(): from_below = lax.ppermute(high, 'gz', forward)  53 us
    ppermute x8, starting transfers between devices, domain_total(): from_low = lax.ppermute(forward, 'gz', ahead)  51.2 us
    pallas_call x2, Pallas kernels, lower_inverse(): pl.pallas_call(_lower_inverse_kernel, out_shape=jax.ShapeDtypeStruct((n,...  31.3 us
    pallas_call x4, Pallas kernels, chebyshev_step(): pl.pallas_call(functools.partial(_step_kernel, first), out_shape=(piece,...  27 us
    ppermute x4, waiting for transfers between devices, rimmed(): from_above = lax.ppermute(low, 'gz', backward)  12.6 us
    ppermute x8, starting transfers between devices, domain_total(): from_high = lax.ppermute(backward, 'gz', behind)  10.5 us
    ppermute x8, waiting for transfers between devices, domain_total(): from_high = lax.ppermute(backward, 'gz', behind)  9.75 us
    ppermute x8, waiting for transfers between devices, domain_total(): from_low = lax.ppermute(forward, 'gz', ahead)  5.42 us
  transfers between devices with their start and end apart: 24, of which 16 were waited for; matrix products, arithmetic and copies ran while one was open for 1% of the time, Pallas kernels for 0%

profile of v16, /device:TPU:0, one launch (start us, length us, event | category | flops | bytes accessed | tf_op | source)
XLA Modules:
  0.0 236.4 jit_solution(4198920551111412157)
XLA Ops:
  0.0 1.5 fusion.11
  1.5 1.3 collective-permute-start.1
  2.8 3.1 %collective-permute-start = (bf16[3,8,64,256]{3,2,1,0:T(8,128)(2,1)S(1)}, bf16[3,8,64,256]{3,2,1,0:T(8,128)(2,1)S(1)}, u32[]{:S(2)}, u32[]{:S(2)}) collective-permute-start(bf16[3,8,64,256]{3,2,1,0:T(8,128)(2,1)S(1)} %get-tuple-element.22.high_ref), channel_id=1, source_target_pairs={{0,1},{1,2},{2,3},{3,4},{4,5},{5,6},{6,7},{7,8},{8,9},{9,10},{10,1... | collective-permute-start | bytes 2359304 | tf_op jit(solution)/shard_map/ppermute | solution.py:220
  6.0 0.7 fusion.12
  9.3 0.6 add_convert_fusion.rim_ref
  9.9 1.6 broadcast_in_dim.8.low_pot_ref.high_pot_ref
  11.6 6.6 %shard_map.37 = (bf16[3,8,64,256]{3,2,1,0:T(8,128)(2,1)}, bf16[3,8,64,256]{3,2,1,0:T(8,128)(2,1)}) custom-call(f32[2]{0:T(128)} %add_convert_fusion.rim_ref, bf16[3,8,64,256]{3,2,1,0:T(8,128)(2,1)} %copy-done.3, bf16[3,8,64,256]{3,2,1,0:T(8,128)(2,1)} %copy-done, bf16[3,8,64,256]{3,2,1,0:T(8,128)(2,1)} %copy-done.1, bf16[3,8,64,256]{3,2,1,0:T(8,128)(2,1)} %copy-done.2, ...), custom_call_target="tpu_custom_call" | custom-call | tf_op jit(solution)/shard_map/pallas_call | solution.py:133
  18.2 16.8 %collective-permute-start.2 = (bf16[3,8,64,256]{3,2,1,0:T(8,128)(2,1)}, bf16[3,8,64,256]{3,2,1,0:T(8,128)(2,1)S(1)}, u32[]{:S(2)}, u32[]{:S(2)}) collective-permute-start(bf16[3,8,64,256]{3,2,1,0:T(8,128)(2,1)} %get-tuple-element.13.high_ref.older_high_ref), channel_id=1, source_target_pairs={{0,1},{1,2},{2,3},{3,4},{4,5},{5,6},{6,7},{7,8},{8,9},{9,10},{10,1... | collective-permute-start | bytes 2359304 | tf_op jit(solution)/shard_map/ppermute | solution.py:220
  35.0 1.3 collective-permute-start.3
  36.3 0.8 collective-permute-done.2.below_ref
  37.1 4.3 %collective-permute-done.3.above_ref = bf16[3,8,64,256]{3,2,1,0:T(8,128)(2,1)S(1)} collective-permute-done((bf16[3,8,64,256]{3,2,1,0:T(8,128)(2,1)}, bf16[3,8,64,256]{3,2,1,0:T(8,128)(2,1)S(1)}, u32[]{:S(2)}, u32[]{:S(2)}) %collective-permute-start.3) | collective-permute-done | bytes 786464 | tf_op jit(solution)/shard_map/ppermute | solution.py:221
  41.4 0.9 copy-done.5
  42.2 6.8 %shard_map.38 = (bf16[3,8,64,256]{3,2,1,0:T(8,128)(2,1)}, bf16[3,8,64,256]{3,2,1,0:T(8,128)(2,1)}) custom-call(f32[2]{0:T(128)} %add_convert_fusion.rim_ref, bf16[3,8,64,256]{3,2,1,0:T(8,128)(2,1)} %copy-done.4, bf16[3,8,64,256]{3,2,1,0:T(8,128)(2,1)} %get-tuple-element.14.low_ref.older_low_ref, ...), custom_call_target="tpu_custom_call" | custom-call | tf_op jit(solution)/shard_map/pallas_call | solution.py:133
  49.0 16.6 %collective-permute-start.4 = (bf16[3,8,64,256]{3,2,1,0:T(8,128)(2,1)}, bf16[3,8,64,256]{3,2,1,0:T(8,128)(2,1)S(1)}, u32[]{:S(2)}, u32[]{:S(2)}) collective-permute-start(bf16[3,8,64,256]{3,2,1,0:T(8,128)(2,1)} %get-tuple-element.15.high_ref.older_high_ref), channel_id=1, source_target_pairs={{0,1},{1,2},{2,3},{3,4},{4,5},{5,6},{6,7},{7,8},{8,9},{9,10},{10,1... | collective-permute-start | bytes 2359304 | tf_op jit(solution)/shard_map/ppermute | solution.py:220
  65.6 1.3 collective-permute-start.5
  66.9 0.8 collective-permute-done.4.below_ref
  67.7 4.2 %collective-permute-done.5.above_ref = bf16[3,8,64,256]{3,2,1,0:T(8,128)(2,1)S(1)} collective-permute-done((bf16[3,8,64,256]{3,2,1,0:T(8,128)(2,1)}, bf16[3,8,64,256]{3,2,1,0:T(8,128)(2,1)S(1)}, u32[]{:S(2)}, u32[]{:S(2)}) %collective-permute-start.5) | collective-permute-done | bytes 786464 | tf_op jit(solution)/shard_map/ppermute | solution.py:221
  71.8 0.9 copy-done.9
  72.7 6.8 %shard_map.39 = (bf16[3,8,64,256]{3,2,1,0:T(8,128)(2,1)}, bf16[3,8,64,256]{3,2,1,0:T(8,128)(2,1)}) custom-call(f32[2]{0:T(128)} %add_convert_fusion.rim_ref, bf16[3,8,64,256]{3,2,1,0:T(8,128)(2,1)} %copy-done.7, bf16[3,8,64,256]{3,2,1,0:T(8,128)(2,1)} %get-tuple-element.16.low_ref.older_low_ref, ...), custom_call_target="tpu_custom_call" | custom-call | tf_op jit(solution)/shard_map/pallas_call | solution.py:133
  79.5 16.6 %collective-permute-start.6 = (bf16[3,8,64,256]{3,2,1,0:T(8,128)(2,1)}, bf16[3,8,64,256]{3,2,1,0:T(8,128)(2,1)S(1)}, u32[]{:S(2)}, u32[]{:S(2)}) collective-permute-start(bf16[3,8,64,256]{3,2,1,0:T(8,128)(2,1)} %get-tuple-element.17.high_ref), channel_id=1, source_target_pairs={{0,1},{1,2},{2,3},{3,4},{4,5},{5,6},{6,7},{7,8},{8,9},{9,10},{10,1... | collective-permute-start | bytes 2359304 | tf_op jit(solution)/shard_map/ppermute | solution.py:220
  96.2 1.3 collective-permute-start.7
  97.5 0.8 collective-permute-done.6.below_ref
  98.2 4.2 %collective-permute-done.7.above_ref = bf16[3,8,64,256]{3,2,1,0:T(8,128)(2,1)S(1)} collective-permute-done((bf16[3,8,64,256]{3,2,1,0:T(8,128)(2,1)}, bf16[3,8,64,256]{3,2,1,0:T(8,128)(2,1)S(1)}, u32[]{:S(2)}, u32[]{:S(2)}) %collective-permute-start.7) | collective-permute-done | bytes 786464 | tf_op jit(solution)/shard_map/ppermute | solution.py:221
  102.4 0.9 copy-done.8
  103.3 6.8 %shard_map.40 = (bf16[3,8,64,256]{3,2,1,0:T(8,128)(2,1)}, bf16[3,8,64,256]{3,2,1,0:T(8,128)(2,1)}) custom-call(f32[2]{0:T(128)} %add_convert_fusion.rim_ref, bf16[3,8,64,256]{3,2,1,0:T(8,128)(2,1)} %copy-done.6, bf16[3,8,64,256]{3,2,1,0:T(8,128)(2,1)} %get-tuple-element.18.low_ref, bf16[3,8,64,256]{3,2,1,0:T(8,128)(2,1)} %get-tuple-element.17.high_ref, ...), custom_call_target="tpu_custom_call" | custom-call | tf_op jit(solution)/shard_map/pallas_call | solution.py:133
  110.1 1.5 pad_maximum_fusion
  111.6 0.4 fusion.2
  112.0 1.3 collective-permute-start.12
  113.3 17.2 %collective-permute-start.8 = (f32[128,256]{1,0:T(8,128)S(1)}, f32[128,256]{1,0:T(8,128)S(1)}, u32[]{:S(2)}, u32[]{:S(2)}) collective-permute-start(f32[128,256]{1,0:T(8,128)S(1)} %fusion.2), channel_id=1, source_target_pairs={{0,1},{1,2},{2,3},{3,4},{4,5},{5,6},{6,7},{7,8},{8,9},{9,10},{10,1... | collective-permute-start | bytes 393224 | tf_op jit(solution)/shard_map/ppermute | solution.py:248
  130.5 0.9 collective-permute-done.8
  131.5 7.6 %collective-permute-start.9 = (f32[128,256]{1,0:T(8,128)S(1)}, f32[128,256]{1,0:T(8,128)S(1)}, u32[]{:S(2)}, u32[]{:S(2)}) collective-permute-start(f32[128,256]{1,0:T(8,128)S(1)} %get-tuple-element.23), channel_id=1, source_target_pairs={{0,2},{1,3},{2,4},{3,5},{4,6},{5,7},{6,8},{7,9},{8,10},{9,11},{10,... | collective-permute-start | bytes 393224 | tf_op jit(solution)/shard_map/ppermute | solution.py:248
  144.1 1.3 collective-permute-start.13
  145.5 5.3 %collective-permute-start.10 = (f32[128,256]{1,0:T(8,128)S(1)}, f32[128,256]{1,0:T(8,128)S(1)}, u32[]{:S(2)}, u32[]{:S(2)}) collective-permute-start(f32[128,256]{1,0:T(8,128)S(1)} %multiply_add_fusion.4), channel_id=1, source_target_pairs={{0,4},{1,5},{2,6},{3,7},{4,8},{5,9},{6,10},{7,11},{8,12},{9,13},{1... | collective-permute-start | bytes 393224 | tf_op jit(solution)/shard_map/ppermute | solution.py:248
  150.7 0.2 collective-permute-done.13
  151.0 1.3 collective-permute-start.14
  152.3 1.3 collective-permute-done.10
  153.6 3.6 %collective-permute-start.11 = (f32[128,256]{1,0:T(8,128)S(1)}, f32[128,256]{1,0:T(8,128)S(1)}, u32[]{:S(2)}, u32[]{:S(2)}) collective-permute-start(f32[128,256]{1,0:T(8,128)S(1)} %multiply_add_fusion.3), channel_id=1, source_target_pairs={{0,8},{1,9},{2,10},{3,11},{4,12},{5,13},{6,14},{7,15},{16,24},{17,... | collective-permute-start | bytes 393224 | tf_op jit(solution)/shard_map/ppermute | solution.py:248
  157.3 0.6 collective-permute-done.14
  157.9 1.5 collective-permute-start.15
  161.9 1.2 fusion.10
  163.8 3.0 %collective-permute-done.15 = f32[128,256]{1,0:T(8,128)S(1)} collective-permute-done((f32[128,256]{1,0:T(8,128)S(1)}, f32[128,256]{1,0:T(8,128)S(1)}, u32[]{:S(2)}, u32[]{:S(2)}) %collective-permute-start.15) | collective-permute-done | bytes 131104 | tf_op jit(solution)/shard_map/ppermute | solution.py:249
  166.8 0.6 slice.25.gram_ref
  167.5 15.6 %shard_map.41 = f32[128,128]{1,0:T(8,128)} custom-call(f32[128,128]{1,0:T(8,128)} %slice.25.gram_ref), custom_call_target="tpu_custom_call" | custom-call | tf_op jit(solution)/shard_map/pallas_call | solution.py:60
  183.1 1.3 convolution_convert_fusion.1
  184.4 0.5 fusion
  184.9 0.4 fusion.13
  185.3 1.3 collective-permute-start.20
  186.6 3.0 %collective-permute-start.16 = (f32[128,128]{1,0:T(8,128)S(1)}, f32[128,128]{1,0:T(8,128)S(1)}, u32[]{:S(2)}, u32[]{:S(2)}) collective-permute-start(f32[128,128]{1,0:T(8,128)S(1)} %fusion.13), channel_id=1, source_target_pairs={{0,1},{1,2},{2,3},{3,4},{4,5},{5,6},{6,7},{7,8},{8,9},{9,10},{10,1... | collective-permute-start | bytes 196616 | tf_op jit(solution)/shard_map/ppermute | solution.py:248
  189.7 0.9 collective-permute-done.16
  190.6 5.7 %collective-permute-start.17 = (f32[128,128]{1,0:T(8,128)S(1)}, f32[128,128]{1,0:T(8,128)S(1)}, u32[]{:S(2)}, u32[]{:S(2)}) collective-permute-start(f32[128,128]{1,0:T(8,128)S(1)} %get-tuple-element.25), channel_id=1, source_target_pairs={{0,2},{1,3},{2,4},{3,5},{4,6},{5,7},{6,8},{7,9},{8,10},{9,11},{10,... | collective-permute-start | bytes 196616 | tf_op jit(solution)/shard_map/ppermute | solution.py:248
  196.2 1.3 collective-permute-start.21
  197.5 1.2 collective-permute-done.17
  198.7 4.4 %collective-permute-start.18 = (f32[128,128]{1,0:T(8,128)S(1)}, f32[128,128]{1,0:T(8,128)S(1)}, u32[]{:S(2)}, u32[]{:S(2)}) collective-permute-start(f32[128,128]{1,0:T(8,128)S(1)} %multiply_add_fusion.10), channel_id=1, source_target_pairs={{0,4},{1,5},{2,6},{3,7},{4,8},{5,9},{6,10},{7,11},{8,12},{9,13},{1... | collective-permute-start | bytes 196616 | tf_op jit(solution)/shard_map/ppermute | solution.py:248
  203.2 1.3 collective-permute-start.22
  204.5 0.6 collective-permute-done.18
  205.0 4.4 %collective-permute-start.19 = (f32[128,128]{1,0:T(8,128)S(1)}, f32[128,128]{1,0:T(8,128)S(1)}, u32[]{:S(2)}, u32[]{:S(2)}) collective-permute-start(f32[128,128]{1,0:T(8,128)S(1)} %multiply_add_fusion.9), channel_id=1, source_target_pairs={{0,8},{1,9},{2,10},{3,11},{4,12},{5,13},{6,14},{7,15},{16,24},{17,... | collective-permute-start | bytes 196616 | tf_op jit(solution)/shard_map/ppermute | solution.py:248
  209.5 1.3 collective-permute-start.23
  210.8 0.6 collective-permute-done.19
  211.3 5.9 %collective-permute-done.23 = f32[128,128]{1,0:T(8,128)S(1)} collective-permute-done((f32[128,128]{1,0:T(8,128)S(1)}, f32[128,128]{1,0:T(8,128)S(1)}, u32[]{:S(2)}, u32[]{:S(2)}) %collective-permute-start.23) | collective-permute-done | bytes 65568 | tf_op jit(solution)/shard_map/ppermute | solution.py:249
  217.3 0.7 subtract_divide_fusion.1.gram_ref
  217.9 15.6 %shard_map.42 = f32[128,128]{1,0:T(8,128)} custom-call(f32[128,128]{1,0:T(8,128)} %subtract_divide_fusion.1.gram_ref), custom_call_target="tpu_custom_call" | custom-call | tf_op jit(solution)/shard_map/pallas_call | solution.py:60
  233.5 1.2 convolution_convert_fusion
  234.8 0.1 pad_maximum_fusion.1
  234.9 1.6 copy.5
  (43 shorter events, 0.3 us)
Async XLA Ops:
  0.0 5.9 %copy-start.11 = (s32[16]{0:T(128)S(1)}, s32[16]{0:T(128)}, u32[]{:S(2)}) copy-start(s32[16]{0:T(128)} %param.5) | copy-start | bytes 196
  0.0 9.3 %copy-start.12 = (f32[6,512]{1,0:T(8,128)S(1)}, f32[6,512]{1,0:T(8,128)}, u32[]{:S(2)}) copy-start(f32[6,512]{1,0:T(8,128)} %param.4) | copy-start | bytes 36868
  1.5 10.1 %copy-start = (bf16[3,8,64,256]{3,2,1,0:T(8,128)(2,1)}, bf16[3,8,64,256]{3,2,1,0:T(8,128)(2,1)S(1)}, u32[]{:S(2)}) copy-start(bf16[3,8,64,256]{3,2,1,0:T(8,128)(2,1)S(1)} %get-tuple-element.21.low_ref) | copy-start | bytes 2359300
  1.5 10.1 %copy-start.1 = (bf16[3,8,64,256]{3,2,1,0:T(8,128)(2,1)}, bf16[3,8,64,256]{3,2,1,0:T(8,128)(2,1)S(1)}, u32[]{:S(2)}) copy-start(bf16[3,8,64,256]{3,2,1,0:T(8,128)(2,1)S(1)} %get-tuple-element.22.high_ref) | copy-start | bytes 2359300
  1.5 8.4 %collective-permute-start.1 = (bf16[3,8,64,256]{3,2,1,0:T(8,128)(2,1)S(1)}, bf16[3,8,64,256]{3,2,1,0:T(8,128)(2,1)S(1)}, u32[]{:S(2)}, u32[]{:S(2)}) collective-permute-start(bf16[3,8,64,256]{3,2,1,0:T(8,128)(2,1)S(1)} %get-tuple-element.21.low_ref), channel_id=1, source_target_pairs={{1,0},{2,1},{3,2},{4,3},{5,4},{6,5},{7,6},{8,7},{9,8},{10,9},{11,1... | collective-permute-start | bytes 2359304 | tf_op jit(solution)/shard_map/ppermute | solution.py:221
  2.8 7.1 %collective-permute-start = (bf16[3,8,64,256]{3,2,1,0:T(8,128)(2,1)S(1)}, bf16[3,8,64,256]{3,2,1,0:T(8,128)(2,1)S(1)}, u32[]{:S(2)}, u32[]{:S(2)}) collective-permute-start(bf16[3,8,64,256]{3,2,1,0:T(8,128)(2,1)S(1)} %get-tuple-element.22.high_ref), channel_id=1, source_target_pairs={{0,1},{1,2},{2,3},{3,4},{4,5},{5,6},{6,7},{7,8},{8,9},{9,10},{10,1... | collective-permute-start | bytes 2359304 | tf_op jit(solution)/shard_map/ppermute | solution.py:220
  9.9 1.7 copy-start.2
  9.9 1.7 copy-start.3
  18.2 18.8 %collective-permute-start.2 = (bf16[3,8,64,256]{3,2,1,0:T(8,128)(2,1)}, bf16[3,8,64,256]{3,2,1,0:T(8,128)(2,1)S(1)}, u32[]{:S(2)}, u32[]{:S(2)}) collective-permute-start(bf16[3,8,64,256]{3,2,1,0:T(8,128)(2,1)} %get-tuple-element.13.high_ref.older_high_ref), channel_id=1, source_target_pairs={{0,1},{1,2},{2,3},{3,4},{4,5},{5,6},{6,7},{7,8},{8,9},{9,10},{10,1... | collective-permute-start | bytes 2359304 | tf_op jit(solution)/shard_map/ppermute | solution.py:220
  35.0 6.3 %collective-permute-start.3 = (bf16[3,8,64,256]{3,2,1,0:T(8,128)(2,1)}, bf16[3,8,64,256]{3,2,1,0:T(8,128)(2,1)S(1)}, u32[]{:S(2)}, u32[]{:S(2)}) collective-permute-start(bf16[3,8,64,256]{3,2,1,0:T(8,128)(2,1)} %get-tuple-element.14.low_ref.older_low_ref), channel_id=1, source_target_pairs={{1,0},{2,1},{3,2},{4,3},{5,4},{6,5},{7,6},{8,7},{9,8},{10,9},{11,1... | collective-permute-start | bytes 2359304 | tf_op jit(solution)/shard_map/ppermute | solution.py:221
  37.1 4.3 %copy-start.4 = (bf16[3,8,64,256]{3,2,1,0:T(8,128)(2,1)}, bf16[3,8,64,256]{3,2,1,0:T(8,128)(2,1)S(1)}, u32[]{:S(2)}) copy-start(bf16[3,8,64,256]{3,2,1,0:T(8,128)(2,1)S(1)} %collective-permute-done.2.below_ref) | copy-start | bytes 2359300
  41.3 0.9 copy-start.5
  49.0 18.6 %collective-permute-start.4 = (bf16[3,8,64,256]{3,2,1,0:T(8,128)(2,1)}, bf16[3,8,64,256]{3,2,1,0:T(8,128)(2,1)S(1)}, u32[]{:S(2)}, u32[]{:S(2)}) collective-permute-start(bf16[3,8,64,256]{3,2,1,0:T(8,128)(2,1)} %get-tuple-element.15.high_ref.older_high_ref), channel_id=1, source_target_pairs={{0,1},{1,2},{2,3},{3,4},{4,5},{5,6},{6,7},{7,8},{8,9},{9,10},{10,1... | collective-permute-start | bytes 2359304 | tf_op jit(solution)/shard_map/ppermute | solution.py:220
  65.6 6.2 %collective-permute-start.5 = (bf16[3,8,64,256]{3,2,1,0:T(8,128)(2,1)}, bf16[3,8,64,256]{3,2,1,0:T(8,128)(2,1)S(1)}, u32[]{:S(2)}, u32[]{:S(2)}) collective-permute-start(bf16[3,8,64,256]{3,2,1,0:T(8,128)(2,1)} %get-tuple-element.16.low_ref.older_low_ref), channel_id=1, source_target_pairs={{1,0},{2,1},{3,2},{4,3},{5,4},{6,5},{7,6},{8,7},{9,8},{10,9},{11,1... | collective-permute-start | bytes 2359304 | tf_op jit(solution)/shard_map/ppermute | solution.py:221
  67.7 4.2 %copy-start.7 = (bf16[3,8,64,256]{3,2,1,0:T(8,128)(2,1)}, bf16[3,8,64,256]{3,2,1,0:T(8,128)(2,1)S(1)}, u32[]{:S(2)}) copy-start(bf16[3,8,64,256]{3,2,1,0:T(8,128)(2,1)S(1)} %collective-permute-done.4.below_ref) | copy-start | bytes 2359300
  71.8 0.9 copy-start.9
  79.5 18.7 %collective-permute-start.6 = (bf16[3,8,64,256]{3,2,1,0:T(8,128)(2,1)}, bf16[3,8,64,256]{3,2,1,0:T(8,128)(2,1)S(1)}, u32[]{:S(2)}, u32[]{:S(2)}) collective-permute-start(bf16[3,8,64,256]{3,2,1,0:T(8,128)(2,1)} %get-tuple-element.17.high_ref), channel_id=1, source_target_pairs={{0,1},{1,2},{2,3},{3,4},{4,5},{5,6},{6,7},{7,8},{8,9},{9,10},{10,1... | collective-permute-start | bytes 2359304 | tf_op jit(solution)/shard_map/ppermute | solution.py:220
  96.2 6.2 %collective-permute-start.7 = (bf16[3,8,64,256]{3,2,1,0:T(8,128)(2,1)}, bf16[3,8,64,256]{3,2,1,0:T(8,128)(2,1)S(1)}, u32[]{:S(2)}, u32[]{:S(2)}) collective-permute-start(bf16[3,8,64,256]{3,2,1,0:T(8,128)(2,1)} %get-tuple-element.18.low_ref), channel_id=1, source_target_pairs={{1,0},{2,1},{3,2},{4,3},{5,4},{6,5},{7,6},{8,7},{9,8},{10,9},{11,1... | collective-permute-start | bytes 2359304 | tf_op jit(solution)/shard_map/ppermute | solution.py:221
  98.2 4.2 %copy-start.6 = (bf16[3,8,64,256]{3,2,1,0:T(8,128)(2,1)}, bf16[3,8,64,256]{3,2,1,0:T(8,128)(2,1)S(1)}, u32[]{:S(2)}) copy-start(bf16[3,8,64,256]{3,2,1,0:T(8,128)(2,1)S(1)} %collective-permute-done.6.below_ref) | copy-start | bytes 2359300
  102.4 0.9 copy-start.8
  112.0 18.5 %collective-permute-start.12 = (f32[128,256]{1,0:T(8,128)S(1)}, f32[128,256]{1,0:T(8,128)S(1)}, u32[]{:S(2)}, u32[]{:S(2)}) collective-permute-start(f32[128,256]{1,0:T(8,128)S(1)} %fusion.2), channel_id=1, source_target_pairs={{1,0},{2,1},{3,2},{4,3},{5,4},{6,5},{7,6},{8,7},{9,8},{10,9},{11,1... | collective-permute-start | bytes 393224 | tf_op jit(solution)/shard_map/ppermute | solution.py:249
  113.3 18.1 %collective-permute-start.8 = (f32[128,256]{1,0:T(8,128)S(1)}, f32[128,256]{1,0:T(8,128)S(1)}, u32[]{:S(2)}, u32[]{:S(2)}) collective-permute-start(f32[128,256]{1,0:T(8,128)S(1)} %fusion.2), channel_id=1, source_target_pairs={{0,1},{1,2},{2,3},{3,4},{4,5},{5,6},{6,7},{7,8},{8,9},{9,10},{10,1... | collective-permute-start | bytes 393224 | tf_op jit(solution)/shard_map/ppermute | solution.py:248
  131.5 13.9 %collective-permute-start.9 = (f32[128,256]{1,0:T(8,128)S(1)}, f32[128,256]{1,0:T(8,128)S(1)}, u32[]{:S(2)}, u32[]{:S(2)}) collective-permute-start(f32[128,256]{1,0:T(8,128)S(1)} %get-tuple-element.23), channel_id=1, source_target_pairs={{0,2},{1,3},{2,4},{3,5},{4,6},{5,7},{6,8},{7,9},{8,10},{9,11},{10,... | collective-permute-start | bytes 393224 | tf_op jit(solution)/shard_map/ppermute | solution.py:248
  144.1 6.9 %collective-permute-start.13 = (f32[128,256]{1,0:T(8,128)S(1)}, f32[128,256]{1,0:T(8,128)S(1)}, u32[]{:S(2)}, u32[]{:S(2)}) collective-permute-start(f32[128,256]{1,0:T(8,128)S(1)} %get-tuple-element.24), channel_id=1, source_target_pairs={{2,0},{3,1},{4,2},{5,3},{6,4},{7,5},{8,6},{9,7},{10,8},{11,9},{12,... | collective-permute-start | bytes 393224 | tf_op jit(solution)/shard_map/ppermute | solution.py:249
  145.5 8.2 %collective-permute-start.10 = (f32[128,256]{1,0:T(8,128)S(1)}, f32[128,256]{1,0:T(8,128)S(1)}, u32[]{:S(2)}, u32[]{:S(2)}) collective-permute-start(f32[128,256]{1,0:T(8,128)S(1)} %multiply_add_fusion.4), channel_id=1, source_target_pairs={{0,4},{1,5},{2,6},{3,7},{4,8},{5,9},{6,10},{7,11},{8,12},{9,13},{1... | collective-permute-start | bytes 393224 | tf_op jit(solution)/shard_map/ppermute | solution.py:248
  151.0 6.9 %collective-permute-start.14 = (f32[128,256]{1,0:T(8,128)S(1)}, f32[128,256]{1,0:T(8,128)S(1)}, u32[]{:S(2)}, u32[]{:S(2)}) collective-permute-start(f32[128,256]{1,0:T(8,128)S(1)} %multiply_add_fusion.1), channel_id=1, source_target_pairs={{4,0},{5,1},{6,2},{7,3},{8,4},{9,5},{10,6},{11,7},{12,8},{13,9},{1... | collective-permute-start | bytes 393224 | tf_op jit(solution)/shard_map/ppermute | solution.py:249
  153.6 10.1 %collective-permute-start.11 = (f32[128,256]{1,0:T(8,128)S(1)}, f32[128,256]{1,0:T(8,128)S(1)}, u32[]{:S(2)}, u32[]{:S(2)}) collective-permute-start(f32[128,256]{1,0:T(8,128)S(1)} %multiply_add_fusion.3), channel_id=1, source_target_pairs={{0,8},{1,9},{2,10},{3,11},{4,12},{5,13},{6,14},{7,15},{16,24},{17,... | collective-permute-start | bytes 393224 | tf_op jit(solution)/shard_map/ppermute | solution.py:248
  157.9 8.9 %collective-permute-start.15 = (f32[128,256]{1,0:T(8,128)S(1)}, f32[128,256]{1,0:T(8,128)S(1)}, u32[]{:S(2)}, u32[]{:S(2)}) collective-permute-start(f32[128,256]{1,0:T(8,128)S(1)} %multiply_add_fusion), channel_id=1, source_target_pairs={{8,0},{9,1},{10,2},{11,3},{12,4},{13,5},{14,6},{15,7},{24,16},{25,... | collective-permute-start | bytes 393224 | tf_op jit(solution)/shard_map/ppermute | solution.py:249
  183.1 1.3 copy-start.10
  185.3 4.3 %collective-permute-start.20 = (f32[128,128]{1,0:T(8,128)S(1)}, f32[128,128]{1,0:T(8,128)S(1)}, u32[]{:S(2)}, u32[]{:S(2)}) collective-permute-start(f32[128,128]{1,0:T(8,128)S(1)} %fusion.13), channel_id=1, source_target_pairs={{1,0},{2,1},{3,2},{4,3},{5,4},{6,5},{7,6},{8,7},{9,8},{10,9},{11,1... | collective-permute-start | bytes 196616 | tf_op jit(solution)/shard_map/ppermute | solution.py:249
  186.6 3.9 %collective-permute-start.16 = (f32[128,128]{1,0:T(8,128)S(1)}, f32[128,128]{1,0:T(8,128)S(1)}, u32[]{:S(2)}, u32[]{:S(2)}) collective-permute-start(f32[128,128]{1,0:T(8,128)S(1)} %fusion.13), channel_id=1, source_target_pairs={{0,1},{1,2},{2,3},{3,4},{4,5},{5,6},{6,7},{7,8},{8,9},{9,10},{10,1... | collective-permute-start | bytes 196616 | tf_op jit(solution)/shard_map/ppermute | solution.py:248
  190.6 8.2 %collective-permute-start.17 = (f32[128,128]{1,0:T(8,128)S(1)}, f32[128,128]{1,0:T(8,128)S(1)}, u32[]{:S(2)}, u32[]{:S(2)}) collective-permute-start(f32[128,128]{1,0:T(8,128)S(1)} %get-tuple-element.25), channel_id=1, source_target_pairs={{0,2},{1,3},{2,4},{3,5},{4,6},{5,7},{6,8},{7,9},{8,10},{9,11},{10,... | collective-permute-start | bytes 196616 | tf_op jit(solution)/shard_map/ppermute | solution.py:248
  196.2 6.9 %collective-permute-start.21 = (f32[128,128]{1,0:T(8,128)S(1)}, f32[128,128]{1,0:T(8,128)S(1)}, u32[]{:S(2)}, u32[]{:S(2)}) collective-permute-start(f32[128,128]{1,0:T(8,128)S(1)} %get-tuple-element.26), channel_id=1, source_target_pairs={{2,0},{3,1},{4,2},{5,3},{6,4},{7,5},{8,6},{9,7},{10,8},{11,9},{12,... | collective-permute-start | bytes 196616 | tf_op jit(solution)/shard_map/ppermute | solution.py:249
  198.7 6.3 %collective-permute-start.18 = (f32[128,128]{1,0:T(8,128)S(1)}, f32[128,128]{1,0:T(8,128)S(1)}, u32[]{:S(2)}, u32[]{:S(2)}) collective-permute-start(f32[128,128]{1,0:T(8,128)S(1)} %multiply_add_fusion.10), channel_id=1, source_target_pairs={{0,4},{1,5},{2,6},{3,7},{4,8},{5,9},{6,10},{7,11},{8,12},{9,13},{1... | collective-permute-start | bytes 196616 | tf_op jit(solution)/shard_map/ppermute | solution.py:248
  203.2 6.3 %collective-permute-start.22 = (f32[128,128]{1,0:T(8,128)S(1)}, f32[128,128]{1,0:T(8,128)S(1)}, u32[]{:S(2)}, u32[]{:S(2)}) collective-permute-start(f32[128,128]{1,0:T(8,128)S(1)} %multiply_add_fusion.7), channel_id=1, source_target_pairs={{4,0},{5,1},{6,2},{7,3},{8,4},{9,5},{10,6},{11,7},{12,8},{13,9},{1... | collective-permute-start | bytes 196616 | tf_op jit(solution)/shard_map/ppermute | solution.py:249
  205.0 6.3 %collective-permute-start.19 = (f32[128,128]{1,0:T(8,128)S(1)}, f32[128,128]{1,0:T(8,128)S(1)}, u32[]{:S(2)}, u32[]{:S(2)}) collective-permute-start(f32[128,128]{1,0:T(8,128)S(1)} %multiply_add_fusion.9), channel_id=1, source_target_pairs={{0,8},{1,9},{2,10},{3,11},{4,12},{5,13},{6,14},{7,15},{16,24},{17,... | collective-permute-start | bytes 196616 | tf_op jit(solution)/shard_map/ppermute | solution.py:248
  209.5 7.8 %collective-permute-start.23 = (f32[128,128]{1,0:T(8,128)S(1)}, f32[128,128]{1,0:T(8,128)S(1)}, u32[]{:S(2)}, u32[]{:S(2)}) collective-permute-start(f32[128,128]{1,0:T(8,128)S(1)} %multiply_add_fusion.6), channel_id=1, source_target_pairs={{8,0},{9,1},{10,2},{11,3},{12,4},{13,5},{14,6},{15,7},{24,16},{25,... | collective-permute-start | bytes 196616 | tf_op jit(solution)/shard_map/ppermute | solution.py:249

commit v17 on v16

--- a/solution.py
+++ b/solution.py
@@ -142,8 +142,8 @@
             spec(above, 0),
             spec(older_low, 0),
             spec(older_high, 1),
-            pl.BlockSpec(block, lambda j: (0, 0, 0, 0)),
-            pl.BlockSpec(block, lambda j: (1, 0, 0, 0)),
+            pl.BlockSpec((half, rows_y, rows_x, 1), lambda j: (0, 0, 0, 0)),
+            pl.BlockSpec((half, rows_y, rows_x, 1), lambda j: (1, 0, 0, 0)),
         ],
         out_specs=(
             pl.BlockSpec(block, lambda j: (0, 0, 0, j)),
@@ -221,7 +221,7 @@
         from_above = lax.ppermute(low, "gz", backward)
         return from_below, from_above
 
-    lanes = jnp.broadcast_to(grid[..., None], grid.shape + (128,))
+    lanes = grid[..., None]
     half = planes // 2
     low, high = waves[:half], waves[half:]
     from_below, from_above = rimmed(low, high)

time: 238 us -> 236 us (level)
  starting transfers between devices: 120 us -> 117 us
  local copies, waits for them, and re-layouts: 8.82 us -> 11.4 us
    ppermute x4, starting transfers between devices: 53 us -> 49.7 us  [rimmed(): from_below = lax.ppermute(high, 'gz', forward)]
    another operation x0 -> x1, local copies, waits for them, and re-layouts: none -> 2.6 us  [shards(): lanes = grid[..., None]]
  transfers between devices with their start and end apart: 24 -> 24, of which waited for: 16 -> 16; matrix products, arithmetic and copies ran while one was open for 1% -> 2% of each run, Pallas kernels for 0% -> 0%
where the time goes in v17:
time: 236 us; the launch traced here: 235 us
  starting transfers between devices  117 us (50%)
  Pallas kernels  57.3 us (24%)
  waiting for transfers between devices  30 us (13%)
  local copies, waits for them, and re-layouts  11.4 us (5%)
  between operations  11.3 us (5%)
  other arithmetic  4.29 us (2%)
  matrix products  3.8 us (2%)
    ppermute x8, starting transfers between devices, domain_total(): from_low = lax.ppermute(forward, 'gz', ahead)  51.2 us
    ppermute x4, starting transfers between devices, rimmed(): from_below = lax.ppermute(high, 'gz', forward)  49.7 us
    pallas_call x2, Pallas kernels, lower_inverse(): pl.pallas_call(_lower_inverse_kernel, out_shape=jax.ShapeDtypeStruct((n,...  31.3 us
    pallas_call x4, Pallas kernels, chebyshev_step(): pl.pallas_call(functools.partial(_step_kernel, first), out_shape=(piece,...  26 us
    ppermute x4, waiting for transfers between devices, rimmed(): from_above = lax.ppermute(low, 'gz', backward)  12.6 us
    ppermute x8, starting transfers between devices, domain_total(): from_high = lax.ppermute(backward, 'gz', behind)  10.5 us
    ppermute x8, waiting for transfers between devices, domain_total(): from_high = lax.ppermute(backward, 'gz', behind)  9.75 us
    ppermute x8, waiting for transfers between devices, domain_total(): from_low = lax.ppermute(forward, 'gz', ahead)  5.42 us
  transfers between devices with their start and end apart: 24, of which 16 were waited for; matrix products, arithmetic and copies ran while one was open for 2% of the time, Pallas kernels for 0%

profile of v17, /device:TPU:0, one launch (start us, length us, event | category | flops | bytes accessed | tf_op | source)
XLA Modules:
  0.0 234.6 jit_solution(8491004408608127345)
XLA Ops:
  0.0 1.5 fusion.11
  1.5 1.3 collective-permute-start.1
  2.8 3.1 %collective-permute-start = (bf16[3,8,64,256]{3,2,1,0:T(8,128)(2,1)S(1)}, bf16[3,8,64,256]{3,2,1,0:T(8,128)(2,1)S(1)}, u32[]{:S(2)}, u32[]{:S(2)}) collective-permute-start(bf16[3,8,64,256]{3,2,1,0:T(8,128)(2,1)S(1)} %get-tuple-element.22.high_ref), channel_id=1, source_target_pairs={{0,1},{1,2},{2,3},{3,4},{4,5},{5,6},{6,7},{7,8},{8,9},{9,10},{10,1... | collective-permute-start | bytes 2359304 | tf_op jit(solution)/shard_map/ppermute | solution.py:220
  6.0 0.7 fusion.12
  9.3 2.6 %broadcast_in_dim_reshape.4.low_pot_ref.high_pot_ref = f32[6,8,64,1]{3,2,1,0:T(8,128)} reshape(f32[6,512]{1,0:T(8,128)S(1)} %copy-done.12) | data formatting | bytes 24576 | tf_op jit(solution)/shard_map/broadcast_in_dim;reshape | solution.py:224
  11.9 0.6 add_convert_fusion.rim_ref
  12.5 0.9 copy-done.2
  13.3 0.9 copy-done.3
  14.2 6.3 %shard_map.37 = (bf16[3,8,64,256]{3,2,1,0:T(8,128)(2,1)}, bf16[3,8,64,256]{3,2,1,0:T(8,128)(2,1)}) custom-call(f32[2]{0:T(128)} %add_convert_fusion.rim_ref, bf16[3,8,64,256]{3,2,1,0:T(8,128)(2,1)} %copy-done.3, bf16[3,8,64,256]{3,2,1,0:T(8,128)(2,1)} %copy-done, bf16[3,8,64,256]{3,2,1,0:T(8,128)(2,1)} %copy-done.1, bf16[3,8,64,256]{3,2,1,0:T(8,128)(2,1)} %copy-done.2, ...), custom_call_target="tpu_custom_call" | custom-call | tf_op jit(solution)/shard_map/pallas_call | solution.py:133
  20.5 13.4 %collective-permute-start.2 = (bf16[3,8,64,256]{3,2,1,0:T(8,128)(2,1)}, bf16[3,8,64,256]{3,2,1,0:T(8,128)(2,1)S(1)}, u32[]{:S(2)}, u32[]{:S(2)}) collective-permute-start(bf16[3,8,64,256]{3,2,1,0:T(8,128)(2,1)} %get-tuple-element.13.high_ref.older_high_ref), channel_id=1, source_target_pairs={{0,1},{1,2},{2,3},{3,4},{4,5},{5,6},{6,7},{7,8},{8,9},{9,10},{10,1... | collective-permute-start | bytes 2359304 | tf_op jit(solution)/shard_map/ppermute | solution.py:220
  34.0 1.3 collective-permute-start.3
  35.3 0.8 collective-permute-done.2.below_ref
  36.0 4.3 %collective-permute-done.3.above_ref = bf16[3,8,64,256]{3,2,1,0:T(8,128)(2,1)S(1)} collective-permute-done((bf16[3,8,64,256]{3,2,1,0:T(8,128)(2,1)}, bf16[3,8,64,256]{3,2,1,0:T(8,128)(2,1)S(1)}, u32[]{:S(2)}, u32[]{:S(2)}) %collective-permute-start.3) | collective-permute-done | bytes 786464 | tf_op jit(solution)/shard_map/ppermute | solution.py:221
  40.3 0.9 copy-done.5
  41.2 6.5 %shard_map.38 = (bf16[3,8,64,256]{3,2,1,0:T(8,128)(2,1)}, bf16[3,8,64,256]{3,2,1,0:T(8,128)(2,1)}) custom-call(f32[2]{0:T(128)} %add_convert_fusion.rim_ref, bf16[3,8,64,256]{3,2,1,0:T(8,128)(2,1)} %copy-done.4, bf16[3,8,64,256]{3,2,1,0:T(8,128)(2,1)} %get-tuple-element.14.low_ref.older_low_ref, ...), custom_call_target="tpu_custom_call" | custom-call | tf_op jit(solution)/shard_map/pallas_call | solution.py:133
  47.7 16.6 %collective-permute-start.4 = (bf16[3,8,64,256]{3,2,1,0:T(8,128)(2,1)}, bf16[3,8,64,256]{3,2,1,0:T(8,128)(2,1)S(1)}, u32[]{:S(2)}, u32[]{:S(2)}) collective-permute-start(bf16[3,8,64,256]{3,2,1,0:T(8,128)(2,1)} %get-tuple-element.15.high_ref.older_high_ref), channel_id=1, source_target_pairs={{0,1},{1,2},{2,3},{3,4},{4,5},{5,6},{6,7},{7,8},{8,9},{9,10},{10,1... | collective-permute-start | bytes 2359304 | tf_op jit(solution)/shard_map/ppermute | solution.py:220
  64.3 1.3 collective-permute-start.5
  65.6 0.8 collective-permute-done.4.below_ref
  66.4 4.2 %collective-permute-done.5.above_ref = bf16[3,8,64,256]{3,2,1,0:T(8,128)(2,1)S(1)} collective-permute-done((bf16[3,8,64,256]{3,2,1,0:T(8,128)(2,1)}, bf16[3,8,64,256]{3,2,1,0:T(8,128)(2,1)S(1)}, u32[]{:S(2)}, u32[]{:S(2)}) %collective-permute-start.5) | collective-permute-done | bytes 786464 | tf_op jit(solution)/shard_map/ppermute | solution.py:221
  70.5 0.9 copy-done.9
  71.4 6.6 %shard_map.39 = (bf16[3,8,64,256]{3,2,1,0:T(8,128)(2,1)}, bf16[3,8,64,256]{3,2,1,0:T(8,128)(2,1)}) custom-call(f32[2]{0:T(128)} %add_convert_fusion.rim_ref, bf16[3,8,64,256]{3,2,1,0:T(8,128)(2,1)} %copy-done.7, bf16[3,8,64,256]{3,2,1,0:T(8,128)(2,1)} %get-tuple-element.16.low_ref.older_low_ref, ...), custom_call_target="tpu_custom_call" | custom-call | tf_op jit(solution)/shard_map/pallas_call | solution.py:133
  78.0 16.6 %collective-permute-start.6 = (bf16[3,8,64,256]{3,2,1,0:T(8,128)(2,1)}, bf16[3,8,64,256]{3,2,1,0:T(8,128)(2,1)S(1)}, u32[]{:S(2)}, u32[]{:S(2)}) collective-permute-start(bf16[3,8,64,256]{3,2,1,0:T(8,128)(2,1)} %get-tuple-element.17.high_ref), channel_id=1, source_target_pairs={{0,1},{1,2},{2,3},{3,4},{4,5},{5,6},{6,7},{7,8},{8,9},{9,10},{10,1... | collective-permute-start | bytes 2359304 | tf_op jit(solution)/shard_map/ppermute | solution.py:220
  94.6 1.3 collective-permute-start.7
  95.9 0.8 collective-permute-done.6.below_ref
  96.7 4.2 %collective-permute-done.7.above_ref = bf16[3,8,64,256]{3,2,1,0:T(8,128)(2,1)S(1)} collective-permute-done((bf16[3,8,64,256]{3,2,1,0:T(8,128)(2,1)}, bf16[3,8,64,256]{3,2,1,0:T(8,128)(2,1)S(1)}, u32[]{:S(2)}, u32[]{:S(2)}) %collective-permute-start.7) | collective-permute-done | bytes 786464 | tf_op jit(solution)/shard_map/ppermute | solution.py:221
  100.8 0.9 copy-done.8
  101.7 6.5 %shard_map.40 = (bf16[3,8,64,256]{3,2,1,0:T(8,128)(2,1)}, bf16[3,8,64,256]{3,2,1,0:T(8,128)(2,1)}) custom-call(f32[2]{0:T(128)} %add_convert_fusion.rim_ref, bf16[3,8,64,256]{3,2,1,0:T(8,128)(2,1)} %copy-done.6, bf16[3,8,64,256]{3,2,1,0:T(8,128)(2,1)} %get-tuple-element.18.low_ref, bf16[3,8,64,256]{3,2,1,0:T(8,128)(2,1)} %get-tuple-element.17.high_ref, ...), custom_call_target="tpu_custom_call" | custom-call | tf_op jit(solution)/shard_map/pallas_call | solution.py:133
  108.3 1.5 pad_maximum_fusion
  109.8 0.4 fusion.2
  110.2 1.3 collective-permute-start.12
  111.5 17.2 %collective-permute-start.8 = (f32[128,256]{1,0:T(8,128)S(1)}, f32[128,256]{1,0:T(8,128)S(1)}, u32[]{:S(2)}, u32[]{:S(2)}) collective-permute-start(f32[128,256]{1,0:T(8,128)S(1)} %fusion.2), channel_id=1, source_target_pairs={{0,1},{1,2},{2,3},{3,4},{4,5},{5,6},{6,7},{7,8},{8,9},{9,10},{10,1... | collective-permute-start | bytes 393224 | tf_op jit(solution)/shard_map/ppermute | solution.py:248
  128.7 0.9 collective-permute-done.8
  129.7 7.6 %collective-permute-start.9 = (f32[128,256]{1,0:T(8,128)S(1)}, f32[128,256]{1,0:T(8,128)S(1)}, u32[]{:S(2)}, u32[]{:S(2)}) collective-permute-start(f32[128,256]{1,0:T(8,128)S(1)} %get-tuple-element.23), channel_id=1, source_target_pairs={{0,2},{1,3},{2,4},{3,5},{4,6},{5,7},{6,8},{7,9},{8,10},{9,11},{10,... | collective-permute-start | bytes 393224 | tf_op jit(solution)/shard_map/ppermute | solution.py:248
  142.3 1.3 collective-permute-start.13
  143.6 5.3 %collective-permute-start.10 = (f32[128,256]{1,0:T(8,128)S(1)}, f32[128,256]{1,0:T(8,128)S(1)}, u32[]{:S(2)}, u32[]{:S(2)}) collective-permute-start(f32[128,256]{1,0:T(8,128)S(1)} %multiply_add_fusion.4), channel_id=1, source_target_pairs={{0,4},{1,5},{2,6},{3,7},{4,8},{5,9},{6,10},{7,11},{8,12},{9,13},{1... | collective-permute-start | bytes 393224 | tf_op jit(solution)/shard_map/ppermute | solution.py:248
  149.2 1.3 collective-permute-start.14
  150.5 1.3 collective-permute-done.10
  151.8 3.6 %collective-permute-start.11 = (f32[128,256]{1,0:T(8,128)S(1)}, f32[128,256]{1,0:T(8,128)S(1)}, u32[]{:S(2)}, u32[]{:S(2)}) collective-permute-start(f32[128,256]{1,0:T(8,128)S(1)} %multiply_add_fusion.3), channel_id=1, source_target_pairs={{0,8},{1,9},{2,10},{3,11},{4,12},{5,13},{6,14},{7,15},{16,24},{17,... | collective-permute-start | bytes 393224 | tf_op jit(solution)/shard_map/ppermute | solution.py:248
  155.5 0.6 collective-permute-done.14
  156.1 1.5 collective-permute-start.15
  160.1 1.2 fusion.10
  162.0 3.0 %collective-permute-done.15 = f32[128,256]{1,0:T(8,128)S(1)} collective-permute-done((f32[128,256]{1,0:T(8,128)S(1)}, f32[128,256]{1,0:T(8,128)S(1)}, u32[]{:S(2)}, u32[]{:S(2)}) %collective-permute-start.15) | collective-permute-done | bytes 131104 | tf_op jit(solution)/shard_map/ppermute | solution.py:249
  165.0 0.6 slice.25.gram_ref
  165.7 15.6 %shard_map.41 = f32[128,128]{1,0:T(8,128)} custom-call(f32[128,128]{1,0:T(8,128)} %slice.25.gram_ref), custom_call_target="tpu_custom_call" | custom-call | tf_op jit(solution)/shard_map/pallas_call | solution.py:60
  181.3 1.3 convolution_convert_fusion.1
  182.6 0.5 fusion
  183.1 0.4 fusion.13
  183.5 1.3 collective-permute-start.20
  184.8 3.0 %collective-permute-start.16 = (f32[128,128]{1,0:T(8,128)S(1)}, f32[128,128]{1,0:T(8,128)S(1)}, u32[]{:S(2)}, u32[]{:S(2)}) collective-permute-start(f32[128,128]{1,0:T(8,128)S(1)} %fusion.13), channel_id=1, source_target_pairs={{0,1},{1,2},{2,3},{3,4},{4,5},{5,6},{6,7},{7,8},{8,9},{9,10},{10,1... | collective-permute-start | bytes 196616 | tf_op jit(solution)/shard_map/ppermute | solution.py:248
  187.9 0.9 collective-permute-done.16
  188.8 5.7 %collective-permute-start.17 = (f32[128,128]{1,0:T(8,128)S(1)}, f32[128,128]{1,0:T(8,128)S(1)}, u32[]{:S(2)}, u32[]{:S(2)}) collective-permute-start(f32[128,128]{1,0:T(8,128)S(1)} %get-tuple-element.25), channel_id=1, source_target_pairs={{0,2},{1,3},{2,4},{3,5},{4,6},{5,7},{6,8},{7,9},{8,10},{9,11},{10,... | collective-permute-start | bytes 196616 | tf_op jit(solution)/shard_map/ppermute | solution.py:248
  194.4 1.3 collective-permute-start.21
  195.7 1.2 collective-permute-done.17
  196.9 4.4 %collective-permute-start.18 = (f32[128,128]{1,0:T(8,128)S(1)}, f32[128,128]{1,0:T(8,128)S(1)}, u32[]{:S(2)}, u32[]{:S(2)}) collective-permute-start(f32[128,128]{1,0:T(8,128)S(1)} %multiply_add_fusion.10), channel_id=1, source_target_pairs={{0,4},{1,5},{2,6},{3,7},{4,8},{5,9},{6,10},{7,11},{8,12},{9,13},{1... | collective-permute-start | bytes 196616 | tf_op jit(solution)/shard_map/ppermute | solution.py:248
  201.4 1.3 collective-permute-start.22
  202.7 0.6 collective-permute-done.18
  203.2 4.4 %collective-permute-start.19 = (f32[128,128]{1,0:T(8,128)S(1)}, f32[128,128]{1,0:T(8,128)S(1)}, u32[]{:S(2)}, u32[]{:S(2)}) collective-permute-start(f32[128,128]{1,0:T(8,128)S(1)} %multiply_add_fusion.9), channel_id=1, source_target_pairs={{0,8},{1,9},{2,10},{3,11},{4,12},{5,13},{6,14},{7,15},{16,24},{17,... | collective-permute-start | bytes 196616 | tf_op jit(solution)/shard_map/ppermute | solution.py:248
  207.7 1.3 collective-permute-start.23
  209.0 0.6 collective-permute-done.19
  209.5 5.9 %collective-permute-done.23 = f32[128,128]{1,0:T(8,128)S(1)} collective-permute-done((f32[128,128]{1,0:T(8,128)S(1)}, f32[128,128]{1,0:T(8,128)S(1)}, u32[]{:S(2)}, u32[]{:S(2)}) %collective-permute-start.23) | collective-permute-done | bytes 65568 | tf_op jit(solution)/shard_map/ppermute | solution.py:249
  215.5 0.7 subtract_divide_fusion.1.gram_ref
  216.1 15.6 %shard_map.42 = f32[128,128]{1,0:T(8,128)} custom-call(f32[128,128]{1,0:T(8,128)} %subtract_divide_fusion.1.gram_ref), custom_call_target="tpu_custom_call" | custom-call | tf_op jit(solution)/shard_map/pallas_call | solution.py:60
  231.7 1.2 convolution_convert_fusion
  233.1 1.6 copy.13
  (42 shorter events, 0.6 us)
Async XLA Ops:
  0.0 5.9 %copy-start.11 = (s32[16]{0:T(128)S(1)}, s32[16]{0:T(128)}, u32[]{:S(2)}) copy-start(s32[16]{0:T(128)} %param.5) | copy-start | bytes 196
  0.0 9.3 %copy-start.12 = (f32[6,512]{1,0:T(8,128)S(1)}, f32[6,512]{1,0:T(8,128)}, u32[]{:S(2)}) copy-start(f32[6,512]{1,0:T(8,128)} %param.4) | copy-start | bytes 36868
  1.5 11.0 %copy-start = (bf16[3,8,64,256]{3,2,1,0:T(8,128)(2,1)}, bf16[3,8,64,256]{3,2,1,0:T(8,128)(2,1)S(1)}, u32[]{:S(2)}) copy-start(bf16[3,8,64,256]{3,2,1,0:T(8,128)(2,1)S(1)} %get-tuple-element.21.low_ref) | copy-start | bytes 2359300
  1.5 11.0 %copy-start.1 = (bf16[3,8,64,256]{3,2,1,0:T(8,128)(2,1)}, bf16[3,8,64,256]{3,2,1,0:T(8,128)(2,1)S(1)}, u32[]{:S(2)}) copy-start(bf16[3,8,64,256]{3,2,1,0:T(8,128)(2,1)S(1)} %get-tuple-element.22.high_ref) | copy-start | bytes 2359300
  1.5 10.9 %collective-permute-start.1 = (bf16[3,8,64,256]{3,2,1,0:T(8,128)(2,1)S(1)}, bf16[3,8,64,256]{3,2,1,0:T(8,128)(2,1)S(1)}, u32[]{:S(2)}, u32[]{:S(2)}) collective-permute-start(bf16[3,8,64,256]{3,2,1,0:T(8,128)(2,1)S(1)} %get-tuple-element.21.low_ref), channel_id=1, source_target_pairs={{1,0},{2,1},{3,2},{4,3},{5,4},{6,5},{7,6},{8,7},{9,8},{10,9},{11,1... | collective-permute-start | bytes 2359304 | tf_op jit(solution)/shard_map/ppermute | solution.py:221
  2.8 9.6 %collective-permute-start = (bf16[3,8,64,256]{3,2,1,0:T(8,128)(2,1)S(1)}, bf16[3,8,64,256]{3,2,1,0:T(8,128)(2,1)S(1)}, u32[]{:S(2)}, u32[]{:S(2)}) collective-permute-start(bf16[3,8,64,256]{3,2,1,0:T(8,128)(2,1)S(1)} %get-tuple-element.22.high_ref), channel_id=1, source_target_pairs={{0,1},{1,2},{2,3},{3,4},{4,5},{5,6},{6,7},{7,8},{8,9},{9,10},{10,1... | collective-permute-start | bytes 2359304 | tf_op jit(solution)/shard_map/ppermute | solution.py:220
  12.5 0.9 copy-start.2
  13.3 0.9 copy-start.3
  20.5 15.5 %collective-permute-start.2 = (bf16[3,8,64,256]{3,2,1,0:T(8,128)(2,1)}, bf16[3,8,64,256]{3,2,1,0:T(8,128)(2,1)S(1)}, u32[]{:S(2)}, u32[]{:S(2)}) collective-permute-start(bf16[3,8,64,256]{3,2,1,0:T(8,128)(2,1)} %get-tuple-element.13.high_ref.older_high_ref), channel_id=1, source_target_pairs={{0,1},{1,2},{2,3},{3,4},{4,5},{5,6},{6,7},{7,8},{8,9},{9,10},{10,1... | collective-permute-start | bytes 2359304 | tf_op jit(solution)/shard_map/ppermute | solution.py:220
  34.0 6.3 %collective-permute-start.3 = (bf16[3,8,64,256]{3,2,1,0:T(8,128)(2,1)}, bf16[3,8,64,256]{3,2,1,0:T(8,128)(2,1)S(1)}, u32[]{:S(2)}, u32[]{:S(2)}) collective-permute-start(bf16[3,8,64,256]{3,2,1,0:T(8,128)(2,1)} %get-tuple-element.14.low_ref.older_low_ref), channel_id=1, source_target_pairs={{1,0},{2,1},{3,2},{4,3},{5,4},{6,5},{7,6},{8,7},{9,8},{10,9},{11,1... | collective-permute-start | bytes 2359304 | tf_op jit(solution)/shard_map/ppermute | solution.py:221
  36.0 4.3 %copy-start.4 = (bf16[3,8,64,256]{3,2,1,0:T(8,128)(2,1)}, bf16[3,8,64,256]{3,2,1,0:T(8,128)(2,1)S(1)}, u32[]{:S(2)}) copy-start(bf16[3,8,64,256]{3,2,1,0:T(8,128)(2,1)S(1)} %collective-permute-done.2.below_ref) | copy-start | bytes 2359300
  40.3 0.9 copy-start.5
  47.7 18.6 %collective-permute-start.4 = (bf16[3,8,64,256]{3,2,1,0:T(8,128)(2,1)}, bf16[3,8,64,256]{3,2,1,0:T(8,128)(2,1)S(1)}, u32[]{:S(2)}, u32[]{:S(2)}) collective-permute-start(bf16[3,8,64,256]{3,2,1,0:T(8,128)(2,1)} %get-tuple-element.15.high_ref.older_high_ref), channel_id=1, source_target_pairs={{0,1},{1,2},{2,3},{3,4},{4,5},{5,6},{6,7},{7,8},{8,9},{9,10},{10,1... | collective-permute-start | bytes 2359304 | tf_op jit(solution)/shard_map/ppermute | solution.py:220
  64.3 6.2 %collective-permute-start.5 = (bf16[3,8,64,256]{3,2,1,0:T(8,128)(2,1)}, bf16[3,8,64,256]{3,2,1,0:T(8,128)(2,1)S(1)}, u32[]{:S(2)}, u32[]{:S(2)}) collective-permute-start(bf16[3,8,64,256]{3,2,1,0:T(8,128)(2,1)} %get-tuple-element.16.low_ref.older_low_ref), channel_id=1, source_target_pairs={{1,0},{2,1},{3,2},{4,3},{5,4},{6,5},{7,6},{8,7},{9,8},{10,9},{11,1... | collective-permute-start | bytes 2359304 | tf_op jit(solution)/shard_map/ppermute | solution.py:221
  66.4 4.2 %copy-start.7 = (bf16[3,8,64,256]{3,2,1,0:T(8,128)(2,1)}, bf16[3,8,64,256]{3,2,1,0:T(8,128)(2,1)S(1)}, u32[]{:S(2)}) copy-start(bf16[3,8,64,256]{3,2,1,0:T(8,128)(2,1)S(1)} %collective-permute-done.4.below_ref) | copy-start | bytes 2359300
  70.5 0.9 copy-start.9
  78.0 18.7 %collective-permute-start.6 = (bf16[3,8,64,256]{3,2,1,0:T(8,128)(2,1)}, bf16[3,8,64,256]{3,2,1,0:T(8,128)(2,1)S(1)}, u32[]{:S(2)}, u32[]{:S(2)}) collective-permute-start(bf16[3,8,64,256]{3,2,1,0:T(8,128)(2,1)} %get-tuple-element.17.high_ref), channel_id=1, source_target_pairs={{0,1},{1,2},{2,3},{3,4},{4,5},{5,6},{6,7},{7,8},{8,9},{9,10},{10,1... | collective-permute-start | bytes 2359304 | tf_op jit(solution)/shard_map/ppermute | solution.py:220
  94.6 6.2 %collective-permute-start.7 = (bf16[3,8,64,256]{3,2,1,0:T(8,128)(2,1)}, bf16[3,8,64,256]{3,2,1,0:T(8,128)(2,1)S(1)}, u32[]{:S(2)}, u32[]{:S(2)}) collective-permute-start(bf16[3,8,64,256]{3,2,1,0:T(8,128)(2,1)} %get-tuple-element.18.low_ref), channel_id=1, source_target_pairs={{1,0},{2,1},{3,2},{4,3},{5,4},{6,5},{7,6},{8,7},{9,8},{10,9},{11,1... | collective-permute-start | bytes 2359304 | tf_op jit(solution)/shard_map/ppermute | solution.py:221
  96.7 4.2 %copy-start.6 = (bf16[3,8,64,256]{3,2,1,0:T(8,128)(2,1)}, bf16[3,8,64,256]{3,2,1,0:T(8,128)(2,1)S(1)}, u32[]{:S(2)}) copy-start(bf16[3,8,64,256]{3,2,1,0:T(8,128)(2,1)S(1)} %collective-permute-done.6.below_ref) | copy-start | bytes 2359300
  100.8 0.9 copy-start.8
  110.2 18.5 %collective-permute-start.12 = (f32[128,256]{1,0:T(8,128)S(1)}, f32[128,256]{1,0:T(8,128)S(1)}, u32[]{:S(2)}, u32[]{:S(2)}) collective-permute-start(f32[128,256]{1,0:T(8,128)S(1)} %fusion.2), channel_id=1, source_target_pairs={{1,0},{2,1},{3,2},{4,3},{5,4},{6,5},{7,6},{8,7},{9,8},{10,9},{11,1... | collective-permute-start | bytes 393224 | tf_op jit(solution)/shard_map/ppermute | solution.py:249
  111.5 18.2 %collective-permute-start.8 = (f32[128,256]{1,0:T(8,128)S(1)}, f32[128,256]{1,0:T(8,128)S(1)}, u32[]{:S(2)}, u32[]{:S(2)}) collective-permute-start(f32[128,256]{1,0:T(8,128)S(1)} %fusion.2), channel_id=1, source_target_pairs={{0,1},{1,2},{2,3},{3,4},{4,5},{5,6},{6,7},{7,8},{8,9},{9,10},{10,1... | collective-permute-start | bytes 393224 | tf_op jit(solution)/shard_map/ppermute | solution.py:248
  129.7 13.9 %collective-permute-start.9 = (f32[128,256]{1,0:T(8,128)S(1)}, f32[128,256]{1,0:T(8,128)S(1)}, u32[]{:S(2)}, u32[]{:S(2)}) collective-permute-start(f32[128,256]{1,0:T(8,128)S(1)} %get-tuple-element.23), channel_id=1, source_target_pairs={{0,2},{1,3},{2,4},{3,5},{4,6},{5,7},{6,8},{7,9},{8,10},{9,11},{10,... | collective-permute-start | bytes 393224 | tf_op jit(solution)/shard_map/ppermute | solution.py:248
  142.3 6.9 %collective-permute-start.13 = (f32[128,256]{1,0:T(8,128)S(1)}, f32[128,256]{1,0:T(8,128)S(1)}, u32[]{:S(2)}, u32[]{:S(2)}) collective-permute-start(f32[128,256]{1,0:T(8,128)S(1)} %get-tuple-element.24), channel_id=1, source_target_pairs={{2,0},{3,1},{4,2},{5,3},{6,4},{7,5},{8,6},{9,7},{10,8},{11,9},{12,... | collective-permute-start | bytes 393224 | tf_op jit(solution)/shard_map/ppermute | solution.py:249
  143.6 8.2 %collective-permute-start.10 = (f32[128,256]{1,0:T(8,128)S(1)}, f32[128,256]{1,0:T(8,128)S(1)}, u32[]{:S(2)}, u32[]{:S(2)}) collective-permute-start(f32[128,256]{1,0:T(8,128)S(1)} %multiply_add_fusion.4), channel_id=1, source_target_pairs={{0,4},{1,5},{2,6},{3,7},{4,8},{5,9},{6,10},{7,11},{8,12},{9,13},{1... | collective-permute-start | bytes 393224 | tf_op jit(solution)/shard_map/ppermute | solution.py:248
  149.2 6.9 %collective-permute-start.14 = (f32[128,256]{1,0:T(8,128)S(1)}, f32[128,256]{1,0:T(8,128)S(1)}, u32[]{:S(2)}, u32[]{:S(2)}) collective-permute-start(f32[128,256]{1,0:T(8,128)S(1)} %multiply_add_fusion.1), channel_id=1, source_target_pairs={{4,0},{5,1},{6,2},{7,3},{8,4},{9,5},{10,6},{11,7},{12,8},{13,9},{1... | collective-permute-start | bytes 393224 | tf_op jit(solution)/shard_map/ppermute | solution.py:249
  151.8 10.1 %collective-permute-start.11 = (f32[128,256]{1,0:T(8,128)S(1)}, f32[128,256]{1,0:T(8,128)S(1)}, u32[]{:S(2)}, u32[]{:S(2)}) collective-permute-start(f32[128,256]{1,0:T(8,128)S(1)} %multiply_add_fusion.3), channel_id=1, source_target_pairs={{0,8},{1,9},{2,10},{3,11},{4,12},{5,13},{6,14},{7,15},{16,24},{17,... | collective-permute-start | bytes 393224 | tf_op jit(solution)/shard_map/ppermute | solution.py:248
  156.1 8.9 %collective-permute-start.15 = (f32[128,256]{1,0:T(8,128)S(1)}, f32[128,256]{1,0:T(8,128)S(1)}, u32[]{:S(2)}, u32[]{:S(2)}) collective-permute-start(f32[128,256]{1,0:T(8,128)S(1)} %multiply_add_fusion), channel_id=1, source_target_pairs={{8,0},{9,1},{10,2},{11,3},{12,4},{13,5},{14,6},{15,7},{24,16},{25,... | collective-permute-start | bytes 393224 | tf_op jit(solution)/shard_map/ppermute | solution.py:249
  181.3 1.3 copy-start.10
  183.5 4.3 %collective-permute-start.20 = (f32[128,128]{1,0:T(8,128)S(1)}, f32[128,128]{1,0:T(8,128)S(1)}, u32[]{:S(2)}, u32[]{:S(2)}) collective-permute-start(f32[128,128]{1,0:T(8,128)S(1)} %fusion.13), channel_id=1, source_target_pairs={{1,0},{2,1},{3,2},{4,3},{5,4},{6,5},{7,6},{8,7},{9,8},{10,9},{11,1... | collective-permute-start | bytes 196616 | tf_op jit(solution)/shard_map/ppermute | solution.py:249
  184.8 3.9 %collective-permute-start.16 = (f32[128,128]{1,0:T(8,128)S(1)}, f32[128,128]{1,0:T(8,128)S(1)}, u32[]{:S(2)}, u32[]{:S(2)}) collective-permute-start(f32[128,128]{1,0:T(8,128)S(1)} %fusion.13), channel_id=1, source_target_pairs={{0,1},{1,2},{2,3},{3,4},{4,5},{5,6},{6,7},{7,8},{8,9},{9,10},{10,1... | collective-permute-start | bytes 196616 | tf_op jit(solution)/shard_map/ppermute | solution.py:248
  188.8 8.2 %collective-permute-start.17 = (f32[128,128]{1,0:T(8,128)S(1)}, f32[128,128]{1,0:T(8,128)S(1)}, u32[]{:S(2)}, u32[]{:S(2)}) collective-permute-start(f32[128,128]{1,0:T(8,128)S(1)} %get-tuple-element.25), channel_id=1, source_target_pairs={{0,2},{1,3},{2,4},{3,5},{4,6},{5,7},{6,8},{7,9},{8,10},{9,11},{10,... | collective-permute-start | bytes 196616 | tf_op jit(solution)/shard_map/ppermute | solution.py:248
  194.4 6.9 %collective-permute-start.21 = (f32[128,128]{1,0:T(8,128)S(1)}, f32[128,128]{1,0:T(8,128)S(1)}, u32[]{:S(2)}, u32[]{:S(2)}) collective-permute-start(f32[128,128]{1,0:T(8,128)S(1)} %get-tuple-element.26), channel_id=1, source_target_pairs={{2,0},{3,1},{4,2},{5,3},{6,4},{7,5},{8,6},{9,7},{10,8},{11,9},{12,... | collective-permute-start | bytes 196616 | tf_op jit(solution)/shard_map/ppermute | solution.py:249
  196.9 6.3 %collective-permute-start.18 = (f32[128,128]{1,0:T(8,128)S(1)}, f32[128,128]{1,0:T(8,128)S(1)}, u32[]{:S(2)}, u32[]{:S(2)}) collective-permute-start(f32[128,128]{1,0:T(8,128)S(1)} %multiply_add_fusion.10), channel_id=1, source_target_pairs={{0,4},{1,5},{2,6},{3,7},{4,8},{5,9},{6,10},{7,11},{8,12},{9,13},{1... | collective-permute-start | bytes 196616 | tf_op jit(solution)/shard_map/ppermute | solution.py:248
  201.4 6.3 %collective-permute-start.22 = (f32[128,128]{1,0:T(8,128)S(1)}, f32[128,128]{1,0:T(8,128)S(1)}, u32[]{:S(2)}, u32[]{:S(2)}) collective-permute-start(f32[128,128]{1,0:T(8,128)S(1)} %multiply_add_fusion.7), channel_id=1, source_target_pairs={{4,0},{5,1},{6,2},{7,3},{8,4},{9,5},{10,6},{11,7},{12,8},{13,9},{1... | collective-permute-start | bytes 196616 | tf_op jit(solution)/shard_map/ppermute | solution.py:249
  203.2 6.3 %collective-permute-start.19 = (f32[128,128]{1,0:T(8,128)S(1)}, f32[128,128]{1,0:T(8,128)S(1)}, u32[]{:S(2)}, u32[]{:S(2)}) collective-permute-start(f32[128,128]{1,0:T(8,128)S(1)} %multiply_add_fusion.9), channel_id=1, source_target_pairs={{0,8},{1,9},{2,10},{3,11},{4,12},{5,13},{6,14},{7,15},{16,24},{17,... | collective-permute-start | bytes 196616 | tf_op jit(solution)/shard_map/ppermute | solution.py:248
  207.7 7.8 %collective-permute-start.23 = (f32[128,128]{1,0:T(8,128)S(1)}, f32[128,128]{1,0:T(8,128)S(1)}, u32[]{:S(2)}, u32[]{:S(2)}) collective-permute-start(f32[128,128]{1,0:T(8,128)S(1)} %multiply_add_fusion.6), channel_id=1, source_target_pairs={{8,0},{9,1},{10,2},{11,3},{12,4},{13,5},{14,6},{15,7},{24,16},{25,... | collective-permute-start | bytes 196616 | tf_op jit(solution)/shard_map/ppermute | solution.py:249
